TPU v7x, 32 devices: a whole 2x2x4 slice. The times are simulated.
32 devices in a mesh: seq: 8 (over y, x, core), panel: 4 (over z).
Axes of the slice: x: 2, y: 2, z: 4, core: 2. Of those that a mesh axis runs over, the one named last changes fastest.
Arguments:
- tokens: bfloat16 [2048, 1024], P('seq', 'panel'), may hold values from -6 to 6
- cotangent: bfloat16 [2048, 1024], P('seq', 'panel'), may hold values from -6 to 6
- in_weight: bfloat16 [3, 1024, 1024], P(None, None, 'panel'), may hold values from -0.1875 to 0.1875
- short_kernel: float32 [3, 3, 1024], P(None, None, 'panel'), may hold values from -1 to 1
- skip_gain: float32 [1024], P('panel'), may hold values from 0.5 to 1.5
- long_filter: float32 [2048, 1024], P('seq', 'panel'), may hold values from -1.25 to 1.25
- out_weight: bfloat16 [1024, 1024], P('panel'), may hold values from -0.1875 to 0.1875
Outputs:
- block_out: bfloat16 [2048, 1024], P('seq', 'panel')
- token_grad: bfloat16 [2048, 1024], P('seq', 'panel')
All inputs are finite; a program needn't handle non-finite values.
Results may differ from a plain program's by a relative error of at most 0.007.
Values may be sent and summed in bfloat16 or wider, within the bound.
No kernel may reach another device: no remote copies, remote signals or barrier semaphores. Data moves between devices by JAX's collectives and lax.ppermute only.
A program may use at most 64 MiB of HBM per device.

v0:
```python
import math

import jax
import jax.numpy as jnp
from jax import lax
from jax.sharding import PartitionSpec as P

HIGHEST = lax.Precision.HIGHEST


def shifted(value, axis, steps):
    count = lax.axis_size(axis)
    initial, last = (max(0, -steps), min(count, count - steps))
    return lax.ppermute(value, axis, [(source, source + steps) for source in range(initial, last)])


def dft_tables(size_count):
    counter = jnp.arange(size_count, dtype=jnp.int32)
    product_mod = counter[:, None] * counter[None, :] % size_count
    phase_angle = -2.0 * math.pi / size_count * product_mod.astype(jnp.float32)
    return (jnp.cos(phase_angle), jnp.sin(phase_angle))


def apply_dft(real_part, imag_part, einsum_form, inverse, table_size=0):
    cos_table, sin_table = dft_tables(table_size)
    cos_real = jnp.einsum(einsum_form, cos_table, real_part, precision=HIGHEST)
    sin_real = jnp.einsum(einsum_form, sin_table, real_part, precision=HIGHEST)
    cos_imag = jnp.einsum(einsum_form, cos_table, imag_part, precision=HIGHEST)
    sin_imag = jnp.einsum(einsum_form, sin_table, imag_part, precision=HIGHEST)
    if inverse:
        return (cos_real + sin_imag, cos_imag - sin_real)
    return (cos_real - sin_imag, cos_imag + sin_real)


def rotate(real_part, imag_part, phase_angle):
    cos_part = jnp.cos(phase_angle)
    sin_part = jnp.sin(phase_angle)
    return (
        real_part * cos_part - imag_part * sin_part,
        real_part * sin_part + imag_part * cos_part,
    )


def multiply(left_spec, right_spec, mirror):
    left_real, left_imag = left_spec
    right_real, right_imag = right_spec
    if mirror:
        right_imag = -right_imag
    return (
        left_real * right_real - left_imag * right_imag,
        left_real * right_imag + left_imag * right_real,
    )


def whole_phases(shard_count, row_count):
    length = shard_count * row_count
    half_angle = -math.pi / length * jnp.arange(length, dtype=jnp.int32).astype(jnp.float32)
    twiddle = (
        jnp.arange(shard_count, dtype=jnp.int32)[:, None]
        * jnp.arange(row_count, dtype=jnp.int32)[None, :]
        % length
    )
    return (half_angle, -2.0 * math.pi / length * twiddle.astype(jnp.float32))


def whole_transform(signal):
    row_count = signal.shape[0]
    shard_count = lax.axis_size("seq")
    columns = lax.all_to_all(signal.T, "seq", split_axis=0, concat_axis=1, tiled=True)
    chan_count, length = columns.shape
    half_angle, twiddle_angle = whole_phases(shard_count, row_count)
    real_part = jnp.stack([columns, columns * jnp.cos(half_angle)[None, :]]).reshape(
        2, chan_count, shard_count, row_count
    )
    imag_part = jnp.stack(
        [jnp.zeros_like(columns), columns * jnp.sin(half_angle)[None, :]]
    ).reshape(2, chan_count, shard_count, row_count)
    real_part, imag_part = apply_dft(real_part, imag_part, "kp,ecpm->eckm", False, shard_count)
    real_part, imag_part = rotate(real_part, imag_part, twiddle_angle)
    return apply_dft(real_part, imag_part, "km,ecpm->ecpk", False, row_count)


def whole_untransform(spectrum):
    real_part, imag_part = spectrum
    chan_count, shard_count, row_count = (
        real_part.shape[1],
        real_part.shape[2],
        real_part.shape[3],
    )
    length = shard_count * row_count
    half_angle, twiddle_angle = whole_phases(shard_count, row_count)
    real_part, imag_part = apply_dft(real_part, imag_part, "km,ecpm->ecpk", True, row_count)
    real_part, imag_part = rotate(real_part, imag_part, -twiddle_angle)
    real_part, imag_part = apply_dft(real_part, imag_part, "kp,ecpm->eckm", True, shard_count)
    real_part = real_part.reshape(2, chan_count, length)
    imag_part = imag_part.reshape(2, chan_count, length)
    odd_term = (
        real_part[1] * jnp.cos(half_angle)[None, :] + imag_part[1] * jnp.sin(half_angle)[None, :]
    )
    columns = (real_part[0] + odd_term) * (0.5 / length)
    return lax.all_to_all(columns, "seq", split_axis=1, concat_axis=0, tiled=True).T


def local(tokens, cotangent, in_weight, short_kernel, skip_gain, long_filter, out_weight):
    row_count = tokens.shape[0]
    tap_count = short_kernel.shape[0]
    forward_fn, inverse_fn = (whole_transform, whole_untransform)
    full_tok, full_cot = (
        lax.all_gather(tokens, "panel", axis=1, tiled=True),
        lax.all_gather(cotangent, "panel", axis=1, tiled=True),
    )
    projected = jnp.einsum(
        "td,jdc->jtc", full_tok, in_weight, preferred_element_type=jnp.float32
    ).astype(jnp.bfloat16)
    before = shifted(projected[:, row_count - (tap_count - 1) :, :], "seq", 1)
    extended = jnp.concatenate([before, projected], axis=1).astype(jnp.float32)
    filtered = short_kernel[0][:, None, :] * extended[:, tap_count - 1 :, :]
    for tap_index in range(1, tap_count):
        filtered = (
            filtered
            + short_kernel[tap_index][:, None, :]
            * extended[:, tap_count - 1 - tap_index : tap_count - 1 - tap_index + row_count, :]
        )
    gate_out, gate_in, value_path = (filtered[0], filtered[1], filtered[2])
    signal = value_path * gate_in
    filt_spec = forward_fn(long_filter)
    conv_state = (
        inverse_fn(multiply(forward_fn(signal), filt_spec, False)) + skip_gain[None, :] * signal
    )
    gated_state = (conv_state * gate_out).astype(jnp.bfloat16)
    partial_value = jnp.dot(gated_state, out_weight, preferred_element_type=jnp.float32)
    block_out = lax.psum_scatter(partial_value, "panel", scatter_dimension=1, tiled=True).astype(
        jnp.bfloat16
    )
    grad_gated = lax.dot_general(
        full_cot, out_weight, (((1,), (1,)), ((), ())), preferred_element_type=jnp.float32
    )
    grad_gate_out = grad_gated * conv_state
    grad_state = grad_gated * gate_out
    grad_signal = (
        inverse_fn(multiply(forward_fn(grad_state), filt_spec, True))
        + skip_gain[None, :] * grad_state
    )
    grad_value = grad_signal * gate_in
    grad_gate_in = grad_signal * value_path
    upstream = jnp.stack([grad_gate_out, grad_gate_in, grad_value])
    after_rim = shifted(upstream[:, : tap_count - 1, :], "seq", -1)
    widened = jnp.concatenate([upstream, after_rim], axis=1)
    grad_projected = short_kernel[0][:, None, :] * widened[:, :row_count, :]
    for tap_index in range(1, tap_count):
        grad_projected = (
            grad_projected
            + short_kernel[tap_index][:, None, :] * widened[:, tap_index : tap_index + row_count, :]
        )
    grad_projected = grad_projected.astype(jnp.bfloat16)
    grad_partial = jnp.einsum(
        "jtc,jdc->td", grad_projected, in_weight, preferred_element_type=jnp.float32
    )
    token_grad = lax.psum_scatter(grad_partial, "panel", scatter_dimension=1, tiled=True).astype(
        jnp.bfloat16
    )
    return (block_out, token_grad)


def solution(mesh):
    placed = (
        P("seq", "panel"),
        P("seq", "panel"),
        P(None, None, "panel"),
        P(None, None, "panel"),
        P("panel"),
        P("seq", "panel"),
        P("panel", None),
    )
    return jax.shard_map(
        local,
        mesh=mesh,
        in_specs=placed,
        out_specs=(P("seq", "panel"), P("seq", "panel")),
        check_vma=False,
    )
```

profile of v0, /device:TPU:0, one launch (start us, length us, event | category | flops | bytes accessed | tf_op | source)
XLA Modules:
  0.0 200.1 jit_solution(18421160317685976978)
XLA Ops:
  7.2 17.7 %all_gather.6 = bf16[256,1024]{1,0:T(8,128)(2,1)S(1)} all-gather(bf16[256,256]{1,0:T(8,128)(2,1)} %param.7), channel_id=1, replica_groups=mesh['seq'=8,'panel'=4] {'panel'}, dimensions={1}, use_global_device_ids=true | all-gather | bytes 655360 | tf_op jit(solution)/shard_map/all_gather | solution.py:109
  25.5 1.3 collective-permute-start
  26.8 0.8 copy.25
  27.7 4.6 %all-to-all-start.1 = ((f32[8,32,256]{2,1,0:T(8,128)}), f32[8,32,256]{2,1,0:T(8,128)S(1)}, u32[]{:S(2)}, u32[]{:S(2)}) async-start(f32[8,32,256]{2,1,0:T(8,128)} %bitcast.25), calls=%async_computation.1 | async-start | bytes 524288 | tf_op jit(solution)/shard_map/all_to_all | solution.py:69
  32.3 17.6 %all_gather.7 = bf16[256,1024]{1,0:T(8,128)(2,1)S(1)} all-gather(bf16[256,256]{1,0:T(8,128)(2,1)S(1)} %copy-done.8), channel_id=1, replica_groups=mesh['seq'=8,'panel'=4] {'panel'}, dimensions={1}, use_global_device_ids=true | all-gather | bytes 655360 | tf_op jit(solution)/shard_map/all_gather | solution.py:110
  50.6 0.8 copy.23
  51.5 3.4 %all-to-all-start = ((f32[8,32,256]{2,1,0:T(8,128)}), f32[8,32,256]{2,1,0:T(8,128)S(1)}, u32[]{:S(2)}, u32[]{:S(2)}) async-start(f32[8,32,256]{2,1,0:T(8,128)} %bitcast.8), calls=%async_computation | async-start | bytes 524288 | tf_op jit(solution)/shard_map/all_to_all | solution.py:69
  55.0 0.9 copy.29
  55.9 5.9 %all-to-all-done = f32[8,32,256]{2,1,0:T(8,128)S(1)} async-done(((f32[8,32,256]{2,1,0:T(8,128)}), f32[8,32,256]{2,1,0:T(8,128)S(1)}, u32[]{:S(2)}, u32[]{:S(2)}) %all-to-all-start) | async-done | bytes 262176 | tf_op jit(solution)/shard_map/all_to_all | solution.py:69
  61.7 4.1 %all-to-all-start.3 = ((f32[8,32,256]{2,1,0:T(8,128)}), f32[8,32,256]{2,1,0:T(8,128)}, u32[]{:S(2)}, u32[]{:S(2)}) async-start(f32[8,32,256]{2,1,0:T(8,128)} %bitcast.44), calls=%async_computation.4 | async-start | bytes 524288 | tf_op jit(solution)/shard_map/all_to_all | solution.py:69
  67.4 1.1 copy.54
  69.3 3.4 %all-to-all-done.3 = f32[8,32,256]{2,1,0:T(8,128)} async-done(((f32[8,32,256]{2,1,0:T(8,128)}), f32[8,32,256]{2,1,0:T(8,128)}, u32[]{:S(2)}, u32[]{:S(2)}) %all-to-all-start.3) | async-done | bytes 262176 | tf_op jit(solution)/shard_map/all_to_all | solution.py:69
  72.7 1.1 copy.52
  74.6 1.2 broadcast_multiply_fusion
  76.8 1.4 multiply_bitcast_fusion.2
  80.0 1.6 fusion.74
  81.6 1.6 fusion.70
  85.8 1.6 fusion.68
  87.4 1.7 fusion.72
  91.8 1.6 fusion.60
  93.4 1.6 fusion.62
  94.9 1.6 convolution_subtract_fusion.9
  96.5 1.6 convolution_add_fusion.9
  98.1 2.0 convolution_add_fusion.8
  100.1 1.6 convolution_subtract_fusion.8
  101.7 1.6 convolution_subtract_fusion.6
  103.3 1.8 multiply_subtract_fusion.1
  105.1 1.6 fusion.66
  106.6 1.6 fusion.64
  108.2 1.6 convolution_add_fusion.7
  109.8 1.6 convolution_subtract_fusion.7
  111.4 0.8 fusion.81
  112.8 1.6 fusion.58
  114.4 1.6 fusion.56
  116.0 1.6 convolution_add_fusion.5
  117.5 1.6 convolution_subtract_fusion.5
  123.9 10.0 %all_to_all.89 = f32[32,8,256]{2,0,1:T(8,128)} all-to-all(f32[32,8,256]{2,0,1:T(8,128)S(1)} %copy.27), channel_id=1, replica_groups=mesh['seq'=8,'panel'=4] {'seq'}, dimensions={1} | all-to-all | bytes 524288 | tf_op jit(solution)/shard_map/all_to_all | solution.py:101
  133.9 1.1 copy.28
  135.0 1.3 fusion.85
  136.4 1.0 copy.31
  137.4 9.3 %all_to_all.90 = f32[32,8,256]{2,0,1:T(8,128)S(1)} all-to-all(f32[32,8,256]{2,0,1:T(8,128)S(1)} %copy.31), channel_id=1, replica_groups=mesh['seq'=8,'panel'=4] {'seq'}, dimensions={1} | all-to-all | bytes 524288 | tf_op jit(solution)/shard_map/all_to_all | solution.py:101
  147.1 1.3 collective-permute-start.1
  148.4 1.8 collective-permute-done.1
  150.2 1.6 convolution_bitcast_fusion
  151.9 11.5 %reduce-scatter.3.cloned.1.call-done = f32[256,256]{1,0:T(8,128)} async-done(((f32[256,1024]{1,0:T(8,128)}), f32[256,256]{1,0:T(8,128)}) %reduce-scatter.3.cloned.1.call-update) | async-done | bytes 262160 | tf_op jit(solution)/shard_map/reduce_scatter | solution.py:132
  163.4 1.6 convert_element_type.211
  165.0 26.5 %reduce-scatter.5.cloned.1.call-done = f32[256,256]{1,0:T(8,128)} async-done(((f32[256,1024]{1,0:T(8,128)}), f32[256,256]{1,0:T(8,128)}) %reduce-scatter.5.cloned.1.call-update) | async-done | bytes 262160 | tf_op jit(solution)/shard_map/reduce_scatter | solution.py:159
  191.5 1.6 convert_element_type.213
  (77 shorter events, 18.4 us)
Async XLA Ops:
  7.2 17.7 %copy-start = (bf16[3,1024,256]{2,1,0:T(8,128)(2,1)S(1)}, bf16[3,1024,256]{2,1,0:T(8,128)(2,1)}, u32[]{:S(2)}) copy-start(bf16[3,1024,256]{2,1,0:T(8,128)(2,1)} %param.9) | copy-start | bytes 4718596
  7.2 19.6 %copy-start.7 = (f32[256,256]{1,0:T(8,128)S(1)}, f32[256,256]{1,0:T(8,128)}, u32[]{:S(2)}) copy-start(f32[256,256]{1,0:T(8,128)} %param.12) | copy-start | bytes 786436
  24.9 7.4 %copy-start.8 = (bf16[256,256]{1,0:T(8,128)(2,1)S(1)}, bf16[256,256]{1,0:T(8,128)(2,1)}, u32[]{:S(2)}) copy-start(bf16[256,256]{1,0:T(8,128)(2,1)} %param.8) | copy-start | bytes 393220
  24.9 24.9 %copy-start.5 = (bf16[256,1024]{1,0:T(8,128)(2,1)S(1)}, bf16[256,1024]{1,0:T(8,128)(2,1)}, u32[]{:S(2)}) copy-start(bf16[256,1024]{1,0:T(8,128)(2,1)} %param.13) | copy-start | bytes 1572868
  25.5 24.7 %copy-start.9 = (f32[3,3,256]{2,1,0:T(4,128)S(1)}, f32[3,3,256]{2,1,0:T(4,128)}, u32[]{:S(2)}) copy-start(f32[3,3,256]{2,1,0:T(4,128)} %param.10) | copy-start | bytes 27652
  25.5 24.7 %collective-permute-start = (bf16[3,2,256]{2,1,0:T(2,128)(2,1)S(1)}, bf16[3,2,256]{2,1,0:T(2,128)(2,1)S(1)}, u32[]{:S(2)}, u32[]{:S(2)}) collective-permute-start(bf16[3,2,256]{2,1,0:T(2,128)(2,1)S(1)} %slice.85), channel_id=1, source_target_pairs={{0,4},{4,8},{8,12},{12,16},{16,20},{20,24},{24,28},{1,5},{5,9},{9,... | collective-permute-start | bytes 9224 | tf_op jit(solution)/shard_map/ppermute | solution.py:14
  27.7 23.8 %all-to-all-start.1 = ((f32[8,32,256]{2,1,0:T(8,128)}), f32[8,32,256]{2,1,0:T(8,128)S(1)}, u32[]{:S(2)}, u32[]{:S(2)}) async-start(f32[8,32,256]{2,1,0:T(8,128)} %bitcast.25), calls=%async_computation.1 | async-start | bytes 524288 | tf_op jit(solution)/shard_map/all_to_all | solution.py:69
  51.5 17.1 %copy-start.1 = (f32[8,32,256]{2,1,0:T(8,128)}, f32[8,32,256]{2,1,0:T(8,128)S(1)}, u32[]{:S(2)}) copy-start(f32[8,32,256]{2,1,0:T(8,128)S(1)} %all-to-all-done.1) | copy-start | bytes 786436
  51.5 10.3 %all-to-all-start = ((f32[8,32,256]{2,1,0:T(8,128)}), f32[8,32,256]{2,1,0:T(8,128)S(1)}, u32[]{:S(2)}, u32[]{:S(2)}) async-start(f32[8,32,256]{2,1,0:T(8,128)} %bitcast.8), calls=%async_computation | async-start | bytes 524288 | tf_op jit(solution)/shard_map/all_to_all | solution.py:69
  61.7 4.7 %copy-start.3 = (f32[8,32,256]{2,1,0:T(8,128)}, f32[8,32,256]{2,1,0:T(8,128)S(1)}, u32[]{:S(2)}) copy-start(f32[8,32,256]{2,1,0:T(8,128)S(1)} %all-to-all-done) | copy-start | bytes 786436
  61.7 11.0 %all-to-all-start.3 = ((f32[8,32,256]{2,1,0:T(8,128)}), f32[8,32,256]{2,1,0:T(8,128)}, u32[]{:S(2)}, u32[]{:S(2)}) async-start(f32[8,32,256]{2,1,0:T(8,128)} %bitcast.44), calls=%async_computation.4 | async-start | bytes 524288 | tf_op jit(solution)/shard_map/all_to_all | solution.py:69
  65.8 97.6 %reduce-scatter.3.cloned.1.call-start = ((), (), s32[]{:S(2)}) async-start(), calls=%async_computation.7 | async-start | bytes 1310720 | tf_op jit(solution)/shard_map/reduce_scatter | solution.py:132
  75.8 1.0 copy-start.2
  75.8 1.0 copy-start.4
  123.0 12.0 %copy-start.6 = (bf16[256,1024]{1,0:T(8,128)(2,1)S(1)}, bf16[256,1024]{1,0:T(8,128)(2,1)}, u32[]{:S(2)}) copy-start(bf16[256,1024]{1,0:T(8,128)(2,1)} %param.13) | copy-start | bytes 1572868
  123.0 12.0 %copy-start.10 = (f32[256]{0:T(256)S(1)}, f32[256]{0:T(256)}, u32[]{:S(2)}) copy-start(f32[256]{0:T(256)} %param.11) | copy-start | bytes 3076
  136.3 55.1 %reduce-scatter.5.cloned.1.call-start = ((), (), s32[]{:S(2)}) async-start(), calls=%async_computation.8 | async-start | bytes 1310720 | tf_op jit(solution)/shard_map/reduce_scatter | solution.py:159
  147.1 3.1 %collective-permute-start.1 = (f32[3,2,256]{2,1,0:T(2,128)S(1)}, f32[3,2,256]{2,1,0:T(2,128)S(1)}, u32[]{:S(2)}, u32[]{:S(2)}) collective-permute-start(f32[3,2,256]{2,1,0:T(2,128)S(1)} %slice.98), channel_id=1, source_target_pairs={{4,0},{8,4},{12,8},{16,12},{20,16},{24,20},{28,24},{5,1},{9,5},{13... | collective-permute-start | bytes 18440 | tf_op jit(solution)/shard_map/ppermute | solution.py:14
Sparse Core Ops, SparseCore 0:
  136.5 26.8 reduce-scatter.2
  165.7 25.7 reduce-scatter.4
where the time goes:
time: 203 us; the launch traced here: 200 us
  blocking collectives  54.6 us (27%)
  waiting for transfers between devices  49.1 us (24%)
  matrix products  48.5 us (24%)
  starting transfers between devices  15.2 us (7%)
  between operations  14.9 us (7%)
  local copies, waits for them, and re-layouts  10.4 us (5%)
  other arithmetic  7.55 us (4%)
    reduce_scatter x1, waiting for transfers between devices, local(): lax.psum_scatter(grad_partial, 'panel', scatter_dimension=1, tiled=True)  26.5 us
    all_to_all x2, blocking collectives, whole_untransform(): lax.all_to_all(columns, 'seq', split_axis=1, concat_axis=0, tiled=True)  19.3 us
    all_gather x1, blocking collectives, local(): lax.all_gather(tokens, 'panel', axis=1, tiled=True)  17.7 us
    all_gather x1, blocking collectives, local(): lax.all_gather(cotangent, 'panel', axis=1, tiled=True)  17.6 us
    all_to_all x3, starting transfers between devices, whole_transform(): lax.all_to_all(signal.T, 'seq', split_axis=0, concat_axis=1, tiled=True)  12.1 us
    dot_general x10, matrix products, apply_dft(): sin_real = jnp.einsum(einsum_form, sin_table, real_part, precision=HIGHEST)  11.5 us
    reduce_scatter x1, waiting for transfers between devices, local(): lax.psum_scatter(partial_value, 'panel', scatter_dimension=1, tiled=True)  11.5 us
    dot_general x10, matrix products, apply_dft(): cos_real = jnp.einsum(einsum_form, cos_table, real_part, precision=HIGHEST)  11.3 us
  transfers between devices with their start and end apart: 7, of which 5 were waited for; matrix products, arithmetic and copies ran while one was open for 5% of the time, Pallas kernels for 0%

commit v1 on v0

v1 whole, which is shorter than its diff:
```python
import math

import jax
import jax.numpy as jnp
from jax import lax
from jax.sharding import PartitionSpec as P

HIGHEST = lax.Precision.HIGHEST
STAGE_A_PRECISION = lax.Precision.HIGHEST
STAGE_B_PRECISION = lax.Precision.HIGHEST


def shifted(value, axis, steps):
    count = lax.axis_size(axis)
    initial, last = (max(0, -steps), min(count, count - steps))
    return lax.ppermute(value, axis, [(source, source + steps) for source in range(initial, last)])


def phase(numer, period):
    return (2.0 * math.pi / period) * (numer % period).astype(jnp.float32)


def transform_tables(shard_count, row_count):
    length = shard_count * row_count
    branch = jnp.arange(2, dtype=jnp.int32)
    shard = jnp.arange(shard_count, dtype=jnp.int32)
    row = jnp.arange(row_count, dtype=jnp.int32)
    theta = -phase(
        (2 * shard[:, None] * shard[None, :])[None] + branch[:, None, None] * shard[None, None, :],
        2 * shard_count,
    )
    stage_a = jnp.stack([jnp.cos(theta), jnp.sin(theta)], axis=1)
    phi = -phase(
        (2 * shard[:, None] * row[None, :])[None] + branch[:, None, None] * row[None, :][None],
        2 * length,
    )
    twiddle = (jnp.cos(phi), jnp.sin(phi))
    psi = -phase(row[:, None] * row[None, :], row_count)
    cos_b, sin_b = jnp.cos(psi), jnp.sin(psi)
    stage_b = jnp.stack(
        [jnp.stack([cos_b, sin_b], axis=1), jnp.stack([-sin_b, cos_b], axis=1)]
    )
    stage_b_inv = jnp.stack(
        [jnp.stack([cos_b, -sin_b], axis=1), jnp.stack([sin_b, cos_b], axis=1)]
    )
    stage_a_inv = stage_a * (0.5 / length)
    return stage_a, twiddle, stage_b, stage_b_inv, stage_a_inv


def complex_scale(value, cos_part, sin_part, axis):
    real_part = lax.index_in_dim(value, 0, axis, keepdims=False)
    imag_part = lax.index_in_dim(value, 1, axis, keepdims=False)
    return jnp.stack(
        [real_part * cos_part - imag_part * sin_part, real_part * sin_part + imag_part * cos_part],
        axis=axis,
    )


def to_columns(rows):
    shard_count = lax.axis_size("seq")
    batch, row_count, _ = rows.shape
    columns = lax.all_to_all(
        jnp.swapaxes(rows, 1, 2), "seq", split_axis=1, concat_axis=2, tiled=True
    )
    return columns.reshape(batch, columns.shape[1], shard_count, row_count)


def to_rows(columns):
    batch, chan_count, shard_count, row_count = columns.shape
    flat = columns.reshape(batch, chan_count, shard_count * row_count)
    rows = lax.all_to_all(flat, "seq", split_axis=2, concat_axis=1, tiled=True)
    return jnp.swapaxes(rows, 1, 2)


def forward_spectrum(columns, tables):
    stage_a, twiddle, stage_b, _, _ = tables
    spread = jnp.einsum("erkp,bcpm->bcerkm", stage_a, columns, precision=STAGE_A_PRECISION)
    spread = complex_scale(spread, twiddle[0], twiddle[1], 3)
    return jnp.einsum("bcerkm,rmsq->bceskq", spread, stage_b, precision=STAGE_B_PRECISION)


def inverse_spectrum(spectrum, tables):
    _, twiddle, _, stage_b_inv, stage_a_inv = tables
    spread = jnp.einsum("bceskq,sqrm->bcerkm", spectrum, stage_b_inv, precision=STAGE_B_PRECISION)
    spread = complex_scale(spread, twiddle[0], -twiddle[1], 3)
    return jnp.einsum("erkp,bcerkm->bcpm", stage_a_inv, spread, precision=STAGE_A_PRECISION)


def local(tokens, cotangent, in_weight, short_kernel, skip_gain, long_filter, out_weight):
    row_count = tokens.shape[0]
    tap_count = short_kernel.shape[0]
    shard_count = lax.axis_size("seq")
    tables = transform_tables(shard_count, row_count)
    filt_spec = forward_spectrum(to_columns(long_filter[None]), tables)
    both = lax.all_gather(
        jnp.concatenate([tokens, cotangent], axis=0), "panel", axis=1, tiled=True
    )
    full_tok, full_cot = both[:row_count], both[row_count:]
    projected = jnp.einsum(
        "td,jdc->jtc", full_tok, in_weight, preferred_element_type=jnp.float32
    ).astype(jnp.bfloat16)
    before = shifted(projected[:, row_count - (tap_count - 1) :, :], "seq", 1)
    extended = jnp.concatenate([before, projected], axis=1).astype(jnp.float32)
    filtered = short_kernel[0][:, None, :] * extended[:, tap_count - 1 :, :]
    for tap_index in range(1, tap_count):
        filtered = (
            filtered
            + short_kernel[tap_index][:, None, :]
            * extended[:, tap_count - 1 - tap_index : tap_count - 1 - tap_index + row_count, :]
        )
    gate_out, gate_in, value_path = (filtered[0], filtered[1], filtered[2])
    signal = value_path * gate_in
    grad_gated = lax.dot_general(
        full_cot, out_weight, (((1,), (1,)), ((), ())), preferred_element_type=jnp.float32
    )
    grad_state = grad_gated * gate_out
    spectra = forward_spectrum(to_columns(jnp.stack([signal, grad_state])), tables)
    filt_real, filt_imag = filt_spec[:, :, :, 0], filt_spec[:, :, :, 1]
    sig_real, sig_imag = spectra[0:1, :, :, 0], spectra[0:1, :, :, 1]
    grad_real, grad_imag = spectra[1:2, :, :, 0], spectra[1:2, :, :, 1]
    product = jnp.concatenate(
        [
            jnp.stack(
                [sig_real * filt_real - sig_imag * filt_imag, sig_real * filt_imag + sig_imag * filt_real],
                axis=3,
            ),
            jnp.stack(
                [grad_real * filt_real + grad_imag * filt_imag, grad_imag * filt_real - grad_real * filt_imag],
                axis=3,
            ),
        ]
    )
    convolved = to_rows(inverse_spectrum(product, tables))
    conv_state = convolved[0] + skip_gain[None, :] * signal
    grad_signal = convolved[1] + skip_gain[None, :] * grad_state
    gated_state = (conv_state * gate_out).astype(jnp.bfloat16)
    partial_value = jnp.dot(gated_state, out_weight, preferred_element_type=jnp.float32)
    block_out = lax.psum_scatter(partial_value, "panel", scatter_dimension=1, tiled=True).astype(
        jnp.bfloat16
    )
    grad_gate_out = grad_gated * conv_state
    grad_value = grad_signal * gate_in
    grad_gate_in = grad_signal * value_path
    upstream = jnp.stack([grad_gate_out, grad_gate_in, grad_value])
    after_rim = shifted(upstream[:, : tap_count - 1, :], "seq", -1)
    widened = jnp.concatenate([upstream, after_rim], axis=1)
    grad_projected = short_kernel[0][:, None, :] * widened[:, :row_count, :]
    for tap_index in range(1, tap_count):
        grad_projected = (
            grad_projected
            + short_kernel[tap_index][:, None, :] * widened[:, tap_index : tap_index + row_count, :]
        )
    grad_projected = grad_projected.astype(jnp.bfloat16)
    grad_partial = jnp.einsum(
        "jtc,jdc->td", grad_projected, in_weight, preferred_element_type=jnp.float32
    )
    token_grad = lax.psum_scatter(grad_partial, "panel", scatter_dimension=1, tiled=True).astype(
        jnp.bfloat16
    )
    return (block_out, token_grad)


def solution(mesh):
    placed = (
        P("seq", "panel"),
        P("seq", "panel"),
        P(None, None, "panel"),
        P(None, None, "panel"),
        P("panel"),
        P("seq", "panel"),
        P("panel", None),
    )
    return jax.shard_map(
        local,
        mesh=mesh,
        in_specs=placed,
        out_specs=(P("seq", "panel"), P("seq", "panel")),
        check_vma=False,
    )
```

time: 203 us -> 172 us (0.85); the launches traced: 200 us -> 172 us
  blocking collectives: 54.6 us -> 12.1 us
  matrix products: 48.5 us -> 21.1 us
  waiting for transfers between devices: 49.1 us -> 75.6 us
  local copies, waits for them, and re-layouts: 10.4 us -> 19.8 us
  other arithmetic: 7.55 us -> 14.9 us
    all_gather x2 -> x0, blocking collectives: 35.3 us -> none  [the longest x1 17.7 us: local(): lax.all_gather(tokens, 'panel', axis=1, tiled=True)]
    dot_general x40 -> x6, matrix products: 44.6 us -> 16.1 us  [the longest x2 6.4 us: forward_spectrum(): jnp.einsum('bcerkm,rmsq->bceskq', spread, stage_b, precision=STAGE_B_PREC...]
    all_gather x0 -> x1, waiting for transfers between devices: none -> 18 us  [local(): lax.all_gather(jnp.concatenate([tokens, cotangent], axis=0), 'panel', axi...]
    unnamed x26 -> x31, local copies, waits for them, and re-layouts: 1.58 us -> 9.84 us
    reduce_scatter x1, waiting for transfers between devices: 11.5 us -> 19.3 us  [local(): lax.psum_scatter(partial_value, 'panel', scatter_dimension=1, tiled=True)]
    all_to_all x2 -> x1, blocking collectives: 19.3 us -> 12.1 us  [to_rows(): rows = lax.all_to_all(flat, 'seq', split_axis=2, concat_axis=1, tiled=True)]
    mul x3 -> x6, other arithmetic: 3.38 us -> 0.19 us  [the longest x2 0.07 us: transform_tables(): 2 * shard[:, None] * shard[None, :]]
    all_to_all x8 -> x3, local copies, waits for them, and re-layouts: 5.85 us -> 4.23 us  [to_rows(): rows = lax.all_to_all(flat, 'seq', split_axis=2, concat_axis=1, tiled=True)]
  transfers between devices with their start and end apart: 7 -> 7, of which waited for: 5 -> 7; matrix products, arithmetic and copies ran while one was open for 5% -> 7% of each run, Pallas kernels for 0% -> 0%
where the time goes in v1:
time: 172 us
  waiting for transfers between devices  75.6 us (44%)
  matrix products  21.1 us (12%)
  local copies, waits for them, and re-layouts  19.8 us (12%)
  other arithmetic  14.9 us (9%)
  between operations  14.1 us (8%)
  starting transfers between devices  14 us (8%)
  blocking collectives  12.1 us (7%)
    reduce_scatter x1, waiting for transfers between devices, local(): lax.psum_scatter(grad_partial, 'panel', scatter_dimension=1, tiled=True)  26.5 us
    reduce_scatter x1, waiting for transfers between devices, local(): lax.psum_scatter(partial_value, 'panel', scatter_dimension=1, tiled=True)  19.3 us
    all_gather x1, waiting for transfers between devices, local(): lax.all_gather(jnp.concatenate([tokens, cotangent], axis=0), 'panel', axi...  18 us
    all_to_all x1, blocking collectives, to_rows(): rows = lax.all_to_all(flat, 'seq', split_axis=2, concat_axis=1, tiled=True)  12.1 us
    all_to_all x2, starting transfers between devices, to_columns(): lax.all_to_all(jnp.swapaxes(rows, 1, 2), 'seq', split_axis=1, concat_axis...  11.2 us
    unnamed x31, local copies, waits for them, and re-layouts  9.84 us
    all_to_all x2, waiting for transfers between devices, to_columns(): lax.all_to_all(jnp.swapaxes(rows, 1, 2), 'seq', split_axis=1, concat_axis...  9.46 us
    dot_general x2, matrix products, forward_spectrum(): jnp.einsum('bcerkm,rmsq->bceskq', spread, stage_b, precision=STAGE_B_PREC...  6.4 us
  transfers between devices with their start and end apart: 7, of which 7 were waited for; matrix products, arithmetic and copies ran while one was open for 7% of the time, Pallas kernels for 0%

profile of v1, /device:TPU:0, one launch (start us, length us, event | category | flops | bytes accessed | tf_op | source)
XLA Modules:
  0.0 171.7 jit_solution(15434371494799115491)
XLA Ops:
  7.2 1.8 %pad_maximum_fusion.10 = bf16[512,256]{1,0:T(8,128)(2,1)} fusion(bf16[256,256]{1,0:T(8,128)(2,1)} %param.8, bf16[256,256]{1,0:T(8,128)(2,1)} %param.7), kind=kLoop, calls=%fused_computation.82 | loop fusion | flops 524288 | bytes 524288 | tf_op jit(solution)/shard_map/concatenate | solution.py:96
  9.0 1.8 %copy.63 = f32[1,256,256]{1,0,2:T(1,128)} copy(f32[1,256,256]{2,1,0:T(8,128)} %bitcast.183) | data formatting | bytes 524288 | tf_op jit(solution)/shard_map/broadcast_in_dim | solution.py:94
  10.9 5.3 %all-to-all-start.1 = ((f32[1,256,256]{2,0,1:T(1,128)}), f32[1,256,256]{2,0,1:T(1,128)S(1)}, u32[]{:S(2)}, u32[]{:S(2)}) async-start(f32[1,256,256]{2,0,1:T(1,128)} %bitcast.32), calls=%async_computation.1 | async-start | bytes 524288 | tf_op jit(solution)/shard_map/all_to_all | solution.py:62
  16.2 1.0 fusion.59
  17.2 1.0 fusion.61
  18.2 1.4 fusion.33
  20.0 3.1 %all-to-all-done.1 = f32[1,256,256]{2,0,1:T(1,128)S(1)} async-done(((f32[1,256,256]{2,0,1:T(1,128)}), f32[1,256,256]{2,0,1:T(1,128)S(1)}, u32[]{:S(2)}, u32[]{:S(2)}) %all-to-all-start.1) | async-done | bytes 262176 | tf_op jit(solution)/shard_map/all_to_all | solution.py:62
  23.1 1.0 convolution_bitcast_fusion.3
  24.1 18.0 %all-gather.2.cloned.1.call-done = bf16[512,1024]{1,0:T(8,128)(2,1)} async-done(((bf16[512,256]{1,0:T(8,128)(2,1)}), bf16[512,1024]{1,0:T(8,128)(2,1)}) %all-gather.2.cloned.1.call-update) | async-done | bytes 1048592 | tf_op jit(solution)/shard_map/all_gather | solution.py:95
  42.2 1.7 fusion.19
  43.9 1.3 collective-permute-start
  45.2 0.3 fusion.35
  45.6 0.4 collective-permute-done
  46.1 0.2 fusion.29
  46.4 0.8 maximum_bitcast_fusion.4
  47.3 2.1 %copy.31 = f32[2,256,256]{2,0,1:T(2,128)} copy(f32[2,256,256]{1,2,0:T(8,128)} %maximum_bitcast_fusion.4) | data formatting | bytes 1048576 | tf_op jit(solution)/shard_map/transpose | solution.py:63
  49.3 5.8 %all-to-all-start = ((f32[2,256,256]{2,0,1:T(2,128)}), f32[2,256,256]{2,0,1:T(2,128)}, u32[]{:S(2)}, u32[]{:S(2)}) async-start(f32[2,256,256]{2,0,1:T(2,128)} %copy.31), calls=%async_computation | async-start | bytes 1048576 | tf_op jit(solution)/shard_map/all_to_all | solution.py:62
  55.1 0.2 reduce-scatter.3.cloned.1.call-start
  55.6 0.8 copy-done.5
  56.6 2.0 %convolution_bitcast_fusion.2 = f32[1,32,2,2,8,256]{5,1,4,2,0,3:T(8,128)S(1)} fusion(f32[32,2,2,8,256]{4,3,0,2,1:T(8,128)S(1)} %maximum_bitcast_fusion.3, f32[1,256,2,256]{3,1,0,2:T(8,128)S(1)} %copy-done.5, f32[1,256,2,256]{3,1,0,2:T(8,128)S(1)} %copy-done.7), kind=kOutput, calls=%fused_computation.16 | convolution fusion | flops 1610874880 | bytes 3145728 | tf_op jit(solution)/shard_map/bcerkm,rmsq->bceskq/dot_general | solution.py:79
  58.6 6.4 %all-to-all-done = f32[2,256,256]{2,0,1:T(2,128)} async-done(((f32[2,256,256]{2,0,1:T(2,128)}), f32[2,256,256]{2,0,1:T(2,128)}, u32[]{:S(2)}, u32[]{:S(2)}) %all-to-all-start) | async-done | bytes 524320 | tf_op jit(solution)/shard_map/all_to_all | solution.py:62
  65.0 2.9 %convolution_bitcast_fusion = f32[2,32,2,2,8,256]{5,4,3,2,1,0:T(8,128)S(1)} fusion(f32[2,8,32,256]{3,0,2,1:T(2,128)} %bitcast.16, f32[2,1,8,8]{3,2,1,0:T(8,128)S(1)} %get-tuple-element.31, f32[2,1,8,8]{3,2,1,0:T(8,128)S(1)} %get-tuple-element.30), kind=kOutput, calls=%fused_computation.14 | convolution fusion | flops 50331904 | bytes 2622464 | tf_op jit(solution)/shard_map/erkp,bcpm->bcerkm/dot_general | solution.py:77
  67.9 0.3 multiply_subtract_fusion.1
  68.2 0.2 pad_maximum_fusion
  68.4 0.8 copy-done.6
  69.4 4.4 %fusion.10 = f32[2,32,2,2,8,256]{5,1,4,2,0,3:T(8,128)S(1)} fusion(f32[2,32,2,2,8,256]{5,4,3,2,1,0:T(8,128)S(1)} %pad_maximum_fusion, f32[1,256,2,256]{3,1,0,2:T(8,128)S(1)} %copy-done.6, f32[1,256,2,256]{3,1,0,2:T(8,128)S(1)} %copy-done.8), kind=kOutput, calls=%fused_computation.12 | convolution fusion | flops 3221487616 | bytes 5242880 | tf_op jit(solution)/shard_map/bcerkm,rmsq->bceskq/dot_general | solution.py:79
  73.8 0.5 multiply_subtract_fusion.3
  74.4 0.9 copy-done.9
  75.5 4.6 %fusion.13 = f32[2,32,2,2,8,256]{5,4,3,2,1,0:T(8,128)S(1)} fusion(f32[2,32,2,2,8,256,1]{5,1,4,2,0,3,6:T(8,128)S(1)} %maximum_bitcast_fusion, f32[1,256,2,256]{3,1,2,0:T(8,128)S(1)} %copy-done.10, f32[1,256,2,256]{3,1,2,0:T(8,128)S(1)} %copy-done.9), kind=kOutput, calls=%fused_computation.13 | convolution fusion | flops 3221487616 | bytes 5242880 | tf_op jit(solution)/shard_map/bceskq,sqrm->bcerkm/dot_general | solution.py:84
  80.1 0.3 multiply_subtract_fusion
  80.4 1.2 fusion.16
  81.7 1.9 %copy.68 = f32[2,32,8,256]{1,0,3,2:T(2,128)} copy(f32[2,32,8,256]{3,2,1,0:T(8,128)S(1)} %fusion.16) | data formatting | bytes 1048576 | tf_op jit(solution)/shard_map/reshape | solution.py:70
  83.5 3.6 %reshape.320 = f32[8,1,16384]{2,1,0:T(1,128)S(1)} reshape(f32[2048,2,32]{2,1,0:T(2,128)} %bitcast.178) | data formatting | bytes 1048576
  87.2 12.1 %all_to_all.48 = f32[8,1,16384]{2,1,0:T(1,128)S(1)} all-to-all(f32[8,1,16384]{2,1,0:T(1,128)S(1)} %reshape.320), channel_id=1, replica_groups=mesh['seq'=8,'panel'=4] {'seq'}, dimensions={0} | all-to-all | bytes 1048576 | tf_op jit(solution)/shard_map/all_to_all | solution.py:71
  99.3 0.5 broadcast.355
  99.8 1.9 %reduce = f32[8,16384]{1,0:T(8,128)S(1)} reduce(f32[8,1,16384]{2,1,0:T(1,128)S(1)} %all_to_all.48, f32[]{:T(128)} %broadcast.355), dimensions={1}, to_apply=%all_to_all.41.reduce_sub_computation | reduce | bytes 1048580 | tf_op jit(solution)/shard_map/all_to_all | solution.py:71
  101.7 3.1 %reshape.321 = f32[2048,2,32]{2,1,0:T(2,128)} reshape(f32[8,16384]{1,0:T(8,128)S(1)} %reduce) | data formatting | bytes 1048576
  104.8 2.7 %copy.70 = f32[2,32,8,256]{3,1,2,0:T(8,128)S(1)} copy(f32[2,32,8,256]{1,0,3,2:T(2,128)} %bitcast.179) | data formatting | bytes 1048576 | tf_op jit(solution)/shard_map/all_to_all | solution.py:71
  107.5 1.0 copy.45
  108.6 1.2 fusion.52
  109.8 1.3 fusion.58
  111.3 1.3 collective-permute-start.1
  112.6 1.8 %collective-permute-done.1 = f32[3,2,256]{2,1,0:T(2,128)S(1)} collective-permute-done((f32[3,2,256]{2,1,0:T(2,128)S(1)}, f32[3,2,256]{2,1,0:T(2,128)S(1)}, u32[]{:S(2)}, u32[]{:S(2)}) %collective-permute-start.1) | collective-permute-done | bytes 6176 | tf_op jit(solution)/shard_map/ppermute | solution.py:16
  114.4 1.6 convolution_bitcast_fusion.1
  116.0 19.3 %reduce-scatter.3.cloned.1.call-done = f32[256,256]{1,0:T(8,128)} async-done(((f32[256,1024]{1,0:T(8,128)}), f32[256,256]{1,0:T(8,128)}) %reduce-scatter.3.cloned.1.call-update) | async-done | bytes 262160 | tf_op jit(solution)/shard_map/reduce_scatter | solution.py:138
  135.4 1.6 convert_element_type.109
  137.0 26.5 %reduce-scatter.5.cloned.1.call-done = f32[256,256]{1,0:T(8,128)} async-done(((f32[256,1024]{1,0:T(8,128)}), f32[256,256]{1,0:T(8,128)}) %reduce-scatter.5.cloned.1.call-update) | async-done | bytes 262160 | tf_op jit(solution)/shard_map/reduce_scatter | solution.py:157
  163.5 1.6 convert_element_type.111
  (50 shorter events, 1.6 us)
Async XLA Ops:
  7.2 35.0 %copy-start = (bf16[3,1024,256]{2,1,0:T(8,128)(2,1)S(1)}, bf16[3,1024,256]{2,1,0:T(8,128)(2,1)}, u32[]{:S(2)}) copy-start(bf16[3,1024,256]{2,1,0:T(8,128)(2,1)} %param.9) | copy-start | bytes 4718596
  7.2 35.0 %all-gather.2.cloned.1.call-start = ((), (), s32[]{:S(2)}) async-start(), calls=%async_computation.5 | async-start | bytes 1310720 | tf_op jit(solution)/shard_map/all_gather | solution.py:95
  10.9 9.0 %copy-start.12 = (f32[3,3,256]{2,1,0:T(4,128)S(1)}, f32[3,3,256]{2,1,0:T(4,128)}, u32[]{:S(2)}) copy-start(f32[3,3,256]{2,1,0:T(4,128)} %param.10) | copy-start | bytes 27652
  10.9 12.2 %all-to-all-start.1 = ((f32[1,256,256]{2,0,1:T(1,128)}), f32[1,256,256]{2,0,1:T(1,128)S(1)}, u32[]{:S(2)}, u32[]{:S(2)}) async-start(f32[1,256,256]{2,0,1:T(1,128)} %bitcast.32), calls=%async_computation.1 | async-start | bytes 524288 | tf_op jit(solution)/shard_map/all_to_all | solution.py:62
  23.1 22.1 %copy-start.3 = (bf16[256,1024]{1,0:T(8,128)(2,1)S(1)}, bf16[256,1024]{1,0:T(8,128)(2,1)}, u32[]{:S(2)}) copy-start(bf16[256,1024]{1,0:T(8,128)(2,1)} %param.13) | copy-start | bytes 1572868
  42.2 3.0 %copy-start.11 = (bf16[512,1024]{1,0:T(8,128)(2,1)S(1)}, bf16[512,1024]{1,0:T(8,128)(2,1)}, u32[]{:S(2)}) copy-start(bf16[512,1024]{1,0:T(8,128)(2,1)} %all-gather.2.cloned.1.call-done) | copy-start | bytes 3145732
  43.9 2.1 %collective-permute-start = (bf16[3,2,256]{2,1,0:T(2,128)(2,1)S(1)}, bf16[3,2,256]{2,1,0:T(2,128)(2,1)S(1)}, u32[]{:S(2)}, u32[]{:S(2)}) collective-permute-start(bf16[3,2,256]{2,1,0:T(2,128)(2,1)S(1)} %slice.120), channel_id=1, source_target_pairs={{0,4},{4,8},{8,12},{12,16},{16,20},{20,24},{24,28},{1,5},{5,9},{9,... | collective-permute-start | bytes 9224 | tf_op jit(solution)/shard_map/ppermute | solution.py:16
  45.5 0.8 copy-start.1
  49.3 15.6 %all-to-all-start = ((f32[2,256,256]{2,0,1:T(2,128)}), f32[2,256,256]{2,0,1:T(2,128)}, u32[]{:S(2)}, u32[]{:S(2)}) async-start(f32[2,256,256]{2,0,1:T(2,128)} %copy.31), calls=%async_computation | async-start | bytes 1048576 | tf_op jit(solution)/shard_map/all_to_all | solution.py:62
  55.1 80.2 %reduce-scatter.3.cloned.1.call-start = ((), (), s32[]{:S(2)}) async-start(), calls=%async_computation.6 | async-start | bytes 1310720 | tf_op jit(solution)/shard_map/reduce_scatter | solution.py:138
  55.4 1.0 copy-start.5
  55.4 1.2 copy-start.7
  68.2 1.0 copy-start.6
  68.2 1.2 copy-start.8
  74.3 1.0 copy-start.9
  74.3 1.2 copy-start.10
  104.8 3.7 %copy-start.2 = (f32[256,256]{1,0:T(8,128)S(1)}, f32[256,256]{1,0:T(8,128)}, u32[]{:S(2)}) copy-start(f32[256,256]{1,0:T(8,128)} %copy-done.1) | copy-start | bytes 786436
  104.8 3.7 %copy-start.13 = (f32[256]{0:T(256)S(1)}, f32[256]{0:T(256)}, u32[]{:S(2)}) copy-start(f32[256]{0:T(256)} %param.11) | copy-start | bytes 3076
  108.6 1.2 copy-start.4
  111.1 52.4 %reduce-scatter.5.cloned.1.call-start = ((), (), s32[]{:S(2)}) async-start(), calls=%async_computation.7 | async-start | bytes 1310720 | tf_op jit(solution)/shard_map/reduce_scatter | solution.py:157
  111.3 3.1 %collective-permute-start.1 = (f32[3,2,256]{2,1,0:T(2,128)S(1)}, f32[3,2,256]{2,1,0:T(2,128)S(1)}, u32[]{:S(2)}, u32[]{:S(2)}) collective-permute-start(f32[3,2,256]{2,1,0:T(2,128)S(1)} %slice.142), channel_id=1, source_target_pairs={{4,0},{8,4},{12,8},{16,12},{20,16},{24,20},{28,24},{5,1},{9,5},{13... | collective-permute-start | bytes 18440 | tf_op jit(solution)/shard_map/ppermute | solution.py:16
Sparse Core Ops, SparseCore 0:
  9.5 32.5 all-gather.1
  111.2 24.1 reduce-scatter.2
  137.7 25.7 reduce-scatter.4

commit v2 on v1

--- a/solution.py
+++ b/solution.py
@@ -7,7 +7,7 @@
 
 HIGHEST = lax.Precision.HIGHEST
 STAGE_A_PRECISION = lax.Precision.HIGHEST
-STAGE_B_PRECISION = lax.Precision.HIGHEST
+STAGE_B_PRECISION = lax.Precision.HIGH
 
 
 def shifted(value, axis, steps):
@@ -67,9 +67,8 @@
 
 def to_rows(columns):
     batch, chan_count, shard_count, row_count = columns.shape
-    flat = columns.reshape(batch, chan_count, shard_count * row_count)
-    rows = lax.all_to_all(flat, "seq", split_axis=2, concat_axis=1, tiled=True)
-    return jnp.swapaxes(rows, 1, 2)
+    rows = lax.all_to_all(columns, "seq", split_axis=2, concat_axis=1, tiled=True)
+    return jnp.swapaxes(rows.reshape(batch, shard_count * chan_count, row_count), 1, 2)
 
 
 def forward_spectrum(columns, tables):
@@ -135,8 +134,8 @@
     grad_signal = convolved[1] + skip_gain[None, :] * grad_state
     gated_state = (conv_state * gate_out).astype(jnp.bfloat16)
     partial_value = jnp.dot(gated_state, out_weight, preferred_element_type=jnp.float32)
-    block_out = lax.psum_scatter(partial_value, "panel", scatter_dimension=1, tiled=True).astype(
-        jnp.bfloat16
+    block_out = lax.psum_scatter(
+        partial_value.astype(jnp.bfloat16), "panel", scatter_dimension=1, tiled=True
     )
     grad_gate_out = grad_gated * conv_state
     grad_value = grad_signal * gate_in
@@ -154,8 +153,8 @@
     grad_partial = jnp.einsum(
         "jtc,jdc->td", grad_projected, in_weight, preferred_element_type=jnp.float32
     )
-    token_grad = lax.psum_scatter(grad_partial, "panel", scatter_dimension=1, tiled=True).astype(
-        jnp.bfloat16
+    token_grad = lax.psum_scatter(
+        grad_partial.astype(jnp.bfloat16), "panel", scatter_dimension=1, tiled=True
     )
     return (block_out, token_grad)
 

time: 172 us -> 146 us (0.85)
  local copies, waits for them, and re-layouts: 19.8 us -> 10 us
  waiting for transfers between devices: 75.6 us -> 67.8 us
  other arithmetic: 14.9 us -> 9.7 us
  matrix products: 21.1 us -> 17.3 us
    reduce_scatter x2, waiting for transfers between devices: 45.9 us -> 37.1 us  [the longest x1 23 us: local(): lax.psum_scatter(grad_partial.astype(jnp.bfloat16), 'panel', scatter_dime...]
    unnamed x31 -> x27, local copies, waits for them, and re-layouts: 9.84 us -> 3.08 us
    all_to_all x3 -> x1, local copies, waits for them, and re-layouts: 4.23 us -> 0.86 us  [to_rows(): lax.all_to_all(columns, 'seq', split_axis=2, concat_axis=1, tiled=True)]
    convert_element_type x2 -> x0, other arithmetic: 3.24 us -> none  [the longest x1 1.62 us: local(): lax.psum_scatter(partial_value, 'panel', scatter_dimension=1, tiled=True)]
    dot_general x2, matrix products: 6.4 us -> 3.81 us  [forward_spectrum(): jnp.einsum('bcerkm,rmsq->bceskq', spread, stage_b, precision=STAGE_B_PREC...]
    dot_general x1, matrix products: 4.62 us -> 2.72 us  [inverse_spectrum(): jnp.einsum('bceskq,sqrm->bcerkm', spectrum, stage_b_inv, precision=STAGE_...]
    all_to_all x1 -> x0, other arithmetic: 1.88 us -> none  [to_rows(): rows = lax.all_to_all(flat, 'seq', split_axis=2, concat_axis=1, tiled=True)]
where the time goes in v2:
time: 146 us; the launch traced here: 145 us
  waiting for transfers between devices  67.8 us (46%)
  matrix products  17.3 us (12%)
  between operations  14.1 us (10%)
  starting transfers between devices  13.9 us (10%)
  blocking collectives  12.1 us (8%)
  local copies, waits for them, and re-layouts  10 us (7%)
  other arithmetic  9.7 us (7%)
    reduce_scatter x1, waiting for transfers between devices, local(): lax.psum_scatter(grad_partial.astype(jnp.bfloat16), 'panel', scatter_dime...  23 us
    all_gather x1, waiting for transfers between devices, local(): lax.all_gather(jnp.concatenate([tokens, cotangent], axis=0), 'panel', axi...  18.1 us
    reduce_scatter x1, waiting for transfers between devices, local(): lax.psum_scatter(partial_value.astype(jnp.bfloat16), 'panel', scatter_dim...  14.1 us
    all_to_all x1, blocking collectives, to_rows(): lax.all_to_all(columns, 'seq', split_axis=2, concat_axis=1, tiled=True)  12.1 us
    all_to_all x2, starting transfers between devices, to_columns(): lax.all_to_all(jnp.swapaxes(rows, 1, 2), 'seq', split_axis=1, concat_axis...  11.1 us
    all_to_all x2, waiting for transfers between devices, to_columns(): lax.all_to_all(jnp.swapaxes(rows, 1, 2), 'seq', split_axis=1, concat_axis...  10.4 us
    dot_general x2, matrix products, forward_spectrum(): jnp.einsum('erkp,bcpm->bcerkm', stage_a, columns, precision=STAGE_A_PRECI...  3.89 us
    dot_general x2, matrix products, forward_spectrum(): jnp.einsum('bcerkm,rmsq->bceskq', spread, stage_b, precision=STAGE_B_PREC...  3.81 us
  transfers between devices with their start and end apart: 7, of which 7 were waited for; matrix products, arithmetic and copies ran while one was open for 7% of the time, Pallas kernels for 0%

profile of v2, /device:TPU:0, one launch (start us, length us, event | category | flops | bytes accessed | tf_op | source)
XLA Modules:
  0.0 145.0 jit_solution(13202346638573220801)
XLA Ops:
  7.2 1.8 %pad_maximum_fusion.10 = bf16[512,256]{1,0:T(8,128)(2,1)} fusion(bf16[256,256]{1,0:T(8,128)(2,1)} %param.8, bf16[256,256]{1,0:T(8,128)(2,1)} %param.7), kind=kLoop, calls=%fused_computation.84 | loop fusion | flops 524288 | bytes 524288 | tf_op jit(solution)/shard_map/concatenate | solution.py:95
  9.0 1.8 %copy.63 = f32[1,256,256]{1,0,2:T(1,128)} copy(f32[1,256,256]{2,1,0:T(8,128)} %bitcast.180) | data formatting | bytes 524288 | tf_op jit(solution)/shard_map/broadcast_in_dim | solution.py:93
  10.8 5.3 %all-to-all-start.1 = ((f32[1,256,256]{2,0,1:T(1,128)}), f32[1,256,256]{2,0,1:T(1,128)S(1)}, u32[]{:S(2)}, u32[]{:S(2)}) async-start(f32[1,256,256]{2,0,1:T(1,128)} %bitcast.32), calls=%async_computation.1 | async-start | bytes 524288 | tf_op jit(solution)/shard_map/all_to_all | solution.py:62
  16.2 1.0 fusion.59
  17.2 1.0 fusion.61
  18.2 1.4 fusion.34
  19.9 0.1 fusion.80
  20.0 3.1 %all-to-all-done.1 = f32[1,256,256]{2,0,1:T(1,128)S(1)} async-done(((f32[1,256,256]{2,0,1:T(1,128)}), f32[1,256,256]{2,0,1:T(1,128)S(1)}, u32[]{:S(2)}, u32[]{:S(2)}) %all-to-all-start.1) | async-done | bytes 262176 | tf_op jit(solution)/shard_map/all_to_all | solution.py:62
  23.1 1.0 convolution_bitcast_fusion.3
  24.1 18.1 %all-gather.2.cloned.1.call-done = bf16[512,1024]{1,0:T(8,128)(2,1)} async-done(((bf16[512,256]{1,0:T(8,128)(2,1)}), bf16[512,1024]{1,0:T(8,128)(2,1)}) %all-gather.2.cloned.1.call-update) | async-done | bytes 1048592 | tf_op jit(solution)/shard_map/all_gather | solution.py:94
  42.2 1.7 %fusion.20 = bf16[3,256,256]{2,1,0:T(8,128)(2,1)S(1)} fusion(bf16[3,1024,256]{2,1,0:T(8,128)(2,1)S(1)} %copy-done, bf16[512,1024]{1,0:T(8,128)(2,1)} %all-gather.2.cloned.1.call-done), kind=kOutput, calls=%fused_computation.22 | convolution fusion | flops 402849792 | bytes 2490368 | tf_op jit(solution)/shard_map/td,jdc->jtc/dot_general | solution.py:98
  43.9 1.3 collective-permute-start
  45.3 0.3 fusion.36
  45.6 0.4 collective-permute-done
  46.1 0.2 fusion.30
  46.5 0.9 maximum_bitcast_fusion.4
  47.3 2.1 %copy.32 = f32[2,256,256]{2,0,1:T(2,128)} copy(f32[2,256,256]{1,2,0:T(8,128)} %maximum_bitcast_fusion.4) | data formatting | bytes 1048576 | tf_op jit(solution)/shard_map/transpose | solution.py:63
  49.4 5.7 %all-to-all-start = ((f32[2,256,256]{2,0,1:T(2,128)}), f32[2,256,256]{2,0,1:T(2,128)}, u32[]{:S(2)}, u32[]{:S(2)}) async-start(f32[2,256,256]{2,0,1:T(2,128)} %copy.32), calls=%async_computation | async-start | bytes 1048576 | tf_op jit(solution)/shard_map/all_to_all | solution.py:62
  55.1 0.2 reduce-scatter.3.cloned.1.call-start
  55.3 0.1 multiply_subtract_fusion.4
  55.5 0.8 copy-done.4
  56.4 0.2 copy-done.6
  56.5 1.1 convolution_bitcast_fusion.2
  57.7 7.2 %all-to-all-done = f32[2,256,256]{2,0,1:T(2,128)} async-done(((f32[2,256,256]{2,0,1:T(2,128)}), f32[2,256,256]{2,0,1:T(2,128)}, u32[]{:S(2)}, u32[]{:S(2)}) %all-to-all-start) | async-done | bytes 524320 | tf_op jit(solution)/shard_map/all_to_all | solution.py:62
  64.9 2.9 %convolution_bitcast_fusion = f32[2,32,2,2,8,256]{5,4,3,2,1,0:T(8,128)S(1)} fusion(f32[2,8,32,256]{3,0,2,1:T(2,128)} %bitcast.16, f32[2,1,8,8]{3,2,1,0:T(8,128)S(1)} %get-tuple-element.31, f32[2,1,8,8]{3,2,1,0:T(8,128)S(1)} %get-tuple-element.30), kind=kOutput, calls=%fused_computation.14 | convolution fusion | flops 50331904 | bytes 2622464 | tf_op jit(solution)/shard_map/erkp,bcpm->bcerkm/dot_general | solution.py:76
  67.8 0.3 multiply_subtract_fusion.1
  68.2 0.2 pad_maximum_fusion
  68.4 0.8 copy-done.5
  69.2 0.2 copy-done.7
  69.4 2.7 %fusion.10 = f32[2,32,2,2,8,256]{5,1,4,2,0,3:T(8,128)S(1)} fusion(f32[2,32,2,2,8,256]{5,4,3,2,1,0:T(8,128)S(1)} %pad_maximum_fusion, f32[1,256,2,256]{3,1,0,2:T(8,128)S(1)} %copy-done.5, f32[1,256,2,256]{3,1,0,2:T(8,128)S(1)} %copy-done.7), kind=kOutput, calls=%fused_computation.12 | convolution fusion | flops 1610874880 | bytes 5242880 | tf_op jit(solution)/shard_map/bcerkm,rmsq->bceskq/dot_general | solution.py:78
  72.1 0.5 multiply_subtract_fusion.3
  72.5 0.1 maximum_bitcast_fusion
  72.7 0.9 copy-done.8
  73.6 0.2 copy-done.9
  73.7 2.7 %fusion.13 = f32[2,32,2,2,8,256]{5,4,3,2,1,0:T(8,128)S(1)} fusion(f32[2,32,2,2,8,256,1]{5,1,4,2,0,3,6:T(8,128)S(1)} %maximum_bitcast_fusion, f32[1,256,2,256]{3,1,2,0:T(8,128)S(1)} %copy-done.9, f32[1,256,2,256]{3,1,2,0:T(8,128)S(1)} %copy-done.8), kind=kOutput, calls=%fused_computation.13 | convolution fusion | flops 1610874880 | bytes 5242880 | tf_op jit(solution)/shard_map/bceskq,sqrm->bcerkm/dot_general | solution.py:83
  76.5 0.3 multiply_subtract_fusion
  76.8 1.2 fusion.17
  78.0 0.2 copy.43
  78.2 12.1 %all_to_all.45 = f32[2,32,8,256]{3,1,0,2:T(8,128)S(1)} all-to-all(f32[2,32,8,256]{3,1,0,2:T(8,128)S(1)} %copy.43), channel_id=1, replica_groups=mesh['seq'=8,'panel'=4] {'seq'}, dimensions={2} | all-to-all | bytes 1048576 | tf_op jit(solution)/shard_map/all_to_all | solution.py:70
  90.4 0.9 copy.44
  91.2 2.1 %copy.45 = f32[2,256,256]{1,2,0:T(8,128)} copy(f32[2,256,256]{2,1,0:T(8,128)} %bitcast.178) | data formatting | bytes 1048576 | tf_op jit(solution)/shard_map/reshape | solution.py:71
  93.3 1.1 fusion.53
  94.4 2.2 %convolution_convert_fusion = bf16[256,1024]{1,0:T(8,128)(2,1)} fusion(bf16[256,1024]{1,0:T(8,128)(2,1)} %param.13, f32[256,256]{1,0:T(8,128)S(1)} %get-tuple-element.15, f32[3,256,256]{2,1,0:T(8,128)S(1)} %fusion.30), kind=kOutput, calls=%fused_computation.19 | convolution fusion | flops 134610944 | bytes 1572864 | tf_op jit(solution)/shard_map/dot_general | solution.py:136
  96.8 1.3 collective-permute-start.1
  98.1 1.8 %collective-permute-done.1 = f32[3,2,256]{2,1,0:T(2,128)S(1)} collective-permute-done((f32[3,2,256]{2,1,0:T(2,128)S(1)}, f32[3,2,256]{2,1,0:T(2,128)S(1)}, u32[]{:S(2)}, u32[]{:S(2)}) %collective-permute-start.1) | collective-permute-done | bytes 6176 | tf_op jit(solution)/shard_map/ppermute | solution.py:16
  99.9 1.5 %fusion.16 = bf16[256,1024]{1,0:T(8,128)(2,1)} fusion(bf16[3,1024,256]{2,1,0:T(8,128)(2,1)S(1)} %copy-done, f32[3,258,256]{2,1,0:T(8,128)S(1)} %pad_maximum_fusion.4, f32[3,256]{1,0:T(4,128)S(1)} %get-tuple-element.25, f32[3,256]{1,0:T(4,128)S(1)} %get-tuple-element.26, f32[3,256]{1,0:T(4,128)S(1)} %get-tuple-element.24, f32[1,256,256]{2,1,0:T(8,128)S(1)} %fusion.52, ...), kind=kOutput, calls=%fused_computation.18 | convolution fusion | flops 404488192 | bytes 4468736 | tf_op jit(solution)/shard_map/jtc,jdc->td/dot_general | solution.py:153
  101.4 14.1 %reduce-scatter.3.cloned.1.call-done = bf16[256,256]{1,0:T(8,128)(2,1)} async-done(((bf16[256,1024]{1,0:T(8,128)(2,1)}), bf16[256,256]{1,0:T(8,128)(2,1)}) %reduce-scatter.3.cloned.1.call-update) | async-done | bytes 131088 | tf_op jit(solution)/shard_map/reduce_scatter | solution.py:137
  115.4 23.0 %reduce-scatter.5.cloned.1.call-done = bf16[256,256]{1,0:T(8,128)(2,1)} async-done(((bf16[256,1024]{1,0:T(8,128)(2,1)}), bf16[256,256]{1,0:T(8,128)(2,1)}) %reduce-scatter.5.cloned.1.call-update) | async-done | bytes 131088 | tf_op jit(solution)/shard_map/reduce_scatter | solution.py:156
  (42 shorter events, 0.8 us)
Async XLA Ops:
  7.2 35.0 %copy-start = (bf16[3,1024,256]{2,1,0:T(8,128)(2,1)S(1)}, bf16[3,1024,256]{2,1,0:T(8,128)(2,1)}, u32[]{:S(2)}) copy-start(bf16[3,1024,256]{2,1,0:T(8,128)(2,1)} %param.9) | copy-start | bytes 4718596
  7.2 35.0 %all-gather.2.cloned.1.call-start = ((), (), s32[]{:S(2)}) async-start(), calls=%async_computation.5 | async-start | bytes 1310720 | tf_op jit(solution)/shard_map/all_gather | solution.py:94
  10.8 9.0 %copy-start.11 = (f32[3,3,256]{2,1,0:T(4,128)S(1)}, f32[3,3,256]{2,1,0:T(4,128)}, u32[]{:S(2)}) copy-start(f32[3,3,256]{2,1,0:T(4,128)} %param.10) | copy-start | bytes 27652
  10.8 12.2 %all-to-all-start.1 = ((f32[1,256,256]{2,0,1:T(1,128)}), f32[1,256,256]{2,0,1:T(1,128)S(1)}, u32[]{:S(2)}, u32[]{:S(2)}) async-start(f32[1,256,256]{2,0,1:T(1,128)} %bitcast.32), calls=%async_computation.1 | async-start | bytes 524288 | tf_op jit(solution)/shard_map/all_to_all | solution.py:62
  23.1 22.2 %copy-start.3 = (bf16[256,1024]{1,0:T(8,128)(2,1)S(1)}, bf16[256,1024]{1,0:T(8,128)(2,1)}, u32[]{:S(2)}) copy-start(bf16[256,1024]{1,0:T(8,128)(2,1)} %param.13) | copy-start | bytes 1572868
  42.2 3.0 %copy-start.10 = (bf16[512,1024]{1,0:T(8,128)(2,1)S(1)}, bf16[512,1024]{1,0:T(8,128)(2,1)}, u32[]{:S(2)}) copy-start(bf16[512,1024]{1,0:T(8,128)(2,1)} %all-gather.2.cloned.1.call-done) | copy-start | bytes 3145732
  43.9 2.1 %collective-permute-start = (bf16[3,2,256]{2,1,0:T(2,128)(2,1)S(1)}, bf16[3,2,256]{2,1,0:T(2,128)(2,1)S(1)}, u32[]{:S(2)}, u32[]{:S(2)}) collective-permute-start(bf16[3,2,256]{2,1,0:T(2,128)(2,1)S(1)} %slice.120), channel_id=1, source_target_pairs={{0,4},{4,8},{8,12},{12,16},{16,20},{20,24},{24,28},{1,5},{5,9},{9,... | collective-permute-start | bytes 9224 | tf_op jit(solution)/shard_map/ppermute | solution.py:16
  45.6 0.8 copy-start.1
  49.4 15.6 %all-to-all-start = ((f32[2,256,256]{2,0,1:T(2,128)}), f32[2,256,256]{2,0,1:T(2,128)}, u32[]{:S(2)}, u32[]{:S(2)}) async-start(f32[2,256,256]{2,0,1:T(2,128)} %copy.32), calls=%async_computation | async-start | bytes 1048576 | tf_op jit(solution)/shard_map/all_to_all | solution.py:62
  55.1 60.3 %reduce-scatter.3.cloned.1.call-start = ((), (), s32[]{:S(2)}) async-start(), calls=%async_computation.6 | async-start | bytes 655360 | tf_op jit(solution)/shard_map/reduce_scatter | solution.py:137
  55.3 1.0 copy-start.4
  55.3 1.2 copy-start.6
  68.2 1.0 copy-start.5
  68.2 1.2 copy-start.7
  72.5 1.0 copy-start.8
  72.5 1.2 copy-start.9
  78.0 15.2 %copy-start.2 = (f32[256,256]{1,0:T(8,128)S(1)}, f32[256,256]{1,0:T(8,128)}, u32[]{:S(2)}) copy-start(f32[256,256]{1,0:T(8,128)} %copy-done.1) | copy-start | bytes 786436
  78.0 15.2 %copy-start.12 = (f32[256]{0:T(256)S(1)}, f32[256]{0:T(256)}, u32[]{:S(2)}) copy-start(f32[256]{0:T(256)} %param.11) | copy-start | bytes 3076
  96.6 41.9 %reduce-scatter.5.cloned.1.call-start = ((), (), s32[]{:S(2)}) async-start(), calls=%async_computation.7 | async-start | bytes 655360 | tf_op jit(solution)/shard_map/reduce_scatter | solution.py:156
  96.8 3.1 %collective-permute-start.1 = (f32[3,2,256]{2,1,0:T(2,128)S(1)}, f32[3,2,256]{2,1,0:T(2,128)S(1)}, u32[]{:S(2)}, u32[]{:S(2)}) collective-permute-start(f32[3,2,256]{2,1,0:T(2,128)S(1)} %slice.142), channel_id=1, source_target_pairs={{4,0},{8,4},{12,8},{16,12},{20,16},{24,20},{28,24},{5,1},{9,5},{13... | collective-permute-start | bytes 18440 | tf_op jit(solution)/shard_map/ppermute | solution.py:16
Sparse Core Ops, SparseCore 0:
  9.5 32.6 all-gather.1
  96.7 18.6 reduce-scatter.2
  118.3 20.1 reduce-scatter.4

commit v3 on v2

--- a/solution.py
+++ b/solution.py
@@ -14,6 +14,31 @@
     count = lax.axis_size(axis)
     initial, last = (max(0, -steps), min(count, count - steps))
     return lax.ppermute(value, axis, [(source, source + steps) for source in range(initial, last)])
+
+
+def panel_gather(value):
+    count = lax.axis_size("panel")
+    me = lax.axis_index("panel")
+    parts = [value] + [
+        lax.ppermute(value, "panel", [(i, (i + k) % count) for i in range(count)])
+        for k in range(count - 1, 0, -1)
+    ]
+    ordered = jnp.roll(jnp.stack(parts), me, axis=0)
+    return jnp.concatenate([ordered[i] for i in range(count)], axis=-1)
+
+
+def panel_reduce_scatter(value):
+    count = lax.axis_size("panel")
+    me = lax.axis_index("panel")
+    rows, cols = value.shape
+    blocks = jnp.roll(value.reshape(rows, count, cols // count), -me, axis=1)
+    total = blocks[:, 0]
+    for k in range(1, count):
+        sent = blocks[:, k].astype(jnp.bfloat16)
+        total = total + lax.ppermute(
+            sent, "panel", [(i, (i + k) % count) for i in range(count)]
+        ).astype(jnp.float32)
+    return total.astype(jnp.bfloat16)
 
 
 def phase(numer, period):
@@ -91,9 +116,7 @@
     shard_count = lax.axis_size("seq")
     tables = transform_tables(shard_count, row_count)
     filt_spec = forward_spectrum(to_columns(long_filter[None]), tables)
-    both = lax.all_gather(
-        jnp.concatenate([tokens, cotangent], axis=0), "panel", axis=1, tiled=True
-    )
+    both = panel_gather(jnp.concatenate([tokens, cotangent], axis=0))
     full_tok, full_cot = both[:row_count], both[row_count:]
     projected = jnp.einsum(
         "td,jdc->jtc", full_tok, in_weight, preferred_element_type=jnp.float32
@@ -134,9 +157,7 @@
     grad_signal = convolved[1] + skip_gain[None, :] * grad_state
     gated_state = (conv_state * gate_out).astype(jnp.bfloat16)
     partial_value = jnp.dot(gated_state, out_weight, preferred_element_type=jnp.float32)
-    block_out = lax.psum_scatter(
-        partial_value.astype(jnp.bfloat16), "panel", scatter_dimension=1, tiled=True
-    )
+    block_out = panel_reduce_scatter(partial_value)
     grad_gate_out = grad_gated * conv_state
     grad_value = grad_signal * gate_in
     grad_gate_in = grad_signal * value_path
@@ -153,9 +174,7 @@
     grad_partial = jnp.einsum(
         "jtc,jdc->td", grad_projected, in_weight, preferred_element_type=jnp.float32
     )
-    token_grad = lax.psum_scatter(
-        grad_partial.astype(jnp.bfloat16), "panel", scatter_dimension=1, tiled=True
-    )
+    token_grad = panel_reduce_scatter(grad_partial)
     return (block_out, token_grad)
 
 

time: 146 us -> 123 us (0.84)
  waiting for transfers between devices: 67.8 us -> 35.4 us
  starting transfers between devices: 13.9 us -> 39.2 us
  local copies, waits for them, and re-layouts: 10 us -> 23.8 us
  between operations: 14.1 us -> 1.2 us
  blocking collectives: 12.1 us -> 0 us
  matrix products: 17.3 us -> 13.6 us
    reduce_scatter x2 -> x0, waiting for transfers between devices: 37.1 us -> none  [the longest x1 23 us: local(): lax.psum_scatter(grad_partial.astype(jnp.bfloat16), 'panel', scatter_dime...]
    ppermute x0 -> x9, starting transfers between devices: none -> 21.9 us  [the longest x6 15.7 us: panel_reduce_scatter(): lax.ppermute(sent, 'panel', [(i, (i + k) % count) for i in range(count)])]
    all_gather x1 -> x0, waiting for transfers between devices: 18.1 us -> none  [local(): lax.all_gather(jnp.concatenate([tokens, cotangent], axis=0), 'panel', axi...]
    ppermute x0 -> x9, waiting for transfers between devices: none -> 16.7 us  [the longest x6 9.53 us: panel_reduce_scatter(): lax.ppermute(sent, 'panel', [(i, (i + k) % count) for i in range(count)])]
    all_to_all x1 -> x0, blocking collectives: 12.1 us -> none  [to_rows(): lax.all_to_all(columns, 'seq', split_axis=2, concat_axis=1, tiled=True)]
    all_to_all x0 -> x1, waiting for transfers between devices: none -> 8.47 us  [to_rows(): lax.all_to_all(columns, 'seq', split_axis=2, concat_axis=1, tiled=True)]
    unnamed x27 -> x41, local copies, waits for them, and re-layouts: 3.08 us -> 10.8 us
    all_to_all x0 -> x1, starting transfers between devices: none -> 4.49 us  [to_rows(): lax.all_to_all(columns, 'seq', split_axis=2, concat_axis=1, tiled=True)]
  transfers between devices with their start and end apart: 7 -> 14, of which waited for: 7 -> 7; matrix products, arithmetic and copies ran while one was open for 7% -> 11% of each run, Pallas kernels for 0% -> 0%
where the time goes in v3:
time: 123 us; the launch traced here: 122 us
  starting transfers between devices  39.2 us (32%)
  waiting for transfers between devices  35.4 us (29%)
  local copies, waits for them, and re-layouts  23.8 us (19%)
  matrix products  13.6 us (11%)
  other arithmetic  8.95 us (7%)
    ppermute x6, starting transfers between devices, panel_reduce_scatter(): lax.ppermute(sent, 'panel', [(i, (i + k) % count) for i in range(count)])  15.7 us
    unnamed x41, local copies, waits for them, and re-layouts  10.8 us
    all_to_all x2, starting transfers between devices, to_columns(): lax.all_to_all(jnp.swapaxes(rows, 1, 2), 'seq', split_axis=1, concat_axis...  10.3 us
    all_to_all x2, waiting for transfers between devices, to_columns(): lax.all_to_all(jnp.swapaxes(rows, 1, 2), 'seq', split_axis=1, concat_axis...  9.82 us
    ppermute x6, waiting for transfers between devices, panel_reduce_scatter(): lax.ppermute(sent, 'panel', [(i, (i + k) % count) for i in range(count)])  9.53 us
    all_to_all x1, waiting for transfers between devices, to_rows(): lax.all_to_all(columns, 'seq', split_axis=2, concat_axis=1, tiled=True)  8.47 us
    ppermute x3, waiting for transfers between devices, panel_gather(): lax.ppermute(value, 'panel', [(i, (i + k) % count) for i in range(count)])  7.13 us
    ppermute x3, starting transfers between devices, panel_gather(): lax.ppermute(value, 'panel', [(i, (i + k) % count) for i in range(count)])  6.14 us
  transfers between devices with their start and end apart: 14, of which 7 were waited for; matrix products, arithmetic and copies ran while one was open for 11% of the time, Pallas kernels for 0%

profile of v3, /device:TPU:0, one launch (start us, length us, event | category | flops | bytes accessed | tf_op | source)
XLA Modules:
  0.0 122.1 jit_solution(12282239528709550268)
XLA Ops:
  0.7 1.0 constant_dynamic-update-slice_fusion.1
  1.7 0.9 constant_dynamic-update-slice_fusion
  2.6 5.1 %collective-permute-start = (bf16[512,256]{1,0:T(8,128)(2,1)S(1)}, bf16[512,256]{1,0:T(8,128)(2,1)S(1)}, u32[]{:S(2)}, u32[]{:S(2)}) collective-permute-start(bf16[512,256]{1,0:T(8,128)(2,1)S(1)} %constant_dynamic-update-slice_fusion), channel_id=1, source_target_pairs={{0,3},{1,0},{2,1},{3,2},{4,7},{5,4},{6,5},{7,6},{8,11},{9,8},{10,9... | collective-permute-start | bytes 786440 | tf_op jit(solution)/shard_map/ppermute | solution.py:23
  7.7 1.0 collective-permute-start.2
  8.8 1.8 %copy.72 = f32[1,256,256]{1,0,2:T(1,128)} copy(f32[1,256,256]{2,1,0:T(8,128)} %bitcast.238) | data formatting | bytes 524288 | tf_op jit(solution)/shard_map/broadcast_in_dim | solution.py:118
  10.6 3.7 %all-to-all-start.1 = ((f32[1,256,256]{2,0,1:T(1,128)}), f32[1,256,256]{2,0,1:T(1,128)S(1)}, u32[]{:S(2)}, u32[]{:S(2)}) async-start(f32[1,256,256]{2,0,1:T(1,128)} %bitcast.40), calls=%async_computation.1 | async-start | bytes 524288 | tf_op jit(solution)/shard_map/all_to_all | solution.py:87
  14.3 0.7 bitcast_dynamic-update-slice_fusion.6
  15.2 1.0 fusion.74
  16.4 1.0 fusion.76
  17.4 1.5 %fusion.35 = (f32[1,256,2,256]{3,1,2,0:T(8,128)}, f32[1,256,2,256]{3,1,0,2:T(8,128)}, f32[1,256,2,256]{3,1,0,2:T(8,128)}, f32[1,256,2,256]{3,1,2,0:T(8,128)}) fusion(f32[256,1,256]{2,0,1:T(8,128)S(1)} %get-tuple-element.45, f32[256,1,256]{2,0,1:T(8,128)S(1)} %fusion.76, f32[256,1,256]{2,0,1:T(8,128)S(1)} %get-tuple-element.44), kind=kLoop, calls=%fused_computation.59 | loop fusion | flops 524288 | bytes 2883584 | tf_op jit(solution)/shard_map/stack | solution.py:68
  18.8 2.3 %all-to-all-done.1 = f32[1,256,256]{2,0,1:T(1,128)S(1)} async-done(((f32[1,256,256]{2,0,1:T(1,128)}), f32[1,256,256]{2,0,1:T(1,128)S(1)}, u32[]{:S(2)}, u32[]{:S(2)}) %all-to-all-start.1) | async-done | bytes 262176 | tf_op jit(solution)/shard_map/all_to_all | solution.py:87
  21.2 1.0 convolution_bitcast_fusion.2
  22.2 0.7 bitcast_dynamic-update-slice_fusion.4
  22.9 7.1 %collective-permute-done.1 = bf16[512,256]{1,0:T(8,128)(2,1)S(1)} collective-permute-done((bf16[512,256]{1,0:T(8,128)(2,1)S(1)}, bf16[512,256]{1,0:T(8,128)(2,1)S(1)}, u32[]{:S(2)}, u32[]{:S(2)}) %collective-permute-start.1) | collective-permute-done | bytes 262176 | tf_op jit(solution)/shard_map/ppermute | solution.py:23
  30.1 0.7 bitcast_dynamic-update-slice_fusion.2
  30.8 1.7 %bitcast_dynamic-update-slice_fusion = bf16[8,512,256]{2,1,0:T(8,128)(2,1)} fusion(bf16[8,512,256]{2,1,0:T(8,128)(2,1)} %bitcast_dynamic-update-slice_fusion.2, bf16[512,256]{1,0:T(8,128)(2,1)} %collective-permute-done.2), kind=kLoop, calls=%fused_computation.112 | loop fusion | bytes 524288
  32.5 0.7 bitcast_dynamic-update-slice_fusion.7
  33.2 0.7 bitcast_dynamic-update-slice_fusion.5
  33.9 0.7 bitcast_dynamic-update-slice_fusion.3
  34.7 1.7 %bitcast_dynamic-update-slice_fusion.1 = bf16[8,512,256]{2,1,0:T(8,128)(2,1)} fusion(bf16[8,512,256]{2,1,0:T(8,128)(2,1)} %bitcast_dynamic-update-slice_fusion.3, bf16[512,256]{1,0:T(8,128)(2,1)} %collective-permute-done.2), kind=kLoop, calls=%fused_computation.113 | loop fusion | bytes 524288 | tf_op jit(solution)/shard_map/jit(_roll_dynamic)/concatenate | solution.py:26
  36.3 1.3 %dynamic-slice_bitcast_fusion.3 = (bf16[512,256]{1,0:T(8,128)(2,1)S(1)}, bf16[512,256]{1,0:T(8,128)(2,1)S(1)}, bf16[512,256]{1,0:T(8,128)(2,1)S(1)}, bf16[512,256]{1,0:T(8,128)(2,1)S(1)}) fusion(bf16[8,512,256]{2,1,0:T(8,128)(2,1)} %bitcast_dynamic-update-slice_fusion.1, s32[]{:T(128)S(6)} %select_n.112, s32[]{:T(128)S(6)} %add.325, s32[]{:T(128)S(6)} %add.324, ...), kind=kLoop, calls=%fused_computation.100 | loop fusion | bytes 2097168 | tf_op jit(solution)/shard_map/squeeze | solution.py:27
  38.3 1.3 %collective-permute-start.3 = (bf16[3,2,256]{2,1,0:T(2,128)(2,1)S(1)}, bf16[3,2,256]{2,1,0:T(2,128)(2,1)S(1)}, u32[]{:S(2)}, u32[]{:S(2)}) collective-permute-start(bf16[3,2,256]{2,1,0:T(2,128)(2,1)S(1)} %slice.174), channel_id=1, source_target_pairs={{0,4},{4,8},{8,12},{12,16},{16,20},{20,24},{24,28},{1,5},{5,9},{9,... | collective-permute-start | bytes 9224 | tf_op jit(solution)/shard_map/ppermute | solution.py:16
  41.5 0.9 maximum_bitcast_fusion.4
  42.4 2.0 %copy.38 = f32[2,256,256]{2,0,1:T(2,128)} copy(f32[2,256,256]{1,2,0:T(8,128)} %maximum_bitcast_fusion.4) | data formatting | bytes 1048576 | tf_op jit(solution)/shard_map/transpose | solution.py:88
  44.4 6.5 %all-to-all-start = ((f32[2,256,256]{2,0,1:T(2,128)}), f32[2,256,256]{2,0,1:T(2,128)}, u32[]{:S(2)}, u32[]{:S(2)}) async-start(f32[2,256,256]{2,0,1:T(2,128)} %copy.38), calls=%async_computation | async-start | bytes 1048576 | tf_op jit(solution)/shard_map/all_to_all | solution.py:87
  51.2 0.8 copy-done.8
  52.2 1.1 convolution_bitcast_fusion.1
  53.3 7.5 %all-to-all-done = f32[2,256,256]{2,0,1:T(2,128)} async-done(((f32[2,256,256]{2,0,1:T(2,128)}), f32[2,256,256]{2,0,1:T(2,128)}, u32[]{:S(2)}, u32[]{:S(2)}) %all-to-all-start) | async-done | bytes 524320 | tf_op jit(solution)/shard_map/all_to_all | solution.py:87
  60.8 2.9 %convolution_bitcast_fusion = f32[2,32,2,2,8,256]{5,4,3,2,1,0:T(8,128)S(1)} fusion(f32[2,8,32,256]{3,0,2,1:T(2,128)} %bitcast.24, f32[2,1,8,8]{3,2,1,0:T(8,128)S(1)} %get-tuple-element.43, f32[2,1,8,8]{3,2,1,0:T(8,128)S(1)} %get-tuple-element.42), kind=kOutput, calls=%fused_computation.18 | convolution fusion | flops 50331904 | bytes 2622464 | tf_op jit(solution)/shard_map/erkp,bcpm->bcerkm/dot_general | solution.py:101
  64.3 0.8 copy-done.9
  65.3 2.7 %fusion.10 = f32[2,32,2,2,8,256]{5,1,4,2,0,3:T(8,128)S(1)} fusion(f32[2,32,2,2,8,256]{5,4,3,2,1,0:T(8,128)S(1)} %pad_maximum_fusion, f32[1,256,2,256]{3,1,0,2:T(8,128)S(1)} %copy-done.9, f32[1,256,2,256]{3,1,0,2:T(8,128)S(1)} %copy-done.11), kind=kOutput, calls=%fused_computation.16 | convolution fusion | flops 1610874880 | bytes 5242880 | tf_op jit(solution)/shard_map/bcerkm,rmsq->bceskq/dot_general | solution.py:103
  68.6 0.9 copy-done.12
  69.6 2.7 %fusion.13 = f32[2,32,2,2,8,256]{5,4,3,2,1,0:T(8,128)S(1)} fusion(f32[2,32,2,2,8,256,1]{5,1,4,2,0,3,6:T(8,128)S(1)} %maximum_bitcast_fusion, f32[1,256,2,256]{3,1,2,0:T(8,128)S(1)} %copy-done.13, f32[1,256,2,256]{3,1,2,0:T(8,128)S(1)} %copy-done.12), kind=kOutput, calls=%fused_computation.17 | convolution fusion | flops 1610874880 | bytes 5242880 | tf_op jit(solution)/shard_map/bceskq,sqrm->bcerkm/dot_general | solution.py:108
  72.7 1.2 fusion.16
  73.9 1.0 copy.49
  74.9 4.5 %all-to-all-start.2 = ((f32[2,32,8,256]{3,1,0,2:T(8,128)}), f32[2,32,8,256]{3,1,0,2:T(8,128)}, u32[]{:S(2)}, u32[]{:S(2)}) async-start(f32[2,32,8,256]{3,1,0,2:T(8,128)} %copy.49), calls=%async_computation.2 | async-start | bytes 1048576 | tf_op jit(solution)/shard_map/all_to_all | solution.py:95
  79.4 1.0 copy.77
  80.4 8.5 %all-to-all-done.2 = f32[2,32,8,256]{3,1,0,2:T(8,128)} async-done(((f32[2,32,8,256]{3,1,0,2:T(8,128)}), f32[2,32,8,256]{3,1,0,2:T(8,128)}, u32[]{:S(2)}, u32[]{:S(2)}) %all-to-all-start.2) | async-done | bytes 524320 | tf_op jit(solution)/shard_map/all_to_all | solution.py:95
  88.9 1.9 %copy.50 = f32[2,32,8,256]{3,1,2,0:T(8,128)} copy(f32[2,32,8,256]{3,1,0,2:T(8,128)} %all-to-all-done.2) | data formatting | bytes 1048576 | tf_op jit(solution)/shard_map/all_to_all | solution.py:95
  90.8 1.2 %copy.51 = f32[2,256,256]{1,2,0:T(8,128)S(1)} copy(f32[2,256,256]{2,1,0:T(8,128)} %bitcast.234) | data formatting | bytes 1048576 | tf_op jit(solution)/shard_map/reshape | solution.py:96
  92.3 1.3 %collective-permute-start.7 = (f32[3,2,256]{2,1,0:T(2,128)S(1)}, f32[3,2,256]{2,1,0:T(2,128)S(1)}, u32[]{:S(2)}, u32[]{:S(2)}) collective-permute-start(f32[3,2,256]{2,1,0:T(2,128)S(1)} %slice.200), channel_id=1, source_target_pairs={{4,0},{8,4},{12,8},{16,12},{20,16},{24,20},{28,24},{5,1},{9,5},{13... | collective-permute-start | bytes 18440 | tf_op jit(solution)/shard_map/ppermute | solution.py:16
  94.5 2.1 %collective-permute-start.5 = (bf16[256,256]{1,0:T(8,128)(2,1)S(1)}, bf16[256,256]{1,0:T(8,128)(2,1)S(1)}, u32[]{:S(2)}, u32[]{:S(2)}) collective-permute-start(bf16[256,256]{1,0:T(8,128)(2,1)S(1)} %get-tuple-element.29), channel_id=1, source_target_pairs={{0,2},{1,3},{2,0},{3,1},{4,6},{5,7},{6,4},{7,5},{8,10},{9,11},{10,... | collective-permute-start | bytes 393224 | tf_op jit(solution)/shard_map/ppermute | solution.py:38
  96.6 2.8 %collective-permute-start.6 = (bf16[256,256]{1,0:T(8,128)(2,1)S(1)}, bf16[256,256]{1,0:T(8,128)(2,1)S(1)}, u32[]{:S(2)}, u32[]{:S(2)}) collective-permute-start(bf16[256,256]{1,0:T(8,128)(2,1)S(1)} %get-tuple-element.28), channel_id=1, source_target_pairs={{0,3},{1,0},{2,1},{3,2},{4,7},{5,4},{6,5},{7,6},{8,11},{9,8},{10,9... | collective-permute-start | bytes 393224 | tf_op jit(solution)/shard_map/ppermute | solution.py:38
  100.6 2.0 %collective-permute-start.8 = (bf16[256,256]{1,0:T(8,128)(2,1)S(1)}, bf16[256,256]{1,0:T(8,128)(2,1)S(1)}, u32[]{:S(2)}, u32[]{:S(2)}) collective-permute-start(bf16[256,256]{1,0:T(8,128)(2,1)S(1)} %get-tuple-element.24), channel_id=1, source_target_pairs={{0,1},{1,2},{2,3},{3,0},{4,5},{5,6},{6,7},{7,4},{8,9},{9,10},{10,1... | collective-permute-start | bytes 393224 | tf_op jit(solution)/shard_map/ppermute | solution.py:38
  102.6 8.5 %collective-permute-start.9 = (bf16[256,256]{1,0:T(8,128)(2,1)S(1)}, bf16[256,256]{1,0:T(8,128)(2,1)S(1)}, u32[]{:S(2)}, u32[]{:S(2)}) collective-permute-start(bf16[256,256]{1,0:T(8,128)(2,1)S(1)} %get-tuple-element.26), channel_id=1, source_target_pairs={{0,2},{1,3},{2,0},{3,1},{4,6},{5,7},{6,4},{7,5},{8,10},{9,11},{10,... | collective-permute-start | bytes 393224 | tf_op jit(solution)/shard_map/ppermute | solution.py:38
  111.1 0.7 fusion.58
  111.9 1.9 %collective-permute-done.8 = bf16[256,256]{1,0:T(8,128)(2,1)S(1)} collective-permute-done((bf16[256,256]{1,0:T(8,128)(2,1)S(1)}, bf16[256,256]{1,0:T(8,128)(2,1)S(1)}, u32[]{:S(2)}, u32[]{:S(2)}) %collective-permute-start.8) | collective-permute-done | bytes 131104 | tf_op jit(solution)/shard_map/ppermute | solution.py:38
  113.7 7.6 %collective-permute-done.9 = bf16[256,256]{1,0:T(8,128)(2,1)S(1)} collective-permute-done((bf16[256,256]{1,0:T(8,128)(2,1)S(1)}, bf16[256,256]{1,0:T(8,128)(2,1)S(1)}, u32[]{:S(2)}, u32[]{:S(2)}) %collective-permute-start.9) | collective-permute-done | bytes 131104 | tf_op jit(solution)/shard_map/ppermute | solution.py:38
  (77 shorter events, 7.9 us)
Async XLA Ops:
  0.6 37.1 %copy-start = (bf16[3,1024,256]{2,1,0:T(8,128)(2,1)S(1)}, bf16[3,1024,256]{2,1,0:T(8,128)(2,1)}, u32[]{:S(2)}) copy-start(bf16[3,1024,256]{2,1,0:T(8,128)(2,1)} %param.11) | copy-start | bytes 4718596
  0.6 15.6 %copy-start.14 = (f32[3,3,256]{2,1,0:T(4,128)S(1)}, f32[3,3,256]{2,1,0:T(4,128)}, u32[]{:S(2)}) copy-start(f32[3,3,256]{2,1,0:T(4,128)} %param.12) | copy-start | bytes 27652
  2.6 19.6 %collective-permute-start = (bf16[512,256]{1,0:T(8,128)(2,1)S(1)}, bf16[512,256]{1,0:T(8,128)(2,1)S(1)}, u32[]{:S(2)}, u32[]{:S(2)}) collective-permute-start(bf16[512,256]{1,0:T(8,128)(2,1)S(1)} %constant_dynamic-update-slice_fusion), channel_id=1, source_target_pairs={{0,3},{1,0},{2,1},{3,2},{4,7},{5,4},{6,5},{7,6},{8,11},{9,8},{10,9... | collective-permute-start | bytes 786440 | tf_op jit(solution)/shard_map/ppermute | solution.py:23
  7.7 22.3 %collective-permute-start.1 = (bf16[512,256]{1,0:T(8,128)(2,1)S(1)}, bf16[512,256]{1,0:T(8,128)(2,1)S(1)}, u32[]{:S(2)}, u32[]{:S(2)}) collective-permute-start(bf16[512,256]{1,0:T(8,128)(2,1)S(1)} %constant_dynamic-update-slice_fusion), channel_id=1, source_target_pairs={{0,2},{1,3},{2,0},{3,1},{4,6},{5,7},{6,4},{7,5},{8,10},{9,11},{10,... | collective-permute-start | bytes 786440 | tf_op jit(solution)/shard_map/ppermute | solution.py:23
  7.7 23.0 %collective-permute-start.2 = (bf16[512,256]{1,0:T(8,128)(2,1)S(1)}, bf16[512,256]{1,0:T(8,128)(2,1)}, u32[]{:S(2)}, u32[]{:S(2)}) collective-permute-start(bf16[512,256]{1,0:T(8,128)(2,1)S(1)} %constant_dynamic-update-slice_fusion), channel_id=1, source_target_pairs={{0,1},{1,2},{2,3},{3,0},{4,5},{5,6},{6,7},{7,4},{8,9},{9,10},{10,1... | collective-permute-start | bytes 786440 | tf_op jit(solution)/shard_map/ppermute | solution.py:23
  10.6 10.6 %all-to-all-start.1 = ((f32[1,256,256]{2,0,1:T(1,128)}), f32[1,256,256]{2,0,1:T(1,128)S(1)}, u32[]{:S(2)}, u32[]{:S(2)}) async-start(f32[1,256,256]{2,0,1:T(1,128)} %bitcast.40), calls=%async_computation.1 | async-start | bytes 524288 | tf_op jit(solution)/shard_map/all_to_all | solution.py:87
  37.6 2.1 %copy-start.5 = (bf16[256,1024]{1,0:T(8,128)(2,1)S(1)}, bf16[256,1024]{1,0:T(8,128)(2,1)}, u32[]{:S(2)}) copy-start(bf16[256,1024]{1,0:T(8,128)(2,1)} %param.15) | copy-start | bytes 1572868
  38.3 2.1 %collective-permute-start.3 = (bf16[3,2,256]{2,1,0:T(2,128)(2,1)S(1)}, bf16[3,2,256]{2,1,0:T(2,128)(2,1)S(1)}, u32[]{:S(2)}, u32[]{:S(2)}) collective-permute-start(bf16[3,2,256]{2,1,0:T(2,128)(2,1)S(1)} %slice.174), channel_id=1, source_target_pairs={{0,4},{4,8},{8,12},{12,16},{16,20},{20,24},{24,28},{1,5},{5,9},{9,... | collective-permute-start | bytes 9224 | tf_op jit(solution)/shard_map/ppermute | solution.py:16
  40.0 0.8 copy-start.1
  40.8 0.7 copy-start.3
  44.4 16.4 %all-to-all-start = ((f32[2,256,256]{2,0,1:T(2,128)}), f32[2,256,256]{2,0,1:T(2,128)}, u32[]{:S(2)}, u32[]{:S(2)}) async-start(f32[2,256,256]{2,0,1:T(2,128)} %copy.38), calls=%async_computation | async-start | bytes 1048576 | tf_op jit(solution)/shard_map/all_to_all | solution.py:87
  51.0 1.0 copy-start.8
  51.0 1.2 copy-start.10
  64.1 1.0 copy-start.9
  64.1 1.2 copy-start.11
  68.4 1.0 copy-start.12
  68.4 1.2 copy-start.13
  72.7 6.7 %copy-start.6 = (bf16[256,1024]{1,0:T(8,128)(2,1)S(1)}, bf16[256,1024]{1,0:T(8,128)(2,1)}, u32[]{:S(2)}) copy-start(bf16[256,1024]{1,0:T(8,128)(2,1)} %param.15) | copy-start | bytes 1572868
  74.9 17.1 %copy-start.2 = (f32[256,256]{1,0:T(8,128)S(1)}, f32[256,256]{1,0:T(8,128)}, u32[]{:S(2)}) copy-start(f32[256,256]{1,0:T(8,128)} %copy-done.1) | copy-start | bytes 786436
  74.9 17.2 %copy-start.15 = (f32[256]{0:T(256)S(1)}, f32[256]{0:T(256)}, u32[]{:S(2)}) copy-start(f32[256]{0:T(256)} %param.13) | copy-start | bytes 3076
  74.9 14.0 %all-to-all-start.2 = ((f32[2,32,8,256]{3,1,0,2:T(8,128)}), f32[2,32,8,256]{3,1,0,2:T(8,128)}, u32[]{:S(2)}, u32[]{:S(2)}) async-start(f32[2,32,8,256]{3,1,0,2:T(8,128)} %copy.49), calls=%async_computation.2 | async-start | bytes 1048576 | tf_op jit(solution)/shard_map/all_to_all | solution.py:95
  92.1 1.6 %copy-start.4 = (f32[1,256,256]{2,1,0:T(8,128)S(1)}, f32[1,256,256]{2,1,0:T(8,128)}, u32[]{:S(2)}) copy-start(f32[1,256,256]{2,1,0:T(8,128)} %copy-done.3) | copy-start | bytes 786436
  92.1 1.6 %copy-start.7 = (bf16[1024,256]{1,0:T(8,128)(2,1)S(1)}, bf16[1024,256]{1,0:T(8,128)(2,1)}, u32[]{:S(2)}) copy-start(bf16[1024,256]{1,0:T(8,128)(2,1)} %copy.77) | copy-start | bytes 1572868
  92.3 7.1 %collective-permute-start.7 = (f32[3,2,256]{2,1,0:T(2,128)S(1)}, f32[3,2,256]{2,1,0:T(2,128)S(1)}, u32[]{:S(2)}, u32[]{:S(2)}) collective-permute-start(f32[3,2,256]{2,1,0:T(2,128)S(1)} %slice.200), channel_id=1, source_target_pairs={{4,0},{8,4},{12,8},{16,12},{20,16},{24,20},{28,24},{5,1},{9,5},{13... | collective-permute-start | bytes 18440 | tf_op jit(solution)/shard_map/ppermute | solution.py:16
  94.3 8.3 %collective-permute-start.4 = (bf16[256,256]{1,0:T(8,128)(2,1)S(1)}, bf16[256,256]{1,0:T(8,128)(2,1)S(1)}, u32[]{:S(2)}, u32[]{:S(2)}) collective-permute-start(bf16[256,256]{1,0:T(8,128)(2,1)S(1)} %get-tuple-element.27), channel_id=1, source_target_pairs={{0,1},{1,2},{2,3},{3,0},{4,5},{5,6},{6,7},{7,4},{8,9},{9,10},{10,1... | collective-permute-start | bytes 393224 | tf_op jit(solution)/shard_map/ppermute | solution.py:38
  94.5 16.7 %collective-permute-start.5 = (bf16[256,256]{1,0:T(8,128)(2,1)S(1)}, bf16[256,256]{1,0:T(8,128)(2,1)S(1)}, u32[]{:S(2)}, u32[]{:S(2)}) collective-permute-start(bf16[256,256]{1,0:T(8,128)(2,1)S(1)} %get-tuple-element.29), channel_id=1, source_target_pairs={{0,2},{1,3},{2,0},{3,1},{4,6},{5,7},{6,4},{7,5},{8,10},{9,11},{10,... | collective-permute-start | bytes 393224 | tf_op jit(solution)/shard_map/ppermute | solution.py:38
  96.6 14.6 %collective-permute-start.6 = (bf16[256,256]{1,0:T(8,128)(2,1)S(1)}, bf16[256,256]{1,0:T(8,128)(2,1)S(1)}, u32[]{:S(2)}, u32[]{:S(2)}) collective-permute-start(bf16[256,256]{1,0:T(8,128)(2,1)S(1)} %get-tuple-element.28), channel_id=1, source_target_pairs={{0,3},{1,0},{2,1},{3,2},{4,7},{5,4},{6,5},{7,6},{8,11},{9,8},{10,9... | collective-permute-start | bytes 393224 | tf_op jit(solution)/shard_map/ppermute | solution.py:38
  100.5 11.4 %collective-permute-start.10 = (bf16[256,256]{1,0:T(8,128)(2,1)S(1)}, bf16[256,256]{1,0:T(8,128)(2,1)S(1)}, u32[]{:S(2)}, u32[]{:S(2)}) collective-permute-start(bf16[256,256]{1,0:T(8,128)(2,1)S(1)} %get-tuple-element.25), channel_id=1, source_target_pairs={{0,3},{1,0},{2,1},{3,2},{4,7},{5,4},{6,5},{7,6},{8,11},{9,8},{10,9... | collective-permute-start | bytes 393224 | tf_op jit(solution)/shard_map/ppermute | solution.py:38
  100.6 13.2 %collective-permute-start.8 = (bf16[256,256]{1,0:T(8,128)(2,1)S(1)}, bf16[256,256]{1,0:T(8,128)(2,1)S(1)}, u32[]{:S(2)}, u32[]{:S(2)}) collective-permute-start(bf16[256,256]{1,0:T(8,128)(2,1)S(1)} %get-tuple-element.24), channel_id=1, source_target_pairs={{0,1},{1,2},{2,3},{3,0},{4,5},{5,6},{6,7},{7,4},{8,9},{9,10},{10,1... | collective-permute-start | bytes 393224 | tf_op jit(solution)/shard_map/ppermute | solution.py:38
  102.6 18.8 %collective-permute-start.9 = (bf16[256,256]{1,0:T(8,128)(2,1)S(1)}, bf16[256,256]{1,0:T(8,128)(2,1)S(1)}, u32[]{:S(2)}, u32[]{:S(2)}) collective-permute-start(bf16[256,256]{1,0:T(8,128)(2,1)S(1)} %get-tuple-element.26), channel_id=1, source_target_pairs={{0,2},{1,3},{2,0},{3,1},{4,6},{5,7},{6,4},{7,5},{8,10},{9,11},{10,... | collective-permute-start | bytes 393224 | tf_op jit(solution)/shard_map/ppermute | solution.py:38

commit v4 on v3

--- a/solution.py
+++ b/solution.py
@@ -16,25 +16,22 @@
     return lax.ppermute(value, axis, [(source, source + steps) for source in range(initial, last)])
 
 
-def panel_gather(value):
+def panel_parts(value):
     count = lax.axis_size("panel")
     me = lax.axis_index("panel")
-    parts = [value] + [
-        lax.ppermute(value, "panel", [(i, (i + k) % count) for i in range(count)])
-        for k in range(count - 1, 0, -1)
-    ]
-    ordered = jnp.roll(jnp.stack(parts), me, axis=0)
-    return jnp.concatenate([ordered[i] for i in range(count)], axis=-1)
-
-
-def panel_reduce_scatter(value):
+    parts = [(value, me)]
+    for k in range(1, count):
+        moved = lax.ppermute(value, "panel", [(i, (i + k) % count) for i in range(count)])
+        parts.append((moved, (me + count - k) % count))
+    return parts
+
+
+def panel_reduce_scatter(block_of):
     count = lax.axis_size("panel")
     me = lax.axis_index("panel")
-    rows, cols = value.shape
-    blocks = jnp.roll(value.reshape(rows, count, cols // count), -me, axis=1)
-    total = blocks[:, 0]
+    total = block_of(me)
     for k in range(1, count):
-        sent = blocks[:, k].astype(jnp.bfloat16)
+        sent = block_of((me + k) % count).astype(jnp.bfloat16)
         total = total + lax.ppermute(
             sent, "panel", [(i, (i + k) % count) for i in range(count)]
         ).astype(jnp.float32)
@@ -116,11 +113,24 @@
     shard_count = lax.axis_size("seq")
     tables = transform_tables(shard_count, row_count)
     filt_spec = forward_spectrum(to_columns(long_filter[None]), tables)
-    both = panel_gather(jnp.concatenate([tokens, cotangent], axis=0))
-    full_tok, full_cot = both[:row_count], both[row_count:]
-    projected = jnp.einsum(
-        "td,jdc->jtc", full_tok, in_weight, preferred_element_type=jnp.float32
-    ).astype(jnp.bfloat16)
+    width = tokens.shape[1]
+    parts = panel_parts(jnp.concatenate([tokens, cotangent], axis=0))
+    projected = 0.0
+    grad_gated = 0.0
+    for part, source in parts:
+        projected = projected + jnp.einsum(
+            "td,jdc->jtc",
+            part[:row_count],
+            lax.dynamic_slice_in_dim(in_weight, source * width, width, axis=1),
+            preferred_element_type=jnp.float32,
+        )
+        grad_gated = grad_gated + lax.dot_general(
+            part[row_count:],
+            lax.dynamic_slice_in_dim(out_weight, source * width, width, axis=1),
+            (((1,), (1,)), ((), ())),
+            preferred_element_type=jnp.float32,
+        )
+    projected = projected.astype(jnp.bfloat16)
     before = shifted(projected[:, row_count - (tap_count - 1) :, :], "seq", 1)
     extended = jnp.concatenate([before, projected], axis=1).astype(jnp.float32)
     filtered = short_kernel[0][:, None, :] * extended[:, tap_count - 1 :, :]
@@ -132,9 +142,6 @@
         )
     gate_out, gate_in, value_path = (filtered[0], filtered[1], filtered[2])
     signal = value_path * gate_in
-    grad_gated = lax.dot_general(
-        full_cot, out_weight, (((1,), (1,)), ((), ())), preferred_element_type=jnp.float32
-    )
     grad_state = grad_gated * gate_out
     spectra = forward_spectrum(to_columns(jnp.stack([signal, grad_state])), tables)
     filt_real, filt_imag = filt_spec[:, :, :, 0], filt_spec[:, :, :, 1]
@@ -156,8 +163,13 @@
     conv_state = convolved[0] + skip_gain[None, :] * signal
     grad_signal = convolved[1] + skip_gain[None, :] * grad_state
     gated_state = (conv_state * gate_out).astype(jnp.bfloat16)
-    partial_value = jnp.dot(gated_state, out_weight, preferred_element_type=jnp.float32)
-    block_out = panel_reduce_scatter(partial_value)
+    block_out = panel_reduce_scatter(
+        lambda dest: jnp.dot(
+            gated_state,
+            lax.dynamic_slice_in_dim(out_weight, dest * width, width, axis=1),
+            preferred_element_type=jnp.float32,
+        )
+    )
     grad_gate_out = grad_gated * conv_state
     grad_value = grad_signal * gate_in
     grad_gate_in = grad_signal * value_path
@@ -171,10 +183,14 @@
             + short_kernel[tap_index][:, None, :] * widened[:, tap_index : tap_index + row_count, :]
         )
     grad_projected = grad_projected.astype(jnp.bfloat16)
-    grad_partial = jnp.einsum(
-        "jtc,jdc->td", grad_projected, in_weight, preferred_element_type=jnp.float32
-    )
-    token_grad = panel_reduce_scatter(grad_partial)
+    token_grad = panel_reduce_scatter(
+        lambda dest: jnp.einsum(
+            "jtc,jdc->td",
+            grad_projected,
+            lax.dynamic_slice_in_dim(in_weight, dest * width, width, axis=1),
+            preferred_element_type=jnp.float32,
+        )
+    )
     return (block_out, token_grad)
 
 

time: 123 us -> 112 us (0.911)
  starting transfers between devices: 39.2 us -> 22.4 us
  blocking collectives: 0 us -> 12.1 us
  matrix products: 13.6 us -> 24.1 us
  local copies, waits for them, and re-layouts: 23.8 us -> 13.5 us
  waiting for transfers between devices: 35.4 us -> 30.4 us
  other arithmetic: 8.95 us -> 7.17 us
    all_to_all x0 -> x1, blocking collectives: none -> 12.1 us  [to_rows(): lax.all_to_all(columns, 'seq', split_axis=2, concat_axis=1, tiled=True)]
    ppermute x6, starting transfers between devices: 15.7 us -> 5.08 us  [panel_reduce_scatter(): lax.ppermute(sent, 'panel', [(i, (i + k) % count) for i in range(count)])]
    dot_general x4 -> x16, matrix products: 1.92 us -> 12.5 us  [the longest x4 5.23 us: local(): lax.dot_general(part[row_count:], lax.dynamic_slice_in_dim(out_weight, so...]
    all_to_all x1 -> x0, waiting for transfers between devices: 8.47 us -> none  [to_rows(): lax.all_to_all(columns, 'seq', split_axis=2, concat_axis=1, tiled=True)]
    ppermute x6, waiting for transfers between devices: 9.53 us -> 15.6 us  [panel_reduce_scatter(): lax.ppermute(sent, 'panel', [(i, (i + k) % count) for i in range(count)])]
    unnamed x41 -> x34, local copies, waits for them, and re-layouts: 10.8 us -> 5.91 us
    all_to_all x1 -> x0, starting transfers between devices: 4.49 us -> none  [to_rows(): lax.all_to_all(columns, 'seq', split_axis=2, concat_axis=1, tiled=True)]
    all_to_all x2, starting transfers between devices: 10.3 us -> 8.04 us  [to_columns(): lax.all_to_all(jnp.swapaxes(rows, 1, 2), 'seq', split_axis=1, concat_axis...]
  transfers between devices with their start and end apart: 14 -> 13, of which waited for: 7 -> 6; matrix products, arithmetic and copies ran while one was open for 11% -> 16% of each run, Pallas kernels for 0% -> 0%
where the time goes in v4:
time: 112 us; the launch traced here: 111 us
  waiting for transfers between devices  30.4 us (27%)
  matrix products  24.1 us (22%)
  starting transfers between devices  22.4 us (20%)
  local copies, waits for them, and re-layouts  13.5 us (12%)
  blocking collectives  12.1 us (11%)
  other arithmetic  7.17 us (6%)
  between operations  1.22 us (1%)
    ppermute x6, waiting for transfers between devices, panel_reduce_scatter(): lax.ppermute(sent, 'panel', [(i, (i + k) % count) for i in range(count)])  15.6 us
    all_to_all x1, blocking collectives, to_rows(): lax.all_to_all(columns, 'seq', split_axis=2, concat_axis=1, tiled=True)  12.1 us
    all_to_all x2, waiting for transfers between devices, to_columns(): lax.all_to_all(jnp.swapaxes(rows, 1, 2), 'seq', split_axis=1, concat_axis...  8.16 us
    all_to_all x2, starting transfers between devices, to_columns(): lax.all_to_all(jnp.swapaxes(rows, 1, 2), 'seq', split_axis=1, concat_axis...  8.04 us
    ppermute x3, waiting for transfers between devices, panel_parts(): lax.ppermute(value, 'panel', [(i, (i + k) % count) for i in range(count)])  6.58 us
    ppermute x3, starting transfers between devices, panel_parts(): lax.ppermute(value, 'panel', [(i, (i + k) % count) for i in range(count)])  6.09 us
    unnamed x34, local copies, waits for them, and re-layouts  5.91 us
    dot_general x4, matrix products, local(): lax.dot_general(part[row_count:], lax.dynamic_slice_in_dim(out_weight, so...  5.23 us
  transfers between devices with their start and end apart: 13, of which 6 were waited for; matrix products, arithmetic and copies ran while one was open for 16% of the time, Pallas kernels for 0%

profile of v4, /device:TPU:0, one launch (start us, length us, event | category | flops | bytes accessed | tf_op | source)
XLA Modules:
  0.0 110.9 jit_solution(5834362679238241478)
XLA Ops:
  0.7 1.7 %constant_dynamic-update-slice_fusion.1 = bf16[512,256]{1,0:T(8,128)(2,1)} fusion(bf16[256,256]{1,0:T(8,128)(2,1)} %param.7), kind=kLoop, calls=%fused_computation.172 | loop fusion | bytes 262144
  2.4 1.6 %constant_dynamic-update-slice_fusion = bf16[512,256]{1,0:T(8,128)(2,1)} fusion(bf16[512,256]{1,0:T(8,128)(2,1)} %constant_dynamic-update-slice_fusion.1, bf16[256,256]{1,0:T(8,128)(2,1)} %param.8), kind=kLoop, calls=%fused_computation.171 | loop fusion | bytes 262144 | tf_op jit(solution)/shard_map/concatenate | solution.py:117
  3.9 3.1 %collective-permute-start = (bf16[512,256]{1,0:T(8,128)(2,1)}, bf16[512,256]{1,0:T(8,128)(2,1)}, u32[]{:S(2)}, u32[]{:S(2)}) collective-permute-start(bf16[512,256]{1,0:T(8,128)(2,1)} %constant_dynamic-update-slice_fusion), channel_id=1, source_target_pairs={{0,1},{1,2},{2,3},{3,0},{4,5},{5,6},{6,7},{7,4},{8,9},{9,10},{10,1... | collective-permute-start | bytes 786440 | tf_op jit(solution)/shard_map/ppermute | solution.py:24
  7.0 2.0 %collective-permute-start.2 = (bf16[512,256]{1,0:T(8,128)(2,1)}, bf16[512,256]{1,0:T(8,128)(2,1)}, u32[]{:S(2)}, u32[]{:S(2)}) collective-permute-start(bf16[512,256]{1,0:T(8,128)(2,1)} %constant_dynamic-update-slice_fusion), channel_id=1, source_target_pairs={{0,3},{1,0},{2,1},{3,2},{4,7},{5,4},{6,5},{7,6},{8,11},{9,8},{10,9... | collective-permute-start | bytes 786440 | tf_op jit(solution)/shard_map/ppermute | solution.py:24
  9.0 1.0 collective-permute-start.1
  10.0 1.8 %copy.63 = f32[1,256,256]{1,0,2:T(1,128)} copy(f32[1,256,256]{2,1,0:T(8,128)} %bitcast.213) | data formatting | bytes 524288 | tf_op jit(solution)/shard_map/broadcast_in_dim | solution.py:115
  11.8 3.7 %all-to-all-start.1 = ((f32[1,256,256]{2,0,1:T(1,128)}), f32[1,256,256]{2,0,1:T(1,128)S(1)}, u32[]{:S(2)}, u32[]{:S(2)}) async-start(f32[1,256,256]{2,0,1:T(1,128)} %bitcast.36), calls=%async_computation.1 | async-start | bytes 524288 | tf_op jit(solution)/shard_map/all_to_all | solution.py:84
  15.7 1.0 fusion.87
  17.0 1.8 %convolution_bitcast_fusion.7 = f32[256,256]{1,0:T(8,128)} fusion(bf16[256,256]{1,0:T(8,128)(2,1)S(1)} %copy-done.11, bf16[256,1024]{1,0:T(8,128)(2,1)} %param.13, s32[]{:T(128)S(6)} %select_n.142), kind=kOutput, calls=%fused_computation.30 | convolution fusion | flops 33554432 | bytes 524292 | tf_op jit(solution)/shard_map/dot_general | solution.py:127
  19.0 1.0 fusion.89
  20.0 1.4 %fusion.40 = (f32[1,256,2,256]{3,1,2,0:T(8,128)}, f32[1,256,2,256]{3,1,0,2:T(8,128)}, f32[1,256,2,256]{3,1,0,2:T(8,128)}, f32[1,256,2,256]{3,1,2,0:T(8,128)}) fusion(f32[256,1,256]{2,0,1:T(8,128)S(1)} %get-tuple-element.35, f32[256,1,256]{2,0,1:T(8,128)S(1)} %fusion.89, f32[256,1,256]{2,0,1:T(8,128)S(1)} %get-tuple-element.34), kind=kLoop, calls=%fused_computation.68 | loop fusion | flops 524288 | bytes 2883584 | tf_op jit(solution)/shard_map/stack | solution.py:65
  21.5 1.0 all-to-all-done.1
  22.4 1.0 convolution_bitcast_fusion.2
  23.4 1.2 %fusion.45 = f32[3,256,256]{1,2,0:T(8,128)S(1)} fusion(bf16[3,1024,256]{2,1,0:T(8,128)(2,1)S(1)} %copy-done, s32[]{:T(128)S(6)} %select_n.148, bf16[512,256]{1,0:T(8,128)(2,1)} %collective-permute-done.2), kind=kOutput, calls=%fused_computation.84 | convolution fusion | flops 100663296 | bytes 1310724 | tf_op jit(solution)/shard_map/td,jdc->jtc/dot_general | solution.py:121
  24.6 1.2 %convolution_add_fusion.1 = f32[3,256,256]{1,2,0:T(8,128)S(1)} fusion(f32[3,256,256]{1,2,0:T(8,128)S(1)} %fusion.52, bf16[3,1024,256]{2,1,0:T(8,128)(2,1)S(1)} %copy-done, s32[]{:T(128)S(6)} %select_n.144, bf16[512,256]{1,0:T(8,128)(2,1)} %collective-permute-done), kind=kOutput, calls=%fused_computation.19 | convolution fusion | flops 100859904 | bytes 2097156 | tf_op jit(solution)/shard_map/td,jdc->jtc/dot_general | solution.py:121
  25.9 6.6 %collective-permute-done.1 = bf16[512,256]{1,0:T(8,128)(2,1)} collective-permute-done((bf16[512,256]{1,0:T(8,128)(2,1)}, bf16[512,256]{1,0:T(8,128)(2,1)}, u32[]{:S(2)}, u32[]{:S(2)}) %collective-permute-start.1) | collective-permute-done | bytes 262176 | tf_op jit(solution)/shard_map/ppermute | solution.py:24
  32.5 1.2 %fusion.21 = bf16[3,256,256]{2,1,0:T(8,128)(2,1)S(1)} fusion(f32[3,256,256]{1,2,0:T(8,128)S(1)} %fusion.45, f32[3,256,256]{1,2,0:T(8,128)S(1)} %convolution_add_fusion.1, bf16[3,1024,256]{2,1,0:T(8,128)(2,1)S(1)} %copy-done, s32[]{:T(128)S(6)} %select_n.146, bf16[512,256]{1,0:T(8,128)(2,1)} %collective-permute-done.1), kind=kOutput, calls=%fused_computation.22 | convolution fusion | flops 101253120 | bytes 2490372 | tf_op jit(solution)/shard_map/td,jdc->jtc/dot_general | solution.py:121
  33.7 1.9 %collective-permute-start.3 = (bf16[3,2,256]{2,1,0:T(2,128)(2,1)S(1)}, bf16[3,2,256]{2,1,0:T(2,128)(2,1)S(1)}, u32[]{:S(2)}, u32[]{:S(2)}) collective-permute-start(bf16[3,2,256]{2,1,0:T(2,128)(2,1)S(1)} %slice.138), channel_id=1, source_target_pairs={{0,4},{4,8},{8,12},{12,16},{16,20},{20,24},{24,28},{1,5},{5,9},{9,... | collective-permute-start | bytes 9224 | tf_op jit(solution)/shard_map/ppermute | solution.py:16
  35.6 1.1 %fusion.83 = f32[256,256]{1,0:T(8,128)S(1)} fusion(bf16[512,256]{1,0:T(8,128)(2,1)} %collective-permute-done.1, bf16[256,1024]{1,0:T(8,128)(2,1)S(1)} %copy-done.3, s32[]{:T(128)S(6)} %select_n.146), kind=kOutput, calls=%fused_computation.124 | convolution fusion | flops 33554432 | bytes 524292 | tf_op jit(solution)/shard_map/dot_general | solution.py:127
  36.7 1.1 %fusion.81 = f32[256,256]{1,0:T(8,128)S(1)} fusion(bf16[512,256]{1,0:T(8,128)(2,1)} %collective-permute-done.2, bf16[256,1024]{1,0:T(8,128)(2,1)S(1)} %copy-done.3, s32[]{:T(128)S(6)} %select_n.148), kind=kOutput, calls=%fused_computation.122 | convolution fusion | flops 33554432 | bytes 524292 | tf_op jit(solution)/shard_map/dot_general | solution.py:127
  37.9 1.1 %fusion.23 = f32[256,256]{1,0:T(8,128)S(1)} fusion(f32[256,256]{1,0:T(8,128)S(1)} %fusion.81, f32[256,256]{1,0:T(8,128)S(1)} %fusion.83, f32[256,256]{1,0:T(8,128)S(1)} %copy-done.9, bf16[512,256]{1,0:T(8,128)(2,1)} %collective-permute-done, bf16[256,1024]{1,0:T(8,128)(2,1)S(1)} %copy-done.3, s32[]{:T(128)S(6)} %select_n.144), kind=kOutput, calls=%fused_computation.29 | convolution fusion | flops 33751040 | bytes 1310724 | tf_op jit(solution)/shard_map/dot_general | solution.py:127
  39.8 0.8 maximum_bitcast_fusion.4
  40.6 2.0 %copy.32 = f32[2,256,256]{2,0,1:T(2,128)} copy(f32[2,256,256]{1,2,0:T(8,128)} %maximum_bitcast_fusion.4) | data formatting | bytes 1048576 | tf_op jit(solution)/shard_map/transpose | solution.py:85
  42.7 4.3 %all-to-all-start = ((f32[2,256,256]{2,0,1:T(2,128)}), f32[2,256,256]{2,0,1:T(2,128)}, u32[]{:S(2)}, u32[]{:S(2)}) async-start(f32[2,256,256]{2,0,1:T(2,128)} %copy.32), calls=%async_computation | async-start | bytes 1048576 | tf_op jit(solution)/shard_map/all_to_all | solution.py:84
  47.2 0.8 copy-done.5
  48.2 1.1 %convolution_bitcast_fusion.1 = f32[1,32,2,2,8,256]{5,1,4,2,0,3:T(8,128)S(1)} fusion(f32[32,2,2,8,256]{4,3,0,2,1:T(8,128)S(1)} %maximum_bitcast_fusion.3, f32[1,256,2,256]{3,1,0,2:T(8,128)S(1)} %copy-done.5, f32[1,256,2,256]{3,1,0,2:T(8,128)S(1)} %copy-done.7), kind=kOutput, calls=%fused_computation.15 | convolution fusion | flops 805568512 | bytes 3145728 | tf_op jit(solution)/shard_map/bcerkm,rmsq->bceskq/dot_general | solution.py:100
  49.3 7.2 %all-to-all-done = f32[2,256,256]{2,0,1:T(2,128)} async-done(((f32[2,256,256]{2,0,1:T(2,128)}), f32[2,256,256]{2,0,1:T(2,128)}, u32[]{:S(2)}, u32[]{:S(2)}) %all-to-all-start) | async-done | bytes 524320 | tf_op jit(solution)/shard_map/all_to_all | solution.py:84
  56.5 2.9 %convolution_bitcast_fusion = f32[2,32,2,2,8,256]{5,4,3,2,1,0:T(8,128)S(1)} fusion(f32[2,8,32,256]{3,0,2,1:T(2,128)} %bitcast.20, f32[2,1,8,8]{3,2,1,0:T(8,128)S(1)} %get-tuple-element.33, f32[2,1,8,8]{3,2,1,0:T(8,128)S(1)} %get-tuple-element.32), kind=kOutput, calls=%fused_computation.14 | convolution fusion | flops 50331904 | bytes 2622464 | tf_op jit(solution)/shard_map/erkp,bcpm->bcerkm/dot_general | solution.py:98
  59.4 0.3 multiply_subtract_fusion.1
  60.0 0.8 copy-done.6
  61.0 2.7 %fusion.10 = f32[2,32,2,2,8,256]{5,1,4,2,0,3:T(8,128)S(1)} fusion(f32[2,32,2,2,8,256]{5,4,3,2,1,0:T(8,128)S(1)} %pad_maximum_fusion, f32[1,256,2,256]{3,1,0,2:T(8,128)S(1)} %copy-done.6, f32[1,256,2,256]{3,1,0,2:T(8,128)S(1)} %copy-done.8), kind=kOutput, calls=%fused_computation.12 | convolution fusion | flops 1610874880 | bytes 5242880 | tf_op jit(solution)/shard_map/bcerkm,rmsq->bceskq/dot_general | solution.py:100
  63.7 0.5 multiply_subtract_fusion.3
  64.3 0.9 copy-done.12
  65.3 2.7 %fusion.13 = f32[2,32,2,2,8,256]{5,4,3,2,1,0:T(8,128)S(1)} fusion(f32[2,32,2,2,8,256,1]{5,1,4,2,0,3,6:T(8,128)S(1)} %maximum_bitcast_fusion, f32[1,256,2,256]{3,1,2,0:T(8,128)S(1)} %copy-done.13, f32[1,256,2,256]{3,1,2,0:T(8,128)S(1)} %copy-done.12), kind=kOutput, calls=%fused_computation.13 | convolution fusion | flops 1610874880 | bytes 5242880 | tf_op jit(solution)/shard_map/bceskq,sqrm->bcerkm/dot_general | solution.py:105
  68.4 1.2 %fusion.18 = f32[2,32,8,256]{3,2,1,0:T(8,128)S(1)} fusion(f32[2,32,2,1,8,256]{5,4,3,2,1,0:T(8,128)S(1)} %get-tuple-element.11, f32[2,32,2,1,8,256]{5,4,3,2,1,0:T(8,128)S(1)} %get-tuple-element.10, f32[2,1,8,8]{3,2,1,0:T(8,128)S(1)} %get-tuple-element.33, f32[2,1,8,8]{3,2,1,0:T(8,128)S(1)} %get-tuple-element.32), kind=kOutput, calls=%fused_computation.21 | convolution fusion | flops 50856448 | bytes 2622464 | tf_op jit(solution)/shard_map/erkp,bcerkm->bcpm/dot_general | solution.py:107
  69.8 12.1 %all_to_all.45 = f32[2,32,8,256]{3,1,0,2:T(8,128)S(1)} all-to-all(f32[2,32,8,256]{3,1,0,2:T(8,128)S(1)} %copy.43), channel_id=1, replica_groups=mesh['seq'=8,'panel'=4] {'seq'}, dimensions={2} | all-to-all | bytes 1048576 | tf_op jit(solution)/shard_map/all_to_all | solution.py:92
  82.0 0.8 copy.44
  82.8 1.2 %copy.45 = f32[2,256,256]{1,2,0:T(8,128)S(1)} copy(f32[2,256,256]{2,1,0:T(8,128)} %bitcast.211) | data formatting | bytes 1048576 | tf_op jit(solution)/shard_map/reshape | solution.py:93
  84.3 0.8 copy-done.4
  85.6 1.3 %collective-permute-start.7 = (f32[3,2,256]{2,1,0:T(2,128)S(1)}, f32[3,2,256]{2,1,0:T(2,128)S(1)}, u32[]{:S(2)}, u32[]{:S(2)}) collective-permute-start(f32[3,2,256]{2,1,0:T(2,128)S(1)} %slice.162), channel_id=1, source_target_pairs={{4,0},{8,4},{12,8},{16,12},{20,16},{24,20},{28,24},{5,1},{9,5},{13... | collective-permute-start | bytes 18440 | tf_op jit(solution)/shard_map/ppermute | solution.py:16
  87.1 2.1 %collective-permute-start.4 = (bf16[256,256]{1,0:T(8,128)(2,1)S(1)}, bf16[256,256]{1,0:T(8,128)(2,1)S(1)}, u32[]{:S(2)}, u32[]{:S(2)}) collective-permute-start(bf16[256,256]{1,0:T(8,128)(2,1)S(1)} %convolution_convert_fusion.2), channel_id=1, source_target_pairs={{0,1},{1,2},{2,3},{3,0},{4,5},{5,6},{6,7},{7,4},{8,9},{9,10},{10,1... | collective-permute-start | bytes 393224 | tf_op jit(solution)/shard_map/ppermute | solution.py:35
  89.2 1.8 %collective-permute-start.6 = (bf16[256,256]{1,0:T(8,128)(2,1)S(1)}, bf16[256,256]{1,0:T(8,128)(2,1)S(1)}, u32[]{:S(2)}, u32[]{:S(2)}) collective-permute-start(bf16[256,256]{1,0:T(8,128)(2,1)S(1)} %convolution_convert_fusion), channel_id=1, source_target_pairs={{0,3},{1,0},{2,1},{3,2},{4,7},{5,4},{6,5},{7,6},{8,11},{9,8},{10,9... | collective-permute-start | bytes 393224 | tf_op jit(solution)/shard_map/ppermute | solution.py:35
  92.0 1.1 %collective-permute-start.9 = (bf16[256,256]{1,0:T(8,128)(2,1)S(1)}, bf16[256,256]{1,0:T(8,128)(2,1)S(1)}, u32[]{:S(2)}, u32[]{:S(2)}) collective-permute-start(bf16[256,256]{1,0:T(8,128)(2,1)S(1)} %fusion.25), channel_id=1, source_target_pairs={{0,2},{1,3},{2,0},{3,1},{4,6},{5,7},{6,4},{7,5},{8,10},{9,11},{10,... | collective-permute-start | bytes 393224 | tf_op jit(solution)/shard_map/ppermute | solution.py:35
  93.4 5.6 %collective-permute-done.5 = bf16[256,256]{1,0:T(8,128)(2,1)S(1)} collective-permute-done((bf16[256,256]{1,0:T(8,128)(2,1)S(1)}, bf16[256,256]{1,0:T(8,128)(2,1)S(1)}, u32[]{:S(2)}, u32[]{:S(2)}) %collective-permute-start.5) | collective-permute-done | bytes 131104 | tf_op jit(solution)/shard_map/ppermute | solution.py:35
  99.1 1.7 %collective-permute-done.6 = bf16[256,256]{1,0:T(8,128)(2,1)S(1)} collective-permute-done((bf16[256,256]{1,0:T(8,128)(2,1)S(1)}, bf16[256,256]{1,0:T(8,128)(2,1)S(1)}, u32[]{:S(2)}, u32[]{:S(2)}) %collective-permute-start.6) | collective-permute-done | bytes 131104 | tf_op jit(solution)/shard_map/ppermute | solution.py:35
  100.8 0.9 add_convert_fusion
  101.6 8.3 %collective-permute-done.9 = bf16[256,256]{1,0:T(8,128)(2,1)S(1)} collective-permute-done((bf16[256,256]{1,0:T(8,128)(2,1)S(1)}, bf16[256,256]{1,0:T(8,128)(2,1)S(1)}, u32[]{:S(2)}, u32[]{:S(2)}) %collective-permute-start.9) | collective-permute-done | bytes 131104 | tf_op jit(solution)/shard_map/ppermute | solution.py:35
  109.9 1.0 fusion.63
  (71 shorter events, 5.0 us)
Async XLA Ops:
  0.6 16.1 %copy-start = (bf16[3,1024,256]{2,1,0:T(8,128)(2,1)S(1)}, bf16[3,1024,256]{2,1,0:T(8,128)(2,1)}, u32[]{:S(2)}) copy-start(bf16[3,1024,256]{2,1,0:T(8,128)(2,1)} %param.9) | copy-start | bytes 4718596
  0.6 16.1 %copy-start.10 = (bf16[256,256]{1,0:T(8,128)(2,1)S(1)}, bf16[256,256]{1,0:T(8,128)(2,1)}, u32[]{:S(2)}) copy-start(bf16[256,256]{1,0:T(8,128)(2,1)} %param.7) | copy-start | bytes 393220
  0.7 16.4 %copy-start.11 = (bf16[256,256]{1,0:T(8,128)(2,1)S(1)}, bf16[256,256]{1,0:T(8,128)(2,1)}, u32[]{:S(2)}) copy-start(bf16[256,256]{1,0:T(8,128)(2,1)} %param.8) | copy-start | bytes 393220
  0.7 16.1 %copy-start.14 = (f32[3,3,256]{2,1,0:T(4,128)S(1)}, f32[3,3,256]{2,1,0:T(4,128)}, u32[]{:S(2)}) copy-start(f32[3,3,256]{2,1,0:T(4,128)} %param.10) | copy-start | bytes 27652
  3.9 20.7 %collective-permute-start = (bf16[512,256]{1,0:T(8,128)(2,1)}, bf16[512,256]{1,0:T(8,128)(2,1)}, u32[]{:S(2)}, u32[]{:S(2)}) collective-permute-start(bf16[512,256]{1,0:T(8,128)(2,1)} %constant_dynamic-update-slice_fusion), channel_id=1, source_target_pairs={{0,1},{1,2},{2,3},{3,0},{4,5},{5,6},{6,7},{7,4},{8,9},{9,10},{10,1... | collective-permute-start | bytes 786440 | tf_op jit(solution)/shard_map/ppermute | solution.py:24
  7.0 16.5 %collective-permute-start.2 = (bf16[512,256]{1,0:T(8,128)(2,1)}, bf16[512,256]{1,0:T(8,128)(2,1)}, u32[]{:S(2)}, u32[]{:S(2)}) collective-permute-start(bf16[512,256]{1,0:T(8,128)(2,1)} %constant_dynamic-update-slice_fusion), channel_id=1, source_target_pairs={{0,3},{1,0},{2,1},{3,2},{4,7},{5,4},{6,5},{7,6},{8,11},{9,8},{10,9... | collective-permute-start | bytes 786440 | tf_op jit(solution)/shard_map/ppermute | solution.py:24
  9.0 23.5 %collective-permute-start.1 = (bf16[512,256]{1,0:T(8,128)(2,1)}, bf16[512,256]{1,0:T(8,128)(2,1)}, u32[]{:S(2)}, u32[]{:S(2)}) collective-permute-start(bf16[512,256]{1,0:T(8,128)(2,1)} %constant_dynamic-update-slice_fusion), channel_id=1, source_target_pairs={{0,2},{1,3},{2,0},{3,1},{4,6},{5,7},{6,4},{7,5},{8,10},{9,11},{10,... | collective-permute-start | bytes 786440 | tf_op jit(solution)/shard_map/ppermute | solution.py:24
  11.8 10.6 %all-to-all-start.1 = ((f32[1,256,256]{2,0,1:T(1,128)}), f32[1,256,256]{2,0,1:T(1,128)S(1)}, u32[]{:S(2)}, u32[]{:S(2)}) async-start(f32[1,256,256]{2,0,1:T(1,128)} %bitcast.36), calls=%async_computation.1 | async-start | bytes 524288 | tf_op jit(solution)/shard_map/all_to_all | solution.py:84
  24.6 11.0 %copy-start.3 = (bf16[256,1024]{1,0:T(8,128)(2,1)S(1)}, bf16[256,1024]{1,0:T(8,128)(2,1)}, u32[]{:S(2)}) copy-start(bf16[256,1024]{1,0:T(8,128)(2,1)} %param.13) | copy-start | bytes 1572868
  25.9 12.0 %copy-start.9 = (f32[256,256]{1,0:T(8,128)S(1)}, f32[256,256]{1,0:T(8,128)}, u32[]{:S(2)}) copy-start(f32[256,256]{1,0:T(8,128)} %convolution_bitcast_fusion.7) | copy-start | bytes 786436
  33.7 5.4 %collective-permute-start.3 = (bf16[3,2,256]{2,1,0:T(2,128)(2,1)S(1)}, bf16[3,2,256]{2,1,0:T(2,128)(2,1)S(1)}, u32[]{:S(2)}, u32[]{:S(2)}) collective-permute-start(bf16[3,2,256]{2,1,0:T(2,128)(2,1)S(1)} %slice.138), channel_id=1, source_target_pairs={{0,4},{4,8},{8,12},{12,16},{16,20},{20,24},{24,28},{1,5},{5,9},{9,... | collective-permute-start | bytes 9224 | tf_op jit(solution)/shard_map/ppermute | solution.py:16
  39.0 0.7 copy-start.1
  42.7 13.9 %all-to-all-start = ((f32[2,256,256]{2,0,1:T(2,128)}), f32[2,256,256]{2,0,1:T(2,128)}, u32[]{:S(2)}, u32[]{:S(2)}) async-start(f32[2,256,256]{2,0,1:T(2,128)} %copy.32), calls=%async_computation | async-start | bytes 1048576 | tf_op jit(solution)/shard_map/all_to_all | solution.py:84
  47.0 1.0 copy-start.5
  47.0 1.2 %copy-start.7 = (f32[1,256,2,256]{3,1,0,2:T(8,128)S(1)}, f32[1,256,2,256]{3,1,0,2:T(8,128)}, u32[]{:S(2)}) copy-start(f32[1,256,2,256]{3,1,0,2:T(8,128)} %get-tuple-element.24) | copy-start | bytes 1572868
  59.8 1.0 copy-start.6
  59.8 1.2 %copy-start.8 = (f32[1,256,2,256]{3,1,0,2:T(8,128)S(1)}, f32[1,256,2,256]{3,1,0,2:T(8,128)}, u32[]{:S(2)}) copy-start(f32[1,256,2,256]{3,1,0,2:T(8,128)} %get-tuple-element.24) | copy-start | bytes 1572868
  64.1 1.0 copy-start.12
  64.2 1.2 %copy-start.13 = (f32[1,256,2,256]{3,1,2,0:T(8,128)S(1)}, f32[1,256,2,256]{3,1,2,0:T(8,128)}, u32[]{:S(2)}) copy-start(f32[1,256,2,256]{3,1,2,0:T(8,128)} %get-tuple-element.25) | copy-start | bytes 1572868
  69.6 14.4 %copy-start.2 = (f32[256,256]{1,0:T(8,128)S(1)}, f32[256,256]{1,0:T(8,128)}, u32[]{:S(2)}) copy-start(f32[256,256]{1,0:T(8,128)} %copy-done.1) | copy-start | bytes 786436
  69.7 14.4 %copy-start.15 = (f32[256]{0:T(256)S(1)}, f32[256]{0:T(256)}, u32[]{:S(2)}) copy-start(f32[256]{0:T(256)} %param.11) | copy-start | bytes 3076
  84.0 1.0 copy-start.4
  85.6 5.5 %collective-permute-start.7 = (f32[3,2,256]{2,1,0:T(2,128)S(1)}, f32[3,2,256]{2,1,0:T(2,128)S(1)}, u32[]{:S(2)}, u32[]{:S(2)}) collective-permute-start(f32[3,2,256]{2,1,0:T(2,128)S(1)} %slice.162), channel_id=1, source_target_pairs={{4,0},{8,4},{12,8},{16,12},{20,16},{24,20},{28,24},{5,1},{9,5},{13... | collective-permute-start | bytes 18440 | tf_op jit(solution)/shard_map/ppermute | solution.py:16
  87.1 12.0 %collective-permute-start.5 = (bf16[256,256]{1,0:T(8,128)(2,1)S(1)}, bf16[256,256]{1,0:T(8,128)(2,1)S(1)}, u32[]{:S(2)}, u32[]{:S(2)}) collective-permute-start(bf16[256,256]{1,0:T(8,128)(2,1)S(1)} %convolution_convert_fusion.1), channel_id=1, source_target_pairs={{0,2},{1,3},{2,0},{3,1},{4,6},{5,7},{6,4},{7,5},{8,10},{9,11},{10,... | collective-permute-start | bytes 393224 | tf_op jit(solution)/shard_map/ppermute | solution.py:35
  87.1 11.9 %collective-permute-start.4 = (bf16[256,256]{1,0:T(8,128)(2,1)S(1)}, bf16[256,256]{1,0:T(8,128)(2,1)S(1)}, u32[]{:S(2)}, u32[]{:S(2)}) collective-permute-start(bf16[256,256]{1,0:T(8,128)(2,1)S(1)} %convolution_convert_fusion.2), channel_id=1, source_target_pairs={{0,1},{1,2},{2,3},{3,0},{4,5},{5,6},{6,7},{7,4},{8,9},{9,10},{10,1... | collective-permute-start | bytes 393224 | tf_op jit(solution)/shard_map/ppermute | solution.py:35
  89.2 11.5 %collective-permute-start.6 = (bf16[256,256]{1,0:T(8,128)(2,1)S(1)}, bf16[256,256]{1,0:T(8,128)(2,1)S(1)}, u32[]{:S(2)}, u32[]{:S(2)}) collective-permute-start(bf16[256,256]{1,0:T(8,128)(2,1)S(1)} %convolution_convert_fusion), channel_id=1, source_target_pairs={{0,3},{1,0},{2,1},{3,2},{4,7},{5,4},{6,5},{7,6},{8,11},{9,8},{10,9... | collective-permute-start | bytes 393224 | tf_op jit(solution)/shard_map/ppermute | solution.py:35
  92.0 17.9 %collective-permute-start.9 = (bf16[256,256]{1,0:T(8,128)(2,1)S(1)}, bf16[256,256]{1,0:T(8,128)(2,1)S(1)}, u32[]{:S(2)}, u32[]{:S(2)}) collective-permute-start(bf16[256,256]{1,0:T(8,128)(2,1)S(1)} %fusion.25), channel_id=1, source_target_pairs={{0,2},{1,3},{2,0},{3,1},{4,6},{5,7},{6,4},{7,5},{8,10},{9,11},{10,... | collective-permute-start | bytes 393224 | tf_op jit(solution)/shard_map/ppermute | solution.py:35
  93.1 16.8 %collective-permute-start.8 = (bf16[256,256]{1,0:T(8,128)(2,1)S(1)}, bf16[256,256]{1,0:T(8,128)(2,1)S(1)}, u32[]{:S(2)}, u32[]{:S(2)}) collective-permute-start(bf16[256,256]{1,0:T(8,128)(2,1)S(1)} %fusion.24), channel_id=1, source_target_pairs={{0,1},{1,2},{2,3},{3,0},{4,5},{5,6},{6,7},{7,4},{8,9},{9,10},{10,1... | collective-permute-start | bytes 393224 | tf_op jit(solution)/shard_map/ppermute | solution.py:35
  99.1 10.9 %collective-permute-start.10 = (bf16[256,256]{1,0:T(8,128)(2,1)S(1)}, bf16[256,256]{1,0:T(8,128)(2,1)S(1)}, u32[]{:S(2)}, u32[]{:S(2)}) collective-permute-start(bf16[256,256]{1,0:T(8,128)(2,1)S(1)} %fusion.26), channel_id=1, source_target_pairs={{0,3},{1,0},{2,1},{3,2},{4,7},{5,4},{6,5},{7,6},{8,11},{9,8},{10,9... | collective-permute-start | bytes 393224 | tf_op jit(solution)/shard_map/ppermute | solution.py:35

commit v5 on v4

--- a/solution.py
+++ b/solution.py
@@ -8,6 +8,7 @@
 HIGHEST = lax.Precision.HIGHEST
 STAGE_A_PRECISION = lax.Precision.HIGHEST
 STAGE_B_PRECISION = lax.Precision.HIGH
+WIRE = jnp.float32
 
 
 def shifted(value, axis, steps):
@@ -78,18 +79,20 @@
     )
 
 
-def to_columns(rows):
+def to_columns(rows, wire=jnp.float32):
     shard_count = lax.axis_size("seq")
     batch, row_count, _ = rows.shape
     columns = lax.all_to_all(
-        jnp.swapaxes(rows, 1, 2), "seq", split_axis=1, concat_axis=2, tiled=True
-    )
+        jnp.swapaxes(rows, 1, 2).astype(wire), "seq", split_axis=1, concat_axis=2, tiled=True
+    ).astype(jnp.float32)
     return columns.reshape(batch, columns.shape[1], shard_count, row_count)
 
 
-def to_rows(columns):
+def to_rows(columns, wire=jnp.float32):
     batch, chan_count, shard_count, row_count = columns.shape
-    rows = lax.all_to_all(columns, "seq", split_axis=2, concat_axis=1, tiled=True)
+    rows = lax.all_to_all(
+        columns.astype(wire), "seq", split_axis=2, concat_axis=1, tiled=True
+    ).astype(jnp.float32)
     return jnp.swapaxes(rows.reshape(batch, shard_count * chan_count, row_count), 1, 2)
 
 
@@ -114,23 +117,24 @@
     tables = transform_tables(shard_count, row_count)
     filt_spec = forward_spectrum(to_columns(long_filter[None]), tables)
     width = tokens.shape[1]
-    parts = panel_parts(jnp.concatenate([tokens, cotangent], axis=0))
     projected = 0.0
-    grad_gated = 0.0
-    for part, source in parts:
+    for part, source in panel_parts(tokens):
         projected = projected + jnp.einsum(
             "td,jdc->jtc",
-            part[:row_count],
+            part,
             lax.dynamic_slice_in_dim(in_weight, source * width, width, axis=1),
             preferred_element_type=jnp.float32,
         )
+    grad_gated = 0.0
+    for part, source in panel_parts(cotangent):
         grad_gated = grad_gated + lax.dot_general(
-            part[row_count:],
+            part,
             lax.dynamic_slice_in_dim(out_weight, source * width, width, axis=1),
             (((1,), (1,)), ((), ())),
             preferred_element_type=jnp.float32,
         )
     projected = projected.astype(jnp.bfloat16)
+
     before = shifted(projected[:, row_count - (tap_count - 1) :, :], "seq", 1)
     extended = jnp.concatenate([before, projected], axis=1).astype(jnp.float32)
     filtered = short_kernel[0][:, None, :] * extended[:, tap_count - 1 :, :]
@@ -143,7 +147,7 @@
     gate_out, gate_in, value_path = (filtered[0], filtered[1], filtered[2])
     signal = value_path * gate_in
     grad_state = grad_gated * gate_out
-    spectra = forward_spectrum(to_columns(jnp.stack([signal, grad_state])), tables)
+    spectra = forward_spectrum(to_columns(jnp.stack([signal, grad_state]), WIRE), tables)
     filt_real, filt_imag = filt_spec[:, :, :, 0], filt_spec[:, :, :, 1]
     sig_real, sig_imag = spectra[0:1, :, :, 0], spectra[0:1, :, :, 1]
     grad_real, grad_imag = spectra[1:2, :, :, 0], spectra[1:2, :, :, 1]
@@ -159,7 +163,7 @@
             ),
         ]
     )
-    convolved = to_rows(inverse_spectrum(product, tables))
+    convolved = to_rows(inverse_spectrum(product, tables), WIRE)
     conv_state = convolved[0] + skip_gain[None, :] * signal
     grad_signal = convolved[1] + skip_gain[None, :] * grad_state
     gated_state = (conv_state * gate_out).astype(jnp.bfloat16)

time: 112 us -> 110 us (0.982)
  waiting for transfers between devices: 30.4 us -> 21.5 us
  starting transfers between devices: 22.4 us -> 28.8 us
  other arithmetic: 7.17 us -> 12.2 us
  local copies, waits for them, and re-layouts: 13.5 us -> 9.98 us
  matrix products: 24.1 us -> 22.7 us
    ppermute x3 -> x6, waiting for transfers between devices: 6.58 us -> 0.68 us  [panel_parts(): lax.ppermute(value, 'panel', [(i, (i + k) % count) for i in range(count)])]
    ppermute x3 -> x6, starting transfers between devices: 6.09 us -> 10.3 us  [panel_parts(): lax.ppermute(value, 'panel', [(i, (i + k) % count) for i in range(count)])]
    all_to_all x2, waiting for transfers between devices: 8.16 us -> 6.19 us  [to_columns(): lax.all_to_all(jnp.swapaxes(rows, 1, 2).astype(wire), 'seq', split_axis=1...]
    ppermute x6, starting transfers between devices: 5.08 us -> 6.97 us  [panel_reduce_scatter(): lax.ppermute(sent, 'panel', [(i, (i + k) % count) for i in range(count)])]
    unnamed x34 -> x27, local copies, waits for them, and re-layouts: 5.91 us -> 4.23 us
    dot_general x8, matrix products: 9.09 us -> 7.42 us  [the longest x4 4.7 us: local(): jnp.einsum('td,jdc->jtc', part, lax.dynamic_slice_in_dim(in_weight, sourc...]
    concatenate x1 -> x0, local copies, waits for them, and re-layouts: 1.55 us -> none  [local(): parts = panel_parts(jnp.concatenate([tokens, cotangent], axis=0))]
    another operation x1, other arithmetic: 1.45 us -> 2.77 us  [transform_tables(): jnp.stack([jnp.stack([cos_b, -sin_b], axis=1), jnp.stack([sin_b, cos_b],...]
  transfers between devices with their start and end apart: 13 -> 16, of which waited for: 6 -> 5; matrix products, arithmetic and copies ran while one was open for 16% -> 24% of each run, Pallas kernels for 0% -> 0%
where the time goes in v5:
time: 110 us; the launch traced here: 108 us
  starting transfers between devices  28.8 us (26%)
  matrix products  22.7 us (21%)
  waiting for transfers between devices  21.5 us (20%)
  other arithmetic  12.2 us (11%)
  blocking collectives  12.1 us (11%)
  local copies, waits for them, and re-layouts  9.98 us (9%)
  between operations  1.2 us (1%)
    ppermute x6, waiting for transfers between devices, panel_reduce_scatter(): lax.ppermute(sent, 'panel', [(i, (i + k) % count) for i in range(count)])  14.6 us
    all_to_all x1, blocking collectives, to_rows(): lax.all_to_all(columns.astype(wire), 'seq', split_axis=2, concat_axis=1,...  12.1 us
    ppermute x6, starting transfers between devices, panel_parts(): lax.ppermute(value, 'panel', [(i, (i + k) % count) for i in range(count)])  10.3 us
    all_to_all x2, starting transfers between devices, to_columns(): lax.all_to_all(jnp.swapaxes(rows, 1, 2).astype(wire), 'seq', split_axis=1...  8.04 us
    ppermute x6, starting transfers between devices, panel_reduce_scatter(): lax.ppermute(sent, 'panel', [(i, (i + k) % count) for i in range(count)])  6.97 us
    all_to_all x2, waiting for transfers between devices, to_columns(): lax.all_to_all(jnp.swapaxes(rows, 1, 2).astype(wire), 'seq', split_axis=1...  6.19 us
    dot_general x4, matrix products, local(): jnp.einsum('td,jdc->jtc', part, lax.dynamic_slice_in_dim(in_weight, sourc...  4.7 us
    unnamed x27, local copies, waits for them, and re-layouts  4.23 us
  transfers between devices with their start and end apart: 16, of which 5 were waited for; matrix products, arithmetic and copies ran while one was open for 24% of the time, Pallas kernels for 0%

profile of v5, /device:TPU:0, one launch (start us, length us, event | category | flops | bytes accessed | tf_op | source)
XLA Modules:
  0.0 108.4 jit_solution(39392062306511381)
XLA Ops:
  0.7 3.1 %collective-permute-start = (bf16[256,256]{1,0:T(8,128)(2,1)}, bf16[256,256]{1,0:T(8,128)(2,1)}, u32[]{:S(2)}, u32[]{:S(2)}) collective-permute-start(bf16[256,256]{1,0:T(8,128)(2,1)} %param.7), channel_id=1, source_target_pairs={{0,1},{1,2},{2,3},{3,0},{4,5},{5,6},{6,7},{7,4},{8,9},{9,10},{10,1... | collective-permute-start | bytes 393224 | tf_op jit(solution)/shard_map/ppermute | solution.py:25
  3.8 2.1 %collective-permute-start.2 = (bf16[256,256]{1,0:T(8,128)(2,1)}, bf16[256,256]{1,0:T(8,128)(2,1)}, u32[]{:S(2)}, u32[]{:S(2)}) collective-permute-start(bf16[256,256]{1,0:T(8,128)(2,1)} %param.7), channel_id=1, source_target_pairs={{0,3},{1,0},{2,1},{3,2},{4,7},{5,4},{6,5},{7,6},{8,11},{9,8},{10,9... | collective-permute-start | bytes 393224 | tf_op jit(solution)/shard_map/ppermute | solution.py:25
  5.9 0.9 collective-permute-start.1
  6.8 1.6 %collective-permute-start.4 = (bf16[256,256]{1,0:T(8,128)(2,1)}, bf16[256,256]{1,0:T(8,128)(2,1)}, u32[]{:S(2)}, u32[]{:S(2)}) collective-permute-start(bf16[256,256]{1,0:T(8,128)(2,1)} %param.8), channel_id=1, source_target_pairs={{0,1},{1,2},{2,3},{3,0},{4,5},{5,6},{6,7},{7,4},{8,9},{9,10},{10,1... | collective-permute-start | bytes 393224 | tf_op jit(solution)/shard_map/ppermute | solution.py:25
  8.4 2.2 %collective-permute-start.6 = (bf16[256,256]{1,0:T(8,128)(2,1)}, bf16[256,256]{1,0:T(8,128)(2,1)}, u32[]{:S(2)}, u32[]{:S(2)}) collective-permute-start(bf16[256,256]{1,0:T(8,128)(2,1)} %param.8), channel_id=1, source_target_pairs={{0,3},{1,0},{2,1},{3,2},{4,7},{5,4},{6,5},{7,6},{8,11},{9,8},{10,9... | collective-permute-start | bytes 393224 | tf_op jit(solution)/shard_map/ppermute | solution.py:25
  10.6 1.8 %copy.63 = f32[1,256,256]{1,0,2:T(1,128)} copy(f32[1,256,256]{2,1,0:T(8,128)} %bitcast.216) | data formatting | bytes 524288 | tf_op jit(solution)/shard_map/broadcast_in_dim | solution.py:118
  12.4 3.7 %all-to-all-start.1 = ((f32[1,256,256]{2,0,1:T(1,128)}), f32[1,256,256]{2,0,1:T(1,128)S(1)}, u32[]{:S(2)}, u32[]{:S(2)}) async-start(f32[1,256,256]{2,0,1:T(1,128)} %bitcast.36), calls=%async_computation.1 | async-start | bytes 524288 | tf_op jit(solution)/shard_map/all_to_all | solution.py:85
  16.8 0.7 iota_multiply_fusion
  17.4 0.6 iota_multiply_fusion.2
  18.0 1.8 %fusion.85 = (f32[256,1,256]{2,0,1:T(8,128)}, f32[256,1,256]{2,0,1:T(8,128)}) fusion(), kind=kLoop, calls=%fused_computation.126 | loop fusion | flops 983040 | bytes 524288 | tf_op jit(solution)/shard_map/sin | solution.py:62
  19.8 1.7 %fusion.87 = f32[256,1,256]{2,0,1:T(8,128)} fusion(), kind=kLoop, calls=%fused_computation.128 | loop fusion | flops 1048576 | bytes 262144 | tf_op jit(solution)/shard_map/neg | solution.py:67
  21.5 0.7 slice_bitcast_fusion.5
  22.2 1.2 %fusion.52 = f32[3,256,256]{1,2,0:T(8,128)S(1)} fusion(bf16[3,1024,256]{2,1,0:T(8,128)(2,1)S(1)} %copy-done, s32[]{:T(128)S(6)} %select_n.148, bf16[256,256]{1,0:T(8,128)(2,1)} %param.7), kind=kOutput, calls=%fused_computation.91 | convolution fusion | flops 100663296 | bytes 1310724 | tf_op jit(solution)/shard_map/td,jdc->jtc/dot_general | solution.py:122
  23.6 0.7 fusion.116
  24.3 0.8 fusion.133
  25.1 2.8 %fusion.40 = (f32[1,256,2,256]{3,1,2,0:T(8,128)}, f32[1,256,2,256]{3,1,0,2:T(8,128)}, f32[1,256,2,256]{3,1,0,2:T(8,128)}, f32[1,256,2,256]{3,1,2,0:T(8,128)}) fusion(f32[256,1,256]{2,0,1:T(8,128)} %get-tuple-element.35, f32[256,1,256]{2,0,1:T(8,128)} %fusion.87, f32[256,1,256]{2,0,1:T(8,128)} %get-tuple-element.34), kind=kLoop, calls=%fused_computation.68 | loop fusion | flops 524288 | bytes 2883584 | tf_op jit(solution)/shard_map/stack | solution.py:66
  28.3 1.2 %convolution_add_fusion.1 = f32[3,256,256]{1,2,0:T(8,128)S(1)} fusion(f32[3,256,256]{1,2,0:T(8,128)S(1)} %fusion.52, bf16[3,1024,256]{2,1,0:T(8,128)(2,1)S(1)} %copy-done, s32[]{:T(128)S(6)} %select_n.150, bf16[256,256]{1,0:T(8,128)(2,1)} %collective-permute-done), kind=kOutput, calls=%fused_computation.19 | convolution fusion | flops 100859904 | bytes 2097156 | tf_op jit(solution)/shard_map/td,jdc->jtc/dot_general | solution.py:122
  29.4 1.2 %fusion.45 = f32[3,256,256]{1,2,0:T(8,128)S(1)} fusion(bf16[3,1024,256]{2,1,0:T(8,128)(2,1)S(1)} %copy-done, s32[]{:T(128)S(6)} %select_n.154, bf16[256,256]{1,0:T(8,128)(2,1)} %collective-permute-done.2), kind=kOutput, calls=%fused_computation.84 | convolution fusion | flops 100663296 | bytes 1310724 | tf_op jit(solution)/shard_map/td,jdc->jtc/dot_general | solution.py:122
  30.6 1.2 %fusion.21 = bf16[3,256,256]{2,1,0:T(8,128)(2,1)S(1)} fusion(f32[3,256,256]{1,2,0:T(8,128)S(1)} %fusion.45, f32[3,256,256]{1,2,0:T(8,128)S(1)} %convolution_add_fusion.1, bf16[3,1024,256]{2,1,0:T(8,128)(2,1)S(1)} %copy-done, s32[]{:T(128)S(6)} %select_n.152, bf16[256,256]{1,0:T(8,128)(2,1)} %collective-permute-done.1), kind=kOutput, calls=%fused_computation.22 | convolution fusion | flops 101253120 | bytes 2490372 | tf_op jit(solution)/shard_map/td,jdc->jtc/dot_general | solution.py:122
  31.8 2.1 %collective-permute-start.3 = (bf16[3,2,256]{2,1,0:T(2,128)(2,1)S(1)}, bf16[3,2,256]{2,1,0:T(2,128)(2,1)S(1)}, u32[]{:S(2)}, u32[]{:S(2)}) collective-permute-start(bf16[3,2,256]{2,1,0:T(2,128)(2,1)S(1)} %slice.111), channel_id=1, source_target_pairs={{0,4},{4,8},{8,12},{12,16},{16,20},{20,24},{24,28},{1,5},{5,9},{9,... | collective-permute-start | bytes 9224 | tf_op jit(solution)/shard_map/ppermute | solution.py:17
  34.0 1.1 %convolution_add_fusion.3 = f32[256,256]{0,1:T(8,128)S(1)} fusion(f32[256,256]{0,1:T(8,128)S(1)} %fusion.97, bf16[256,256]{1,0:T(8,128)(2,1)} %collective-permute-done.4, bf16[256,1024]{1,0:T(8,128)(2,1)S(1)} %copy-done.3, s32[]{:T(128)S(6)} %select_n.150), kind=kOutput, calls=%fused_computation.30 | convolution fusion | flops 33619968 | bytes 786436 | tf_op jit(solution)/shard_map/dot_general | solution.py:130
  35.1 1.1 %fusion.89 = f32[256,256]{0,1:T(8,128)S(1)} fusion(bf16[256,256]{1,0:T(8,128)(2,1)} %collective-permute-done.6, bf16[256,1024]{1,0:T(8,128)(2,1)S(1)} %copy-done.3, s32[]{:T(128)S(6)} %select_n.154), kind=kOutput, calls=%fused_computation.130 | convolution fusion | flops 33554432 | bytes 524292 | tf_op jit(solution)/shard_map/dot_general | solution.py:130
  36.3 0.7 collective-permute-done.5
  38.0 1.0 copy.32
  39.0 4.3 %all-to-all-start = ((f32[2,256,256]{2,0,1:T(2,128)}), f32[2,256,256]{2,0,1:T(2,128)}, u32[]{:S(2)}, u32[]{:S(2)}) async-start(f32[2,256,256]{2,0,1:T(2,128)} %copy.32), calls=%async_computation | async-start | bytes 1048576 | tf_op jit(solution)/shard_map/all_to_all | solution.py:85
  43.4 1.0 convolution_bitcast_fusion.2
  44.6 0.8 copy-done.5
  45.6 1.1 %convolution_bitcast_fusion.1 = f32[1,32,2,2,8,256]{5,1,4,2,0,3:T(8,128)S(1)} fusion(f32[32,2,2,8,256]{4,3,0,2,1:T(8,128)S(1)} %maximum_bitcast_fusion.3, f32[1,256,2,256]{3,1,0,2:T(8,128)S(1)} %copy-done.5, f32[1,256,2,256]{3,1,0,2:T(8,128)S(1)} %copy-done.7), kind=kOutput, calls=%fused_computation.15 | convolution fusion | flops 805568512 | bytes 3145728 | tf_op jit(solution)/shard_map/bcerkm,rmsq->bceskq/dot_general | solution.py:103
  46.7 6.2 %all-to-all-done = f32[2,256,256]{2,0,1:T(2,128)} async-done(((f32[2,256,256]{2,0,1:T(2,128)}), f32[2,256,256]{2,0,1:T(2,128)}, u32[]{:S(2)}, u32[]{:S(2)}) %all-to-all-start) | async-done | bytes 524320 | tf_op jit(solution)/shard_map/all_to_all | solution.py:85
  52.9 2.9 %convolution_bitcast_fusion = f32[2,32,2,2,8,256]{5,4,3,2,1,0:T(8,128)S(1)} fusion(f32[2,8,32,256]{3,0,2,1:T(2,128)} %bitcast.20, f32[2,1,8,8]{3,2,1,0:T(8,128)S(1)} %get-tuple-element.33, f32[2,1,8,8]{3,2,1,0:T(8,128)S(1)} %get-tuple-element.32), kind=kOutput, calls=%fused_computation.14 | convolution fusion | flops 50331904 | bytes 2622464 | tf_op jit(solution)/shard_map/erkp,bcpm->bcerkm/dot_general | solution.py:101
  56.4 0.8 copy-done.6
  57.4 2.7 %fusion.10 = f32[2,32,2,2,8,256]{5,1,4,2,0,3:T(8,128)S(1)} fusion(f32[2,32,2,2,8,256]{5,4,3,2,1,0:T(8,128)S(1)} %pad_maximum_fusion, f32[1,256,2,256]{3,1,0,2:T(8,128)S(1)} %copy-done.6, f32[1,256,2,256]{3,1,0,2:T(8,128)S(1)} %copy-done.8), kind=kOutput, calls=%fused_computation.12 | convolution fusion | flops 1610874880 | bytes 5242880 | tf_op jit(solution)/shard_map/bcerkm,rmsq->bceskq/dot_general | solution.py:103
  60.7 0.9 copy-done.9
  61.7 2.7 %fusion.13 = f32[2,32,2,2,8,256]{5,4,3,2,1,0:T(8,128)S(1)} fusion(f32[2,32,2,2,8,256,1]{5,1,4,2,0,3,6:T(8,128)S(1)} %maximum_bitcast_fusion, f32[1,256,2,256]{3,1,2,0:T(8,128)S(1)} %copy-done.10, f32[1,256,2,256]{3,1,2,0:T(8,128)S(1)} %copy-done.9), kind=kOutput, calls=%fused_computation.13 | convolution fusion | flops 1610874880 | bytes 5242880 | tf_op jit(solution)/shard_map/bceskq,sqrm->bcerkm/dot_general | solution.py:108
  64.8 1.4 %fusion.18 = f32[2,32,8,256]{3,2,1,0:T(8,128)S(1)} fusion(f32[2,32,2,1,8,256]{5,4,3,2,1,0:T(8,128)S(1)} %get-tuple-element.11, f32[2,32,2,1,8,256]{5,4,3,2,1,0:T(8,128)S(1)} %get-tuple-element.10, f32[2,1,8,8]{3,2,1,0:T(8,128)S(1)} %get-tuple-element.33, f32[2,1,8,8]{3,2,1,0:T(8,128)S(1)} %get-tuple-element.32), kind=kOutput, calls=%fused_computation.21 | convolution fusion | flops 50856448 | bytes 2622464 | tf_op jit(solution)/shard_map/erkp,bcerkm->bcpm/dot_general | solution.py:110
  66.4 12.1 %all_to_all.45 = f32[2,32,8,256]{3,1,0,2:T(8,128)S(1)} all-to-all(f32[2,32,8,256]{3,1,0,2:T(8,128)S(1)} %copy.43), channel_id=1, replica_groups=mesh['seq'=8,'panel'=4] {'seq'}, dimensions={2} | all-to-all | bytes 1048576 | tf_op jit(solution)/shard_map/all_to_all | solution.py:93
  78.6 0.8 copy.44
  79.4 1.2 %copy.45 = f32[2,256,256]{1,2,0:T(8,128)S(1)} copy(f32[2,256,256]{2,1,0:T(8,128)} %bitcast.214) | data formatting | bytes 1048576 | tf_op jit(solution)/shard_map/reshape | solution.py:96
  80.8 0.8 copy-done.4
  82.1 1.3 %collective-permute-start.10 = (f32[3,2,256]{2,1,0:T(2,128)S(1)}, f32[3,2,256]{2,1,0:T(2,128)S(1)}, u32[]{:S(2)}, u32[]{:S(2)}) collective-permute-start(f32[3,2,256]{2,1,0:T(2,128)S(1)} %slice.132), channel_id=1, source_target_pairs={{4,0},{8,4},{12,8},{16,12},{20,16},{24,20},{28,24},{5,1},{9,5},{13... | collective-permute-start | bytes 18440 | tf_op jit(solution)/shard_map/ppermute | solution.py:17
  83.6 2.5 %collective-permute-start.8 = (bf16[256,256]{1,0:T(8,128)(2,1)S(1)}, bf16[256,256]{1,0:T(8,128)(2,1)S(1)}, u32[]{:S(2)}, u32[]{:S(2)}) collective-permute-start(bf16[256,256]{1,0:T(8,128)(2,1)S(1)} %convolution_convert_fusion.1), channel_id=1, source_target_pairs={{0,2},{1,3},{2,0},{3,1},{4,6},{5,7},{6,4},{7,5},{8,10},{9,11},{10,... | collective-permute-start | bytes 393224 | tf_op jit(solution)/shard_map/ppermute | solution.py:36
  86.2 3.8 %collective-permute-start.9 = (bf16[256,256]{1,0:T(8,128)(2,1)S(1)}, bf16[256,256]{1,0:T(8,128)(2,1)S(1)}, u32[]{:S(2)}, u32[]{:S(2)}) collective-permute-start(bf16[256,256]{1,0:T(8,128)(2,1)S(1)} %convolution_convert_fusion), channel_id=1, source_target_pairs={{0,3},{1,0},{2,1},{3,2},{4,7},{5,4},{6,5},{7,6},{8,11},{9,8},{10,9... | collective-permute-start | bytes 393224 | tf_op jit(solution)/shard_map/ppermute | solution.py:36
  91.0 0.6 collective-permute-start.11
  91.9 4.3 %collective-permute-done.8 = bf16[256,256]{1,0:T(8,128)(2,1)S(1)} collective-permute-done((bf16[256,256]{1,0:T(8,128)(2,1)S(1)}, bf16[256,256]{1,0:T(8,128)(2,1)S(1)}, u32[]{:S(2)}, u32[]{:S(2)}) %collective-permute-start.8) | collective-permute-done | bytes 131104 | tf_op jit(solution)/shard_map/ppermute | solution.py:36
  96.2 1.7 %collective-permute-done.9 = bf16[256,256]{1,0:T(8,128)(2,1)S(1)} collective-permute-done((bf16[256,256]{1,0:T(8,128)(2,1)S(1)}, bf16[256,256]{1,0:T(8,128)(2,1)S(1)}, u32[]{:S(2)}, u32[]{:S(2)}) %collective-permute-start.9) | collective-permute-done | bytes 131104 | tf_op jit(solution)/shard_map/ppermute | solution.py:36
  97.9 0.9 add_convert_fusion
  98.8 8.6 %collective-permute-done.12 = bf16[256,256]{1,0:T(8,128)(2,1)S(1)} collective-permute-done((bf16[256,256]{1,0:T(8,128)(2,1)S(1)}, bf16[256,256]{1,0:T(8,128)(2,1)S(1)}, u32[]{:S(2)}, u32[]{:S(2)}) %collective-permute-start.12) | collective-permute-done | bytes 131104 | tf_op jit(solution)/shard_map/ppermute | solution.py:36
  107.4 1.0 fusion.63
  (69 shorter events, 6.8 us)
Async XLA Ops:
  0.6 21.5 %copy-start = (bf16[3,1024,256]{2,1,0:T(8,128)(2,1)S(1)}, bf16[3,1024,256]{2,1,0:T(8,128)(2,1)}, u32[]{:S(2)}) copy-start(bf16[3,1024,256]{2,1,0:T(8,128)(2,1)} %param.9) | copy-start | bytes 4718596
  0.6 22.7 %copy-start.11 = (bf16[256,256]{1,0:T(8,128)(2,1)S(1)}, bf16[256,256]{1,0:T(8,128)(2,1)}, u32[]{:S(2)}) copy-start(bf16[256,256]{1,0:T(8,128)(2,1)} %param.8) | copy-start | bytes 393220
  0.7 22.7 %copy-start.3 = (bf16[256,1024]{1,0:T(8,128)(2,1)S(1)}, bf16[256,1024]{1,0:T(8,128)(2,1)}, u32[]{:S(2)}) copy-start(bf16[256,1024]{1,0:T(8,128)(2,1)} %param.13) | copy-start | bytes 1572868
  0.7 27.2 %collective-permute-start = (bf16[256,256]{1,0:T(8,128)(2,1)}, bf16[256,256]{1,0:T(8,128)(2,1)}, u32[]{:S(2)}, u32[]{:S(2)}) collective-permute-start(bf16[256,256]{1,0:T(8,128)(2,1)} %param.7), channel_id=1, source_target_pairs={{0,1},{1,2},{2,3},{3,0},{4,5},{5,6},{6,7},{7,4},{8,9},{9,10},{10,1... | collective-permute-start | bytes 393224 | tf_op jit(solution)/shard_map/ppermute | solution.py:25
  3.8 25.7 %collective-permute-start.2 = (bf16[256,256]{1,0:T(8,128)(2,1)}, bf16[256,256]{1,0:T(8,128)(2,1)}, u32[]{:S(2)}, u32[]{:S(2)}) collective-permute-start(bf16[256,256]{1,0:T(8,128)(2,1)} %param.7), channel_id=1, source_target_pairs={{0,3},{1,0},{2,1},{3,2},{4,7},{5,4},{6,5},{7,6},{8,11},{9,8},{10,9... | collective-permute-start | bytes 393224 | tf_op jit(solution)/shard_map/ppermute | solution.py:25
  5.9 24.8 %collective-permute-start.1 = (bf16[256,256]{1,0:T(8,128)(2,1)}, bf16[256,256]{1,0:T(8,128)(2,1)}, u32[]{:S(2)}, u32[]{:S(2)}) collective-permute-start(bf16[256,256]{1,0:T(8,128)(2,1)} %param.7), channel_id=1, source_target_pairs={{0,2},{1,3},{2,0},{3,1},{4,6},{5,7},{6,4},{7,5},{8,10},{9,11},{10,... | collective-permute-start | bytes 393224 | tf_op jit(solution)/shard_map/ppermute | solution.py:25
  6.8 27.2 %collective-permute-start.4 = (bf16[256,256]{1,0:T(8,128)(2,1)}, bf16[256,256]{1,0:T(8,128)(2,1)}, u32[]{:S(2)}, u32[]{:S(2)}) collective-permute-start(bf16[256,256]{1,0:T(8,128)(2,1)} %param.8), channel_id=1, source_target_pairs={{0,1},{1,2},{2,3},{3,0},{4,5},{5,6},{6,7},{7,4},{8,9},{9,10},{10,1... | collective-permute-start | bytes 393224 | tf_op jit(solution)/shard_map/ppermute | solution.py:25
  8.4 26.7 %collective-permute-start.6 = (bf16[256,256]{1,0:T(8,128)(2,1)}, bf16[256,256]{1,0:T(8,128)(2,1)}, u32[]{:S(2)}, u32[]{:S(2)}) collective-permute-start(bf16[256,256]{1,0:T(8,128)(2,1)} %param.8), channel_id=1, source_target_pairs={{0,3},{1,0},{2,1},{3,2},{4,7},{5,4},{6,5},{7,6},{8,11},{9,8},{10,9... | collective-permute-start | bytes 393224 | tf_op jit(solution)/shard_map/ppermute | solution.py:25
  12.4 26.6 %all-to-all-start.1 = ((f32[1,256,256]{2,0,1:T(1,128)}), f32[1,256,256]{2,0,1:T(1,128)S(1)}, u32[]{:S(2)}, u32[]{:S(2)}) async-start(f32[1,256,256]{2,0,1:T(1,128)} %bitcast.36), calls=%async_computation.1 | async-start | bytes 524288 | tf_op jit(solution)/shard_map/all_to_all | solution.py:85
  27.9 9.1 %collective-permute-start.5 = (bf16[256,256]{1,0:T(8,128)(2,1)}, bf16[256,256]{1,0:T(8,128)(2,1)S(1)}, u32[]{:S(2)}, u32[]{:S(2)}) collective-permute-start(bf16[256,256]{1,0:T(8,128)(2,1)} %param.8), channel_id=1, source_target_pairs={{0,2},{1,3},{2,0},{3,1},{4,6},{5,7},{6,4},{7,5},{8,10},{9,11},{10,... | collective-permute-start | bytes 393224 | tf_op jit(solution)/shard_map/ppermute | solution.py:25
  31.8 5.4 %collective-permute-start.3 = (bf16[3,2,256]{2,1,0:T(2,128)(2,1)S(1)}, bf16[3,2,256]{2,1,0:T(2,128)(2,1)S(1)}, u32[]{:S(2)}, u32[]{:S(2)}) collective-permute-start(bf16[3,2,256]{2,1,0:T(2,128)(2,1)S(1)} %slice.111), channel_id=1, source_target_pairs={{0,4},{4,8},{8,12},{12,16},{16,20},{20,24},{24,28},{1,5},{5,9},{9,... | collective-permute-start | bytes 9224 | tf_op jit(solution)/shard_map/ppermute | solution.py:17
  37.2 0.7 copy-start.1
  39.0 13.9 %all-to-all-start = ((f32[2,256,256]{2,0,1:T(2,128)}), f32[2,256,256]{2,0,1:T(2,128)}, u32[]{:S(2)}, u32[]{:S(2)}) async-start(f32[2,256,256]{2,0,1:T(2,128)} %copy.32), calls=%async_computation | async-start | bytes 1048576 | tf_op jit(solution)/shard_map/all_to_all | solution.py:85
  44.4 1.0 copy-start.5
  44.4 1.2 %copy-start.7 = (f32[1,256,2,256]{3,1,0,2:T(8,128)S(1)}, f32[1,256,2,256]{3,1,0,2:T(8,128)}, u32[]{:S(2)}) copy-start(f32[1,256,2,256]{3,1,0,2:T(8,128)} %get-tuple-element.24) | copy-start | bytes 1572868
  56.2 1.0 copy-start.6
  56.2 1.2 %copy-start.8 = (f32[1,256,2,256]{3,1,0,2:T(8,128)S(1)}, f32[1,256,2,256]{3,1,0,2:T(8,128)}, u32[]{:S(2)}) copy-start(f32[1,256,2,256]{3,1,0,2:T(8,128)} %get-tuple-element.24) | copy-start | bytes 1572868
  60.5 1.0 copy-start.9
  60.5 1.2 %copy-start.10 = (f32[1,256,2,256]{3,1,2,0:T(8,128)S(1)}, f32[1,256,2,256]{3,1,2,0:T(8,128)}, u32[]{:S(2)}) copy-start(f32[1,256,2,256]{3,1,2,0:T(8,128)} %get-tuple-element.25) | copy-start | bytes 1572868
  66.2 14.4 %copy-start.2 = (f32[256,256]{1,0:T(8,128)S(1)}, f32[256,256]{1,0:T(8,128)}, u32[]{:S(2)}) copy-start(f32[256,256]{1,0:T(8,128)} %copy-done.1) | copy-start | bytes 786436
  66.2 14.4 %copy-start.12 = (f32[256]{0:T(256)S(1)}, f32[256]{0:T(256)}, u32[]{:S(2)}) copy-start(f32[256]{0:T(256)} %param.11) | copy-start | bytes 3076
  80.6 1.0 copy-start.4
  82.1 7.9 %collective-permute-start.10 = (f32[3,2,256]{2,1,0:T(2,128)S(1)}, f32[3,2,256]{2,1,0:T(2,128)S(1)}, u32[]{:S(2)}, u32[]{:S(2)}) collective-permute-start(f32[3,2,256]{2,1,0:T(2,128)S(1)} %slice.132), channel_id=1, source_target_pairs={{4,0},{8,4},{12,8},{16,12},{20,16},{24,20},{28,24},{5,1},{9,5},{13... | collective-permute-start | bytes 18440 | tf_op jit(solution)/shard_map/ppermute | solution.py:17
  83.6 12.6 %collective-permute-start.8 = (bf16[256,256]{1,0:T(8,128)(2,1)S(1)}, bf16[256,256]{1,0:T(8,128)(2,1)S(1)}, u32[]{:S(2)}, u32[]{:S(2)}) collective-permute-start(bf16[256,256]{1,0:T(8,128)(2,1)S(1)} %convolution_convert_fusion.1), channel_id=1, source_target_pairs={{0,2},{1,3},{2,0},{3,1},{4,6},{5,7},{6,4},{7,5},{8,10},{9,11},{10,... | collective-permute-start | bytes 393224 | tf_op jit(solution)/shard_map/ppermute | solution.py:36
  86.2 10.1 %collective-permute-start.7 = (bf16[256,256]{1,0:T(8,128)(2,1)S(1)}, bf16[256,256]{1,0:T(8,128)(2,1)S(1)}, u32[]{:S(2)}, u32[]{:S(2)}) collective-permute-start(bf16[256,256]{1,0:T(8,128)(2,1)S(1)} %convolution_convert_fusion.2), channel_id=1, source_target_pairs={{0,1},{1,2},{2,3},{3,0},{4,5},{5,6},{6,7},{7,4},{8,9},{9,10},{10,1... | collective-permute-start | bytes 393224 | tf_op jit(solution)/shard_map/ppermute | solution.py:36
  86.2 11.8 %collective-permute-start.9 = (bf16[256,256]{1,0:T(8,128)(2,1)S(1)}, bf16[256,256]{1,0:T(8,128)(2,1)S(1)}, u32[]{:S(2)}, u32[]{:S(2)}) collective-permute-start(bf16[256,256]{1,0:T(8,128)(2,1)S(1)} %convolution_convert_fusion), channel_id=1, source_target_pairs={{0,3},{1,0},{2,1},{3,2},{4,7},{5,4},{6,5},{7,6},{8,11},{9,8},{10,9... | collective-permute-start | bytes 393224 | tf_op jit(solution)/shard_map/ppermute | solution.py:36
  91.0 16.4 %collective-permute-start.12 = (bf16[256,256]{1,0:T(8,128)(2,1)S(1)}, bf16[256,256]{1,0:T(8,128)(2,1)S(1)}, u32[]{:S(2)}, u32[]{:S(2)}) collective-permute-start(bf16[256,256]{1,0:T(8,128)(2,1)S(1)} %fusion.25), channel_id=1, source_target_pairs={{0,2},{1,3},{2,0},{3,1},{4,6},{5,7},{6,4},{7,5},{8,10},{9,11},{10,... | collective-permute-start | bytes 393224 | tf_op jit(solution)/shard_map/ppermute | solution.py:36
  91.0 16.4 %collective-permute-start.11 = (bf16[256,256]{1,0:T(8,128)(2,1)S(1)}, bf16[256,256]{1,0:T(8,128)(2,1)S(1)}, u32[]{:S(2)}, u32[]{:S(2)}) collective-permute-start(bf16[256,256]{1,0:T(8,128)(2,1)S(1)} %fusion.24), channel_id=1, source_target_pairs={{0,1},{1,2},{2,3},{3,0},{4,5},{5,6},{6,7},{7,4},{8,9},{9,10},{10,1... | collective-permute-start | bytes 393224 | tf_op jit(solution)/shard_map/ppermute | solution.py:36
  96.2 11.2 %collective-permute-start.13 = (bf16[256,256]{1,0:T(8,128)(2,1)S(1)}, bf16[256,256]{1,0:T(8,128)(2,1)S(1)}, u32[]{:S(2)}, u32[]{:S(2)}) collective-permute-start(bf16[256,256]{1,0:T(8,128)(2,1)S(1)} %fusion.26), channel_id=1, source_target_pairs={{0,3},{1,0},{2,1},{3,2},{4,7},{5,4},{6,5},{7,6},{8,11},{9,8},{10,9... | collective-permute-start | bytes 393224 | tf_op jit(solution)/shard_map/ppermute | solution.py:36

commit v6 on v5

--- a/solution.py
+++ b/solution.py
@@ -8,7 +8,7 @@
 HIGHEST = lax.Precision.HIGHEST
 STAGE_A_PRECISION = lax.Precision.HIGHEST
 STAGE_B_PRECISION = lax.Precision.HIGH
-WIRE = jnp.float32
+WIRE = jnp.bfloat16
 
 
 def shifted(value, axis, steps):

time: 110 us -> 103 us (0.936)
  waiting for transfers between devices: 21.5 us -> 18.7 us
  blocking collectives: 12.1 us -> 9.32 us
  matrix products: 22.7 us -> 21.5 us
    all_to_all x1, blocking collectives: 12.1 us -> 9.32 us  [to_rows(): lax.all_to_all(columns.astype(wire), 'seq', split_axis=2, concat_axis=1,...]
    all_to_all x2, waiting for transfers between devices: 6.19 us -> 3.38 us  [to_columns(): lax.all_to_all(jnp.swapaxes(rows, 1, 2).astype(wire), 'seq', split_axis=1...]
    reshape x1 -> x0, local copies, waits for them, and re-layouts: 1.24 us -> none  [to_rows(): rows.reshape(batch, shard_count * chan_count, row_count)]
  transfers between devices with their start and end apart: 16 -> 16, of which waited for: 5 -> 5; matrix products, arithmetic and copies ran while one was open for 24% -> 25% of each run, Pallas kernels for 0% -> 0%
where the time goes in v6:
time: 103 us; the launch traced here: 101 us
  starting transfers between devices  28.8 us (28%)
  matrix products  21.5 us (21%)
  waiting for transfers between devices  18.7 us (18%)
  other arithmetic  13 us (13%)
  blocking collectives  9.32 us (9%)
  local copies, waits for them, and re-layouts  8.92 us (9%)
  between operations  1.2 us (1%)
    ppermute x6, waiting for transfers between devices, panel_reduce_scatter(): lax.ppermute(sent, 'panel', [(i, (i + k) % count) for i in range(count)])  14.6 us
    ppermute x6, starting transfers between devices, panel_parts(): lax.ppermute(value, 'panel', [(i, (i + k) % count) for i in range(count)])  10.3 us
    all_to_all x1, blocking collectives, to_rows(): lax.all_to_all(columns.astype(wire), 'seq', split_axis=2, concat_axis=1,...  9.32 us
    all_to_all x2, starting transfers between devices, to_columns(): lax.all_to_all(jnp.swapaxes(rows, 1, 2).astype(wire), 'seq', split_axis=1...  7.95 us
    ppermute x6, starting transfers between devices, panel_reduce_scatter(): lax.ppermute(sent, 'panel', [(i, (i + k) % count) for i in range(count)])  7.07 us
    dot_general x4, matrix products, local(): jnp.einsum('td,jdc->jtc', part, lax.dynamic_slice_in_dim(in_weight, sourc...  4.7 us
    unnamed x27, local copies, waits for them, and re-layouts  4.24 us
    dot_general x2, matrix products, forward_spectrum(): jnp.einsum('bcerkm,rmsq->bceskq', spread, stage_b, precision=STAGE_B_PREC...  3.81 us
  transfers between devices with their start and end apart: 16, of which 5 were waited for; matrix products, arithmetic and copies ran while one was open for 25% of the time, Pallas kernels for 0%

profile of v6, /device:TPU:0, one launch (start us, length us, event | category | flops | bytes accessed | tf_op | source)
XLA Modules:
  0.0 101.4 jit_solution(3250132800332185401)
XLA Ops:
  0.7 3.1 %collective-permute-start = (bf16[256,256]{1,0:T(8,128)(2,1)}, bf16[256,256]{1,0:T(8,128)(2,1)}, u32[]{:S(2)}, u32[]{:S(2)}) collective-permute-start(bf16[256,256]{1,0:T(8,128)(2,1)} %param.7), channel_id=1, source_target_pairs={{0,1},{1,2},{2,3},{3,0},{4,5},{5,6},{6,7},{7,4},{8,9},{9,10},{10,1... | collective-permute-start | bytes 393224 | tf_op jit(solution)/shard_map/ppermute | solution.py:25
  3.8 2.1 %collective-permute-start.2 = (bf16[256,256]{1,0:T(8,128)(2,1)}, bf16[256,256]{1,0:T(8,128)(2,1)}, u32[]{:S(2)}, u32[]{:S(2)}) collective-permute-start(bf16[256,256]{1,0:T(8,128)(2,1)} %param.7), channel_id=1, source_target_pairs={{0,3},{1,0},{2,1},{3,2},{4,7},{5,4},{6,5},{7,6},{8,11},{9,8},{10,9... | collective-permute-start | bytes 393224 | tf_op jit(solution)/shard_map/ppermute | solution.py:25
  5.9 0.9 collective-permute-start.1
  6.8 1.6 %collective-permute-start.4 = (bf16[256,256]{1,0:T(8,128)(2,1)}, bf16[256,256]{1,0:T(8,128)(2,1)}, u32[]{:S(2)}, u32[]{:S(2)}) collective-permute-start(bf16[256,256]{1,0:T(8,128)(2,1)} %param.8), channel_id=1, source_target_pairs={{0,1},{1,2},{2,3},{3,0},{4,5},{5,6},{6,7},{7,4},{8,9},{9,10},{10,1... | collective-permute-start | bytes 393224 | tf_op jit(solution)/shard_map/ppermute | solution.py:25
  8.4 2.2 %collective-permute-start.6 = (bf16[256,256]{1,0:T(8,128)(2,1)}, bf16[256,256]{1,0:T(8,128)(2,1)}, u32[]{:S(2)}, u32[]{:S(2)}) collective-permute-start(bf16[256,256]{1,0:T(8,128)(2,1)} %param.8), channel_id=1, source_target_pairs={{0,3},{1,0},{2,1},{3,2},{4,7},{5,4},{6,5},{7,6},{8,11},{9,8},{10,9... | collective-permute-start | bytes 393224 | tf_op jit(solution)/shard_map/ppermute | solution.py:25
  10.6 1.8 %copy.63 = f32[1,256,256]{1,0,2:T(1,128)} copy(f32[1,256,256]{2,1,0:T(8,128)} %bitcast.221) | data formatting | bytes 524288 | tf_op jit(solution)/shard_map/broadcast_in_dim | solution.py:118
  12.4 3.7 %all-to-all-start.1 = ((f32[1,256,256]{2,0,1:T(1,128)}), f32[1,256,256]{2,0,1:T(1,128)S(1)}, u32[]{:S(2)}, u32[]{:S(2)}) async-start(f32[1,256,256]{2,0,1:T(1,128)} %bitcast.36), calls=%async_computation.1 | async-start | bytes 524288 | tf_op jit(solution)/shard_map/all_to_all | solution.py:85
  16.8 0.7 iota_multiply_fusion
  17.4 0.6 iota_multiply_fusion.2
  18.0 1.8 %fusion.91 = (f32[256,1,256]{2,0,1:T(8,128)}, f32[256,1,256]{2,0,1:T(8,128)}) fusion(), kind=kLoop, calls=%fused_computation.130 | loop fusion | flops 983040 | bytes 524288 | tf_op jit(solution)/shard_map/sin | solution.py:62
  19.8 1.7 %fusion.93 = f32[256,1,256]{2,0,1:T(8,128)} fusion(), kind=kLoop, calls=%fused_computation.132 | loop fusion | flops 1048576 | bytes 262144 | tf_op jit(solution)/shard_map/neg | solution.py:67
  21.5 0.7 slice_bitcast_fusion.5
  22.2 1.2 %fusion.56 = f32[3,256,256]{1,2,0:T(8,128)S(1)} fusion(bf16[3,1024,256]{2,1,0:T(8,128)(2,1)S(1)} %copy-done, s32[]{:T(128)S(6)} %select_n.148, bf16[256,256]{1,0:T(8,128)(2,1)} %param.7), kind=kOutput, calls=%fused_computation.90 | convolution fusion | flops 100663296 | bytes 1310724 | tf_op jit(solution)/shard_map/td,jdc->jtc/dot_general | solution.py:122
  23.6 0.7 fusion.121
  24.3 0.8 fusion.138
  25.1 2.8 %fusion.46 = (f32[1,256,2,256]{3,1,2,0:T(8,128)}, f32[1,256,2,256]{3,1,0,2:T(8,128)}, f32[1,256,2,256]{3,1,0,2:T(8,128)}, f32[1,256,2,256]{3,1,2,0:T(8,128)}) fusion(f32[256,1,256]{2,0,1:T(8,128)} %get-tuple-element.35, f32[256,1,256]{2,0,1:T(8,128)} %fusion.93, f32[256,1,256]{2,0,1:T(8,128)} %get-tuple-element.34), kind=kLoop, calls=%fused_computation.70 | loop fusion | flops 524288 | bytes 2883584 | tf_op jit(solution)/shard_map/stack | solution.py:66
  28.3 1.2 %convolution_add_fusion.1 = f32[3,256,256]{1,2,0:T(8,128)S(1)} fusion(f32[3,256,256]{1,2,0:T(8,128)S(1)} %fusion.56, bf16[3,1024,256]{2,1,0:T(8,128)(2,1)S(1)} %copy-done, s32[]{:T(128)S(6)} %select_n.150, bf16[256,256]{1,0:T(8,128)(2,1)} %collective-permute-done), kind=kOutput, calls=%fused_computation.19 | convolution fusion | flops 100859904 | bytes 2097156 | tf_op jit(solution)/shard_map/td,jdc->jtc/dot_general | solution.py:122
  29.4 1.2 %fusion.49 = f32[3,256,256]{1,2,0:T(8,128)S(1)} fusion(bf16[3,1024,256]{2,1,0:T(8,128)(2,1)S(1)} %copy-done, s32[]{:T(128)S(6)} %select_n.154, bf16[256,256]{1,0:T(8,128)(2,1)} %collective-permute-done.2), kind=kOutput, calls=%fused_computation.83 | convolution fusion | flops 100663296 | bytes 1310724 | tf_op jit(solution)/shard_map/td,jdc->jtc/dot_general | solution.py:122
  30.6 1.2 %fusion.21 = bf16[3,256,256]{2,1,0:T(8,128)(2,1)S(1)} fusion(f32[3,256,256]{1,2,0:T(8,128)S(1)} %fusion.49, f32[3,256,256]{1,2,0:T(8,128)S(1)} %convolution_add_fusion.1, bf16[3,1024,256]{2,1,0:T(8,128)(2,1)S(1)} %copy-done, s32[]{:T(128)S(6)} %select_n.152, bf16[256,256]{1,0:T(8,128)(2,1)} %collective-permute-done.1), kind=kOutput, calls=%fused_computation.22 | convolution fusion | flops 101253120 | bytes 2490372 | tf_op jit(solution)/shard_map/td,jdc->jtc/dot_general | solution.py:122
  31.8 2.1 %collective-permute-start.3 = (bf16[3,2,256]{2,1,0:T(2,128)(2,1)S(1)}, bf16[3,2,256]{2,1,0:T(2,128)(2,1)S(1)}, u32[]{:S(2)}, u32[]{:S(2)}) collective-permute-start(bf16[3,2,256]{2,1,0:T(2,128)(2,1)S(1)} %slice.111), channel_id=1, source_target_pairs={{0,4},{4,8},{8,12},{12,16},{16,20},{20,24},{24,28},{1,5},{5,9},{9,... | collective-permute-start | bytes 9224 | tf_op jit(solution)/shard_map/ppermute | solution.py:17
  34.0 1.1 %convolution_add_fusion.3 = f32[256,256]{0,1:T(8,128)S(1)} fusion(f32[256,256]{0,1:T(8,128)S(1)} %fusion.103, bf16[256,256]{1,0:T(8,128)(2,1)} %collective-permute-done.4, bf16[256,1024]{1,0:T(8,128)(2,1)S(1)} %copy-done.3, s32[]{:T(128)S(6)} %select_n.150), kind=kOutput, calls=%fused_computation.31 | convolution fusion | flops 33619968 | bytes 786436 | tf_op jit(solution)/shard_map/dot_general | solution.py:130
  35.1 1.1 %fusion.95 = f32[256,256]{0,1:T(8,128)S(1)} fusion(bf16[256,256]{1,0:T(8,128)(2,1)} %collective-permute-done.6, bf16[256,1024]{1,0:T(8,128)(2,1)S(1)} %copy-done.3, s32[]{:T(128)S(6)} %select_n.154), kind=kOutput, calls=%fused_computation.134 | convolution fusion | flops 33554432 | bytes 524292 | tf_op jit(solution)/shard_map/dot_general | solution.py:130
  36.3 0.7 collective-permute-done.5
  38.0 0.9 copy.32
  38.9 4.2 %all-to-all-start = ((bf16[2,256,256]{2,0,1:T(2,128)(2,1)}), bf16[2,256,256]{2,0,1:T(2,128)(2,1)}, u32[]{:S(2)}, u32[]{:S(2)}) async-start(bf16[2,256,256]{2,0,1:T(2,128)(2,1)} %copy.32), calls=%async_computation | async-start | bytes 524288 | tf_op jit(solution)/shard_map/all_to_all | solution.py:85
  43.2 1.0 convolution_bitcast_fusion.2
  44.4 0.8 copy-done.5
  45.3 1.1 %convolution_bitcast_fusion.1 = f32[1,32,2,2,8,256]{5,1,4,2,0,3:T(8,128)S(1)} fusion(f32[32,2,2,8,256]{4,3,0,2,1:T(8,128)S(1)} %maximum_bitcast_fusion.3, f32[1,256,2,256]{3,1,0,2:T(8,128)S(1)} %copy-done.5, f32[1,256,2,256]{3,1,0,2:T(8,128)S(1)} %copy-done.7), kind=kOutput, calls=%fused_computation.15 | convolution fusion | flops 805568512 | bytes 3145728 | tf_op jit(solution)/shard_map/bcerkm,rmsq->bceskq/dot_general | solution.py:103
  46.5 3.4 %all-to-all-done = bf16[2,256,256]{2,0,1:T(2,128)(2,1)} async-done(((bf16[2,256,256]{2,0,1:T(2,128)(2,1)}), bf16[2,256,256]{2,0,1:T(2,128)(2,1)}, u32[]{:S(2)}, u32[]{:S(2)}) %all-to-all-start) | async-done | bytes 262176 | tf_op jit(solution)/shard_map/all_to_all | solution.py:85
  49.9 2.0 %convolution_bitcast_fusion = f32[2,32,2,2,8,256]{5,4,3,2,1,0:T(8,128)S(1)} fusion(bf16[2,8,32,256]{3,0,2,1:T(2,128)(2,1)} %bitcast.20, f32[2,1,8,8]{3,2,1,0:T(8,128)S(1)} %get-tuple-element.33, f32[2,1,8,8]{3,2,1,0:T(8,128)S(1)} %get-tuple-element.32), kind=kOutput, calls=%fused_computation.14 | convolution fusion | flops 50331904 | bytes 2360320 | tf_op jit(solution)/shard_map/erkp,bcpm->bcerkm/dot_general | solution.py:101
  52.4 0.8 copy-done.6
  53.4 2.7 %fusion.10 = f32[2,32,2,2,8,256]{5,1,4,2,0,3:T(8,128)S(1)} fusion(f32[2,32,2,2,8,256]{5,4,3,2,1,0:T(8,128)S(1)} %pad_maximum_fusion, f32[1,256,2,256]{3,1,0,2:T(8,128)S(1)} %copy-done.6, f32[1,256,2,256]{3,1,0,2:T(8,128)S(1)} %copy-done.8), kind=kOutput, calls=%fused_computation.12 | convolution fusion | flops 1610874880 | bytes 5242880 | tf_op jit(solution)/shard_map/bcerkm,rmsq->bceskq/dot_general | solution.py:103
  56.7 0.9 copy-done.9
  57.7 2.7 %fusion.13 = f32[2,32,2,2,8,256]{5,4,3,2,1,0:T(8,128)S(1)} fusion(f32[2,32,2,2,8,256,1]{5,1,4,2,0,3,6:T(8,128)S(1)} %maximum_bitcast_fusion, f32[1,256,2,256]{3,1,2,0:T(8,128)S(1)} %copy-done.10, f32[1,256,2,256]{3,1,2,0:T(8,128)S(1)} %copy-done.9), kind=kOutput, calls=%fused_computation.13 | convolution fusion | flops 1610874880 | bytes 5242880 | tf_op jit(solution)/shard_map/bceskq,sqrm->bcerkm/dot_general | solution.py:108
  60.8 1.2 %fusion.27 = bf16[2,32,8,256]{3,2,1,0:T(8,128)(2,1)S(1)} fusion(f32[2,32,2,1,8,256]{5,4,3,2,1,0:T(8,128)S(1)} %get-tuple-element.11, f32[2,32,2,1,8,256]{5,4,3,2,1,0:T(8,128)S(1)} %get-tuple-element.10, f32[2,1,8,8]{3,2,1,0:T(8,128)S(1)} %get-tuple-element.33, f32[2,1,8,8]{3,2,1,0:T(8,128)S(1)} %get-tuple-element.32), kind=kOutput, calls=%fused_computation.32 | convolution fusion | flops 50987520 | bytes 2360320 | tf_op jit(solution)/shard_map/erkp,bcerkm->bcpm/dot_general | solution.py:110
  62.1 9.3 %all_to_all.39 = bf16[2,32,8,256]{3,1,0,2:T(8,128)(2,1)S(1)} all-to-all(bf16[2,32,8,256]{3,1,0,2:T(8,128)(2,1)S(1)} %copy.43), channel_id=1, replica_groups=mesh['seq'=8,'panel'=4] {'seq'}, dimensions={2} | all-to-all | bytes 524288 | tf_op jit(solution)/shard_map/all_to_all | solution.py:93
  71.4 0.8 bitcast_convert_fusion
  72.2 1.2 %copy.45 = f32[2,256,256]{1,2,0:T(8,128)S(1)} copy(f32[2,256,256]{2,1,0:T(8,128)} %bitcast.219) | data formatting | bytes 1048576 | tf_op jit(solution)/shard_map/transpose | solution.py:96
  73.7 0.8 copy-done.4
  75.0 1.3 %collective-permute-start.10 = (f32[3,2,256]{2,1,0:T(2,128)S(1)}, f32[3,2,256]{2,1,0:T(2,128)S(1)}, u32[]{:S(2)}, u32[]{:S(2)}) collective-permute-start(f32[3,2,256]{2,1,0:T(2,128)S(1)} %slice.132), channel_id=1, source_target_pairs={{4,0},{8,4},{12,8},{16,12},{20,16},{24,20},{28,24},{5,1},{9,5},{13... | collective-permute-start | bytes 18440 | tf_op jit(solution)/shard_map/ppermute | solution.py:17
  76.5 2.6 %collective-permute-start.8 = (bf16[256,256]{1,0:T(8,128)(2,1)S(1)}, bf16[256,256]{1,0:T(8,128)(2,1)S(1)}, u32[]{:S(2)}, u32[]{:S(2)}) collective-permute-start(bf16[256,256]{1,0:T(8,128)(2,1)S(1)} %convolution_convert_fusion.1), channel_id=1, source_target_pairs={{0,2},{1,3},{2,0},{3,1},{4,6},{5,7},{6,4},{7,5},{8,10},{9,11},{10,... | collective-permute-start | bytes 393224 | tf_op jit(solution)/shard_map/ppermute | solution.py:36
  79.1 3.8 %collective-permute-start.9 = (bf16[256,256]{1,0:T(8,128)(2,1)S(1)}, bf16[256,256]{1,0:T(8,128)(2,1)S(1)}, u32[]{:S(2)}, u32[]{:S(2)}) collective-permute-start(bf16[256,256]{1,0:T(8,128)(2,1)S(1)} %convolution_convert_fusion), channel_id=1, source_target_pairs={{0,3},{1,0},{2,1},{3,2},{4,7},{5,4},{6,5},{7,6},{8,11},{9,8},{10,9... | collective-permute-start | bytes 393224 | tf_op jit(solution)/shard_map/ppermute | solution.py:36
  84.0 0.6 collective-permute-start.11
  84.9 4.3 %collective-permute-done.8 = bf16[256,256]{1,0:T(8,128)(2,1)S(1)} collective-permute-done((bf16[256,256]{1,0:T(8,128)(2,1)S(1)}, bf16[256,256]{1,0:T(8,128)(2,1)S(1)}, u32[]{:S(2)}, u32[]{:S(2)}) %collective-permute-start.8) | collective-permute-done | bytes 131104 | tf_op jit(solution)/shard_map/ppermute | solution.py:36
  89.2 1.7 %collective-permute-done.9 = bf16[256,256]{1,0:T(8,128)(2,1)S(1)} collective-permute-done((bf16[256,256]{1,0:T(8,128)(2,1)S(1)}, bf16[256,256]{1,0:T(8,128)(2,1)S(1)}, u32[]{:S(2)}, u32[]{:S(2)}) %collective-permute-start.9) | collective-permute-done | bytes 131104 | tf_op jit(solution)/shard_map/ppermute | solution.py:36
  90.9 0.9 add_convert_fusion
  91.8 8.6 %collective-permute-done.12 = bf16[256,256]{1,0:T(8,128)(2,1)S(1)} collective-permute-done((bf16[256,256]{1,0:T(8,128)(2,1)S(1)}, bf16[256,256]{1,0:T(8,128)(2,1)S(1)}, u32[]{:S(2)}, u32[]{:S(2)}) %collective-permute-start.12) | collective-permute-done | bytes 131104 | tf_op jit(solution)/shard_map/ppermute | solution.py:36
  100.4 1.0 fusion.67
  (69 shorter events, 6.6 us)
Async XLA Ops:
  0.6 21.6 %copy-start = (bf16[3,1024,256]{2,1,0:T(8,128)(2,1)S(1)}, bf16[3,1024,256]{2,1,0:T(8,128)(2,1)}, u32[]{:S(2)}) copy-start(bf16[3,1024,256]{2,1,0:T(8,128)(2,1)} %param.9) | copy-start | bytes 4718596
  0.6 22.7 %copy-start.11 = (bf16[256,256]{1,0:T(8,128)(2,1)S(1)}, bf16[256,256]{1,0:T(8,128)(2,1)}, u32[]{:S(2)}) copy-start(bf16[256,256]{1,0:T(8,128)(2,1)} %param.8) | copy-start | bytes 393220
  0.7 22.7 %copy-start.3 = (bf16[256,1024]{1,0:T(8,128)(2,1)S(1)}, bf16[256,1024]{1,0:T(8,128)(2,1)}, u32[]{:S(2)}) copy-start(bf16[256,1024]{1,0:T(8,128)(2,1)} %param.13) | copy-start | bytes 1572868
  0.7 27.2 %collective-permute-start = (bf16[256,256]{1,0:T(8,128)(2,1)}, bf16[256,256]{1,0:T(8,128)(2,1)}, u32[]{:S(2)}, u32[]{:S(2)}) collective-permute-start(bf16[256,256]{1,0:T(8,128)(2,1)} %param.7), channel_id=1, source_target_pairs={{0,1},{1,2},{2,3},{3,0},{4,5},{5,6},{6,7},{7,4},{8,9},{9,10},{10,1... | collective-permute-start | bytes 393224 | tf_op jit(solution)/shard_map/ppermute | solution.py:25
  3.8 25.7 %collective-permute-start.2 = (bf16[256,256]{1,0:T(8,128)(2,1)}, bf16[256,256]{1,0:T(8,128)(2,1)}, u32[]{:S(2)}, u32[]{:S(2)}) collective-permute-start(bf16[256,256]{1,0:T(8,128)(2,1)} %param.7), channel_id=1, source_target_pairs={{0,3},{1,0},{2,1},{3,2},{4,7},{5,4},{6,5},{7,6},{8,11},{9,8},{10,9... | collective-permute-start | bytes 393224 | tf_op jit(solution)/shard_map/ppermute | solution.py:25
  5.9 24.8 %collective-permute-start.1 = (bf16[256,256]{1,0:T(8,128)(2,1)}, bf16[256,256]{1,0:T(8,128)(2,1)}, u32[]{:S(2)}, u32[]{:S(2)}) collective-permute-start(bf16[256,256]{1,0:T(8,128)(2,1)} %param.7), channel_id=1, source_target_pairs={{0,2},{1,3},{2,0},{3,1},{4,6},{5,7},{6,4},{7,5},{8,10},{9,11},{10,... | collective-permute-start | bytes 393224 | tf_op jit(solution)/shard_map/ppermute | solution.py:25
  6.8 27.2 %collective-permute-start.4 = (bf16[256,256]{1,0:T(8,128)(2,1)}, bf16[256,256]{1,0:T(8,128)(2,1)}, u32[]{:S(2)}, u32[]{:S(2)}) collective-permute-start(bf16[256,256]{1,0:T(8,128)(2,1)} %param.8), channel_id=1, source_target_pairs={{0,1},{1,2},{2,3},{3,0},{4,5},{5,6},{6,7},{7,4},{8,9},{9,10},{10,1... | collective-permute-start | bytes 393224 | tf_op jit(solution)/shard_map/ppermute | solution.py:25
  8.4 26.7 %collective-permute-start.6 = (bf16[256,256]{1,0:T(8,128)(2,1)}, bf16[256,256]{1,0:T(8,128)(2,1)}, u32[]{:S(2)}, u32[]{:S(2)}) collective-permute-start(bf16[256,256]{1,0:T(8,128)(2,1)} %param.8), channel_id=1, source_target_pairs={{0,3},{1,0},{2,1},{3,2},{4,7},{5,4},{6,5},{7,6},{8,11},{9,8},{10,9... | collective-permute-start | bytes 393224 | tf_op jit(solution)/shard_map/ppermute | solution.py:25
  12.4 26.5 %all-to-all-start.1 = ((f32[1,256,256]{2,0,1:T(1,128)}), f32[1,256,256]{2,0,1:T(1,128)S(1)}, u32[]{:S(2)}, u32[]{:S(2)}) async-start(f32[1,256,256]{2,0,1:T(1,128)} %bitcast.36), calls=%async_computation.1 | async-start | bytes 524288 | tf_op jit(solution)/shard_map/all_to_all | solution.py:85
  27.9 9.1 %collective-permute-start.5 = (bf16[256,256]{1,0:T(8,128)(2,1)}, bf16[256,256]{1,0:T(8,128)(2,1)S(1)}, u32[]{:S(2)}, u32[]{:S(2)}) collective-permute-start(bf16[256,256]{1,0:T(8,128)(2,1)} %param.8), channel_id=1, source_target_pairs={{0,2},{1,3},{2,0},{3,1},{4,6},{5,7},{6,4},{7,5},{8,10},{9,11},{10,... | collective-permute-start | bytes 393224 | tf_op jit(solution)/shard_map/ppermute | solution.py:25
  31.8 5.4 %collective-permute-start.3 = (bf16[3,2,256]{2,1,0:T(2,128)(2,1)S(1)}, bf16[3,2,256]{2,1,0:T(2,128)(2,1)S(1)}, u32[]{:S(2)}, u32[]{:S(2)}) collective-permute-start(bf16[3,2,256]{2,1,0:T(2,128)(2,1)S(1)} %slice.111), channel_id=1, source_target_pairs={{0,4},{4,8},{8,12},{12,16},{16,20},{20,24},{24,28},{1,5},{5,9},{9,... | collective-permute-start | bytes 9224 | tf_op jit(solution)/shard_map/ppermute | solution.py:17
  37.2 0.7 copy-start.1
  38.9 11.0 %all-to-all-start = ((bf16[2,256,256]{2,0,1:T(2,128)(2,1)}), bf16[2,256,256]{2,0,1:T(2,128)(2,1)}, u32[]{:S(2)}, u32[]{:S(2)}) async-start(bf16[2,256,256]{2,0,1:T(2,128)(2,1)} %copy.32), calls=%async_computation | async-start | bytes 524288 | tf_op jit(solution)/shard_map/all_to_all | solution.py:85
  44.1 1.0 %copy-start.5 = (f32[1,256,2,256]{3,1,0,2:T(8,128)S(1)}, f32[1,256,2,256]{3,1,0,2:T(8,128)}, u32[]{:S(2)}) copy-start(f32[1,256,2,256]{3,1,0,2:T(8,128)} %get-tuple-element.21) | copy-start | bytes 1572868
  44.1 1.2 %copy-start.7 = (f32[1,256,2,256]{3,1,0,2:T(8,128)S(1)}, f32[1,256,2,256]{3,1,0,2:T(8,128)}, u32[]{:S(2)}) copy-start(f32[1,256,2,256]{3,1,0,2:T(8,128)} %get-tuple-element.24) | copy-start | bytes 1572868
  52.2 1.0 %copy-start.6 = (f32[1,256,2,256]{3,1,0,2:T(8,128)S(1)}, f32[1,256,2,256]{3,1,0,2:T(8,128)}, u32[]{:S(2)}) copy-start(f32[1,256,2,256]{3,1,0,2:T(8,128)} %get-tuple-element.21) | copy-start | bytes 1572868
  52.2 1.2 %copy-start.8 = (f32[1,256,2,256]{3,1,0,2:T(8,128)S(1)}, f32[1,256,2,256]{3,1,0,2:T(8,128)}, u32[]{:S(2)}) copy-start(f32[1,256,2,256]{3,1,0,2:T(8,128)} %get-tuple-element.24) | copy-start | bytes 1572868
  56.5 1.0 %copy-start.9 = (f32[1,256,2,256]{3,1,2,0:T(8,128)S(1)}, f32[1,256,2,256]{3,1,2,0:T(8,128)}, u32[]{:S(2)}) copy-start(f32[1,256,2,256]{3,1,2,0:T(8,128)} %get-tuple-element.20) | copy-start | bytes 1572868
  56.5 1.2 %copy-start.10 = (f32[1,256,2,256]{3,1,2,0:T(8,128)S(1)}, f32[1,256,2,256]{3,1,2,0:T(8,128)}, u32[]{:S(2)}) copy-start(f32[1,256,2,256]{3,1,2,0:T(8,128)} %get-tuple-element.25) | copy-start | bytes 1572868
  60.8 12.7 %copy-start.2 = (f32[256,256]{1,0:T(8,128)S(1)}, f32[256,256]{1,0:T(8,128)}, u32[]{:S(2)}) copy-start(f32[256,256]{1,0:T(8,128)} %copy-done.1) | copy-start | bytes 786436
  60.8 12.7 %copy-start.12 = (f32[256]{0:T(256)S(1)}, f32[256]{0:T(256)}, u32[]{:S(2)}) copy-start(f32[256]{0:T(256)} %param.11) | copy-start | bytes 3076
  73.5 1.0 %copy-start.4 = (bf16[256,1024]{1,0:T(8,128)(2,1)S(1)}, bf16[256,1024]{1,0:T(8,128)(2,1)}, u32[]{:S(2)}) copy-start(bf16[256,1024]{1,0:T(8,128)(2,1)} %param.13) | copy-start | bytes 1572868
  75.0 8.0 %collective-permute-start.10 = (f32[3,2,256]{2,1,0:T(2,128)S(1)}, f32[3,2,256]{2,1,0:T(2,128)S(1)}, u32[]{:S(2)}, u32[]{:S(2)}) collective-permute-start(f32[3,2,256]{2,1,0:T(2,128)S(1)} %slice.132), channel_id=1, source_target_pairs={{4,0},{8,4},{12,8},{16,12},{20,16},{24,20},{28,24},{5,1},{9,5},{13... | collective-permute-start | bytes 18440 | tf_op jit(solution)/shard_map/ppermute | solution.py:17
  76.5 12.7 %collective-permute-start.8 = (bf16[256,256]{1,0:T(8,128)(2,1)S(1)}, bf16[256,256]{1,0:T(8,128)(2,1)S(1)}, u32[]{:S(2)}, u32[]{:S(2)}) collective-permute-start(bf16[256,256]{1,0:T(8,128)(2,1)S(1)} %convolution_convert_fusion.1), channel_id=1, source_target_pairs={{0,2},{1,3},{2,0},{3,1},{4,6},{5,7},{6,4},{7,5},{8,10},{9,11},{10,... | collective-permute-start | bytes 393224 | tf_op jit(solution)/shard_map/ppermute | solution.py:36
  79.1 10.1 %collective-permute-start.7 = (bf16[256,256]{1,0:T(8,128)(2,1)S(1)}, bf16[256,256]{1,0:T(8,128)(2,1)S(1)}, u32[]{:S(2)}, u32[]{:S(2)}) collective-permute-start(bf16[256,256]{1,0:T(8,128)(2,1)S(1)} %convolution_convert_fusion.2), channel_id=1, source_target_pairs={{0,1},{1,2},{2,3},{3,0},{4,5},{5,6},{6,7},{7,4},{8,9},{9,10},{10,1... | collective-permute-start | bytes 393224 | tf_op jit(solution)/shard_map/ppermute | solution.py:36
  79.1 11.8 %collective-permute-start.9 = (bf16[256,256]{1,0:T(8,128)(2,1)S(1)}, bf16[256,256]{1,0:T(8,128)(2,1)S(1)}, u32[]{:S(2)}, u32[]{:S(2)}) collective-permute-start(bf16[256,256]{1,0:T(8,128)(2,1)S(1)} %convolution_convert_fusion), channel_id=1, source_target_pairs={{0,3},{1,0},{2,1},{3,2},{4,7},{5,4},{6,5},{7,6},{8,11},{9,8},{10,9... | collective-permute-start | bytes 393224 | tf_op jit(solution)/shard_map/ppermute | solution.py:36
  83.9 16.5 %collective-permute-start.12 = (bf16[256,256]{1,0:T(8,128)(2,1)S(1)}, bf16[256,256]{1,0:T(8,128)(2,1)S(1)}, u32[]{:S(2)}, u32[]{:S(2)}) collective-permute-start(bf16[256,256]{1,0:T(8,128)(2,1)S(1)} %fusion.31), channel_id=1, source_target_pairs={{0,2},{1,3},{2,0},{3,1},{4,6},{5,7},{6,4},{7,5},{8,10},{9,11},{10,... | collective-permute-start | bytes 393224 | tf_op jit(solution)/shard_map/ppermute | solution.py:36
  84.0 16.4 %collective-permute-start.11 = (bf16[256,256]{1,0:T(8,128)(2,1)S(1)}, bf16[256,256]{1,0:T(8,128)(2,1)S(1)}, u32[]{:S(2)}, u32[]{:S(2)}) collective-permute-start(bf16[256,256]{1,0:T(8,128)(2,1)S(1)} %fusion.30), channel_id=1, source_target_pairs={{0,1},{1,2},{2,3},{3,0},{4,5},{5,6},{6,7},{7,4},{8,9},{9,10},{10,1... | collective-permute-start | bytes 393224 | tf_op jit(solution)/shard_map/ppermute | solution.py:36
  89.2 11.2 %collective-permute-start.13 = (bf16[256,256]{1,0:T(8,128)(2,1)S(1)}, bf16[256,256]{1,0:T(8,128)(2,1)S(1)}, u32[]{:S(2)}, u32[]{:S(2)}) collective-permute-start(bf16[256,256]{1,0:T(8,128)(2,1)S(1)} %fusion.32), channel_id=1, source_target_pairs={{0,3},{1,0},{2,1},{3,2},{4,7},{5,4},{6,5},{7,6},{8,11},{9,8},{10,9... | collective-permute-start | bytes 393224 | tf_op jit(solution)/shard_map/ppermute | solution.py:36

commit v7 on v6

--- a/solution.py
+++ b/solution.py
@@ -17,13 +17,26 @@
     return lax.ppermute(value, axis, [(source, source + steps) for source in range(initial, last)])
 
 
+def panel_shift(value, steps):
+    count = lax.axis_size("panel")
+    return lax.ppermute(value, "panel", [(i, (i + steps) % count) for i in range(count)])
+
+
 def panel_parts(value):
     count = lax.axis_size("panel")
     me = lax.axis_index("panel")
     parts = [(value, me)]
-    for k in range(1, count):
-        moved = lax.ppermute(value, "panel", [(i, (i + k) % count) for i in range(count)])
-        parts.append((moved, (me + count - k) % count))
+    left, right = value, value
+    for distance in range(1, (count + 1) // 2):
+        left, right = panel_shift(left, 1), panel_shift(right, -1)
+        parts.append((left, (me + count - distance) % count))
+        parts.append((right, (me + distance) % count))
+    if count % 2 == 0 and count > 1:
+        half = value.shape[0] // 2
+        far = jnp.concatenate(
+            [panel_shift(left[:half], 1), panel_shift(right[half:], -1)], axis=0
+        )
+        parts.append((far, (me + count // 2) % count))
     return parts
 
 

time: 103 us -> 113 us (1.097)
  starting transfers between devices: 28.8 us -> 37.3 us
  local copies, waits for them, and re-layouts: 8.92 us -> 12 us
    ppermute x6 -> x8, starting transfers between devices: 10.3 us -> 16.7 us  [panel_shift(): lax.ppermute(value, 'panel', [(i, (i + steps) % count) for i in range(cou...]
    slice x0 -> x4, local copies, waits for them, and re-layouts: none -> 2.54 us  [the longest x2 1.69 us: panel_parts(): right[half:]]
    all_to_all x2, starting transfers between devices: 7.95 us -> 9.97 us  [to_columns(): lax.all_to_all(jnp.swapaxes(rows, 1, 2).astype(wire), 'seq', split_axis=1...]
    dot_general x4, matrix products: 4.7 us -> 2.89 us  [local(): jnp.einsum('td,jdc->jtc', part, lax.dynamic_slice_in_dim(in_weight, sourc...]
    unnamed x27 -> x39, local copies, waits for them, and re-layouts: 4.24 us -> 4.19 us
  transfers between devices with their start and end apart: 16 -> 18, of which waited for: 5 -> 5; matrix products, arithmetic and copies ran while one was open for 25% -> 25% of each run, Pallas kernels for 0% -> 0%
where the time goes in v7:
time: 113 us; the launch traced here: 111 us
  starting transfers between devices  37.3 us (33%)
  matrix products  20.6 us (18%)
  waiting for transfers between devices  17.7 us (16%)
  other arithmetic  13.1 us (12%)
  local copies, waits for them, and re-layouts  12 us (11%)
  blocking collectives  9.32 us (8%)
  between operations  1.28 us (1%)
    ppermute x8, starting transfers between devices, panel_shift(): lax.ppermute(value, 'panel', [(i, (i + steps) % count) for i in range(cou...  16.7 us
    ppermute x6, waiting for transfers between devices, panel_reduce_scatter(): lax.ppermute(sent, 'panel', [(i, (i + k) % count) for i in range(count)])  14 us
    all_to_all x2, starting transfers between devices, to_columns(): lax.all_to_all(jnp.swapaxes(rows, 1, 2).astype(wire), 'seq', split_axis=1...  9.97 us
    all_to_all x1, blocking collectives, to_rows(): lax.all_to_all(columns.astype(wire), 'seq', split_axis=2, concat_axis=1,...  9.32 us
    ppermute x6, starting transfers between devices, panel_reduce_scatter(): lax.ppermute(sent, 'panel', [(i, (i + k) % count) for i in range(count)])  8.01 us
    unnamed x39, local copies, waits for them, and re-layouts  4.19 us
    dot_general x2, matrix products, forward_spectrum(): jnp.einsum('bcerkm,rmsq->bceskq', spread, stage_b, precision=STAGE_B_PREC...  3.83 us
    dot_general x4, matrix products, local(): lax.dot_general(part, lax.dynamic_slice_in_dim(out_weight, source * width...  3.63 us
  transfers between devices with their start and end apart: 18, of which 5 were waited for; matrix products, arithmetic and copies ran while one was open for 25% of the time, Pallas kernels for 0%

profile of v7, /device:TPU:0, one launch (start us, length us, event | category | flops | bytes accessed | tf_op | source)
XLA Modules:
  0.0 111.3 jit_solution(8142680390693819738)
XLA Ops:
  0.7 3.1 %collective-permute-start = (bf16[256,256]{1,0:T(8,128)(2,1)}, bf16[256,256]{1,0:T(8,128)(2,1)S(1)}, u32[]{:S(2)}, u32[]{:S(2)}) collective-permute-start(bf16[256,256]{1,0:T(8,128)(2,1)} %param.7), channel_id=1, source_target_pairs={{0,1},{1,2},{2,3},{3,0},{4,5},{5,6},{6,7},{7,4},{8,9},{9,10},{10,1... | collective-permute-start | bytes 393224 | tf_op jit(solution)/shard_map/ppermute | solution.py:22
  3.8 2.1 %collective-permute-start.1 = (bf16[256,256]{1,0:T(8,128)(2,1)}, bf16[256,256]{1,0:T(8,128)(2,1)}, u32[]{:S(2)}, u32[]{:S(2)}) collective-permute-start(bf16[256,256]{1,0:T(8,128)(2,1)} %param.7), channel_id=1, source_target_pairs={{0,3},{1,0},{2,1},{3,2},{4,7},{5,4},{6,5},{7,6},{8,11},{9,8},{10,9... | collective-permute-start | bytes 393224 | tf_op jit(solution)/shard_map/ppermute | solution.py:22
  5.9 3.8 %collective-permute-start.6 = (bf16[256,256]{1,0:T(8,128)(2,1)}, bf16[256,256]{1,0:T(8,128)(2,1)}, u32[]{:S(2)}, u32[]{:S(2)}) collective-permute-start(bf16[256,256]{1,0:T(8,128)(2,1)} %param.8), channel_id=1, source_target_pairs={{0,3},{1,0},{2,1},{3,2},{4,7},{5,4},{6,5},{7,6},{8,11},{9,8},{10,9... | collective-permute-start | bytes 393224 | tf_op jit(solution)/shard_map/ppermute | solution.py:22
  9.7 1.8 %copy.63 = f32[1,256,256]{1,0,2:T(1,128)} copy(f32[1,256,256]{2,1,0:T(8,128)} %bitcast.222) | data formatting | bytes 524288 | tf_op jit(solution)/shard_map/broadcast_in_dim | solution.py:131
  11.5 3.9 %all-to-all-start.1 = ((f32[1,256,256]{2,0,1:T(1,128)}), f32[1,256,256]{2,0,1:T(1,128)S(1)}, u32[]{:S(2)}, u32[]{:S(2)}) async-start(f32[1,256,256]{2,0,1:T(1,128)} %bitcast.36), calls=%async_computation.1 | async-start | bytes 524288 | tf_op jit(solution)/shard_map/all_to_all | solution.py:98
  15.5 0.7 iota_multiply_fusion
  16.7 1.8 %fusion.96 = (f32[256,1,256]{2,0,1:T(8,128)}, f32[256,1,256]{2,0,1:T(8,128)}) fusion(), kind=kLoop, calls=%fused_computation.136 | loop fusion | flops 983040 | bytes 524288 | tf_op jit(solution)/shard_map/sin | solution.py:75
  18.5 1.7 %fusion.98 = f32[256,1,256]{2,0,1:T(8,128)} fusion(), kind=kLoop, calls=%fused_computation.138 | loop fusion | flops 1048576 | bytes 262144 | tf_op jit(solution)/shard_map/neg | solution.py:80
  20.1 1.3 %slice_bitcast_fusion.5 = (f32[3,256]{1,0:T(4,128)}, f32[3,256]{1,0:T(4,128)}, f32[3,256]{1,0:T(4,128)}) fusion(f32[3,3,256]{2,1,0:T(4,128)} %param.10), kind=kLoop, calls=%fused_computation.181 | loop fusion | bytes 18432 | tf_op jit(solution)/shard_map/mul | solution.py:153
  21.5 1.2 %fusion.56 = f32[3,256,256]{1,2,0:T(8,128)S(1)} fusion(bf16[3,1024,256]{2,1,0:T(8,128)(2,1)S(1)} %copy-done, s32[]{:T(128)S(6)} %select_n.148, bf16[256,256]{1,0:T(8,128)(2,1)} %param.7), kind=kOutput, calls=%fused_computation.90 | convolution fusion | flops 100663296 | bytes 1310724 | tf_op jit(solution)/shard_map/td,jdc->jtc/dot_general | solution.py:135
  22.7 1.1 %fusion.107 = f32[256,256]{0,1:T(8,128)S(1)} fusion(bf16[256,256]{1,0:T(8,128)(2,1)} %param.8, bf16[256,1024]{1,0:T(8,128)(2,1)S(1)} %copy-done.3, s32[]{:T(128)S(6)} %select_n.148), kind=kOutput, calls=%fused_computation.147 | convolution fusion | flops 33554432 | bytes 524292 | tf_op jit(solution)/shard_map/dot_general | solution.py:143
  24.5 1.4 %fusion.142 = (f32[2,8,256]{2,1,0:T(8,128)}, f32[2,8,256]{2,1,0:T(8,128)}, f32[2,8,256]{2,1,0:T(8,128)S(1)}) fusion(s32[2,256]{1,0:T(2,128)} %iota_multiply_fusion.2, s32[8,256]{1,0:T(8,128)} %iota_multiply_fusion), kind=kLoop, calls=%fused_computation.201 | loop fusion | flops 65536 | bytes 59392 | tf_op jit(solution)/shard_map/neg | solution.py:122
  25.9 2.8 %fusion.46 = (f32[1,256,2,256]{3,1,2,0:T(8,128)}, f32[1,256,2,256]{3,1,0,2:T(8,128)}, f32[1,256,2,256]{3,1,0,2:T(8,128)}, f32[1,256,2,256]{3,1,2,0:T(8,128)}) fusion(f32[256,1,256]{2,0,1:T(8,128)} %get-tuple-element.35, f32[256,1,256]{2,0,1:T(8,128)} %fusion.98, f32[256,1,256]{2,0,1:T(8,128)} %get-tuple-element.34), kind=kLoop, calls=%fused_computation.70 | loop fusion | flops 524288 | bytes 2883584 | tf_op jit(solution)/shard_map/stack | solution.py:79
  28.7 0.8 slice.128
  29.6 3.8 %collective-permute-start.3 = (bf16[128,256]{1,0:T(8,128)(2,1)S(1)}, bf16[128,256]{1,0:T(8,128)(2,1)S(1)}, u32[]{:S(2)}, u32[]{:S(2)}) collective-permute-start(bf16[128,256]{1,0:T(8,128)(2,1)S(1)} %slice.128), channel_id=1, source_target_pairs={{0,3},{1,0},{2,1},{3,2},{4,7},{5,4},{6,5},{7,6},{8,11},{9,8},{10,9... | collective-permute-start | bytes 196616 | tf_op jit(solution)/shard_map/ppermute | solution.py:22
  33.4 0.8 slice.135
  34.2 0.8 slice.136
  35.1 3.8 %collective-permute-start.8 = (bf16[128,256]{1,0:T(8,128)(2,1)S(1)}, bf16[128,256]{1,0:T(8,128)(2,1)S(1)}, u32[]{:S(2)}, u32[]{:S(2)}) collective-permute-start(bf16[128,256]{1,0:T(8,128)(2,1)S(1)} %slice.136), channel_id=1, source_target_pairs={{0,3},{1,0},{2,1},{3,2},{4,7},{5,4},{6,5},{7,6},{8,11},{9,8},{10,9... | collective-permute-start | bytes 196616 | tf_op jit(solution)/shard_map/ppermute | solution.py:22
  39.2 1.1 %convolution_add_fusion.3 = f32[256,256]{0,1:T(8,128)S(1)} fusion(f32[256,256]{0,1:T(8,128)S(1)} %fusion.107, bf16[256,256]{1,0:T(8,128)(2,1)} %collective-permute-done.5, bf16[256,1024]{1,0:T(8,128)(2,1)S(1)} %copy-done.3, s32[]{:T(128)S(6)} %select_n.150), kind=kOutput, calls=%fused_computation.31 | convolution fusion | flops 33619968 | bytes 786436 | tf_op jit(solution)/shard_map/dot_general | solution.py:143
  40.6 1.2 %fusion.21 = bf16[3,256,256]{2,1,0:T(8,128)(2,1)S(1)} fusion(f32[3,256,256]{1,2,0:T(8,128)S(1)} %fusion.49, f32[3,256,256]{1,2,0:T(8,128)S(1)} %convolution_add_fusion.1, bf16[3,1024,256]{2,1,0:T(8,128)(2,1)S(1)} %copy-done, s32[]{:T(128)S(6)} %select_n.152, bf16[256,256]{1,0:T(8,128)(2,1)} %collective-permute-done.1), kind=kOutput, calls=%fused_computation.22 | convolution fusion | flops 101253120 | bytes 2490372 | tf_op jit(solution)/shard_map/td,jdc->jtc/dot_general | solution.py:135
  41.8 1.3 %collective-permute-start.4 = (bf16[3,2,256]{2,1,0:T(2,128)(2,1)S(1)}, bf16[3,2,256]{2,1,0:T(2,128)(2,1)S(1)}, u32[]{:S(2)}, u32[]{:S(2)}) collective-permute-start(bf16[3,2,256]{2,1,0:T(2,128)(2,1)S(1)} %slice.129), channel_id=1, source_target_pairs={{0,4},{4,8},{8,12},{12,16},{16,20},{20,24},{24,28},{1,5},{5,9},{9,... | collective-permute-start | bytes 9224 | tf_op jit(solution)/shard_map/ppermute | solution.py:17
  43.4 1.1 %fusion.26 = f32[256,256]{1,0:T(8,128)S(1)} fusion(f32[256,256]{1,0:T(8,128)S(1)} %fusion.89, f32[256,256]{0,1:T(8,128)S(1)} %convolution_add_fusion.3, bf16[256,256]{1,0:T(8,128)(2,1)} %collective-permute-done.6, bf16[256,1024]{1,0:T(8,128)(2,1)S(1)} %copy-done.3, s32[]{:T(128)S(6)} %select_n.152), kind=kOutput, calls=%fused_computation.30 | convolution fusion | flops 33685504 | bytes 1048580 | tf_op jit(solution)/shard_map/dot_general | solution.py:143
  45.4 0.9 copy.32
  46.2 6.1 %all-to-all-start = ((bf16[2,256,256]{2,0,1:T(2,128)(2,1)}), bf16[2,256,256]{2,0,1:T(2,128)(2,1)}, u32[]{:S(2)}, u32[]{:S(2)}) async-start(bf16[2,256,256]{2,0,1:T(2,128)(2,1)} %copy.32), calls=%async_computation | async-start | bytes 524288 | tf_op jit(solution)/shard_map/all_to_all | solution.py:98
  52.4 1.0 convolution_bitcast_fusion.2
  53.6 0.8 copy-done.5
  54.6 1.1 %convolution_bitcast_fusion.1 = f32[1,32,2,2,8,256]{5,1,4,2,0,3:T(8,128)S(1)} fusion(f32[32,2,2,8,256]{4,3,0,2,1:T(8,128)S(1)} %maximum_bitcast_fusion.3, f32[1,256,2,256]{3,1,0,2:T(8,128)S(1)} %copy-done.5, f32[1,256,2,256]{3,1,0,2:T(8,128)S(1)} %copy-done.7), kind=kOutput, calls=%fused_computation.15 | convolution fusion | flops 805568512 | bytes 3145728 | tf_op jit(solution)/shard_map/bcerkm,rmsq->bceskq/dot_general | solution.py:116
  55.7 3.6 %all-to-all-done = bf16[2,256,256]{2,0,1:T(2,128)(2,1)} async-done(((bf16[2,256,256]{2,0,1:T(2,128)(2,1)}), bf16[2,256,256]{2,0,1:T(2,128)(2,1)}, u32[]{:S(2)}, u32[]{:S(2)}) %all-to-all-start) | async-done | bytes 262176 | tf_op jit(solution)/shard_map/all_to_all | solution.py:98
  59.4 2.0 %convolution_bitcast_fusion = f32[2,32,2,2,8,256]{5,4,3,2,1,0:T(8,128)S(1)} fusion(bf16[2,8,32,256]{3,0,2,1:T(2,128)(2,1)} %bitcast.20, f32[2,1,8,8]{3,2,1,0:T(8,128)S(1)} %copy-done.13, f32[2,1,8,8]{3,2,1,0:T(8,128)S(1)} %copy-done.12), kind=kOutput, calls=%fused_computation.14 | convolution fusion | flops 50331904 | bytes 2360320 | tf_op jit(solution)/shard_map/erkp,bcpm->bcerkm/dot_general | solution.py:114
  61.9 0.8 copy-done.6
  62.9 2.7 %fusion.10 = f32[2,32,2,2,8,256]{5,1,4,2,0,3:T(8,128)S(1)} fusion(f32[2,32,2,2,8,256]{5,4,3,2,1,0:T(8,128)S(1)} %pad_maximum_fusion, f32[1,256,2,256]{3,1,0,2:T(8,128)S(1)} %copy-done.6, f32[1,256,2,256]{3,1,0,2:T(8,128)S(1)} %copy-done.8), kind=kOutput, calls=%fused_computation.12 | convolution fusion | flops 1610874880 | bytes 5242880 | tf_op jit(solution)/shard_map/bcerkm,rmsq->bceskq/dot_general | solution.py:116
  66.2 0.9 copy-done.9
  67.2 2.7 %fusion.13 = f32[2,32,2,2,8,256]{5,4,3,2,1,0:T(8,128)S(1)} fusion(f32[2,32,2,2,8,256,1]{5,1,4,2,0,3,6:T(8,128)S(1)} %maximum_bitcast_fusion, f32[1,256,2,256]{3,1,2,0:T(8,128)S(1)} %copy-done.10, f32[1,256,2,256]{3,1,2,0:T(8,128)S(1)} %copy-done.9), kind=kOutput, calls=%fused_computation.13 | convolution fusion | flops 1610874880 | bytes 5242880 | tf_op jit(solution)/shard_map/bceskq,sqrm->bcerkm/dot_general | solution.py:121
  70.3 1.2 %fusion.27 = bf16[2,32,8,256]{3,2,1,0:T(8,128)(2,1)S(1)} fusion(f32[2,32,2,1,8,256]{5,4,3,2,1,0:T(8,128)S(1)} %get-tuple-element.11, f32[2,32,2,1,8,256]{5,4,3,2,1,0:T(8,128)S(1)} %get-tuple-element.10, f32[2,1,8,8]{3,2,1,0:T(8,128)S(1)} %copy-done.13, f32[2,1,8,8]{3,2,1,0:T(8,128)S(1)} %copy-done.12), kind=kOutput, calls=%fused_computation.32 | convolution fusion | flops 50987520 | bytes 2360320 | tf_op jit(solution)/shard_map/erkp,bcerkm->bcpm/dot_general | solution.py:123
  71.6 9.3 %all_to_all.39 = bf16[2,32,8,256]{3,1,0,2:T(8,128)(2,1)S(1)} all-to-all(bf16[2,32,8,256]{3,1,0,2:T(8,128)(2,1)S(1)} %copy.43), channel_id=1, replica_groups=mesh['seq'=8,'panel'=4] {'seq'}, dimensions={2} | all-to-all | bytes 524288 | tf_op jit(solution)/shard_map/all_to_all | solution.py:106
  80.9 0.9 bitcast_convert_fusion
  81.8 1.2 %copy.45 = f32[2,256,256]{1,2,0:T(8,128)S(1)} copy(f32[2,256,256]{2,1,0:T(8,128)} %bitcast.220) | data formatting | bytes 1048576 | tf_op jit(solution)/shard_map/transpose | solution.py:109
  83.3 0.8 copy-done.4
  84.6 1.3 %collective-permute-start.12 = (f32[3,2,256]{2,1,0:T(2,128)S(1)}, f32[3,2,256]{2,1,0:T(2,128)S(1)}, u32[]{:S(2)}, u32[]{:S(2)}) collective-permute-start(f32[3,2,256]{2,1,0:T(2,128)S(1)} %slice.152), channel_id=1, source_target_pairs={{4,0},{8,4},{12,8},{16,12},{20,16},{24,20},{28,24},{5,1},{9,5},{13... | collective-permute-start | bytes 18440 | tf_op jit(solution)/shard_map/ppermute | solution.py:17
  86.7 3.3 %collective-permute-start.11 = (bf16[256,256]{1,0:T(8,128)(2,1)S(1)}, bf16[256,256]{1,0:T(8,128)(2,1)S(1)}, u32[]{:S(2)}, u32[]{:S(2)}) collective-permute-start(bf16[256,256]{1,0:T(8,128)(2,1)S(1)} %convolution_convert_fusion), channel_id=1, source_target_pairs={{0,3},{1,0},{2,1},{3,2},{4,7},{5,4},{6,5},{7,6},{8,11},{9,8},{10,9... | collective-permute-start | bytes 393224 | tf_op jit(solution)/shard_map/ppermute | solution.py:49
  91.6 1.5 %collective-permute-start.14 = (bf16[256,256]{1,0:T(8,128)(2,1)S(1)}, bf16[256,256]{1,0:T(8,128)(2,1)S(1)}, u32[]{:S(2)}, u32[]{:S(2)}) collective-permute-start(bf16[256,256]{1,0:T(8,128)(2,1)S(1)} %fusion.31), channel_id=1, source_target_pairs={{0,2},{1,3},{2,0},{3,1},{4,6},{5,7},{6,4},{7,5},{8,10},{9,11},{10,... | collective-permute-start | bytes 393224 | tf_op jit(solution)/shard_map/ppermute | solution.py:49
  93.4 0.9 collective-permute-done.9
  94.3 2.0 %collective-permute-start.15 = (bf16[256,256]{1,0:T(8,128)(2,1)S(1)}, bf16[256,256]{1,0:T(8,128)(2,1)S(1)}, u32[]{:S(2)}, u32[]{:S(2)}) collective-permute-start(bf16[256,256]{1,0:T(8,128)(2,1)S(1)} %fusion.32), channel_id=1, source_target_pairs={{0,3},{1,0},{2,1},{3,2},{4,7},{5,4},{6,5},{7,6},{8,11},{9,8},{10,9... | collective-permute-start | bytes 393224 | tf_op jit(solution)/shard_map/ppermute | solution.py:49
  96.3 2.8 %collective-permute-done.10 = bf16[256,256]{1,0:T(8,128)(2,1)S(1)} collective-permute-done((bf16[256,256]{1,0:T(8,128)(2,1)S(1)}, bf16[256,256]{1,0:T(8,128)(2,1)S(1)}, u32[]{:S(2)}, u32[]{:S(2)}) %collective-permute-start.10) | collective-permute-done | bytes 131104 | tf_op jit(solution)/shard_map/ppermute | solution.py:49
  99.1 0.9 add_convert_fusion
  99.9 2.8 %collective-permute-done.13 = bf16[256,256]{1,0:T(8,128)(2,1)S(1)} collective-permute-done((bf16[256,256]{1,0:T(8,128)(2,1)S(1)}, bf16[256,256]{1,0:T(8,128)(2,1)S(1)}, u32[]{:S(2)}, u32[]{:S(2)}) %collective-permute-start.13) | collective-permute-done | bytes 131104 | tf_op jit(solution)/shard_map/ppermute | solution.py:49
  102.7 7.5 %collective-permute-done.14 = bf16[256,256]{1,0:T(8,128)(2,1)S(1)} collective-permute-done((bf16[256,256]{1,0:T(8,128)(2,1)S(1)}, bf16[256,256]{1,0:T(8,128)(2,1)S(1)}, u32[]{:S(2)}, u32[]{:S(2)}) %collective-permute-start.14) | collective-permute-done | bytes 131104 | tf_op jit(solution)/shard_map/ppermute | solution.py:49
  110.3 1.0 fusion.67
  (89 shorter events, 8.5 us)
Async XLA Ops:
  0.6 20.8 %copy-start = (bf16[3,1024,256]{2,1,0:T(8,128)(2,1)S(1)}, bf16[3,1024,256]{2,1,0:T(8,128)(2,1)}, u32[]{:S(2)}) copy-start(bf16[3,1024,256]{2,1,0:T(8,128)(2,1)} %param.9) | copy-start | bytes 4718596
  0.6 22.0 %copy-start.3 = (bf16[256,1024]{1,0:T(8,128)(2,1)S(1)}, bf16[256,1024]{1,0:T(8,128)(2,1)}, u32[]{:S(2)}) copy-start(bf16[256,1024]{1,0:T(8,128)(2,1)} %param.13) | copy-start | bytes 1572868
  0.7 28.0 %collective-permute-start = (bf16[256,256]{1,0:T(8,128)(2,1)}, bf16[256,256]{1,0:T(8,128)(2,1)S(1)}, u32[]{:S(2)}, u32[]{:S(2)}) collective-permute-start(bf16[256,256]{1,0:T(8,128)(2,1)} %param.7), channel_id=1, source_target_pairs={{0,1},{1,2},{2,3},{3,0},{4,5},{5,6},{6,7},{7,4},{8,9},{9,10},{10,1... | collective-permute-start | bytes 393224 | tf_op jit(solution)/shard_map/ppermute | solution.py:22
  3.8 24.9 %collective-permute-start.1 = (bf16[256,256]{1,0:T(8,128)(2,1)}, bf16[256,256]{1,0:T(8,128)(2,1)}, u32[]{:S(2)}, u32[]{:S(2)}) collective-permute-start(bf16[256,256]{1,0:T(8,128)(2,1)} %param.7), channel_id=1, source_target_pairs={{0,3},{1,0},{2,1},{3,2},{4,7},{5,4},{6,5},{7,6},{8,11},{9,8},{10,9... | collective-permute-start | bytes 393224 | tf_op jit(solution)/shard_map/ppermute | solution.py:22
  5.9 27.5 %collective-permute-start.5 = (bf16[256,256]{1,0:T(8,128)(2,1)}, bf16[256,256]{1,0:T(8,128)(2,1)}, u32[]{:S(2)}, u32[]{:S(2)}) collective-permute-start(bf16[256,256]{1,0:T(8,128)(2,1)} %param.8), channel_id=1, source_target_pairs={{0,1},{1,2},{2,3},{3,0},{4,5},{5,6},{6,7},{7,4},{8,9},{9,10},{10,1... | collective-permute-start | bytes 393224 | tf_op jit(solution)/shard_map/ppermute | solution.py:22
  5.9 28.4 %collective-permute-start.6 = (bf16[256,256]{1,0:T(8,128)(2,1)}, bf16[256,256]{1,0:T(8,128)(2,1)}, u32[]{:S(2)}, u32[]{:S(2)}) collective-permute-start(bf16[256,256]{1,0:T(8,128)(2,1)} %param.8), channel_id=1, source_target_pairs={{0,3},{1,0},{2,1},{3,2},{4,7},{5,4},{6,5},{7,6},{8,11},{9,8},{10,9... | collective-permute-start | bytes 393224 | tf_op jit(solution)/shard_map/ppermute | solution.py:22
  11.5 34.8 %all-to-all-start.1 = ((f32[1,256,256]{2,0,1:T(1,128)}), f32[1,256,256]{2,0,1:T(1,128)S(1)}, u32[]{:S(2)}, u32[]{:S(2)}) async-start(f32[1,256,256]{2,0,1:T(1,128)} %bitcast.36), calls=%async_computation.1 | async-start | bytes 524288 | tf_op jit(solution)/shard_map/all_to_all | solution.py:98
  28.6 11.7 %collective-permute-start.2 = (bf16[128,256]{1,0:T(8,128)(2,1)S(1)}, bf16[128,256]{1,0:T(8,128)(2,1)S(1)}, u32[]{:S(2)}, u32[]{:S(2)}) collective-permute-start(bf16[128,256]{1,0:T(8,128)(2,1)S(1)} %slice.127), channel_id=1, source_target_pairs={{0,1},{1,2},{2,3},{3,0},{4,5},{5,6},{6,7},{7,4},{8,9},{9,10},{10,1... | collective-permute-start | bytes 196616 | tf_op jit(solution)/shard_map/ppermute | solution.py:22
  29.6 10.8 %collective-permute-start.3 = (bf16[128,256]{1,0:T(8,128)(2,1)S(1)}, bf16[128,256]{1,0:T(8,128)(2,1)S(1)}, u32[]{:S(2)}, u32[]{:S(2)}) collective-permute-start(bf16[128,256]{1,0:T(8,128)(2,1)S(1)} %slice.128), channel_id=1, source_target_pairs={{0,3},{1,0},{2,1},{3,2},{4,7},{5,4},{6,5},{7,6},{8,11},{9,8},{10,9... | collective-permute-start | bytes 196616 | tf_op jit(solution)/shard_map/ppermute | solution.py:22
  34.2 8.9 %collective-permute-start.7 = (bf16[128,256]{1,0:T(8,128)(2,1)S(1)}, bf16[128,256]{1,0:T(8,128)(2,1)S(1)}, u32[]{:S(2)}, u32[]{:S(2)}) collective-permute-start(bf16[128,256]{1,0:T(8,128)(2,1)S(1)} %slice.135), channel_id=1, source_target_pairs={{0,1},{1,2},{2,3},{3,0},{4,5},{5,6},{6,7},{7,4},{8,9},{9,10},{10,1... | collective-permute-start | bytes 196616 | tf_op jit(solution)/shard_map/ppermute | solution.py:22
  35.1 8.1 %collective-permute-start.8 = (bf16[128,256]{1,0:T(8,128)(2,1)S(1)}, bf16[128,256]{1,0:T(8,128)(2,1)S(1)}, u32[]{:S(2)}, u32[]{:S(2)}) collective-permute-start(bf16[128,256]{1,0:T(8,128)(2,1)S(1)} %slice.136), channel_id=1, source_target_pairs={{0,3},{1,0},{2,1},{3,2},{4,7},{5,4},{6,5},{7,6},{8,11},{9,8},{10,9... | collective-permute-start | bytes 196616 | tf_op jit(solution)/shard_map/ppermute | solution.py:22
  40.6 4.1 %copy-start.15 = (f32[3,256]{1,0:T(4,128)S(1)}, f32[3,256]{1,0:T(4,128)}, u32[]{:S(2)}) copy-start(f32[3,256]{1,0:T(4,128)} %get-tuple-element.26) | copy-start | bytes 9220
  40.6 4.1 %copy-start.16 = (f32[3,256]{1,0:T(4,128)S(1)}, f32[3,256]{1,0:T(4,128)}, u32[]{:S(2)}) copy-start(f32[3,256]{1,0:T(4,128)} %get-tuple-element.27) | copy-start | bytes 9220
  40.6 4.1 %copy-start.17 = (f32[3,256]{1,0:T(4,128)S(1)}, f32[3,256]{1,0:T(4,128)}, u32[]{:S(2)}) copy-start(f32[3,256]{1,0:T(4,128)} %get-tuple-element.28) | copy-start | bytes 9220
  41.8 2.7 %collective-permute-start.4 = (bf16[3,2,256]{2,1,0:T(2,128)(2,1)S(1)}, bf16[3,2,256]{2,1,0:T(2,128)(2,1)S(1)}, u32[]{:S(2)}, u32[]{:S(2)}) collective-permute-start(bf16[3,2,256]{2,1,0:T(2,128)(2,1)S(1)} %slice.129), channel_id=1, source_target_pairs={{0,4},{4,8},{8,12},{12,16},{16,20},{20,24},{24,28},{1,5},{5,9},{9,... | collective-permute-start | bytes 9224 | tf_op jit(solution)/shard_map/ppermute | solution.py:17
  44.5 0.7 copy-start.1
  45.2 7.1 %copy-start.12 = (f32[2,1,8,8]{3,2,1,0:T(8,128)S(1)}, f32[2,1,8,8]{3,2,1,0:T(8,128)}, u32[]{:S(2)}) copy-start(f32[2,1,8,8]{3,2,1,0:T(8,128)} %get-tuple-element.32) | copy-start | bytes 1540
  45.2 7.1 %copy-start.13 = (f32[2,1,8,8]{3,2,1,0:T(8,128)S(1)}, f32[2,1,8,8]{3,2,1,0:T(8,128)}, u32[]{:S(2)}) copy-start(f32[2,1,8,8]{3,2,1,0:T(8,128)} %get-tuple-element.33) | copy-start | bytes 1540
  45.3 8.1 %copy-start.11 = (f32[2,8,256]{2,1,0:T(8,128)S(1)}, f32[2,8,256]{2,1,0:T(8,128)}, u32[]{:S(2)}) copy-start(f32[2,8,256]{2,1,0:T(8,128)} %get-tuple-element.30) | copy-start | bytes 49156
  46.2 13.1 %all-to-all-start = ((bf16[2,256,256]{2,0,1:T(2,128)(2,1)}), bf16[2,256,256]{2,0,1:T(2,128)(2,1)}, u32[]{:S(2)}, u32[]{:S(2)}) async-start(bf16[2,256,256]{2,0,1:T(2,128)(2,1)} %copy.32), calls=%async_computation | async-start | bytes 524288 | tf_op jit(solution)/shard_map/all_to_all | solution.py:98
  53.4 1.0 copy-start.5
  53.4 1.2 %copy-start.7 = (f32[1,256,2,256]{3,1,0,2:T(8,128)S(1)}, f32[1,256,2,256]{3,1,0,2:T(8,128)}, u32[]{:S(2)}) copy-start(f32[1,256,2,256]{3,1,0,2:T(8,128)} %get-tuple-element.24) | copy-start | bytes 1572868
  61.7 1.0 copy-start.6
  61.7 1.2 %copy-start.8 = (f32[1,256,2,256]{3,1,0,2:T(8,128)S(1)}, f32[1,256,2,256]{3,1,0,2:T(8,128)}, u32[]{:S(2)}) copy-start(f32[1,256,2,256]{3,1,0,2:T(8,128)} %get-tuple-element.24) | copy-start | bytes 1572868
  66.0 1.0 copy-start.9
  66.0 1.2 %copy-start.10 = (f32[1,256,2,256]{3,1,2,0:T(8,128)S(1)}, f32[1,256,2,256]{3,1,2,0:T(8,128)}, u32[]{:S(2)}) copy-start(f32[1,256,2,256]{3,1,2,0:T(8,128)} %get-tuple-element.25) | copy-start | bytes 1572868
  67.2 2.7 %copy-start.14 = (f32[2,8,256]{2,1,0:T(8,128)S(1)}, f32[2,8,256]{2,1,0:T(8,128)}, u32[]{:S(2)}) copy-start(f32[2,8,256]{2,1,0:T(8,128)} %get-tuple-element.29) | copy-start | bytes 49156
  70.3 12.7 %copy-start.2 = (f32[256,256]{1,0:T(8,128)S(1)}, f32[256,256]{1,0:T(8,128)}, u32[]{:S(2)}) copy-start(f32[256,256]{1,0:T(8,128)} %copy-done.1) | copy-start | bytes 786436
  70.3 12.7 %copy-start.18 = (f32[256]{0:T(256)S(1)}, f32[256]{0:T(256)}, u32[]{:S(2)}) copy-start(f32[256]{0:T(256)} %param.11) | copy-start | bytes 3076
  83.0 1.0 copy-start.4
  84.6 5.4 %collective-permute-start.12 = (f32[3,2,256]{2,1,0:T(2,128)S(1)}, f32[3,2,256]{2,1,0:T(2,128)S(1)}, u32[]{:S(2)}, u32[]{:S(2)}) collective-permute-start(f32[3,2,256]{2,1,0:T(2,128)S(1)} %slice.152), channel_id=1, source_target_pairs={{4,0},{8,4},{12,8},{16,12},{20,16},{24,20},{28,24},{5,1},{9,5},{13... | collective-permute-start | bytes 18440 | tf_op jit(solution)/shard_map/ppermute | solution.py:17
  86.1 8.3 %collective-permute-start.9 = (bf16[256,256]{1,0:T(8,128)(2,1)S(1)}, bf16[256,256]{1,0:T(8,128)(2,1)S(1)}, u32[]{:S(2)}, u32[]{:S(2)}) collective-permute-start(bf16[256,256]{1,0:T(8,128)(2,1)S(1)} %convolution_convert_fusion.2), channel_id=1, source_target_pairs={{0,1},{1,2},{2,3},{3,0},{4,5},{5,6},{6,7},{7,4},{8,9},{9,10},{10,1... | collective-permute-start | bytes 393224 | tf_op jit(solution)/shard_map/ppermute | solution.py:49
  86.1 12.9 %collective-permute-start.10 = (bf16[256,256]{1,0:T(8,128)(2,1)S(1)}, bf16[256,256]{1,0:T(8,128)(2,1)S(1)}, u32[]{:S(2)}, u32[]{:S(2)}) collective-permute-start(bf16[256,256]{1,0:T(8,128)(2,1)S(1)} %convolution_convert_fusion.1), channel_id=1, source_target_pairs={{0,2},{1,3},{2,0},{3,1},{4,6},{5,7},{6,4},{7,5},{8,10},{9,11},{10,... | collective-permute-start | bytes 393224 | tf_op jit(solution)/shard_map/ppermute | solution.py:49
  86.7 12.4 %collective-permute-start.11 = (bf16[256,256]{1,0:T(8,128)(2,1)S(1)}, bf16[256,256]{1,0:T(8,128)(2,1)S(1)}, u32[]{:S(2)}, u32[]{:S(2)}) collective-permute-start(bf16[256,256]{1,0:T(8,128)(2,1)S(1)} %convolution_convert_fusion), channel_id=1, source_target_pairs={{0,3},{1,0},{2,1},{3,2},{4,7},{5,4},{6,5},{7,6},{8,11},{9,8},{10,9... | collective-permute-start | bytes 393224 | tf_op jit(solution)/shard_map/ppermute | solution.py:49
  90.9 11.8 %collective-permute-start.13 = (bf16[256,256]{1,0:T(8,128)(2,1)S(1)}, bf16[256,256]{1,0:T(8,128)(2,1)S(1)}, u32[]{:S(2)}, u32[]{:S(2)}) collective-permute-start(bf16[256,256]{1,0:T(8,128)(2,1)S(1)} %fusion.30), channel_id=1, source_target_pairs={{0,1},{1,2},{2,3},{3,0},{4,5},{5,6},{6,7},{7,4},{8,9},{9,10},{10,1... | collective-permute-start | bytes 393224 | tf_op jit(solution)/shard_map/ppermute | solution.py:49
  91.6 18.7 %collective-permute-start.14 = (bf16[256,256]{1,0:T(8,128)(2,1)S(1)}, bf16[256,256]{1,0:T(8,128)(2,1)S(1)}, u32[]{:S(2)}, u32[]{:S(2)}) collective-permute-start(bf16[256,256]{1,0:T(8,128)(2,1)S(1)} %fusion.31), channel_id=1, source_target_pairs={{0,2},{1,3},{2,0},{3,1},{4,6},{5,7},{6,4},{7,5},{8,10},{9,11},{10,... | collective-permute-start | bytes 393224 | tf_op jit(solution)/shard_map/ppermute | solution.py:49
  94.3 15.9 %collective-permute-start.15 = (bf16[256,256]{1,0:T(8,128)(2,1)S(1)}, bf16[256,256]{1,0:T(8,128)(2,1)S(1)}, u32[]{:S(2)}, u32[]{:S(2)}) collective-permute-start(bf16[256,256]{1,0:T(8,128)(2,1)S(1)} %fusion.32), channel_id=1, source_target_pairs={{0,3},{1,0},{2,1},{3,2},{4,7},{5,4},{6,5},{7,6},{8,11},{9,8},{10,9... | collective-permute-start | bytes 393224 | tf_op jit(solution)/shard_map/ppermute | solution.py:49

commit v8 on v6

--- a/solution.py
+++ b/solution.py
@@ -167,13 +167,6 @@
     conv_state = convolved[0] + skip_gain[None, :] * signal
     grad_signal = convolved[1] + skip_gain[None, :] * grad_state
     gated_state = (conv_state * gate_out).astype(jnp.bfloat16)
-    block_out = panel_reduce_scatter(
-        lambda dest: jnp.dot(
-            gated_state,
-            lax.dynamic_slice_in_dim(out_weight, dest * width, width, axis=1),
-            preferred_element_type=jnp.float32,
-        )
-    )
     grad_gate_out = grad_gated * conv_state
     grad_value = grad_signal * gate_in
     grad_gate_in = grad_signal * value_path
@@ -187,15 +180,24 @@
             + short_kernel[tap_index][:, None, :] * widened[:, tap_index : tap_index + row_count, :]
         )
     grad_projected = grad_projected.astype(jnp.bfloat16)
-    token_grad = panel_reduce_scatter(
-        lambda dest: jnp.einsum(
-            "jtc,jdc->td",
-            grad_projected,
-            lax.dynamic_slice_in_dim(in_weight, dest * width, width, axis=1),
-            preferred_element_type=jnp.float32,
-        )
-    )
-    return (block_out, token_grad)
+    outputs = panel_reduce_scatter(
+        lambda dest: jnp.stack(
+            [
+                jnp.dot(
+                    gated_state,
+                    lax.dynamic_slice_in_dim(out_weight, dest * width, width, axis=1),
+                    preferred_element_type=jnp.float32,
+                ),
+                jnp.einsum(
+                    "jtc,jdc->td",
+                    grad_projected,
+                    lax.dynamic_slice_in_dim(in_weight, dest * width, width, axis=1),
+                    preferred_element_type=jnp.float32,
+                ),
+            ]
+        )
+    )
+    return (outputs[0], outputs[1])
 
 
 def solution(mesh):

time: 103 us -> 107 us (1.039)
  the two profiles are of different devices: /device:TPU:0 before, /device:TPU:9 now
where the time goes in v8:
time: 107 us; the launch traced here: 106 us
  starting transfers between devices  26.8 us (25%)
  waiting for transfers between devices  25.7 us (24%)
  matrix products  20.1 us (19%)
  other arithmetic  14.4 us (13%)
  local copies, waits for them, and re-layouts  9.61 us (9%)
  blocking collectives  8.73 us (8%)
  between operations  1.2 us (1%)
    ppermute x3, waiting for transfers between devices, panel_reduce_scatter(): lax.ppermute(sent, 'panel', [(i, (i + k) % count) for i in range(count)])  22 us
    all_to_all x2, starting transfers between devices, to_columns(): lax.all_to_all(jnp.swapaxes(rows, 1, 2).astype(wire), 'seq', split_axis=1...  9.98 us
    all_to_all x1, blocking collectives, to_rows(): lax.all_to_all(columns.astype(wire), 'seq', split_axis=2, concat_axis=1,...  8.73 us
    ppermute x2, starting transfers between devices, shifted(): lax.ppermute(value, axis, [(source, source + steps) for source in range(i...  6.96 us
    ppermute x6, starting transfers between devices, panel_parts(): lax.ppermute(value, 'panel', [(i, (i + k) % count) for i in range(count)])  5.83 us
    dot_general x4, matrix products, local(): jnp.einsum('td,jdc->jtc', part, lax.dynamic_slice_in_dim(in_weight, sourc...  4.7 us
    ppermute x3, starting transfers between devices, panel_reduce_scatter(): lax.ppermute(sent, 'panel', [(i, (i + k) % count) for i in range(count)])  4 us
    dot_general x2, matrix products, forward_spectrum(): jnp.einsum('bcerkm,rmsq->bceskq', spread, stage_b, precision=STAGE_B_PREC...  3.81 us
  transfers between devices with their start and end apart: 13, of which 5 were waited for; matrix products, arithmetic and copies ran while one was open for 22% of the time, Pallas kernels for 0%

profile of v8, /device:TPU:9, one launch (start us, length us, event | category | flops | bytes accessed | tf_op | source)
XLA Modules:
  0.0 106.5 jit_solution(7018787121254648654)
XLA Ops:
  0.7 1.3 %collective-permute-start = (bf16[256,256]{1,0:T(8,128)(2,1)}, bf16[256,256]{1,0:T(8,128)(2,1)}, u32[]{:S(2)}, u32[]{:S(2)}) collective-permute-start(bf16[256,256]{1,0:T(8,128)(2,1)} %param.7), channel_id=1, source_target_pairs={{0,1},{1,2},{2,3},{3,0},{4,5},{5,6},{6,7},{7,4},{8,9},{9,10},{10,1... | collective-permute-start | bytes 393224 | tf_op jit(solution)/shard_map/ppermute | solution.py:25
  2.2 2.3 %collective-permute-start.1 = (bf16[256,256]{1,0:T(8,128)(2,1)}, bf16[256,256]{1,0:T(8,128)(2,1)}, u32[]{:S(2)}, u32[]{:S(2)}) collective-permute-start(bf16[256,256]{1,0:T(8,128)(2,1)} %param.7), channel_id=1, source_target_pairs={{0,2},{1,3},{2,0},{3,1},{4,6},{5,7},{6,4},{7,5},{8,10},{9,11},{10,... | collective-permute-start | bytes 393224 | tf_op jit(solution)/shard_map/ppermute | solution.py:25
  4.5 1.0 collective-permute-start.4
  5.5 0.5 collective-permute-start.6
  6.0 1.8 %copy.63 = f32[1,256,256]{1,0,2:T(1,128)} copy(f32[1,256,256]{2,1,0:T(8,128)} %bitcast.238) | data formatting | bytes 524288 | tf_op jit(solution)/shard_map/broadcast_in_dim | solution.py:118
  7.7 5.8 %all-to-all-start.1 = ((f32[1,256,256]{2,0,1:T(1,128)}), f32[1,256,256]{2,0,1:T(1,128)S(1)}, u32[]{:S(2)}, u32[]{:S(2)}) async-start(f32[1,256,256]{2,0,1:T(1,128)} %bitcast.36), calls=%async_computation.1 | async-start | bytes 524288 | tf_op jit(solution)/shard_map/all_to_all | solution.py:85
  13.5 0.6 iota_multiply_fusion.3
  14.2 0.7 iota_multiply_fusion
  14.9 0.6 iota_multiply_fusion.2
  15.5 1.8 %fusion.88 = (f32[256,1,256]{2,0,1:T(8,128)}, f32[256,1,256]{2,0,1:T(8,128)}) fusion(), kind=kLoop, calls=%fused_computation.141 | loop fusion | flops 983040 | bytes 524288 | tf_op jit(solution)/shard_map/sin | solution.py:62
  17.2 1.7 %fusion.90 = f32[256,1,256]{2,0,1:T(8,128)} fusion(), kind=kLoop, calls=%fused_computation.143 | loop fusion | flops 1048576 | bytes 262144 | tf_op jit(solution)/shard_map/neg | solution.py:67
  18.9 0.7 slice_bitcast_fusion.7
  19.6 1.2 %fusion.65 = f32[3,256,256]{1,2,0:T(8,128)S(1)} fusion(bf16[3,1024,256]{2,1,0:T(8,128)(2,1)S(1)} %copy-done, s32[]{:T(128)S(6)} %select_n.142, bf16[256,256]{1,0:T(8,128)(2,1)} %param.7), kind=kOutput, calls=%fused_computation.101 | convolution fusion | flops 100663296 | bytes 1310724 | tf_op jit(solution)/shard_map/td,jdc->jtc/dot_general | solution.py:122
  21.1 0.7 fusion.117
  21.8 0.8 fusion.134
  22.6 2.8 %fusion.52 = (f32[1,256,2,256]{3,1,2,0:T(8,128)}, f32[1,256,2,256]{3,1,0,2:T(8,128)}, f32[1,256,2,256]{3,1,0,2:T(8,128)}, f32[1,256,2,256]{3,1,2,0:T(8,128)}) fusion(f32[256,1,256]{2,0,1:T(8,128)} %get-tuple-element.35, f32[256,1,256]{2,0,1:T(8,128)} %fusion.90, f32[256,1,256]{2,0,1:T(8,128)} %get-tuple-element.34), kind=kLoop, calls=%fused_computation.77 | loop fusion | flops 524288 | bytes 2883584 | tf_op jit(solution)/shard_map/stack | solution.py:66
  25.4 0.5 collective-permute-start.5
  25.9 1.2 %convolution_add_fusion.1 = f32[3,256,256]{1,2,0:T(8,128)S(1)} fusion(f32[3,256,256]{1,2,0:T(8,128)S(1)} %fusion.65, bf16[3,1024,256]{2,1,0:T(8,128)(2,1)S(1)} %copy-done, s32[]{:T(128)S(6)} %select_n.144, bf16[256,256]{1,0:T(8,128)(2,1)} %collective-permute-done), kind=kOutput, calls=%fused_computation.19 | convolution fusion | flops 100859904 | bytes 2097156 | tf_op jit(solution)/shard_map/td,jdc->jtc/dot_general | solution.py:122
  27.1 1.2 %fusion.58 = f32[3,256,256]{1,2,0:T(8,128)S(1)} fusion(bf16[3,1024,256]{2,1,0:T(8,128)(2,1)S(1)} %copy-done, s32[]{:T(128)S(6)} %select_n.148, bf16[256,256]{1,0:T(8,128)(2,1)} %collective-permute-done.2), kind=kOutput, calls=%fused_computation.94 | convolution fusion | flops 100663296 | bytes 1310724 | tf_op jit(solution)/shard_map/td,jdc->jtc/dot_general | solution.py:122
  28.3 1.2 %fusion.21 = bf16[3,256,256]{2,1,0:T(8,128)(2,1)S(1)} fusion(f32[3,256,256]{1,2,0:T(8,128)S(1)} %fusion.58, f32[3,256,256]{1,2,0:T(8,128)S(1)} %convolution_add_fusion.1, bf16[3,1024,256]{2,1,0:T(8,128)(2,1)S(1)} %copy-done, s32[]{:T(128)S(6)} %select_n.146, bf16[256,256]{1,0:T(8,128)(2,1)} %collective-permute-done.1), kind=kOutput, calls=%fused_computation.22 | convolution fusion | flops 101253120 | bytes 2490372 | tf_op jit(solution)/shard_map/td,jdc->jtc/dot_general | solution.py:122
  29.5 3.8 %collective-permute-start.3 = (bf16[3,2,256]{2,1,0:T(2,128)(2,1)S(1)}, bf16[3,2,256]{2,1,0:T(2,128)(2,1)S(1)}, u32[]{:S(2)}, u32[]{:S(2)}) collective-permute-start(bf16[3,2,256]{2,1,0:T(2,128)(2,1)S(1)} %slice.119), channel_id=1, source_target_pairs={{0,4},{4,8},{8,12},{12,16},{16,20},{20,24},{24,28},{1,5},{5,9},{9,... | collective-permute-start | bytes 9224 | tf_op jit(solution)/shard_map/ppermute | solution.py:17
  33.3 1.1 %convolution_add_fusion.3 = f32[256,256]{0,1:T(8,128)S(1)} fusion(f32[256,256]{0,1:T(8,128)S(1)} %fusion.99, bf16[256,256]{1,0:T(8,128)(2,1)} %collective-permute-done.4, bf16[256,1024]{1,0:T(8,128)(2,1)S(1)} %copy-done.3, s32[]{:T(128)S(6)} %select_n.144), kind=kOutput, calls=%fused_computation.31 | convolution fusion | flops 33619968 | bytes 786436 | tf_op jit(solution)/shard_map/dot_general | solution.py:130
  34.5 1.1 %fusion.92 = f32[256,256]{0,1:T(8,128)S(1)} fusion(bf16[256,256]{1,0:T(8,128)(2,1)} %collective-permute-done.6, bf16[256,1024]{1,0:T(8,128)(2,1)S(1)} %copy-done.3, s32[]{:T(128)S(6)} %select_n.148), kind=kOutput, calls=%fused_computation.145 | convolution fusion | flops 33554432 | bytes 524292 | tf_op jit(solution)/shard_map/dot_general | solution.py:130
  36.7 0.9 copy.32
  37.6 4.2 %all-to-all-start = ((bf16[2,256,256]{2,0,1:T(2,128)(2,1)}), bf16[2,256,256]{2,0,1:T(2,128)(2,1)}, u32[]{:S(2)}, u32[]{:S(2)}) async-start(bf16[2,256,256]{2,0,1:T(2,128)(2,1)} %copy.32), calls=%async_computation | async-start | bytes 524288 | tf_op jit(solution)/shard_map/all_to_all | solution.py:85
  41.8 1.0 convolution_bitcast_fusion.2
  43.0 0.8 copy-done.5
  44.0 1.1 %convolution_bitcast_fusion.1 = f32[1,32,2,2,8,256]{5,1,4,2,0,3:T(8,128)S(1)} fusion(f32[32,2,2,8,256]{4,3,0,2,1:T(8,128)S(1)} %maximum_bitcast_fusion.3, f32[1,256,2,256]{3,1,0,2:T(8,128)S(1)} %copy-done.5, f32[1,256,2,256]{3,1,0,2:T(8,128)S(1)} %copy-done.7), kind=kOutput, calls=%fused_computation.15 | convolution fusion | flops 805568512 | bytes 3145728 | tf_op jit(solution)/shard_map/bcerkm,rmsq->bceskq/dot_general | solution.py:103
  45.1 2.0 %all-to-all-done = bf16[2,256,256]{2,0,1:T(2,128)(2,1)} async-done(((bf16[2,256,256]{2,0,1:T(2,128)(2,1)}), bf16[2,256,256]{2,0,1:T(2,128)(2,1)}, u32[]{:S(2)}, u32[]{:S(2)}) %all-to-all-start) | async-done | bytes 262176 | tf_op jit(solution)/shard_map/all_to_all | solution.py:85
  47.2 2.0 %convolution_bitcast_fusion = f32[2,32,2,2,8,256]{5,4,3,2,1,0:T(8,128)S(1)} fusion(bf16[2,8,32,256]{3,0,2,1:T(2,128)(2,1)} %bitcast.20, f32[2,1,8,8]{3,2,1,0:T(8,128)S(1)} %get-tuple-element.33, f32[2,1,8,8]{3,2,1,0:T(8,128)S(1)} %get-tuple-element.32), kind=kOutput, calls=%fused_computation.14 | convolution fusion | flops 50331904 | bytes 2360320 | tf_op jit(solution)/shard_map/erkp,bcpm->bcerkm/dot_general | solution.py:101
  49.7 0.8 copy-done.6
  50.7 2.7 %fusion.10 = f32[2,32,2,2,8,256]{5,1,4,2,0,3:T(8,128)S(1)} fusion(f32[2,32,2,2,8,256]{5,4,3,2,1,0:T(8,128)S(1)} %pad_maximum_fusion, f32[1,256,2,256]{3,1,0,2:T(8,128)S(1)} %copy-done.6, f32[1,256,2,256]{3,1,0,2:T(8,128)S(1)} %copy-done.8), kind=kOutput, calls=%fused_computation.12 | convolution fusion | flops 1610874880 | bytes 5242880 | tf_op jit(solution)/shard_map/bcerkm,rmsq->bceskq/dot_general | solution.py:103
  53.3 0.5 multiply_subtract_fusion.3
  54.0 0.9 copy-done.9
  55.0 2.7 %fusion.13 = f32[2,32,2,2,8,256]{5,4,3,2,1,0:T(8,128)S(1)} fusion(f32[2,32,2,2,8,256,1]{5,1,4,2,0,3,6:T(8,128)S(1)} %maximum_bitcast_fusion, f32[1,256,2,256]{3,1,2,0:T(8,128)S(1)} %copy-done.10, f32[1,256,2,256]{3,1,2,0:T(8,128)S(1)} %copy-done.9), kind=kOutput, calls=%fused_computation.13 | convolution fusion | flops 1610874880 | bytes 5242880 | tf_op jit(solution)/shard_map/bceskq,sqrm->bcerkm/dot_general | solution.py:108
  58.1 1.2 %fusion.27 = bf16[2,32,8,256]{3,2,1,0:T(8,128)(2,1)S(1)} fusion(f32[2,32,2,1,8,256]{5,4,3,2,1,0:T(8,128)S(1)} %get-tuple-element.11, f32[2,32,2,1,8,256]{5,4,3,2,1,0:T(8,128)S(1)} %get-tuple-element.10, f32[2,1,8,8]{3,2,1,0:T(8,128)S(1)} %get-tuple-element.33, f32[2,1,8,8]{3,2,1,0:T(8,128)S(1)} %get-tuple-element.32), kind=kOutput, calls=%fused_computation.33 | convolution fusion | flops 50987520 | bytes 2360320 | tf_op jit(solution)/shard_map/erkp,bcerkm->bcpm/dot_general | solution.py:110
  59.4 8.7 %all_to_all.39 = bf16[2,32,8,256]{3,1,0,2:T(8,128)(2,1)S(1)} all-to-all(bf16[2,32,8,256]{3,1,0,2:T(8,128)(2,1)S(1)} %copy.43), channel_id=1, replica_groups=mesh['seq'=8,'panel'=4] {'seq'}, dimensions={2} | all-to-all | bytes 524288 | tf_op jit(solution)/shard_map/all_to_all | solution.py:93
  68.1 0.8 bitcast_convert_fusion
  69.0 2.0 %copy.45 = f32[2,256,256]{1,2,0:T(8,128)} copy(f32[2,256,256]{2,1,0:T(8,128)} %bitcast.235) | data formatting | bytes 1048576 | tf_op jit(solution)/shard_map/transpose | solution.py:96
  71.0 1.1 %multiply_convert_fusion = (bf16[256,256]{1,0:T(8,128)(2,1)S(1)}, f32[256,256]{1,0:T(8,128)S(1)}, f32[1,256,256]{2,1,0:T(8,128)S(1)}, f32[256,256]{1,0:T(8,128)S(1)}) fusion(f32[3,256,256]{2,1,0:T(8,128)S(1)} %fusion.48, f32[256]{0:T(256)S(1)} %copy-done.12, f32[2,256,256]{2,1,0:T(8,128)} %bitcast.236, f32[256,256]{1,0:T(8,128)S(1)} %copy-done.2), kind=kLoop, calls=%fused_computation.128 | loop fusion | flops 589824 | bytes 2491392 | tf_op jit(solution)/shard_map/convert_element_type | solution.py:169
  72.7 3.1 %collective-permute-start.7 = (f32[3,2,256]{2,1,0:T(2,128)S(1)}, f32[3,2,256]{2,1,0:T(2,128)S(1)}, u32[]{:S(2)}, u32[]{:S(2)}) collective-permute-start(f32[3,2,256]{2,1,0:T(2,128)S(1)} %slice.140), channel_id=1, source_target_pairs={{4,0},{8,4},{12,8},{16,12},{20,16},{24,20},{28,24},{5,1},{9,5},{13... | collective-permute-start | bytes 18440 | tf_op jit(solution)/shard_map/ppermute | solution.py:17
  76.1 1.6 %collective-permute-done.7 = f32[3,2,256]{2,1,0:T(2,128)S(1)} collective-permute-done((f32[3,2,256]{2,1,0:T(2,128)S(1)}, f32[3,2,256]{2,1,0:T(2,128)S(1)}, u32[]{:S(2)}, u32[]{:S(2)}) %collective-permute-start.7) | collective-permute-done | bytes 6176 | tf_op jit(solution)/shard_map/ppermute | solution.py:17
  79.0 2.7 %collective-permute-start.8 = (bf16[2,256,256]{2,1,0:T(8,128)(2,1)S(1)}, bf16[2,256,256]{2,1,0:T(8,128)(2,1)S(1)}, u32[]{:S(2)}, u32[]{:S(2)}) collective-permute-start(bf16[2,256,256]{2,1,0:T(8,128)(2,1)S(1)} %pad_maximum_fusion.10), channel_id=1, source_target_pairs={{0,1},{1,2},{2,3},{3,0},{4,5},{5,6},{6,7},{7,4},{8,9},{9,10},{10,1... | collective-permute-start | bytes 786440 | tf_op jit(solution)/shard_map/ppermute | solution.py:36
  81.7 1.1 collective-permute-start.9
  83.6 15.5 %collective-permute-done.8 = bf16[2,256,256]{2,1,0:T(8,128)(2,1)S(1)} collective-permute-done((bf16[2,256,256]{2,1,0:T(8,128)(2,1)S(1)}, bf16[2,256,256]{2,1,0:T(8,128)(2,1)S(1)}, u32[]{:S(2)}, u32[]{:S(2)}) %collective-permute-start.8) | collective-permute-done | bytes 262176 | tf_op jit(solution)/shard_map/ppermute | solution.py:36
  99.0 5.4 %collective-permute-done.9 = bf16[2,256,256]{2,1,0:T(8,128)(2,1)S(1)} collective-permute-done((bf16[2,256,256]{2,1,0:T(8,128)(2,1)S(1)}, bf16[2,256,256]{2,1,0:T(8,128)(2,1)S(1)}, u32[]{:S(2)}, u32[]{:S(2)}) %collective-permute-start.9) | collective-permute-done | bytes 262176 | tf_op jit(solution)/shard_map/ppermute | solution.py:36
  104.5 1.1 %collective-permute-done.10 = bf16[2,256,256]{2,1,0:T(8,128)(2,1)S(1)} collective-permute-done((bf16[2,256,256]{2,1,0:T(8,128)(2,1)S(1)}, bf16[2,256,256]{2,1,0:T(8,128)(2,1)S(1)}, u32[]{:S(2)}, u32[]{:S(2)}) %collective-permute-start.10) | collective-permute-done | bytes 262176 | tf_op jit(solution)/shard_map/ppermute | solution.py:36
  105.7 0.7 slice_bitcast_fusion.3
  (69 shorter events, 6.2 us)
Async XLA Ops:
  0.6 19.0 %copy-start = (bf16[3,1024,256]{2,1,0:T(8,128)(2,1)S(1)}, bf16[3,1024,256]{2,1,0:T(8,128)(2,1)}, u32[]{:S(2)}) copy-start(bf16[3,1024,256]{2,1,0:T(8,128)(2,1)} %param.9) | copy-start | bytes 4718596
  0.6 20.2 %copy-start.11 = (bf16[256,256]{1,0:T(8,128)(2,1)S(1)}, bf16[256,256]{1,0:T(8,128)(2,1)}, u32[]{:S(2)}) copy-start(bf16[256,256]{1,0:T(8,128)(2,1)} %param.8) | copy-start | bytes 393220
  0.7 20.2 %copy-start.3 = (bf16[256,1024]{1,0:T(8,128)(2,1)S(1)}, bf16[256,1024]{1,0:T(8,128)(2,1)}, u32[]{:S(2)}) copy-start(bf16[256,1024]{1,0:T(8,128)(2,1)} %param.13) | copy-start | bytes 1572868
  0.7 24.7 %collective-permute-start = (bf16[256,256]{1,0:T(8,128)(2,1)}, bf16[256,256]{1,0:T(8,128)(2,1)}, u32[]{:S(2)}, u32[]{:S(2)}) collective-permute-start(bf16[256,256]{1,0:T(8,128)(2,1)} %param.7), channel_id=1, source_target_pairs={{0,1},{1,2},{2,3},{3,0},{4,5},{5,6},{6,7},{7,4},{8,9},{9,10},{10,1... | collective-permute-start | bytes 393224 | tf_op jit(solution)/shard_map/ppermute | solution.py:25
  2.0 25.1 %collective-permute-start.2 = (bf16[256,256]{1,0:T(8,128)(2,1)}, bf16[256,256]{1,0:T(8,128)(2,1)}, u32[]{:S(2)}, u32[]{:S(2)}) collective-permute-start(bf16[256,256]{1,0:T(8,128)(2,1)} %param.7), channel_id=1, source_target_pairs={{0,3},{1,0},{2,1},{3,2},{4,7},{5,4},{6,5},{7,6},{8,11},{9,8},{10,9... | collective-permute-start | bytes 393224 | tf_op jit(solution)/shard_map/ppermute | solution.py:25
  2.2 26.1 %collective-permute-start.1 = (bf16[256,256]{1,0:T(8,128)(2,1)}, bf16[256,256]{1,0:T(8,128)(2,1)}, u32[]{:S(2)}, u32[]{:S(2)}) collective-permute-start(bf16[256,256]{1,0:T(8,128)(2,1)} %param.7), channel_id=1, source_target_pairs={{0,2},{1,3},{2,0},{3,1},{4,6},{5,7},{6,4},{7,5},{8,10},{9,11},{10,... | collective-permute-start | bytes 393224 | tf_op jit(solution)/shard_map/ppermute | solution.py:25
  4.5 28.8 %collective-permute-start.4 = (bf16[256,256]{1,0:T(8,128)(2,1)}, bf16[256,256]{1,0:T(8,128)(2,1)}, u32[]{:S(2)}, u32[]{:S(2)}) collective-permute-start(bf16[256,256]{1,0:T(8,128)(2,1)} %param.8), channel_id=1, source_target_pairs={{0,1},{1,2},{2,3},{3,0},{4,5},{5,6},{6,7},{7,4},{8,9},{9,10},{10,1... | collective-permute-start | bytes 393224 | tf_op jit(solution)/shard_map/ppermute | solution.py:25
  5.5 29.0 %collective-permute-start.6 = (bf16[256,256]{1,0:T(8,128)(2,1)}, bf16[256,256]{1,0:T(8,128)(2,1)}, u32[]{:S(2)}, u32[]{:S(2)}) collective-permute-start(bf16[256,256]{1,0:T(8,128)(2,1)} %param.8), channel_id=1, source_target_pairs={{0,3},{1,0},{2,1},{3,2},{4,7},{5,4},{6,5},{7,6},{8,11},{9,8},{10,9... | collective-permute-start | bytes 393224 | tf_op jit(solution)/shard_map/ppermute | solution.py:25
  7.7 29.9 %all-to-all-start.1 = ((f32[1,256,256]{2,0,1:T(1,128)}), f32[1,256,256]{2,0,1:T(1,128)S(1)}, u32[]{:S(2)}, u32[]{:S(2)}) async-start(f32[1,256,256]{2,0,1:T(1,128)} %bitcast.36), calls=%async_computation.1 | async-start | bytes 524288 | tf_op jit(solution)/shard_map/all_to_all | solution.py:85
  25.4 10.3 %collective-permute-start.5 = (bf16[256,256]{1,0:T(8,128)(2,1)}, bf16[256,256]{1,0:T(8,128)(2,1)S(1)}, u32[]{:S(2)}, u32[]{:S(2)}) collective-permute-start(bf16[256,256]{1,0:T(8,128)(2,1)} %param.8), channel_id=1, source_target_pairs={{0,2},{1,3},{2,0},{3,1},{4,6},{5,7},{6,4},{7,5},{8,10},{9,11},{10,... | collective-permute-start | bytes 393224 | tf_op jit(solution)/shard_map/ppermute | solution.py:25
  29.5 6.4 %collective-permute-start.3 = (bf16[3,2,256]{2,1,0:T(2,128)(2,1)S(1)}, bf16[3,2,256]{2,1,0:T(2,128)(2,1)S(1)}, u32[]{:S(2)}, u32[]{:S(2)}) collective-permute-start(bf16[3,2,256]{2,1,0:T(2,128)(2,1)S(1)} %slice.119), channel_id=1, source_target_pairs={{0,4},{4,8},{8,12},{12,16},{16,20},{20,24},{24,28},{1,5},{5,9},{9,... | collective-permute-start | bytes 9224 | tf_op jit(solution)/shard_map/ppermute | solution.py:17
  35.9 0.7 copy-start.1
  37.6 9.6 %all-to-all-start = ((bf16[2,256,256]{2,0,1:T(2,128)(2,1)}), bf16[2,256,256]{2,0,1:T(2,128)(2,1)}, u32[]{:S(2)}, u32[]{:S(2)}) async-start(bf16[2,256,256]{2,0,1:T(2,128)(2,1)} %copy.32), calls=%async_computation | async-start | bytes 524288 | tf_op jit(solution)/shard_map/all_to_all | solution.py:85
  42.8 1.0 copy-start.5
  42.8 1.2 %copy-start.7 = (f32[1,256,2,256]{3,1,0,2:T(8,128)S(1)}, f32[1,256,2,256]{3,1,0,2:T(8,128)}, u32[]{:S(2)}) copy-start(f32[1,256,2,256]{3,1,0,2:T(8,128)} %get-tuple-element.24) | copy-start | bytes 1572868
  49.5 1.0 copy-start.6
  49.5 1.2 %copy-start.8 = (f32[1,256,2,256]{3,1,0,2:T(8,128)S(1)}, f32[1,256,2,256]{3,1,0,2:T(8,128)}, u32[]{:S(2)}) copy-start(f32[1,256,2,256]{3,1,0,2:T(8,128)} %get-tuple-element.24) | copy-start | bytes 1572868
  53.8 1.0 copy-start.9
  53.8 1.2 %copy-start.10 = (f32[1,256,2,256]{3,1,2,0:T(8,128)S(1)}, f32[1,256,2,256]{3,1,2,0:T(8,128)}, u32[]{:S(2)}) copy-start(f32[1,256,2,256]{3,1,2,0:T(8,128)} %get-tuple-element.25) | copy-start | bytes 1572868
  58.1 12.9 %copy-start.2 = (f32[256,256]{1,0:T(8,128)S(1)}, f32[256,256]{1,0:T(8,128)}, u32[]{:S(2)}) copy-start(f32[256,256]{1,0:T(8,128)} %copy-done.1) | copy-start | bytes 786436
  58.1 12.9 %copy-start.12 = (f32[256]{0:T(256)S(1)}, f32[256]{0:T(256)}, u32[]{:S(2)}) copy-start(f32[256]{0:T(256)} %param.11) | copy-start | bytes 3076
  68.1 4.0 %copy-start.4 = (bf16[256,1024]{1,0:T(8,128)(2,1)S(1)}, bf16[256,1024]{1,0:T(8,128)(2,1)}, u32[]{:S(2)}) copy-start(bf16[256,1024]{1,0:T(8,128)(2,1)} %param.13) | copy-start | bytes 1572868
  72.7 4.9 %collective-permute-start.7 = (f32[3,2,256]{2,1,0:T(2,128)S(1)}, f32[3,2,256]{2,1,0:T(2,128)S(1)}, u32[]{:S(2)}, u32[]{:S(2)}) collective-permute-start(f32[3,2,256]{2,1,0:T(2,128)S(1)} %slice.140), channel_id=1, source_target_pairs={{4,0},{8,4},{12,8},{16,12},{20,16},{24,20},{28,24},{5,1},{9,5},{13... | collective-permute-start | bytes 18440 | tf_op jit(solution)/shard_map/ppermute | solution.py:17
  79.0 20.0 %collective-permute-start.8 = (bf16[2,256,256]{2,1,0:T(8,128)(2,1)S(1)}, bf16[2,256,256]{2,1,0:T(8,128)(2,1)S(1)}, u32[]{:S(2)}, u32[]{:S(2)}) collective-permute-start(bf16[2,256,256]{2,1,0:T(8,128)(2,1)S(1)} %pad_maximum_fusion.10), channel_id=1, source_target_pairs={{0,1},{1,2},{2,3},{3,0},{4,5},{5,6},{6,7},{7,4},{8,9},{9,10},{10,1... | collective-permute-start | bytes 786440 | tf_op jit(solution)/shard_map/ppermute | solution.py:36
  81.7 22.7 %collective-permute-start.9 = (bf16[2,256,256]{2,1,0:T(8,128)(2,1)S(1)}, bf16[2,256,256]{2,1,0:T(8,128)(2,1)S(1)}, u32[]{:S(2)}, u32[]{:S(2)}) collective-permute-start(bf16[2,256,256]{2,1,0:T(8,128)(2,1)S(1)} %pad_maximum_fusion.11), channel_id=1, source_target_pairs={{0,2},{1,3},{2,0},{3,1},{4,6},{5,7},{6,4},{7,5},{8,10},{9,11},{10,... | collective-permute-start | bytes 786440 | tf_op jit(solution)/shard_map/ppermute | solution.py:36
  82.8 22.8 %collective-permute-start.10 = (bf16[2,256,256]{2,1,0:T(8,128)(2,1)S(1)}, bf16[2,256,256]{2,1,0:T(8,128)(2,1)S(1)}, u32[]{:S(2)}, u32[]{:S(2)}) collective-permute-start(bf16[2,256,256]{2,1,0:T(8,128)(2,1)S(1)} %pad_maximum_fusion.12), channel_id=1, source_target_pairs={{0,3},{1,0},{2,1},{3,2},{4,7},{5,4},{6,5},{7,6},{8,11},{9,8},{10,9... | collective-permute-start | bytes 786440 | tf_op jit(solution)/shard_map/ppermute | solution.py:36

commit v9 on v6

--- a/solution.py
+++ b/solution.py
@@ -5,7 +5,7 @@
 from jax import lax
 from jax.sharding import PartitionSpec as P
 
-HIGHEST = lax.Precision.HIGHEST
+
 STAGE_A_PRECISION = lax.Precision.HIGHEST
 STAGE_B_PRECISION = lax.Precision.HIGH
 WIRE = jnp.bfloat16
@@ -110,7 +110,7 @@
     return jnp.einsum("erkp,bcerkm->bcpm", stage_a_inv, spread, precision=STAGE_A_PRECISION)
 
 
-def local(tokens, cotangent, in_weight, short_kernel, skip_gain, long_filter, out_weight):
+def local_body(tokens, cotangent, in_weight, short_kernel, skip_gain, long_filter, out_weight):
     row_count = tokens.shape[0]
     tap_count = short_kernel.shape[0]
     shard_count = lax.axis_size("seq")
@@ -118,7 +118,9 @@
     filt_spec = forward_spectrum(to_columns(long_filter[None]), tables)
     width = tokens.shape[1]
     projected = 0.0
-    for part, source in panel_parts(tokens):
+    token_parts = panel_parts(tokens)
+    cotangent_parts = panel_parts(cotangent)
+    for part, source in token_parts:
         projected = projected + jnp.einsum(
             "td,jdc->jtc",
             part,
@@ -126,7 +128,7 @@
             preferred_element_type=jnp.float32,
         )
     grad_gated = 0.0
-    for part, source in panel_parts(cotangent):
+    for part, source in cotangent_parts:
         grad_gated = grad_gated + lax.dot_general(
             part,
             lax.dynamic_slice_in_dim(out_weight, source * width, width, axis=1),
@@ -147,7 +149,12 @@
     gate_out, gate_in, value_path = (filtered[0], filtered[1], filtered[2])
     signal = value_path * gate_in
     grad_state = grad_gated * gate_out
-    spectra = forward_spectrum(to_columns(jnp.stack([signal, grad_state]), WIRE), tables)
+    spectra = jnp.concatenate(
+        [
+            forward_spectrum(to_columns(signal[None], WIRE), tables),
+            forward_spectrum(to_columns(grad_state[None], WIRE), tables),
+        ]
+    )
     filt_real, filt_imag = filt_spec[:, :, :, 0], filt_spec[:, :, :, 1]
     sig_real, sig_imag = spectra[0:1, :, :, 0], spectra[0:1, :, :, 1]
     grad_real, grad_imag = spectra[1:2, :, :, 0], spectra[1:2, :, :, 1]
@@ -209,7 +216,7 @@
         P("panel", None),
     )
     return jax.shard_map(
-        local,
+        local_body,
         mesh=mesh,
         in_specs=placed,
         out_specs=(P("seq", "panel"), P("seq", "panel")),

time: 103 us -> 127 us (1.23)
  starting transfers between devices: 28.8 us -> 39.5 us
  local copies, waits for them, and re-layouts: 8.92 us -> 15.6 us
  matrix products: 21.5 us -> 26 us
  other arithmetic: 13 us -> 17.3 us
  waiting for transfers between devices: 18.7 us -> 17.3 us
    ppermute x6, starting transfers between devices: 7.07 us -> 12.9 us  [panel_reduce_scatter(): lax.ppermute(sent, 'panel', [(i, (i + k) % count) for i in range(count)])]
    unnamed x27 -> x46, local copies, waits for them, and re-layouts: 4.24 us -> 9.44 us
    unnamed x0 -> x2, other arithmetic: none -> 4.63 us
    all_to_all x2 -> x3, starting transfers between devices: 7.95 us -> 12.3 us  [to_columns(): lax.all_to_all(jnp.swapaxes(rows, 1, 2).astype(wire), 'seq', split_axis=1...]
    dot_general x16, matrix products: 10.8 us -> 13.2 us  [the longest x4 5.09 us: local_body(): lax.dot_general(part, lax.dynamic_slice_in_dim(out_weight, source * width...]
    ppermute x6, waiting for transfers between devices: 14.6 us -> 12.6 us  [panel_reduce_scatter(): lax.ppermute(sent, 'panel', [(i, (i + k) % count) for i in range(count)])]
    sub x3 -> x2, other arithmetic: 0.79 us -> 2.14 us  [complex_scale(): real_part * cos_part - imag_part * sin_part]
    all_to_all x2 -> x3, waiting for transfers between devices: 3.38 us -> 4.7 us  [to_columns(): lax.all_to_all(jnp.swapaxes(rows, 1, 2).astype(wire), 'seq', split_axis=1...]
  transfers between devices with their start and end apart: 16 -> 17, of which waited for: 5 -> 4; matrix products, arithmetic and copies ran while one was open for 25% -> 30% of each run, Pallas kernels for 0% -> 0%
where the time goes in v9:
time: 127 us; the launch traced here: 126 us
  starting transfers between devices  39.5 us (31%)
  matrix products  26 us (20%)
  other arithmetic  17.3 us (14%)
  waiting for transfers between devices  17.3 us (14%)
  local copies, waits for them, and re-layouts  15.6 us (12%)
  blocking collectives  9.32 us (7%)
  between operations  1.31 us (1%)
    ppermute x6, starting transfers between devices, panel_reduce_scatter(): lax.ppermute(sent, 'panel', [(i, (i + k) % count) for i in range(count)])  12.9 us
    ppermute x6, waiting for transfers between devices, panel_reduce_scatter(): lax.ppermute(sent, 'panel', [(i, (i + k) % count) for i in range(count)])  12.6 us
    all_to_all x3, starting transfers between devices, to_columns(): lax.all_to_all(jnp.swapaxes(rows, 1, 2).astype(wire), 'seq', split_axis=1...  12.3 us
    ppermute x6, starting transfers between devices, panel_parts(): lax.ppermute(value, 'panel', [(i, (i + k) % count) for i in range(count)])  11 us
    unnamed x46, local copies, waits for them, and re-layouts  9.44 us
    all_to_all x1, blocking collectives, to_rows(): lax.all_to_all(columns.astype(wire), 'seq', split_axis=2, concat_axis=1,...  9.32 us
    dot_general x4, matrix products, local_body(): lax.dot_general(part, lax.dynamic_slice_in_dim(out_weight, source * width...  5.09 us
    dot_general x4, matrix products, local_body(): jnp.einsum('td,jdc->jtc', part, lax.dynamic_slice_in_dim(in_weight, sourc...  4.76 us
  transfers between devices with their start and end apart: 17, of which 4 were waited for; matrix products, arithmetic and copies ran while one was open for 30% of the time, Pallas kernels for 0%

profile of v9, /device:TPU:0, one launch (start us, length us, event | category | flops | bytes accessed | tf_op | source)
XLA Modules:
  0.0 126.3 jit_solution(10853493897643169414)
XLA Ops:
  0.7 5.1 %collective-permute-start.2 = (bf16[256,256]{1,0:T(8,128)(2,1)}, bf16[256,256]{1,0:T(8,128)(2,1)}, u32[]{:S(2)}, u32[]{:S(2)}) collective-permute-start(bf16[256,256]{1,0:T(8,128)(2,1)} %param.7), channel_id=1, source_target_pairs={{0,3},{1,0},{2,1},{3,2},{4,7},{5,4},{6,5},{7,6},{8,11},{9,8},{10,9... | collective-permute-start | bytes 393224 | tf_op jit(solution)/shard_map/ppermute | solution.py:25
  5.8 1.0 collective-permute-start.1
  6.8 2.8 %collective-permute-start.6 = (bf16[256,256]{1,0:T(8,128)(2,1)}, bf16[256,256]{1,0:T(8,128)(2,1)}, u32[]{:S(2)}, u32[]{:S(2)}) collective-permute-start(bf16[256,256]{1,0:T(8,128)(2,1)} %param.8), channel_id=1, source_target_pairs={{0,3},{1,0},{2,1},{3,2},{4,7},{5,4},{6,5},{7,6},{8,11},{9,8},{10,9... | collective-permute-start | bytes 393224 | tf_op jit(solution)/shard_map/ppermute | solution.py:25
  10.2 1.8 %copy.68 = f32[1,256,256]{1,0,2:T(1,128)} copy(f32[1,256,256]{2,1,0:T(8,128)} %bitcast.255) | data formatting | bytes 524288 | tf_op jit(solution)/shard_map/broadcast_in_dim | solution.py:118
  12.0 4.1 %all-to-all-start.1 = ((f32[1,256,256]{2,0,1:T(1,128)}), f32[1,256,256]{2,0,1:T(1,128)}, u32[]{:S(2)}, u32[]{:S(2)}) async-start(f32[1,256,256]{2,0,1:T(1,128)} %bitcast.33), calls=%async_computation.1 | async-start | bytes 524288 | tf_op jit(solution)/shard_map/all_to_all | solution.py:85
  16.3 1.8 %fusion.87 = (f32[256,1,256]{2,0,1:T(8,128)}, f32[256,1,256]{2,0,1:T(8,128)}) fusion(), kind=kLoop, calls=%fused_computation.134 | loop fusion | flops 983040 | bytes 524288 | tf_op jit(solution)/shard_map/sin | solution.py:62
  18.0 1.7 %fusion.89 = f32[256,1,256]{2,0,1:T(8,128)} fusion(), kind=kLoop, calls=%fused_computation.136 | loop fusion | flops 1048576 | bytes 262144 | tf_op jit(solution)/shard_map/neg | solution.py:67
  19.7 1.3 %slice_bitcast_fusion.5 = (f32[3,256]{1,0:T(4,128)}, f32[3,256]{1,0:T(4,128)}, f32[3,256]{1,0:T(4,128)}) fusion(f32[3,3,256]{2,1,0:T(4,128)} %param.10), kind=kLoop, calls=%fused_computation.181 | loop fusion | bytes 18432 | tf_op jit(solution)/shard_map/mul | solution.py:142
  21.1 1.2 fusion.49
  22.3 1.9 %fusion.99 = f32[256,256]{0,1:T(8,128)} fusion(bf16[256,256]{1,0:T(8,128)(2,1)S(1)} %copy-done.9, bf16[256,1024]{1,0:T(8,128)(2,1)} %param.13, s32[]{:T(128)S(6)} %select_n.157), kind=kOutput, calls=%fused_computation.146 | convolution fusion | flops 33554432 | bytes 524292 | tf_op jit(solution)/shard_map/dot_general | solution.py:132
  24.9 2.5 %fusion.39 = (f32[1,256,2,256]{3,1,2,0:T(8,128)}, f32[1,256,2,256]{3,1,0,2:T(8,128)S(1)}, f32[1,256,2,256]{3,1,0,2:T(8,128)S(1)}, f32[1,256,2,256]{3,1,2,0:T(8,128)}) fusion(f32[256,1,256]{2,0,1:T(8,128)} %get-tuple-element.45, f32[256,1,256]{2,0,1:T(8,128)} %fusion.89, f32[256,1,256]{2,0,1:T(8,128)} %get-tuple-element.44), kind=kLoop, calls=%fused_computation.68 | loop fusion | flops 524288 | bytes 2883584 | tf_op jit(solution)/shard_map/stack | solution.py:66
  27.4 1.5 %collective-permute-start.5 = (bf16[256,256]{1,0:T(8,128)(2,1)S(1)}, bf16[256,256]{1,0:T(8,128)(2,1)S(1)}, u32[]{:S(2)}, u32[]{:S(2)}) collective-permute-start(bf16[256,256]{1,0:T(8,128)(2,1)S(1)} %copy-done.9), channel_id=1, source_target_pairs={{0,2},{1,3},{2,0},{3,1},{4,6},{5,7},{6,4},{7,5},{8,10},{9,11},{10,... | collective-permute-start | bytes 393224 | tf_op jit(solution)/shard_map/ppermute | solution.py:25
  28.9 1.2 convolution_add_fusion.1
  30.1 1.2 fusion.42
  31.3 1.2 fusion.13
  32.6 1.9 %collective-permute-start.3 = (bf16[3,2,256]{2,1,0:T(2,128)(2,1)S(1)}, bf16[3,2,256]{2,1,0:T(2,128)(2,1)S(1)}, u32[]{:S(2)}, u32[]{:S(2)}) collective-permute-start(bf16[3,2,256]{2,1,0:T(2,128)(2,1)S(1)} %slice.119), channel_id=1, source_target_pairs={{0,4},{4,8},{8,12},{12,16},{16,20},{20,24},{24,28},{1,5},{5,9},{9,... | collective-permute-start | bytes 9224 | tf_op jit(solution)/shard_map/ppermute | solution.py:17
  34.6 1.1 convolution_add_fusion.3
  35.7 1.1 fusion.91
  36.9 1.0 fusion.18
  39.6 2.3 %reduce = bf16[256,256]{1,0:T(8,128)(2,1)S(1)} reduce(bf16[256,1,256]{2,1,0:T(2,128)(2,1)} %bitcast.248, bf16[]{:T(256)} %broadcast.391), dimensions={1}, to_apply=%bitcast.225.reduce_sub_computation | reduce | bytes 262146
  42.6 1.0 convert_bitcast_fusion
  44.5 2.3 %reduce.1 = bf16[256,256]{1,0:T(8,128)(2,1)S(1)} reduce(bf16[256,1,256]{2,1,0:T(2,128)(2,1)} %bitcast.249, bf16[]{:T(256)} %broadcast.391), dimensions={1}, to_apply=%bitcast.223.reduce_sub_computation | reduce | bytes 262146
  47.5 4.3 %all-to-all-start = ((bf16[8,2,4096]{2,1,0:T(2,128)(2,1)}), bf16[8,2,4096]{2,1,0:T(2,128)(2,1)S(1)}, u32[]{:S(2)}, u32[]{:S(2)}) async-start(bf16[8,2,4096]{2,1,0:T(2,128)(2,1)} %reshape.390), calls=%async_computation | async-start | bytes 262144 | tf_op jit(solution)/shard_map/all_to_all | solution.py:85
  51.8 1.0 copy.71
  52.8 2.0 %convolution_bitcast_fusion.3 = f32[1,32,2,2,8,256]{5,4,3,2,1,0:T(8,128)} fusion(f32[1,8,32,256]{3,2,1,0:T(8,128)S(1)} %bitcast.252, f32[2,1,8,8]{3,2,1,0:T(8,128)S(1)} %get-tuple-element.41, f32[2,1,8,8]{3,2,1,0:T(8,128)S(1)} %get-tuple-element.40), kind=kOutput, calls=%fused_computation.11 | convolution fusion | flops 25166080 | bytes 1311744 | tf_op jit(solution)/shard_map/erkp,bcpm->bcerkm/dot_general | solution.py:101
  54.8 2.6 %all-to-all-done = bf16[8,2,4096]{2,1,0:T(2,128)(2,1)S(1)} async-done(((bf16[8,2,4096]{2,1,0:T(2,128)(2,1)}), bf16[8,2,4096]{2,1,0:T(2,128)(2,1)S(1)}, u32[]{:S(2)}, u32[]{:S(2)}) %all-to-all-start) | async-done | bytes 131104 | tf_op jit(solution)/shard_map/all_to_all | solution.py:85
  57.3 4.0 %all-to-all-start.2 = ((bf16[8,2,4096]{2,1,0:T(2,128)(2,1)}), bf16[8,2,4096]{2,1,0:T(2,128)(2,1)}, u32[]{:S(2)}, u32[]{:S(2)}) async-start(bf16[8,2,4096]{2,1,0:T(2,128)(2,1)} %reshape.388), calls=%async_computation.2 | async-start | bytes 262144 | tf_op jit(solution)/shard_map/all_to_all | solution.py:85
  62.2 1.0 copy.70
  63.1 1.5 %convolution_bitcast_fusion.5 = f32[1,32,2,2,8,256]{5,4,3,2,1,0:T(8,128)} fusion(bf16[1,8,32,256]{3,2,1,0:T(8,128)(2,1)S(1)} %bitcast.253, f32[2,1,8,8]{3,2,1,0:T(8,128)S(1)} %get-tuple-element.41, f32[2,1,8,8]{3,2,1,0:T(8,128)S(1)} %get-tuple-element.40), kind=kOutput, calls=%fused_computation.13 | convolution fusion | flops 25166080 | bytes 1180672 | tf_op jit(solution)/shard_map/erkp,bcpm->bcerkm/dot_general | solution.py:101
  64.7 2.1 %all-to-all-done.2 = bf16[8,2,4096]{2,1,0:T(2,128)(2,1)} async-done(((bf16[8,2,4096]{2,1,0:T(2,128)(2,1)}), bf16[8,2,4096]{2,1,0:T(2,128)(2,1)}, u32[]{:S(2)}, u32[]{:S(2)}) %all-to-all-start.2) | async-done | bytes 131104 | tf_op jit(solution)/shard_map/all_to_all | solution.py:85
  66.8 2.0 %reshape.389 = bf16[256,1,256]{2,1,0:T(2,128)(2,1)} reshape(bf16[8,2,4096]{2,1,0:T(2,128)(2,1)} %all-to-all-done.2) | data formatting | bytes 262144
  68.8 1.1 copy.72
  70.5 1.7 %multiply_subtract_fusion.5 = (f32[1,32,2,1,8,256]{5,4,3,2,1,0:T(8,128)S(1)}, f32[1,32,2,1,8,256]{5,4,3,2,1,0:T(8,128)S(1)}, f32[1,32,2,1,8,256]{5,4,3,2,1,0:T(8...) fusion(f32[1,32,2,2,8,256]{5,4,3,2,1,0:T(8,128)} %convolution_b, ...), kind=kLoop, calls=%fused_computation.79 | loop fusion | flops 2359296 | bytes 6324224 | tf_op jit(solution)/shard_map/sub | solution.py:77
  72.3 1.5 %convolution_bitcast_fusion.4 = f32[1,32,2,2,8,256]{5,1,4,2,3,0:T(8,128)S(1)} fusion(f32[32,2,2,8,256]{4,3,2,1,0:T(8,128)S(1)} %get-tuple-element.42, f32[1,256,2,256]{3,1,0,2:T(8,128)S(1)} %get-tuple-element.25, f32[1,256,2,256]{3,1,0,2:T(8,128)S(1)} %get-tuple-element.28), kind=kOutput, calls=%fused_computation.12 | convolution fusion | flops 805568512 | bytes 3145728 | tf_op jit(solution)/shard_map/bcerkm,rmsq->bceskq/dot_general | solution.py:103
  73.8 1.5 %convolution_bitcast_fusion.2 = f32[1,32,2,2,8,256]{5,1,4,2,3,0:T(8,128)S(1)} fusion(f32[32,2,2,8,256]{4,3,2,1,0:T(8,128)S(1)} %get-tuple-element.43, f32[1,256,2,256]{3,1,0,2:T(8,128)S(1)} %get-tuple-element.25, f32[1,256,2,256]{3,1,0,2:T(8,128)S(1)} %get-tuple-element.28), kind=kOutput, calls=%fused_computation.10 | convolution fusion | flops 805568512 | bytes 3145728 | tf_op jit(solution)/shard_map/bcerkm,rmsq->bceskq/dot_general | solution.py:103
  75.4 1.4 %convolution_bitcast_fusion = f32[1,32,2,2,8,256]{5,1,4,2,3,0:T(8,128)S(1)} fusion(f32[32,2,2,8,256]{4,3,2,1,0:T(8,128)S(1)} %maximum_bitcast_fusion.4, f32[1,256,2,256]{3,1,0,2:T(8,128)S(1)} %get-tuple-element.25, f32[1,256,2,256]{3,1,0,2:T(8,128)S(1)} %get-tuple-element.28), kind=kOutput, calls=%fused_computation.8 | convolution fusion | flops 805568512 | bytes 3145728 | tf_op jit(solution)/shard_map/bcerkm,rmsq->bceskq/dot_general | solution.py:103
  78.1 1.9 %fusion.5 = f32[2,32,2,2,8,256]{5,1,4,2,0,3:T(8,128)S(1)} fusion(f32[1,32,2,1,8,256]{5,1,4,2,3,0:T(8,128)S(1)} %get-tuple-element.20, f32[1,32,2,1,8,256]{5,1,4,2,3,0:T(8,128)S(1)} %get-tuple-element.21, f32[1,32,2,1,8,256]{5,1,4,2,3,0:T(8,128)S(1)} %get-tuple-element.9, f32[1,32,2,1,8,256]{5,1,4,2,3,0:T(8,128)S(1)} %get-tuple-element.8, ...), kind=kOutput, calls=%fused_computation.7 | convolution fusion | flops 1612447744 | bytes 5242880 | tf_op jit(solution)/shard_map/bceskq,sqrm->bcerkm/dot_general | solution.py:108
  80.7 2.4 %fusion.19 = bf16[2,32,8,256]{3,2,1,0:T(8,128)(2,1)S(1)} fusion(f32[2,32,2,2,8,256]{5,1,4,2,0,3:T(8,128)S(1)} %pad_maximum_fusion, f32[2,1,8,8]{3,2,1,0:T(8,128)S(1)} %get-tuple-element.41, f32[2,1,8,8]{3,2,1,0:T(8,128)S(1)} %get-tuple-element.40), kind=kOutput, calls=%fused_computation.29 | convolution fusion | flops 50463232 | bytes 2360320 | tf_op jit(solution)/shard_map/erkp,bcerkm->bcpm/dot_general | solution.py:110
  83.2 9.3 %all_to_all.54 = bf16[2,32,8,256]{3,1,0,2:T(8,128)(2,1)S(1)} all-to-all(bf16[2,32,8,256]{3,1,0,2:T(8,128)(2,1)S(1)} %copy.52), channel_id=1, replica_groups=mesh['seq'=8,'panel'=4] {'seq'}, dimensions={2} | all-to-all | bytes 524288 | tf_op jit(solution)/shard_map/all_to_all | solution.py:93
  93.3 1.2 copy.54
  96.1 1.3 %collective-permute-start.10 = (f32[3,2,256]{2,1,0:T(2,128)S(1)}, f32[3,2,256]{2,1,0:T(2,128)S(1)}, u32[]{:S(2)}, u32[]{:S(2)}) collective-permute-start(f32[3,2,256]{2,1,0:T(2,128)S(1)} %slice.142), channel_id=1, source_target_pairs={{4,0},{8,4},{12,8},{16,12},{20,16},{24,20},{28,24},{5,1},{9,5},{13... | collective-permute-start | bytes 18440 | tf_op jit(solution)/shard_map/ppermute | solution.py:17
  97.6 3.0 %collective-permute-start.9 = (bf16[256,256]{1,0:T(8,128)(2,1)S(1)}, bf16[256,256]{1,0:T(8,128)(2,1)S(1)}, u32[]{:S(2)}, u32[]{:S(2)}) collective-permute-start(bf16[256,256]{1,0:T(8,128)(2,1)S(1)} %convolution_convert_fusion), channel_id=1, source_target_pairs={{0,3},{1,0},{2,1},{3,2},{4,7},{5,4},{6,5},{7,6},{8,11},{9,8},{10,9... | collective-permute-start | bytes 393224 | tf_op jit(solution)/shard_map/ppermute | solution.py:36
  100.6 0.9 collective-permute-start.8
  102.5 3.9 %collective-permute-start.13 = (bf16[256,256]{1,0:T(8,128)(2,1)S(1)}, bf16[256,256]{1,0:T(8,128)(2,1)S(1)}, u32[]{:S(2)}, u32[]{:S(2)}) collective-permute-start(bf16[256,256]{1,0:T(8,128)(2,1)S(1)} %fusion.24), channel_id=1, source_target_pairs={{0,3},{1,0},{2,1},{3,2},{4,7},{5,4},{6,5},{7,6},{8,11},{9,8},{10,9... | collective-permute-start | bytes 393224 | tf_op jit(solution)/shard_map/ppermute | solution.py:36
  106.9 5.0 %collective-permute-start.11 = (bf16[256,256]{1,0:T(8,128)(2,1)S(1)}, bf16[256,256]{1,0:T(8,128)(2,1)S(1)}, u32[]{:S(2)}, u32[]{:S(2)}) collective-permute-start(bf16[256,256]{1,0:T(8,128)(2,1)S(1)} %fusion.22), channel_id=1, source_target_pairs={{0,1},{1,2},{2,3},{3,0},{4,5},{5,6},{6,7},{7,4},{8,9},{9,10},{10,1... | collective-permute-start | bytes 393224 | tf_op jit(solution)/shard_map/ppermute | solution.py:36
  111.8 7.9 %collective-permute-done.8 = bf16[256,256]{1,0:T(8,128)(2,1)S(1)} collective-permute-done((bf16[256,256]{1,0:T(8,128)(2,1)S(1)}, bf16[256,256]{1,0:T(8,128)(2,1)S(1)}, u32[]{:S(2)}, u32[]{:S(2)}) %collective-permute-start.8) | collective-permute-done | bytes 131104 | tf_op jit(solution)/shard_map/ppermute | solution.py:36
  120.6 4.7 %collective-permute-done.12 = bf16[256,256]{1,0:T(8,128)(2,1)S(1)} collective-permute-done((bf16[256,256]{1,0:T(8,128)(2,1)S(1)}, bf16[256,256]{1,0:T(8,128)(2,1)S(1)}, u32[]{:S(2)}, u32[]{:S(2)}) %collective-permute-start.12) | collective-permute-done | bytes 131104 | tf_op jit(solution)/shard_map/ppermute | solution.py:36
  125.3 1.0 fusion.60
  (93 shorter events, 14.0 us)
Async XLA Ops:
  0.6 20.4 %copy-start = (bf16[3,1024,256]{2,1,0:T(8,128)(2,1)S(1)}, bf16[3,1024,256]{2,1,0:T(8,128)(2,1)}, u32[]{:S(2)}) copy-start(bf16[3,1024,256]{2,1,0:T(8,128)(2,1)} %param.9) | copy-start | bytes 4718596
  0.6 21.6 %copy-start.9 = (bf16[256,256]{1,0:T(8,128)(2,1)S(1)}, bf16[256,256]{1,0:T(8,128)(2,1)}, u32[]{:S(2)}) copy-start(bf16[256,256]{1,0:T(8,128)(2,1)} %param.8) | copy-start | bytes 393220
  0.7 29.4 %collective-permute-start.2 = (bf16[256,256]{1,0:T(8,128)(2,1)}, bf16[256,256]{1,0:T(8,128)(2,1)}, u32[]{:S(2)}, u32[]{:S(2)}) collective-permute-start(bf16[256,256]{1,0:T(8,128)(2,1)} %param.7), channel_id=1, source_target_pairs={{0,3},{1,0},{2,1},{3,2},{4,7},{5,4},{6,5},{7,6},{8,11},{9,8},{10,9... | collective-permute-start | bytes 393224 | tf_op jit(solution)/shard_map/ppermute | solution.py:25
  5.8 21.6 %collective-permute-start = (bf16[256,256]{1,0:T(8,128)(2,1)}, bf16[256,256]{1,0:T(8,128)(2,1)}, u32[]{:S(2)}, u32[]{:S(2)}) collective-permute-start(bf16[256,256]{1,0:T(8,128)(2,1)} %param.7), channel_id=1, source_target_pairs={{0,1},{1,2},{2,3},{3,0},{4,5},{5,6},{6,7},{7,4},{8,9},{9,10},{10,1... | collective-permute-start | bytes 393224 | tf_op jit(solution)/shard_map/ppermute | solution.py:25
  5.8 25.6 %collective-permute-start.1 = (bf16[256,256]{1,0:T(8,128)(2,1)}, bf16[256,256]{1,0:T(8,128)(2,1)}, u32[]{:S(2)}, u32[]{:S(2)}) collective-permute-start(bf16[256,256]{1,0:T(8,128)(2,1)} %param.7), channel_id=1, source_target_pairs={{0,2},{1,3},{2,0},{3,1},{4,6},{5,7},{6,4},{7,5},{8,10},{9,11},{10,... | collective-permute-start | bytes 393224 | tf_op jit(solution)/shard_map/ppermute | solution.py:25
  6.8 28.9 %collective-permute-start.6 = (bf16[256,256]{1,0:T(8,128)(2,1)}, bf16[256,256]{1,0:T(8,128)(2,1)}, u32[]{:S(2)}, u32[]{:S(2)}) collective-permute-start(bf16[256,256]{1,0:T(8,128)(2,1)} %param.8), channel_id=1, source_target_pairs={{0,3},{1,0},{2,1},{3,2},{4,7},{5,4},{6,5},{7,6},{8,11},{9,8},{10,9... | collective-permute-start | bytes 393224 | tf_op jit(solution)/shard_map/ppermute | solution.py:25
  9.6 24.9 %collective-permute-start.4 = (bf16[256,256]{1,0:T(8,128)(2,1)}, bf16[256,256]{1,0:T(8,128)(2,1)}, u32[]{:S(2)}, u32[]{:S(2)}) collective-permute-start(bf16[256,256]{1,0:T(8,128)(2,1)} %param.8), channel_id=1, source_target_pairs={{0,1},{1,2},{2,3},{3,0},{4,5},{5,6},{6,7},{7,4},{8,9},{9,10},{10,1... | collective-permute-start | bytes 393224 | tf_op jit(solution)/shard_map/ppermute | solution.py:25
  12.0 35.5 %all-to-all-start.1 = ((f32[1,256,256]{2,0,1:T(1,128)}), f32[1,256,256]{2,0,1:T(1,128)}, u32[]{:S(2)}, u32[]{:S(2)}) async-start(f32[1,256,256]{2,0,1:T(1,128)} %bitcast.33), calls=%async_computation.1 | async-start | bytes 524288 | tf_op jit(solution)/shard_map/all_to_all | solution.py:85
  27.4 9.4 %collective-permute-start.5 = (bf16[256,256]{1,0:T(8,128)(2,1)S(1)}, bf16[256,256]{1,0:T(8,128)(2,1)S(1)}, u32[]{:S(2)}, u32[]{:S(2)}) collective-permute-start(bf16[256,256]{1,0:T(8,128)(2,1)S(1)} %copy-done.9), channel_id=1, source_target_pairs={{0,2},{1,3},{2,0},{3,1},{4,6},{5,7},{6,4},{7,5},{8,10},{9,11},{10,... | collective-permute-start | bytes 393224 | tf_op jit(solution)/shard_map/ppermute | solution.py:25
  30.1 4.5 %copy-start.3 = (bf16[256,1024]{1,0:T(8,128)(2,1)S(1)}, bf16[256,1024]{1,0:T(8,128)(2,1)}, u32[]{:S(2)}) copy-start(bf16[256,1024]{1,0:T(8,128)(2,1)} %param.13) | copy-start | bytes 1572868
  30.1 4.5 %copy-start.5 = (f32[256,256]{0,1:T(8,128)S(1)}, f32[256,256]{0,1:T(8,128)}, u32[]{:S(2)}) copy-start(f32[256,256]{0,1:T(8,128)} %fusion.99) | copy-start | bytes 786436
  32.5 5.4 %copy-start.12 = (f32[3,256]{1,0:T(4,128)S(1)}, f32[3,256]{1,0:T(4,128)}, u32[]{:S(2)}) copy-start(f32[3,256]{1,0:T(4,128)} %get-tuple-element.34) | copy-start | bytes 9220
  32.5 5.4 %copy-start.14 = (f32[3,256]{1,0:T(4,128)S(1)}, f32[3,256]{1,0:T(4,128)}, u32[]{:S(2)}) copy-start(f32[3,256]{1,0:T(4,128)} %get-tuple-element.35) | copy-start | bytes 9220
  32.6 5.4 %copy-start.16 = (f32[3,256]{1,0:T(4,128)S(1)}, f32[3,256]{1,0:T(4,128)}, u32[]{:S(2)}) copy-start(f32[3,256]{1,0:T(4,128)} %get-tuple-element.36) | copy-start | bytes 9220
  32.6 5.3 %collective-permute-start.3 = (bf16[3,2,256]{2,1,0:T(2,128)(2,1)S(1)}, bf16[3,2,256]{2,1,0:T(2,128)(2,1)S(1)}, u32[]{:S(2)}, u32[]{:S(2)}) collective-permute-start(bf16[3,2,256]{2,1,0:T(2,128)(2,1)S(1)} %slice.119), channel_id=1, source_target_pairs={{0,4},{4,8},{8,12},{12,16},{16,20},{20,24},{24,28},{1,5},{5,9},{9,... | collective-permute-start | bytes 9224 | tf_op jit(solution)/shard_map/ppermute | solution.py:17
  47.5 9.8 %all-to-all-start = ((bf16[8,2,4096]{2,1,0:T(2,128)(2,1)}), bf16[8,2,4096]{2,1,0:T(2,128)(2,1)S(1)}, u32[]{:S(2)}, u32[]{:S(2)}) async-start(bf16[8,2,4096]{2,1,0:T(2,128)(2,1)} %reshape.390), calls=%async_computation | async-start | bytes 262144 | tf_op jit(solution)/shard_map/all_to_all | solution.py:85
  57.3 9.5 %all-to-all-start.2 = ((bf16[8,2,4096]{2,1,0:T(2,128)(2,1)}), bf16[8,2,4096]{2,1,0:T(2,128)(2,1)}, u32[]{:S(2)}, u32[]{:S(2)}) async-start(bf16[8,2,4096]{2,1,0:T(2,128)(2,1)} %reshape.388), calls=%async_computation.2 | async-start | bytes 262144 | tf_op jit(solution)/shard_map/all_to_all | solution.py:85
  62.2 8.3 %copy-start.8 = (f32[2,8,256]{2,1,0:T(8,128)S(1)}, f32[2,8,256]{2,1,0:T(8,128)}, u32[]{:S(2)}) copy-start(f32[2,8,256]{2,1,0:T(8,128)} %get-tuple-element.39) | copy-start | bytes 49156
  62.2 8.3 %copy-start.11 = (f32[2,8,256]{2,1,0:T(8,128)S(1)}, f32[2,8,256]{2,1,0:T(8,128)}, u32[]{:S(2)}) copy-start(f32[2,8,256]{2,1,0:T(8,128)} %get-tuple-element.38) | copy-start | bytes 49156
  68.8 1.6 %copy-start.1 = (f32[1,32,2,2,8,256]{5,4,3,2,1,0:T(8,128)S(1)}, f32[1,32,2,2,8,256]{5,4,3,2,1,0:T(8,128)}, u32[]{:S(2)}) copy-start(f32[1,32,2,2,8,256]{5,4,3,2,1,0:T(8,128)} %convolution_bitcast_fusion.3) | copy-start | bytes 3145732
  76.9 1.0 copy-start.6
  76.9 1.2 copy-start.7
  78.1 1.9 %copy-start.10 = (f32[2,8,256]{2,1,0:T(8,128)S(1)}, f32[2,8,256]{2,1,0:T(8,128)}, u32[]{:S(2)}) copy-start(f32[2,8,256]{2,1,0:T(8,128)} %get-tuple-element.37) | copy-start | bytes 49156
  80.7 13.9 %copy-start.2 = (f32[256,256]{1,0:T(8,128)S(1)}, f32[256,256]{1,0:T(8,128)}, u32[]{:S(2)}) copy-start(f32[256,256]{1,0:T(8,128)} %fusion.18) | copy-start | bytes 786436
  80.7 13.9 %copy-start.18 = (f32[256]{0:T(256)S(1)}, f32[256]{0:T(256)}, u32[]{:S(2)}) copy-start(f32[256]{0:T(256)} %param.11) | copy-start | bytes 3076
  94.6 1.0 copy-start.4
  95.6 6.0 %copy-start.13 = (f32[3,256]{1,0:T(4,128)S(1)}, f32[3,256]{1,0:T(4,128)}, u32[]{:S(2)}) copy-start(f32[3,256]{1,0:T(4,128)} %get-tuple-element.34) | copy-start | bytes 9220
  95.6 6.0 %copy-start.15 = (f32[3,256]{1,0:T(4,128)S(1)}, f32[3,256]{1,0:T(4,128)}, u32[]{:S(2)}) copy-start(f32[3,256]{1,0:T(4,128)} %get-tuple-element.35) | copy-start | bytes 9220
  95.6 6.0 %copy-start.17 = (f32[3,256]{1,0:T(4,128)S(1)}, f32[3,256]{1,0:T(4,128)}, u32[]{:S(2)}) copy-start(f32[3,256]{1,0:T(4,128)} %get-tuple-element.36) | copy-start | bytes 9220
  96.1 5.4 %collective-permute-start.10 = (f32[3,2,256]{2,1,0:T(2,128)S(1)}, f32[3,2,256]{2,1,0:T(2,128)S(1)}, u32[]{:S(2)}, u32[]{:S(2)}) collective-permute-start(f32[3,2,256]{2,1,0:T(2,128)S(1)} %slice.142), channel_id=1, source_target_pairs={{4,0},{8,4},{12,8},{16,12},{20,16},{24,20},{28,24},{5,1},{9,5},{13... | collective-permute-start | bytes 18440 | tf_op jit(solution)/shard_map/ppermute | solution.py:17
  97.6 9.3 %collective-permute-start.9 = (bf16[256,256]{1,0:T(8,128)(2,1)S(1)}, bf16[256,256]{1,0:T(8,128)(2,1)S(1)}, u32[]{:S(2)}, u32[]{:S(2)}) collective-permute-start(bf16[256,256]{1,0:T(8,128)(2,1)S(1)} %convolution_convert_fusion), channel_id=1, source_target_pairs={{0,3},{1,0},{2,1},{3,2},{4,7},{5,4},{6,5},{7,6},{8,11},{9,8},{10,9... | collective-permute-start | bytes 393224 | tf_op jit(solution)/shard_map/ppermute | solution.py:36
  100.6 19.2 %collective-permute-start.8 = (bf16[256,256]{1,0:T(8,128)(2,1)S(1)}, bf16[256,256]{1,0:T(8,128)(2,1)S(1)}, u32[]{:S(2)}, u32[]{:S(2)}) collective-permute-start(bf16[256,256]{1,0:T(8,128)(2,1)S(1)} %convolution_convert_fusion.1), channel_id=1, source_target_pairs={{0,2},{1,3},{2,0},{3,1},{4,6},{5,7},{6,4},{7,5},{8,10},{9,11},{10,... | collective-permute-start | bytes 393224 | tf_op jit(solution)/shard_map/ppermute | solution.py:36
  101.5 18.2 %collective-permute-start.7 = (bf16[256,256]{1,0:T(8,128)(2,1)S(1)}, bf16[256,256]{1,0:T(8,128)(2,1)S(1)}, u32[]{:S(2)}, u32[]{:S(2)}) collective-permute-start(bf16[256,256]{1,0:T(8,128)(2,1)S(1)} %convolution_convert_fusion.2), channel_id=1, source_target_pairs={{0,1},{1,2},{2,3},{3,0},{4,5},{5,6},{6,7},{7,4},{8,9},{9,10},{10,1... | collective-permute-start | bytes 393224 | tf_op jit(solution)/shard_map/ppermute | solution.py:36
  102.5 18.1 %collective-permute-start.13 = (bf16[256,256]{1,0:T(8,128)(2,1)S(1)}, bf16[256,256]{1,0:T(8,128)(2,1)S(1)}, u32[]{:S(2)}, u32[]{:S(2)}) collective-permute-start(bf16[256,256]{1,0:T(8,128)(2,1)S(1)} %fusion.24), channel_id=1, source_target_pairs={{0,3},{1,0},{2,1},{3,2},{4,7},{5,4},{6,5},{7,6},{8,11},{9,8},{10,9... | collective-permute-start | bytes 393224 | tf_op jit(solution)/shard_map/ppermute | solution.py:36
  106.4 19.0 %collective-permute-start.12 = (bf16[256,256]{1,0:T(8,128)(2,1)S(1)}, bf16[256,256]{1,0:T(8,128)(2,1)S(1)}, u32[]{:S(2)}, u32[]{:S(2)}) collective-permute-start(bf16[256,256]{1,0:T(8,128)(2,1)S(1)} %fusion.23), channel_id=1, source_target_pairs={{0,2},{1,3},{2,0},{3,1},{4,6},{5,7},{6,4},{7,5},{8,10},{9,11},{10,... | collective-permute-start | bytes 393224 | tf_op jit(solution)/shard_map/ppermute | solution.py:36
  106.9 18.4 %collective-permute-start.11 = (bf16[256,256]{1,0:T(8,128)(2,1)S(1)}, bf16[256,256]{1,0:T(8,128)(2,1)S(1)}, u32[]{:S(2)}, u32[]{:S(2)}) collective-permute-start(bf16[256,256]{1,0:T(8,128)(2,1)S(1)} %fusion.22), channel_id=1, source_target_pairs={{0,1},{1,2},{2,3},{3,0},{4,5},{5,6},{6,7},{7,4},{8,9},{9,10},{10,1... | collective-permute-start | bytes 393224 | tf_op jit(solution)/shard_map/ppermute | solution.py:36

commit v10 on v6

--- a/solution.py
+++ b/solution.py
@@ -36,7 +36,24 @@
         total = total + lax.ppermute(
             sent, "panel", [(i, (i + k) % count) for i in range(count)]
         ).astype(jnp.float32)
-    return total.astype(jnp.bfloat16)
+    return total
+
+
+def halo_to_previous(halo):
+    seq_count, count = lax.axis_size("seq"), lax.axis_size("panel")
+    me = lax.axis_index("panel")
+    rows, cols = halo.shape
+    width = cols // count
+    total = 0.0
+    for k in range(count):
+        sent = lax.dynamic_slice_in_dim(halo, ((me + k) % count) * width, width, axis=1)
+        pairs = [
+            (s * count + p, (s - 1) * count + (p + k) % count)
+            for s in range(1, seq_count)
+            for p in range(count)
+        ]
+        total = total + lax.ppermute(sent, ("seq", "panel"), pairs)
+    return total
 
 
 def phase(numer, period):
@@ -173,18 +190,35 @@
             lax.dynamic_slice_in_dim(out_weight, dest * width, width, axis=1),
             preferred_element_type=jnp.float32,
         )
-    )
+    ).astype(jnp.bfloat16)
     grad_gate_out = grad_gated * conv_state
     grad_value = grad_signal * gate_in
     grad_gate_in = grad_signal * value_path
     upstream = jnp.stack([grad_gate_out, grad_gate_in, grad_value])
-    after_rim = shifted(upstream[:, : tap_count - 1, :], "seq", -1)
-    widened = jnp.concatenate([upstream, after_rim], axis=1)
-    grad_projected = short_kernel[0][:, None, :] * widened[:, :row_count, :]
+    rim = tap_count - 1
+    halo_proj = jnp.stack(
+        [
+            sum(
+                short_kernel[tap_index][:, None, :]
+                * upstream[:, tap_index - rim + rim_row : tap_index - rim + rim_row + 1, :]
+                for tap_index in range(rim - rim_row, tap_count)
+            )[:, 0, :]
+            for rim_row in range(rim)
+        ],
+        axis=1,
+    )
+    halo_grad = jnp.einsum(
+        "jrc,jdc->rd",
+        halo_proj,
+        in_weight.astype(jnp.float32),
+        precision=HIGHEST,
+        preferred_element_type=jnp.float32,
+    )
+    halo_in = halo_to_previous(halo_grad)
+    grad_projected = short_kernel[0][:, None, :] * upstream
     for tap_index in range(1, tap_count):
-        grad_projected = (
-            grad_projected
-            + short_kernel[tap_index][:, None, :] * widened[:, tap_index : tap_index + row_count, :]
+        grad_projected = grad_projected + short_kernel[tap_index][:, None, :] * jnp.pad(
+            upstream[:, tap_index:, :], ((0, 0), (0, tap_index), (0, 0))
         )
     grad_projected = grad_projected.astype(jnp.bfloat16)
     token_grad = panel_reduce_scatter(
@@ -195,6 +229,9 @@
             preferred_element_type=jnp.float32,
         )
     )
+    token_grad = jnp.concatenate(
+        [token_grad[: row_count - rim], token_grad[row_count - rim :] + halo_in]
+    ).astype(jnp.bfloat16)
     return (block_out, token_grad)
 
 

time: 103 us -> 112 us (1.087)
  the two profiles are of different devices: /device:TPU:0 before, /device:TPU:13 now
where the time goes in v10:
time: 112 us; the launch traced here: 111 us
  starting transfers between devices  47.7 us (43%)
  matrix products  22.1 us (20%)
  waiting for transfers between devices  16.5 us (15%)
  other arithmetic  13.6 us (12%)
  local copies, waits for them, and re-layouts  9.56 us (9%)
  between operations  1.29 us (1%)
    ppermute x4, starting transfers between devices, halo_to_previous(): total = total + lax.ppermute(sent, ('seq', 'panel'), pairs)  16.3 us
    all_to_all x2, starting transfers between devices, to_columns(): lax.all_to_all(jnp.swapaxes(rows, 1, 2).astype(wire), 'seq', split_axis=1...  10.1 us
    ppermute x6, waiting for transfers between devices, panel_reduce_scatter(): lax.ppermute(sent, 'panel', [(i, (i + k) % count) for i in range(count)])  9.73 us
    ppermute x6, starting transfers between devices, panel_reduce_scatter(): lax.ppermute(sent, 'panel', [(i, (i + k) % count) for i in range(count)])  6.61 us
    ppermute x6, starting transfers between devices, panel_parts(): lax.ppermute(value, 'panel', [(i, (i + k) % count) for i in range(count)])  5.82 us
    all_to_all x1, starting transfers between devices, to_rows(): lax.all_to_all(columns.astype(wire), 'seq', split_axis=2, concat_axis=1,...  5.29 us
    dot_general x4, matrix products, local(): jnp.einsum('td,jdc->jtc', part, lax.dynamic_slice_in_dim(in_weight, sourc...  4.7 us
    all_to_all x1, waiting for transfers between devices, to_rows(): lax.all_to_all(columns.astype(wire), 'seq', split_axis=2, concat_axis=1,...  4.59 us
  transfers between devices with their start and end apart: 20, of which 6 were waited for; matrix products, arithmetic and copies ran while one was open for 24% of the time, Pallas kernels for 0%

profile of v10, /device:TPU:13, one launch (start us, length us, event | category | flops | bytes accessed | tf_op | source)
XLA Modules:
  0.0 110.8 jit_solution(11495891932524446402)
XLA Ops:
  0.7 1.3 %collective-permute-start = (bf16[256,256]{1,0:T(8,128)(2,1)}, bf16[256,256]{1,0:T(8,128)(2,1)}, u32[]{:S(2)}, u32[]{:S(2)}) collective-permute-start(bf16[256,256]{1,0:T(8,128)(2,1)} %param.7), channel_id=1, source_target_pairs={{0,1},{1,2},{2,3},{3,0},{4,5},{5,6},{6,7},{7,4},{8,9},{9,10},{10,1... | collective-permute-start | bytes 393224 | tf_op jit(solution)/shard_map/ppermute | solution.py:25
  2.2 2.3 %collective-permute-start.1 = (bf16[256,256]{1,0:T(8,128)(2,1)}, bf16[256,256]{1,0:T(8,128)(2,1)}, u32[]{:S(2)}, u32[]{:S(2)}) collective-permute-start(bf16[256,256]{1,0:T(8,128)(2,1)} %param.7), channel_id=1, source_target_pairs={{0,2},{1,3},{2,0},{3,1},{4,6},{5,7},{6,4},{7,5},{8,10},{9,11},{10,... | collective-permute-start | bytes 393224 | tf_op jit(solution)/shard_map/ppermute | solution.py:25
  4.5 1.0 collective-permute-start.4
  6.0 1.8 %copy.69 = f32[1,256,256]{1,0,2:T(1,128)} copy(f32[1,256,256]{2,1,0:T(8,128)} %bitcast.232) | data formatting | bytes 524288 | tf_op jit(solution)/shard_map/broadcast_in_dim | solution.py:135
  7.8 5.9 %all-to-all-start.1 = ((f32[1,256,256]{2,0,1:T(1,128)}), f32[1,256,256]{2,0,1:T(1,128)S(1)}, u32[]{:S(2)}, u32[]{:S(2)}) async-start(f32[1,256,256]{2,0,1:T(1,128)} %bitcast.34), calls=%async_computation.1 | async-start | bytes 524288 | tf_op jit(solution)/shard_map/all_to_all | solution.py:102
  15.5 1.8 %fusion.76 = (f32[256,1,256]{2,0,1:T(8,128)}, f32[256,1,256]{2,0,1:T(8,128)}) fusion(), kind=kLoop, calls=%fused_computation.125 | loop fusion | flops 983040 | bytes 524288 | tf_op jit(solution)/shard_map/sin | solution.py:79
  17.3 1.7 %fusion.78 = f32[256,1,256]{2,0,1:T(8,128)} fusion(), kind=kLoop, calls=%fused_computation.127 | loop fusion | flops 1048576 | bytes 262144 | tf_op jit(solution)/shard_map/neg | solution.py:84
  19.0 1.3 %fusion.142 = (f32[1,3,256]{2,1,0:T(4,128)}, f32[3,256]{1,0:T(4,128)S(1)}, f32[3,256]{1,0:T(4,128)S(1)}, f32[1,3,256]{2,1,0:T(4,128)}, f32[3,256]{1,0:T(4,128)S(1)}) fusion(f32[3,3,256]{2,1,0:T(4,128)} %param.10), kind=kLoop, calls=%fused_computation.215 | loop fusion | bytes 24576 | tf_op jit(solution)/shard_map/slice | solution.py:161
  20.3 1.2 %fusion.53 = f32[3,256,256]{1,2,0:T(8,128)S(1)} fusion(bf16[3,1024,256]{2,1,0:T(8,128)(2,1)S(1)} %copy-done, s32[]{:T(128)S(6)} %select_n.164, bf16[256,256]{1,0:T(8,128)(2,1)} %param.7), kind=kOutput, calls=%fused_computation.86 | convolution fusion | flops 100663296 | bytes 1310724 | tf_op jit(solution)/shard_map/td,jdc->jtc/dot_general | solution.py:139
  22.5 0.8 fusion.131
  23.3 2.8 %fusion.43 = (f32[1,256,2,256]{3,1,2,0:T(8,128)}, f32[1,256,2,256]{3,1,0,2:T(8,128)}, f32[1,256,2,256]{3,1,0,2:T(8,128)}, f32[1,256,2,256]{3,1,2,0:T(8,128)}) fusion(f32[256,1,256]{2,0,1:T(8,128)} %get-tuple-element.43, f32[256,1,256]{2,0,1:T(8,128)} %fusion.78, f32[256,1,256]{2,0,1:T(8,128)} %get-tuple-element.42), kind=kLoop, calls=%fused_computation.66 | loop fusion | flops 524288 | bytes 2883584 | tf_op jit(solution)/shard_map/stack | solution.py:83
  26.5 1.2 %convolution_add_fusion.1 = f32[3,256,256]{1,2,0:T(8,128)S(1)} fusion(f32[3,256,256]{1,2,0:T(8,128)S(1)} %fusion.53, bf16[3,1024,256]{2,1,0:T(8,128)(2,1)S(1)} %copy-done, s32[]{:T(128)S(6)} %select_n.166, bf16[256,256]{1,0:T(8,128)(2,1)} %collective-permute-done), kind=kOutput, calls=%fused_computation.19 | convolution fusion | flops 100859904 | bytes 2097156 | tf_op jit(solution)/shard_map/td,jdc->jtc/dot_general | solution.py:139
  27.7 1.2 %fusion.46 = f32[3,256,256]{1,2,0:T(8,128)S(1)} fusion(bf16[3,1024,256]{2,1,0:T(8,128)(2,1)S(1)} %copy-done, s32[]{:T(128)S(6)} %select_n.170, bf16[256,256]{1,0:T(8,128)(2,1)} %collective-permute-done.2), kind=kOutput, calls=%fused_computation.79 | convolution fusion | flops 100663296 | bytes 1310724 | tf_op jit(solution)/shard_map/td,jdc->jtc/dot_general | solution.py:139
  28.9 1.2 %fusion.21 = bf16[3,256,256]{2,1,0:T(8,128)(2,1)S(1)} fusion(f32[3,256,256]{1,2,0:T(8,128)S(1)} %fusion.46, f32[3,256,256]{1,2,0:T(8,128)S(1)} %convolution_add_fusion.1, bf16[3,1024,256]{2,1,0:T(8,128)(2,1)S(1)} %copy-done, s32[]{:T(128)S(6)} %select_n.168, bf16[256,256]{1,0:T(8,128)(2,1)} %collective-permute-done.1), kind=kOutput, calls=%fused_computation.22 | convolution fusion | flops 101253120 | bytes 2490372 | tf_op jit(solution)/shard_map/td,jdc->jtc/dot_general | solution.py:139
  30.1 3.7 %collective-permute-start.3 = (bf16[3,2,256]{2,1,0:T(2,128)(2,1)S(1)}, bf16[3,2,256]{2,1,0:T(2,128)(2,1)S(1)}, u32[]{:S(2)}, u32[]{:S(2)}) collective-permute-start(bf16[3,2,256]{2,1,0:T(2,128)(2,1)S(1)} %slice.128), channel_id=1, source_target_pairs={{0,4},{4,8},{8,12},{12,16},{16,20},{20,24},{24,28},{1,5},{5,9},{9,... | collective-permute-start | bytes 9224 | tf_op jit(solution)/shard_map/ppermute | solution.py:17
  33.8 1.1 %convolution_add_fusion.3 = f32[256,256]{0,1:T(8,128)S(1)} fusion(f32[256,256]{0,1:T(8,128)S(1)} %fusion.88, bf16[256,256]{1,0:T(8,128)(2,1)} %collective-permute-done.4, bf16[256,1024]{1,0:T(8,128)(2,1)S(1)} %copy-done.3, s32[]{:T(128)S(6)} %select_n.166), kind=kOutput, calls=%fused_computation.31 | convolution fusion | flops 33619968 | bytes 786436 | tf_op jit(solution)/shard_map/dot_general | solution.py:147
  35.0 1.1 %fusion.80 = f32[256,256]{0,1:T(8,128)S(1)} fusion(bf16[256,256]{1,0:T(8,128)(2,1)} %collective-permute-done.6, bf16[256,1024]{1,0:T(8,128)(2,1)S(1)} %copy-done.3, s32[]{:T(128)S(6)} %select_n.170), kind=kOutput, calls=%fused_computation.129 | convolution fusion | flops 33554432 | bytes 524292 | tf_op jit(solution)/shard_map/dot_general | solution.py:147
  37.2 0.9 copy.38
  38.1 4.2 %all-to-all-start = ((bf16[2,256,256]{2,0,1:T(2,128)(2,1)}), bf16[2,256,256]{2,0,1:T(2,128)(2,1)}, u32[]{:S(2)}, u32[]{:S(2)}) async-start(bf16[2,256,256]{2,0,1:T(2,128)(2,1)} %copy.38), calls=%async_computation | async-start | bytes 524288 | tf_op jit(solution)/shard_map/all_to_all | solution.py:102
  42.3 1.0 convolution_bitcast_fusion.2
  43.5 0.8 copy-done.5
  44.4 1.1 %convolution_bitcast_fusion.1 = f32[1,32,2,2,8,256]{5,1,4,2,0,3:T(8,128)S(1)} fusion(f32[32,2,2,8,256]{4,3,0,2,1:T(8,128)S(1)} %maximum_bitcast_fusion.3, f32[1,256,2,256]{3,1,0,2:T(8,128)S(1)} %copy-done.5, f32[1,256,2,256]{3,1,0,2:T(8,128)S(1)} %copy-done.7), kind=kOutput, calls=%fused_computation.15 | convolution fusion | flops 805568512 | bytes 3145728 | tf_op jit(solution)/shard_map/bcerkm,rmsq->bceskq/dot_general | solution.py:120
  45.6 0.7 all-to-all-done
  46.3 2.0 %convolution_bitcast_fusion = f32[2,32,2,2,8,256]{5,4,3,2,1,0:T(8,128)S(1)} fusion(bf16[2,8,32,256]{3,0,2,1:T(2,128)(2,1)} %bitcast.18, f32[2,1,8,8]{3,2,1,0:T(8,128)S(1)} %get-tuple-element.41, f32[2,1,8,8]{3,2,1,0:T(8,128)S(1)} %get-tuple-element.40), kind=kOutput, calls=%fused_computation.14 | convolution fusion | flops 50331904 | bytes 2360320 | tf_op jit(solution)/shard_map/erkp,bcpm->bcerkm/dot_general | solution.py:118
  48.8 0.8 copy-done.6
  49.8 2.7 %fusion.10 = f32[2,32,2,2,8,256]{5,1,4,2,0,3:T(8,128)S(1)} fusion(f32[2,32,2,2,8,256]{5,4,3,2,1,0:T(8,128)S(1)} %pad_maximum_fusion, f32[1,256,2,256]{3,1,0,2:T(8,128)S(1)} %copy-done.6, f32[1,256,2,256]{3,1,0,2:T(8,128)S(1)} %copy-done.8), kind=kOutput, calls=%fused_computation.12 | convolution fusion | flops 1610874880 | bytes 5242880 | tf_op jit(solution)/shard_map/bcerkm,rmsq->bceskq/dot_general | solution.py:120
  53.1 0.9 copy-done.9
  54.2 2.7 %fusion.13 = f32[2,32,2,2,8,256]{5,4,3,2,1,0:T(8,128)S(1)} fusion(f32[2,32,2,2,8,256,1]{5,1,4,2,0,3,6:T(8,128)S(1)} %maximum_bitcast_fusion, f32[1,256,2,256]{3,1,2,0:T(8,128)S(1)} %copy-done.10, f32[1,256,2,256]{3,1,2,0:T(8,128)S(1)} %copy-done.9), kind=kOutput, calls=%fused_computation.13 | convolution fusion | flops 1610874880 | bytes 5242880 | tf_op jit(solution)/shard_map/bceskq,sqrm->bcerkm/dot_general | solution.py:125
  57.3 1.2 %fusion.27 = bf16[2,32,8,256]{3,2,1,0:T(8,128)(2,1)S(1)} fusion(f32[2,32,2,1,8,256]{5,4,3,2,1,0:T(8,128)S(1)} %get-tuple-element.11, f32[2,32,2,1,8,256]{5,4,3,2,1,0:T(8,128)S(1)} %get-tuple-element.10, f32[2,1,8,8]{3,2,1,0:T(8,128)S(1)} %get-tuple-element.41, f32[2,1,8,8]{3,2,1,0:T(8,128)S(1)} %get-tuple-element.40), kind=kOutput, calls=%fused_computation.32 | convolution fusion | flops 50987520 | bytes 2360320 | tf_op jit(solution)/shard_map/erkp,bcerkm->bcpm/dot_general | solution.py:127
  58.5 0.8 copy.49
  59.3 5.3 %all-to-all-start.2 = ((bf16[2,32,8,256]{3,1,0,2:T(8,128)(2,1)}), bf16[2,32,8,256]{3,1,0,2:T(8,128)(2,1)S(1)}, u32[]{:S(2)}, u32[]{:S(2)}) async-start(bf16[2,32,8,256]{3,1,0,2:T(8,128)(2,1)} %copy.49), calls=%async_computation.2 | async-start | bytes 524288 | tf_op jit(solution)/shard_map/all_to_all | solution.py:110
  64.6 4.6 %all-to-all-done.2 = bf16[2,32,8,256]{3,1,0,2:T(8,128)(2,1)S(1)} async-done(((bf16[2,32,8,256]{3,1,0,2:T(8,128)(2,1)}), bf16[2,32,8,256]{3,1,0,2:T(8,128)(2,1)S(1)}, u32[]{:S(2)}, u32[]{:S(2)}) %all-to-all-start.2) | async-done | bytes 262176 | tf_op jit(solution)/shard_map/all_to_all | solution.py:110
  69.1 0.8 bitcast_convert_fusion
  70.0 1.2 %copy.51 = f32[2,256,256]{1,2,0:T(8,128)S(1)} copy(f32[2,256,256]{2,1,0:T(8,128)} %bitcast.230) | data formatting | bytes 1048576 | tf_op jit(solution)/shard_map/transpose | solution.py:113
  73.3 1.9 %collective-permute-start.11 = (bf16[256,256]{1,0:T(8,128)(2,1)S(1)}, bf16[256,256]{1,0:T(8,128)(2,1)S(1)}, u32[]{:S(2)}, u32[]{:S(2)}) collective-permute-start(bf16[256,256]{1,0:T(8,128)(2,1)S(1)} %fusion.31), channel_id=1, source_target_pairs={{0,2},{1,3},{2,0},{3,1},{4,6},{5,7},{6,4},{7,5},{8,10},{9,11},{10,... | collective-permute-start | bytes 393224 | tf_op jit(solution)/shard_map/ppermute | solution.py:36
  75.2 1.0 collective-permute-start.10
  76.2 1.0 collective-permute-start.12
  77.2 1.3 %convolution_bitcast_fusion.7 = f32[2,1024]{1,0:T(2,128)S(1)} fusion(bf16[3,1024,256]{2,1,0:T(8,128)(2,1)S(1)} %copy-done, f32[3,1,256]{2,1,0:T(1,128)S(1)} %get-tuple-element.19, f32[3,1,256]{2,1,0:T(1,128)S(1)} %get-tuple-element.18), kind=kOutput, calls=%fused_computation.39 | convolution fusion | flops 18875904 | bytes 1587200 | tf_op jit(solution)/shard_map/jrc,jdc->rd/dot_general | solution.py:210
  78.5 3.7 %collective-permute-start.13 = (f32[2,256]{1,0:T(2,128)S(1)}, f32[2,256]{1,0:T(2,128)S(1)}, u32[]{:S(2)}, u32[]{:S(2)}) collective-permute-start(f32[2,256]{1,0:T(2,128)S(1)} %get-tuple-element.39), channel_id=1, source_target_pairs={{4,0},{5,1},{6,2},{7,3},{8,4},{9,5},{10,6},{11,7},{12,8},{13,9},{1... | collective-permute-start | bytes 6152 | tf_op jit(solution)/shard_map/ppermute | solution.py:55
  82.2 2.7 %collective-permute-start.14 = (f32[2,256]{1,0:T(2,128)S(1)}, f32[2,256]{1,0:T(2,128)S(1)}, u32[]{:S(2)}, u32[]{:S(2)}) collective-permute-start(f32[2,256]{1,0:T(2,128)S(1)} %get-tuple-element.36), channel_id=1, source_target_pairs={{4,1},{5,2},{6,3},{7,0},{8,5},{9,6},{10,7},{11,4},{12,9},{13,10},{... | collective-permute-start | bytes 6152 | tf_op jit(solution)/shard_map/ppermute | solution.py:55
  85.1 7.9 %collective-permute-start.15 = (f32[2,256]{1,0:T(2,128)S(1)}, f32[2,256]{1,0:T(2,128)S(1)}, u32[]{:S(2)}, u32[]{:S(2)}) collective-permute-start(f32[2,256]{1,0:T(2,128)S(1)} %get-tuple-element.38), channel_id=1, source_target_pairs={{4,2},{5,3},{6,0},{7,1},{8,6},{9,7},{10,4},{11,5},{12,10},{13,11},... | collective-permute-start | bytes 6152 | tf_op jit(solution)/shard_map/ppermute | solution.py:55
  93.1 1.9 %collective-permute-start.16 = (f32[2,256]{1,0:T(2,128)S(1)}, f32[2,256]{1,0:T(2,128)S(1)}, u32[]{:S(2)}, u32[]{:S(2)}) collective-permute-start(f32[2,256]{1,0:T(2,128)S(1)} %get-tuple-element.37), channel_id=1, source_target_pairs={{4,3},{5,0},{6,1},{7,2},{8,7},{9,4},{10,5},{11,6},{12,11},{13,8},{... | collective-permute-start | bytes 6152 | tf_op jit(solution)/shard_map/ppermute | solution.py:55
  95.7 2.1 %collective-permute-start.7 = (bf16[256,256]{1,0:T(8,128)(2,1)S(1)}, bf16[256,256]{1,0:T(8,128)(2,1)S(1)}, u32[]{:S(2)}, u32[]{:S(2)}) collective-permute-start(bf16[256,256]{1,0:T(8,128)(2,1)S(1)} %convolution_convert_fusion.2), channel_id=1, source_target_pairs={{0,1},{1,2},{2,3},{3,0},{4,5},{5,6},{6,7},{7,4},{8,9},{9,10},{10,1... | collective-permute-start | bytes 393224 | tf_op jit(solution)/shard_map/ppermute | solution.py:36
  98.1 1.4 %collective-permute-done.16 = f32[2,256]{1,0:T(2,128)S(1)} collective-permute-done((f32[2,256]{1,0:T(2,128)S(1)}, f32[2,256]{1,0:T(2,128)S(1)}, u32[]{:S(2)}, u32[]{:S(2)}) %collective-permute-start.16) | collective-permute-done | bytes 2080 | tf_op jit(solution)/shard_map/ppermute | solution.py:55
  100.2 0.9 collective-permute-done.8
  101.1 5.5 %collective-permute-done.7 = bf16[256,256]{1,0:T(8,128)(2,1)S(1)} collective-permute-done((bf16[256,256]{1,0:T(8,128)(2,1)S(1)}, bf16[256,256]{1,0:T(8,128)(2,1)S(1)}, u32[]{:S(2)}, u32[]{:S(2)}) %collective-permute-start.7) | collective-permute-done | bytes 131104 | tf_op jit(solution)/shard_map/ppermute | solution.py:36
  106.5 3.4 %collective-permute-done.9 = bf16[256,256]{1,0:T(8,128)(2,1)S(1)} collective-permute-done((bf16[256,256]{1,0:T(8,128)(2,1)S(1)}, bf16[256,256]{1,0:T(8,128)(2,1)S(1)}, u32[]{:S(2)}, u32[]{:S(2)}) %collective-permute-start.9) | collective-permute-done | bytes 131104 | tf_op jit(solution)/shard_map/ppermute | solution.py:36
  109.9 0.9 add_convert_fusion.1
  (86 shorter events, 10.9 us)
Async XLA Ops:
  0.6 19.7 %copy-start = (bf16[3,1024,256]{2,1,0:T(8,128)(2,1)S(1)}, bf16[3,1024,256]{2,1,0:T(8,128)(2,1)}, u32[]{:S(2)}) copy-start(bf16[3,1024,256]{2,1,0:T(8,128)(2,1)} %param.9) | copy-start | bytes 4718596
  0.6 20.9 %copy-start.11 = (bf16[256,256]{1,0:T(8,128)(2,1)S(1)}, bf16[256,256]{1,0:T(8,128)(2,1)}, u32[]{:S(2)}) copy-start(bf16[256,256]{1,0:T(8,128)(2,1)} %param.8) | copy-start | bytes 393220
  0.7 20.9 %copy-start.3 = (bf16[256,1024]{1,0:T(8,128)(2,1)S(1)}, bf16[256,1024]{1,0:T(8,128)(2,1)}, u32[]{:S(2)}) copy-start(bf16[256,1024]{1,0:T(8,128)(2,1)} %param.13) | copy-start | bytes 1572868
  0.7 25.4 %collective-permute-start = (bf16[256,256]{1,0:T(8,128)(2,1)}, bf16[256,256]{1,0:T(8,128)(2,1)}, u32[]{:S(2)}, u32[]{:S(2)}) collective-permute-start(bf16[256,256]{1,0:T(8,128)(2,1)} %param.7), channel_id=1, source_target_pairs={{0,1},{1,2},{2,3},{3,0},{4,5},{5,6},{6,7},{7,4},{8,9},{9,10},{10,1... | collective-permute-start | bytes 393224 | tf_op jit(solution)/shard_map/ppermute | solution.py:25
  2.0 25.7 %collective-permute-start.2 = (bf16[256,256]{1,0:T(8,128)(2,1)}, bf16[256,256]{1,0:T(8,128)(2,1)}, u32[]{:S(2)}, u32[]{:S(2)}) collective-permute-start(bf16[256,256]{1,0:T(8,128)(2,1)} %param.7), channel_id=1, source_target_pairs={{0,3},{1,0},{2,1},{3,2},{4,7},{5,4},{6,5},{7,6},{8,11},{9,8},{10,9... | collective-permute-start | bytes 393224 | tf_op jit(solution)/shard_map/ppermute | solution.py:25
  2.2 26.7 %collective-permute-start.1 = (bf16[256,256]{1,0:T(8,128)(2,1)}, bf16[256,256]{1,0:T(8,128)(2,1)}, u32[]{:S(2)}, u32[]{:S(2)}) collective-permute-start(bf16[256,256]{1,0:T(8,128)(2,1)} %param.7), channel_id=1, source_target_pairs={{0,2},{1,3},{2,0},{3,1},{4,6},{5,7},{6,4},{7,5},{8,10},{9,11},{10,... | collective-permute-start | bytes 393224 | tf_op jit(solution)/shard_map/ppermute | solution.py:25
  4.5 29.3 %collective-permute-start.4 = (bf16[256,256]{1,0:T(8,128)(2,1)}, bf16[256,256]{1,0:T(8,128)(2,1)}, u32[]{:S(2)}, u32[]{:S(2)}) collective-permute-start(bf16[256,256]{1,0:T(8,128)(2,1)} %param.8), channel_id=1, source_target_pairs={{0,1},{1,2},{2,3},{3,0},{4,5},{5,6},{6,7},{7,4},{8,9},{9,10},{10,1... | collective-permute-start | bytes 393224 | tf_op jit(solution)/shard_map/ppermute | solution.py:25
  5.5 29.5 %collective-permute-start.6 = (bf16[256,256]{1,0:T(8,128)(2,1)}, bf16[256,256]{1,0:T(8,128)(2,1)}, u32[]{:S(2)}, u32[]{:S(2)}) collective-permute-start(bf16[256,256]{1,0:T(8,128)(2,1)} %param.8), channel_id=1, source_target_pairs={{0,3},{1,0},{2,1},{3,2},{4,7},{5,4},{6,5},{7,6},{8,11},{9,8},{10,9... | collective-permute-start | bytes 393224 | tf_op jit(solution)/shard_map/ppermute | solution.py:25
  7.8 30.3 %all-to-all-start.1 = ((f32[1,256,256]{2,0,1:T(1,128)}), f32[1,256,256]{2,0,1:T(1,128)S(1)}, u32[]{:S(2)}, u32[]{:S(2)}) async-start(f32[1,256,256]{2,0,1:T(1,128)} %bitcast.34), calls=%async_computation.1 | async-start | bytes 524288 | tf_op jit(solution)/shard_map/all_to_all | solution.py:102
  26.0 10.1 %collective-permute-start.5 = (bf16[256,256]{1,0:T(8,128)(2,1)}, bf16[256,256]{1,0:T(8,128)(2,1)S(1)}, u32[]{:S(2)}, u32[]{:S(2)}) collective-permute-start(bf16[256,256]{1,0:T(8,128)(2,1)} %param.8), channel_id=1, source_target_pairs={{0,2},{1,3},{2,0},{3,1},{4,6},{5,7},{6,4},{7,5},{8,10},{9,11},{10,... | collective-permute-start | bytes 393224 | tf_op jit(solution)/shard_map/ppermute | solution.py:25
  30.1 6.2 %collective-permute-start.3 = (bf16[3,2,256]{2,1,0:T(2,128)(2,1)S(1)}, bf16[3,2,256]{2,1,0:T(2,128)(2,1)S(1)}, u32[]{:S(2)}, u32[]{:S(2)}) collective-permute-start(bf16[3,2,256]{2,1,0:T(2,128)(2,1)S(1)} %slice.128), channel_id=1, source_target_pairs={{0,4},{4,8},{8,12},{12,16},{16,20},{20,24},{24,28},{1,5},{5,9},{9,... | collective-permute-start | bytes 9224 | tf_op jit(solution)/shard_map/ppermute | solution.py:17
  36.4 0.7 copy-start.1
  38.1 8.3 %all-to-all-start = ((bf16[2,256,256]{2,0,1:T(2,128)(2,1)}), bf16[2,256,256]{2,0,1:T(2,128)(2,1)}, u32[]{:S(2)}, u32[]{:S(2)}) async-start(bf16[2,256,256]{2,0,1:T(2,128)(2,1)} %copy.38), calls=%async_computation | async-start | bytes 524288 | tf_op jit(solution)/shard_map/all_to_all | solution.py:102
  43.2 1.0 copy-start.5
  43.3 1.2 %copy-start.7 = (f32[1,256,2,256]{3,1,0,2:T(8,128)S(1)}, f32[1,256,2,256]{3,1,0,2:T(8,128)}, u32[]{:S(2)}) copy-start(f32[1,256,2,256]{3,1,0,2:T(8,128)} %get-tuple-element.26) | copy-start | bytes 1572868
  48.6 1.0 copy-start.6
  48.6 1.2 %copy-start.8 = (f32[1,256,2,256]{3,1,0,2:T(8,128)S(1)}, f32[1,256,2,256]{3,1,0,2:T(8,128)}, u32[]{:S(2)}) copy-start(f32[1,256,2,256]{3,1,0,2:T(8,128)} %get-tuple-element.26) | copy-start | bytes 1572868
  53.0 1.0 copy-start.9
  53.0 1.2 %copy-start.10 = (f32[1,256,2,256]{3,1,2,0:T(8,128)S(1)}, f32[1,256,2,256]{3,1,2,0:T(8,128)}, u32[]{:S(2)}) copy-start(f32[1,256,2,256]{3,1,2,0:T(8,128)} %get-tuple-element.27) | copy-start | bytes 1572868
  57.3 14.0 %copy-start.2 = (f32[256,256]{1,0:T(8,128)S(1)}, f32[256,256]{1,0:T(8,128)}, u32[]{:S(2)}) copy-start(f32[256,256]{1,0:T(8,128)} %copy-done.1) | copy-start | bytes 786436
  57.3 14.0 %copy-start.14 = (f32[256]{0:T(256)S(1)}, f32[256]{0:T(256)}, u32[]{:S(2)}) copy-start(f32[256]{0:T(256)} %param.11) | copy-start | bytes 3076
  59.3 9.9 %all-to-all-start.2 = ((bf16[2,32,8,256]{3,1,0,2:T(8,128)(2,1)}), bf16[2,32,8,256]{3,1,0,2:T(8,128)(2,1)S(1)}, u32[]{:S(2)}, u32[]{:S(2)}) async-start(bf16[2,32,8,256]{3,1,0,2:T(8,128)(2,1)} %copy.49), calls=%async_computation.2 | async-start | bytes 524288 | tf_op jit(solution)/shard_map/all_to_all | solution.py:110
  71.6 1.2 %copy-start.4 = (bf16[256,1024]{1,0:T(8,128)(2,1)S(1)}, bf16[256,1024]{1,0:T(8,128)(2,1)}, u32[]{:S(2)}) copy-start(bf16[256,1024]{1,0:T(8,128)(2,1)} %param.13) | copy-start | bytes 1572868
  71.9 5.3 %copy-start.12 = (f32[1,3,256]{2,1,0:T(4,128)S(1)}, f32[1,3,256]{2,1,0:T(4,128)}, u32[]{:S(2)}) copy-start(f32[1,3,256]{2,1,0:T(4,128)} %get-tuple-element.28) | copy-start | bytes 9220
  71.9 5.3 %copy-start.13 = (f32[1,3,256]{2,1,0:T(4,128)S(1)}, f32[1,3,256]{2,1,0:T(4,128)}, u32[]{:S(2)}) copy-start(f32[1,3,256]{2,1,0:T(4,128)} %get-tuple-element.31) | copy-start | bytes 9220
  73.3 11.9 %collective-permute-start.11 = (bf16[256,256]{1,0:T(8,128)(2,1)S(1)}, bf16[256,256]{1,0:T(8,128)(2,1)S(1)}, u32[]{:S(2)}, u32[]{:S(2)}) collective-permute-start(bf16[256,256]{1,0:T(8,128)(2,1)S(1)} %fusion.31), channel_id=1, source_target_pairs={{0,2},{1,3},{2,0},{3,1},{4,6},{5,7},{6,4},{7,5},{8,10},{9,11},{10,... | collective-permute-start | bytes 393224 | tf_op jit(solution)/shard_map/ppermute | solution.py:36
  75.2 17.9 %collective-permute-start.10 = (bf16[256,256]{1,0:T(8,128)(2,1)S(1)}, bf16[256,256]{1,0:T(8,128)(2,1)S(1)}, u32[]{:S(2)}, u32[]{:S(2)}) collective-permute-start(bf16[256,256]{1,0:T(8,128)(2,1)S(1)} %fusion.30), channel_id=1, source_target_pairs={{0,1},{1,2},{2,3},{3,0},{4,5},{5,6},{6,7},{7,4},{8,9},{9,10},{10,1... | collective-permute-start | bytes 393224 | tf_op jit(solution)/shard_map/ppermute | solution.py:36
  76.2 18.8 %collective-permute-start.12 = (bf16[256,256]{1,0:T(8,128)(2,1)S(1)}, bf16[256,256]{1,0:T(8,128)(2,1)S(1)}, u32[]{:S(2)}, u32[]{:S(2)}) collective-permute-start(bf16[256,256]{1,0:T(8,128)(2,1)S(1)} %fusion.32), channel_id=1, source_target_pairs={{0,3},{1,0},{2,1},{3,2},{4,7},{5,4},{6,5},{7,6},{8,11},{9,8},{10,9... | collective-permute-start | bytes 393224 | tf_op jit(solution)/shard_map/ppermute | solution.py:36
  78.5 17.2 %collective-permute-start.13 = (f32[2,256]{1,0:T(2,128)S(1)}, f32[2,256]{1,0:T(2,128)S(1)}, u32[]{:S(2)}, u32[]{:S(2)}) collective-permute-start(f32[2,256]{1,0:T(2,128)S(1)} %get-tuple-element.39), channel_id=1, source_target_pairs={{4,0},{5,1},{6,2},{7,3},{8,4},{9,5},{10,6},{11,7},{12,8},{13,9},{1... | collective-permute-start | bytes 6152 | tf_op jit(solution)/shard_map/ppermute | solution.py:55
  82.2 15.6 %collective-permute-start.14 = (f32[2,256]{1,0:T(2,128)S(1)}, f32[2,256]{1,0:T(2,128)S(1)}, u32[]{:S(2)}, u32[]{:S(2)}) collective-permute-start(f32[2,256]{1,0:T(2,128)S(1)} %get-tuple-element.36), channel_id=1, source_target_pairs={{4,1},{5,2},{6,3},{7,0},{8,5},{9,6},{10,7},{11,4},{12,9},{13,10},{... | collective-permute-start | bytes 6152 | tf_op jit(solution)/shard_map/ppermute | solution.py:55
  85.1 13.0 %collective-permute-start.15 = (f32[2,256]{1,0:T(2,128)S(1)}, f32[2,256]{1,0:T(2,128)S(1)}, u32[]{:S(2)}, u32[]{:S(2)}) collective-permute-start(f32[2,256]{1,0:T(2,128)S(1)} %get-tuple-element.38), channel_id=1, source_target_pairs={{4,2},{5,3},{6,0},{7,1},{8,6},{9,7},{10,4},{11,5},{12,10},{13,11},... | collective-permute-start | bytes 6152 | tf_op jit(solution)/shard_map/ppermute | solution.py:55
  93.1 6.4 %collective-permute-start.16 = (f32[2,256]{1,0:T(2,128)S(1)}, f32[2,256]{1,0:T(2,128)S(1)}, u32[]{:S(2)}, u32[]{:S(2)}) collective-permute-start(f32[2,256]{1,0:T(2,128)S(1)} %get-tuple-element.37), channel_id=1, source_target_pairs={{4,3},{5,0},{6,1},{7,2},{8,7},{9,4},{10,5},{11,6},{12,11},{13,8},{... | collective-permute-start | bytes 6152 | tf_op jit(solution)/shard_map/ppermute | solution.py:55
  95.0 6.0 %collective-permute-start.8 = (bf16[256,256]{1,0:T(8,128)(2,1)S(1)}, bf16[256,256]{1,0:T(8,128)(2,1)S(1)}, u32[]{:S(2)}, u32[]{:S(2)}) collective-permute-start(bf16[256,256]{1,0:T(8,128)(2,1)S(1)} %convolution_convert_fusion.1), channel_id=1, source_target_pairs={{0,2},{1,3},{2,0},{3,1},{4,6},{5,7},{6,4},{7,5},{8,10},{9,11},{10,... | collective-permute-start | bytes 393224 | tf_op jit(solution)/shard_map/ppermute | solution.py:36
  95.7 10.8 %collective-permute-start.7 = (bf16[256,256]{1,0:T(8,128)(2,1)S(1)}, bf16[256,256]{1,0:T(8,128)(2,1)S(1)}, u32[]{:S(2)}, u32[]{:S(2)}) collective-permute-start(bf16[256,256]{1,0:T(8,128)(2,1)S(1)} %convolution_convert_fusion.2), channel_id=1, source_target_pairs={{0,1},{1,2},{2,3},{3,0},{4,5},{5,6},{6,7},{7,4},{8,9},{9,10},{10,1... | collective-permute-start | bytes 393224 | tf_op jit(solution)/shard_map/ppermute | solution.py:36
  97.8 12.1 %collective-permute-start.9 = (bf16[256,256]{1,0:T(8,128)(2,1)S(1)}, bf16[256,256]{1,0:T(8,128)(2,1)S(1)}, u32[]{:S(2)}, u32[]{:S(2)}) collective-permute-start(bf16[256,256]{1,0:T(8,128)(2,1)S(1)} %convolution_convert_fusion), channel_id=1, source_target_pairs={{0,3},{1,0},{2,1},{3,2},{4,7},{5,4},{6,5},{7,6},{8,11},{9,8},{10,9... | collective-permute-start | bytes 393224 | tf_op jit(solution)/shard_map/ppermute | solution.py:36

commit v11 on v6

--- a/solution.py
+++ b/solution.py
@@ -6,7 +6,7 @@
 from jax.sharding import PartitionSpec as P
 
 HIGHEST = lax.Precision.HIGHEST
-STAGE_A_PRECISION = lax.Precision.HIGHEST
+STAGE_A_PRECISION = lax.Precision.HIGH
 STAGE_B_PRECISION = lax.Precision.HIGH
 WIRE = jnp.bfloat16
 

time: 103 us -> 102 us (level)
  matrix products: 21.5 us -> 20.3 us
where the time goes in v11:
time: 102 us; the launch traced here: 101 us
  starting transfers between devices  28.8 us (28%)
  matrix products  20.3 us (20%)
  waiting for transfers between devices  19.1 us (19%)
  other arithmetic  13 us (13%)
  blocking collectives  9.32 us (9%)
  local copies, waits for them, and re-layouts  8.92 us (9%)
  between operations  1.2 us (1%)
    ppermute x6, waiting for transfers between devices, panel_reduce_scatter(): lax.ppermute(sent, 'panel', [(i, (i + k) % count) for i in range(count)])  14.6 us
    ppermute x6, starting transfers between devices, panel_parts(): lax.ppermute(value, 'panel', [(i, (i + k) % count) for i in range(count)])  10.3 us
    all_to_all x1, blocking collectives, to_rows(): lax.all_to_all(columns.astype(wire), 'seq', split_axis=2, concat_axis=1,...  9.32 us
    all_to_all x2, starting transfers between devices, to_columns(): lax.all_to_all(jnp.swapaxes(rows, 1, 2).astype(wire), 'seq', split_axis=1...  7.95 us
    ppermute x6, starting transfers between devices, panel_reduce_scatter(): lax.ppermute(sent, 'panel', [(i, (i + k) % count) for i in range(count)])  7.07 us
    dot_general x4, matrix products, local(): jnp.einsum('td,jdc->jtc', part, lax.dynamic_slice_in_dim(in_weight, sourc...  4.7 us
    unnamed x27, local copies, waits for them, and re-layouts  4.24 us
    dot_general x2, matrix products, forward_spectrum(): jnp.einsum('bcerkm,rmsq->bceskq', spread, stage_b, precision=STAGE_B_PREC...  3.81 us
  transfers between devices with their start and end apart: 16, of which 5 were waited for; matrix products, arithmetic and copies ran while one was open for 25% of the time, Pallas kernels for 0%

profile of v11, /device:TPU:0, one launch (start us, length us, event | category | flops | bytes accessed | tf_op | source)
XLA Modules:
  0.0 100.6 jit_solution(12889472377933342648)
XLA Ops:
  0.7 3.1 %collective-permute-start = (bf16[256,256]{1,0:T(8,128)(2,1)}, bf16[256,256]{1,0:T(8,128)(2,1)}, u32[]{:S(2)}, u32[]{:S(2)}) collective-permute-start(bf16[256,256]{1,0:T(8,128)(2,1)} %param.7), channel_id=1, source_target_pairs={{0,1},{1,2},{2,3},{3,0},{4,5},{5,6},{6,7},{7,4},{8,9},{9,10},{10,1... | collective-permute-start | bytes 393224 | tf_op jit(solution)/shard_map/ppermute | solution.py:25
  3.8 2.1 %collective-permute-start.2 = (bf16[256,256]{1,0:T(8,128)(2,1)}, bf16[256,256]{1,0:T(8,128)(2,1)}, u32[]{:S(2)}, u32[]{:S(2)}) collective-permute-start(bf16[256,256]{1,0:T(8,128)(2,1)} %param.7), channel_id=1, source_target_pairs={{0,3},{1,0},{2,1},{3,2},{4,7},{5,4},{6,5},{7,6},{8,11},{9,8},{10,9... | collective-permute-start | bytes 393224 | tf_op jit(solution)/shard_map/ppermute | solution.py:25
  5.9 0.9 collective-permute-start.1
  6.8 1.6 %collective-permute-start.4 = (bf16[256,256]{1,0:T(8,128)(2,1)}, bf16[256,256]{1,0:T(8,128)(2,1)}, u32[]{:S(2)}, u32[]{:S(2)}) collective-permute-start(bf16[256,256]{1,0:T(8,128)(2,1)} %param.8), channel_id=1, source_target_pairs={{0,1},{1,2},{2,3},{3,0},{4,5},{5,6},{6,7},{7,4},{8,9},{9,10},{10,1... | collective-permute-start | bytes 393224 | tf_op jit(solution)/shard_map/ppermute | solution.py:25
  8.4 2.2 %collective-permute-start.6 = (bf16[256,256]{1,0:T(8,128)(2,1)}, bf16[256,256]{1,0:T(8,128)(2,1)}, u32[]{:S(2)}, u32[]{:S(2)}) collective-permute-start(bf16[256,256]{1,0:T(8,128)(2,1)} %param.8), channel_id=1, source_target_pairs={{0,3},{1,0},{2,1},{3,2},{4,7},{5,4},{6,5},{7,6},{8,11},{9,8},{10,9... | collective-permute-start | bytes 393224 | tf_op jit(solution)/shard_map/ppermute | solution.py:25
  10.6 1.8 %copy.63 = f32[1,256,256]{1,0,2:T(1,128)} copy(f32[1,256,256]{2,1,0:T(8,128)} %bitcast.221) | data formatting | bytes 524288 | tf_op jit(solution)/shard_map/broadcast_in_dim | solution.py:118
  12.4 3.7 %all-to-all-start.1 = ((f32[1,256,256]{2,0,1:T(1,128)}), f32[1,256,256]{2,0,1:T(1,128)S(1)}, u32[]{:S(2)}, u32[]{:S(2)}) async-start(f32[1,256,256]{2,0,1:T(1,128)} %bitcast.36), calls=%async_computation.1 | async-start | bytes 524288 | tf_op jit(solution)/shard_map/all_to_all | solution.py:85
  16.8 0.7 iota_multiply_fusion
  17.4 0.6 iota_multiply_fusion.2
  18.0 1.8 %fusion.91 = (f32[256,1,256]{2,0,1:T(8,128)}, f32[256,1,256]{2,0,1:T(8,128)}) fusion(), kind=kLoop, calls=%fused_computation.130 | loop fusion | flops 983040 | bytes 524288 | tf_op jit(solution)/shard_map/sin | solution.py:62
  19.8 1.7 %fusion.93 = f32[256,1,256]{2,0,1:T(8,128)} fusion(), kind=kLoop, calls=%fused_computation.132 | loop fusion | flops 1048576 | bytes 262144 | tf_op jit(solution)/shard_map/neg | solution.py:67
  21.5 0.7 slice_bitcast_fusion.5
  22.2 1.2 %fusion.56 = f32[3,256,256]{1,2,0:T(8,128)S(1)} fusion(bf16[3,1024,256]{2,1,0:T(8,128)(2,1)S(1)} %copy-done, s32[]{:T(128)S(6)} %select_n.148, bf16[256,256]{1,0:T(8,128)(2,1)} %param.7), kind=kOutput, calls=%fused_computation.90 | convolution fusion | flops 100663296 | bytes 1310724 | tf_op jit(solution)/shard_map/td,jdc->jtc/dot_general | solution.py:122
  23.6 0.7 fusion.121
  24.3 0.8 fusion.138
  25.1 2.8 %fusion.46 = (f32[1,256,2,256]{3,1,2,0:T(8,128)}, f32[1,256,2,256]{3,1,0,2:T(8,128)}, f32[1,256,2,256]{3,1,0,2:T(8,128)}, f32[1,256,2,256]{3,1,2,0:T(8,128)}) fusion(f32[256,1,256]{2,0,1:T(8,128)} %get-tuple-element.35, f32[256,1,256]{2,0,1:T(8,128)} %fusion.93, f32[256,1,256]{2,0,1:T(8,128)} %get-tuple-element.34), kind=kLoop, calls=%fused_computation.70 | loop fusion | flops 524288 | bytes 2883584 | tf_op jit(solution)/shard_map/stack | solution.py:66
  28.3 1.2 %convolution_add_fusion.1 = f32[3,256,256]{1,2,0:T(8,128)S(1)} fusion(f32[3,256,256]{1,2,0:T(8,128)S(1)} %fusion.56, bf16[3,1024,256]{2,1,0:T(8,128)(2,1)S(1)} %copy-done, s32[]{:T(128)S(6)} %select_n.150, bf16[256,256]{1,0:T(8,128)(2,1)} %collective-permute-done), kind=kOutput, calls=%fused_computation.19 | convolution fusion | flops 100859904 | bytes 2097156 | tf_op jit(solution)/shard_map/td,jdc->jtc/dot_general | solution.py:122
  29.4 1.2 %fusion.49 = f32[3,256,256]{1,2,0:T(8,128)S(1)} fusion(bf16[3,1024,256]{2,1,0:T(8,128)(2,1)S(1)} %copy-done, s32[]{:T(128)S(6)} %select_n.154, bf16[256,256]{1,0:T(8,128)(2,1)} %collective-permute-done.2), kind=kOutput, calls=%fused_computation.83 | convolution fusion | flops 100663296 | bytes 1310724 | tf_op jit(solution)/shard_map/td,jdc->jtc/dot_general | solution.py:122
  30.6 1.2 %fusion.21 = bf16[3,256,256]{2,1,0:T(8,128)(2,1)S(1)} fusion(f32[3,256,256]{1,2,0:T(8,128)S(1)} %fusion.49, f32[3,256,256]{1,2,0:T(8,128)S(1)} %convolution_add_fusion.1, bf16[3,1024,256]{2,1,0:T(8,128)(2,1)S(1)} %copy-done, s32[]{:T(128)S(6)} %select_n.152, bf16[256,256]{1,0:T(8,128)(2,1)} %collective-permute-done.1), kind=kOutput, calls=%fused_computation.22 | convolution fusion | flops 101253120 | bytes 2490372 | tf_op jit(solution)/shard_map/td,jdc->jtc/dot_general | solution.py:122
  31.8 2.1 %collective-permute-start.3 = (bf16[3,2,256]{2,1,0:T(2,128)(2,1)S(1)}, bf16[3,2,256]{2,1,0:T(2,128)(2,1)S(1)}, u32[]{:S(2)}, u32[]{:S(2)}) collective-permute-start(bf16[3,2,256]{2,1,0:T(2,128)(2,1)S(1)} %slice.111), channel_id=1, source_target_pairs={{0,4},{4,8},{8,12},{12,16},{16,20},{20,24},{24,28},{1,5},{5,9},{9,... | collective-permute-start | bytes 9224 | tf_op jit(solution)/shard_map/ppermute | solution.py:17
  34.0 1.1 %convolution_add_fusion.3 = f32[256,256]{0,1:T(8,128)S(1)} fusion(f32[256,256]{0,1:T(8,128)S(1)} %fusion.103, bf16[256,256]{1,0:T(8,128)(2,1)} %collective-permute-done.4, bf16[256,1024]{1,0:T(8,128)(2,1)S(1)} %copy-done.3, s32[]{:T(128)S(6)} %select_n.150), kind=kOutput, calls=%fused_computation.31 | convolution fusion | flops 33619968 | bytes 786436 | tf_op jit(solution)/shard_map/dot_general | solution.py:130
  35.1 1.1 %fusion.95 = f32[256,256]{0,1:T(8,128)S(1)} fusion(bf16[256,256]{1,0:T(8,128)(2,1)} %collective-permute-done.6, bf16[256,1024]{1,0:T(8,128)(2,1)S(1)} %copy-done.3, s32[]{:T(128)S(6)} %select_n.154), kind=kOutput, calls=%fused_computation.134 | convolution fusion | flops 33554432 | bytes 524292 | tf_op jit(solution)/shard_map/dot_general | solution.py:130
  36.3 0.7 collective-permute-done.5
  38.0 0.9 copy.32
  38.9 4.2 %all-to-all-start = ((bf16[2,256,256]{2,0,1:T(2,128)(2,1)}), bf16[2,256,256]{2,0,1:T(2,128)(2,1)}, u32[]{:S(2)}, u32[]{:S(2)}) async-start(bf16[2,256,256]{2,0,1:T(2,128)(2,1)} %copy.32), calls=%async_computation | async-start | bytes 524288 | tf_op jit(solution)/shard_map/all_to_all | solution.py:85
  43.2 0.6 convolution_bitcast_fusion.2
  44.0 0.8 copy-done.5
  44.9 1.1 %convolution_bitcast_fusion.1 = f32[1,32,2,2,8,256]{5,1,4,2,0,3:T(8,128)S(1)} fusion(f32[32,2,2,8,256]{4,3,0,2,1:T(8,128)S(1)} %maximum_bitcast_fusion.3, f32[1,256,2,256]{3,1,0,2:T(8,128)S(1)} %copy-done.5, f32[1,256,2,256]{3,1,0,2:T(8,128)S(1)} %copy-done.7), kind=kOutput, calls=%fused_computation.15 | convolution fusion | flops 805568512 | bytes 3145728 | tf_op jit(solution)/shard_map/bcerkm,rmsq->bceskq/dot_general | solution.py:103
  46.1 3.8 %all-to-all-done = bf16[2,256,256]{2,0,1:T(2,128)(2,1)} async-done(((bf16[2,256,256]{2,0,1:T(2,128)(2,1)}), bf16[2,256,256]{2,0,1:T(2,128)(2,1)}, u32[]{:S(2)}, u32[]{:S(2)}) %all-to-all-start) | async-done | bytes 262176 | tf_op jit(solution)/shard_map/all_to_all | solution.py:85
  49.9 1.7 %convolution_bitcast_fusion = f32[2,32,2,2,8,256]{5,4,3,2,1,0:T(8,128)S(1)} fusion(bf16[2,8,32,256]{3,0,2,1:T(2,128)(2,1)} %bitcast.20, f32[2,1,8,8]{3,2,1,0:T(8,128)S(1)} %get-tuple-element.33, f32[2,1,8,8]{3,2,1,0:T(8,128)S(1)} %get-tuple-element.32), kind=kOutput, calls=%fused_computation.14 | convolution fusion | flops 25166080 | bytes 2360320 | tf_op jit(solution)/shard_map/erkp,bcpm->bcerkm/dot_general | solution.py:101
  52.1 0.8 copy-done.6
  53.1 2.7 %fusion.10 = f32[2,32,2,2,8,256]{5,1,4,2,0,3:T(8,128)S(1)} fusion(f32[2,32,2,2,8,256]{5,4,3,2,1,0:T(8,128)S(1)} %pad_maximum_fusion, f32[1,256,2,256]{3,1,0,2:T(8,128)S(1)} %copy-done.6, f32[1,256,2,256]{3,1,0,2:T(8,128)S(1)} %copy-done.8), kind=kOutput, calls=%fused_computation.12 | convolution fusion | flops 1610874880 | bytes 5242880 | tf_op jit(solution)/shard_map/bcerkm,rmsq->bceskq/dot_general | solution.py:103
  56.5 0.9 copy-done.9
  57.5 2.7 %fusion.13 = f32[2,32,2,2,8,256]{5,4,3,2,1,0:T(8,128)S(1)} fusion(f32[2,32,2,2,8,256,1]{5,1,4,2,0,3,6:T(8,128)S(1)} %maximum_bitcast_fusion, f32[1,256,2,256]{3,1,2,0:T(8,128)S(1)} %copy-done.10, f32[1,256,2,256]{3,1,2,0:T(8,128)S(1)} %copy-done.9), kind=kOutput, calls=%fused_computation.13 | convolution fusion | flops 1610874880 | bytes 5242880 | tf_op jit(solution)/shard_map/bceskq,sqrm->bcerkm/dot_general | solution.py:108
  60.6 0.7 fusion.27
  61.3 9.3 %all_to_all.39 = bf16[2,32,8,256]{3,1,0,2:T(8,128)(2,1)S(1)} all-to-all(bf16[2,32,8,256]{3,1,0,2:T(8,128)(2,1)S(1)} %copy.43), channel_id=1, replica_groups=mesh['seq'=8,'panel'=4] {'seq'}, dimensions={2} | all-to-all | bytes 524288 | tf_op jit(solution)/shard_map/all_to_all | solution.py:93
  70.6 0.8 bitcast_convert_fusion
  71.5 1.2 %copy.45 = f32[2,256,256]{1,2,0:T(8,128)S(1)} copy(f32[2,256,256]{2,1,0:T(8,128)} %bitcast.219) | data formatting | bytes 1048576 | tf_op jit(solution)/shard_map/transpose | solution.py:96
  72.9 0.8 copy-done.4
  74.2 1.3 %collective-permute-start.10 = (f32[3,2,256]{2,1,0:T(2,128)S(1)}, f32[3,2,256]{2,1,0:T(2,128)S(1)}, u32[]{:S(2)}, u32[]{:S(2)}) collective-permute-start(f32[3,2,256]{2,1,0:T(2,128)S(1)} %slice.132), channel_id=1, source_target_pairs={{4,0},{8,4},{12,8},{16,12},{20,16},{24,20},{28,24},{5,1},{9,5},{13... | collective-permute-start | bytes 18440 | tf_op jit(solution)/shard_map/ppermute | solution.py:17
  75.7 2.6 %collective-permute-start.8 = (bf16[256,256]{1,0:T(8,128)(2,1)S(1)}, bf16[256,256]{1,0:T(8,128)(2,1)S(1)}, u32[]{:S(2)}, u32[]{:S(2)}) collective-permute-start(bf16[256,256]{1,0:T(8,128)(2,1)S(1)} %convolution_convert_fusion.1), channel_id=1, source_target_pairs={{0,2},{1,3},{2,0},{3,1},{4,6},{5,7},{6,4},{7,5},{8,10},{9,11},{10,... | collective-permute-start | bytes 393224 | tf_op jit(solution)/shard_map/ppermute | solution.py:36
  78.4 3.8 %collective-permute-start.9 = (bf16[256,256]{1,0:T(8,128)(2,1)S(1)}, bf16[256,256]{1,0:T(8,128)(2,1)S(1)}, u32[]{:S(2)}, u32[]{:S(2)}) collective-permute-start(bf16[256,256]{1,0:T(8,128)(2,1)S(1)} %convolution_convert_fusion), channel_id=1, source_target_pairs={{0,3},{1,0},{2,1},{3,2},{4,7},{5,4},{6,5},{7,6},{8,11},{9,8},{10,9... | collective-permute-start | bytes 393224 | tf_op jit(solution)/shard_map/ppermute | solution.py:36
  83.2 0.6 collective-permute-start.11
  84.1 4.3 %collective-permute-done.8 = bf16[256,256]{1,0:T(8,128)(2,1)S(1)} collective-permute-done((bf16[256,256]{1,0:T(8,128)(2,1)S(1)}, bf16[256,256]{1,0:T(8,128)(2,1)S(1)}, u32[]{:S(2)}, u32[]{:S(2)}) %collective-permute-start.8) | collective-permute-done | bytes 131104 | tf_op jit(solution)/shard_map/ppermute | solution.py:36
  88.4 1.7 %collective-permute-done.9 = bf16[256,256]{1,0:T(8,128)(2,1)S(1)} collective-permute-done((bf16[256,256]{1,0:T(8,128)(2,1)S(1)}, bf16[256,256]{1,0:T(8,128)(2,1)S(1)}, u32[]{:S(2)}, u32[]{:S(2)}) %collective-permute-start.9) | collective-permute-done | bytes 131104 | tf_op jit(solution)/shard_map/ppermute | solution.py:36
  90.1 0.9 add_convert_fusion
  91.0 8.6 %collective-permute-done.12 = bf16[256,256]{1,0:T(8,128)(2,1)S(1)} collective-permute-done((bf16[256,256]{1,0:T(8,128)(2,1)S(1)}, bf16[256,256]{1,0:T(8,128)(2,1)S(1)}, u32[]{:S(2)}, u32[]{:S(2)}) %collective-permute-start.12) | collective-permute-done | bytes 131104 | tf_op jit(solution)/shard_map/ppermute | solution.py:36
  99.6 1.0 fusion.67
  (69 shorter events, 6.6 us)
Async XLA Ops:
  0.6 21.6 %copy-start = (bf16[3,1024,256]{2,1,0:T(8,128)(2,1)S(1)}, bf16[3,1024,256]{2,1,0:T(8,128)(2,1)}, u32[]{:S(2)}) copy-start(bf16[3,1024,256]{2,1,0:T(8,128)(2,1)} %param.9) | copy-start | bytes 4718596
  0.6 22.7 %copy-start.11 = (bf16[256,256]{1,0:T(8,128)(2,1)S(1)}, bf16[256,256]{1,0:T(8,128)(2,1)}, u32[]{:S(2)}) copy-start(bf16[256,256]{1,0:T(8,128)(2,1)} %param.8) | copy-start | bytes 393220
  0.7 22.7 %copy-start.3 = (bf16[256,1024]{1,0:T(8,128)(2,1)S(1)}, bf16[256,1024]{1,0:T(8,128)(2,1)}, u32[]{:S(2)}) copy-start(bf16[256,1024]{1,0:T(8,128)(2,1)} %param.13) | copy-start | bytes 1572868
  0.7 27.2 %collective-permute-start = (bf16[256,256]{1,0:T(8,128)(2,1)}, bf16[256,256]{1,0:T(8,128)(2,1)}, u32[]{:S(2)}, u32[]{:S(2)}) collective-permute-start(bf16[256,256]{1,0:T(8,128)(2,1)} %param.7), channel_id=1, source_target_pairs={{0,1},{1,2},{2,3},{3,0},{4,5},{5,6},{6,7},{7,4},{8,9},{9,10},{10,1... | collective-permute-start | bytes 393224 | tf_op jit(solution)/shard_map/ppermute | solution.py:25
  3.8 25.7 %collective-permute-start.2 = (bf16[256,256]{1,0:T(8,128)(2,1)}, bf16[256,256]{1,0:T(8,128)(2,1)}, u32[]{:S(2)}, u32[]{:S(2)}) collective-permute-start(bf16[256,256]{1,0:T(8,128)(2,1)} %param.7), channel_id=1, source_target_pairs={{0,3},{1,0},{2,1},{3,2},{4,7},{5,4},{6,5},{7,6},{8,11},{9,8},{10,9... | collective-permute-start | bytes 393224 | tf_op jit(solution)/shard_map/ppermute | solution.py:25
  5.9 24.8 %collective-permute-start.1 = (bf16[256,256]{1,0:T(8,128)(2,1)}, bf16[256,256]{1,0:T(8,128)(2,1)}, u32[]{:S(2)}, u32[]{:S(2)}) collective-permute-start(bf16[256,256]{1,0:T(8,128)(2,1)} %param.7), channel_id=1, source_target_pairs={{0,2},{1,3},{2,0},{3,1},{4,6},{5,7},{6,4},{7,5},{8,10},{9,11},{10,... | collective-permute-start | bytes 393224 | tf_op jit(solution)/shard_map/ppermute | solution.py:25
  6.8 27.2 %collective-permute-start.4 = (bf16[256,256]{1,0:T(8,128)(2,1)}, bf16[256,256]{1,0:T(8,128)(2,1)}, u32[]{:S(2)}, u32[]{:S(2)}) collective-permute-start(bf16[256,256]{1,0:T(8,128)(2,1)} %param.8), channel_id=1, source_target_pairs={{0,1},{1,2},{2,3},{3,0},{4,5},{5,6},{6,7},{7,4},{8,9},{9,10},{10,1... | collective-permute-start | bytes 393224 | tf_op jit(solution)/shard_map/ppermute | solution.py:25
  8.4 26.7 %collective-permute-start.6 = (bf16[256,256]{1,0:T(8,128)(2,1)}, bf16[256,256]{1,0:T(8,128)(2,1)}, u32[]{:S(2)}, u32[]{:S(2)}) collective-permute-start(bf16[256,256]{1,0:T(8,128)(2,1)} %param.8), channel_id=1, source_target_pairs={{0,3},{1,0},{2,1},{3,2},{4,7},{5,4},{6,5},{7,6},{8,11},{9,8},{10,9... | collective-permute-start | bytes 393224 | tf_op jit(solution)/shard_map/ppermute | solution.py:25
  12.4 26.5 %all-to-all-start.1 = ((f32[1,256,256]{2,0,1:T(1,128)}), f32[1,256,256]{2,0,1:T(1,128)S(1)}, u32[]{:S(2)}, u32[]{:S(2)}) async-start(f32[1,256,256]{2,0,1:T(1,128)} %bitcast.36), calls=%async_computation.1 | async-start | bytes 524288 | tf_op jit(solution)/shard_map/all_to_all | solution.py:85
  27.9 9.1 %collective-permute-start.5 = (bf16[256,256]{1,0:T(8,128)(2,1)}, bf16[256,256]{1,0:T(8,128)(2,1)S(1)}, u32[]{:S(2)}, u32[]{:S(2)}) collective-permute-start(bf16[256,256]{1,0:T(8,128)(2,1)} %param.8), channel_id=1, source_target_pairs={{0,2},{1,3},{2,0},{3,1},{4,6},{5,7},{6,4},{7,5},{8,10},{9,11},{10,... | collective-permute-start | bytes 393224 | tf_op jit(solution)/shard_map/ppermute | solution.py:25
  31.8 5.4 %collective-permute-start.3 = (bf16[3,2,256]{2,1,0:T(2,128)(2,1)S(1)}, bf16[3,2,256]{2,1,0:T(2,128)(2,1)S(1)}, u32[]{:S(2)}, u32[]{:S(2)}) collective-permute-start(bf16[3,2,256]{2,1,0:T(2,128)(2,1)S(1)} %slice.111), channel_id=1, source_target_pairs={{0,4},{4,8},{8,12},{12,16},{16,20},{20,24},{24,28},{1,5},{5,9},{9,... | collective-permute-start | bytes 9224 | tf_op jit(solution)/shard_map/ppermute | solution.py:17
  37.2 0.7 copy-start.1
  38.9 11.0 %all-to-all-start = ((bf16[2,256,256]{2,0,1:T(2,128)(2,1)}), bf16[2,256,256]{2,0,1:T(2,128)(2,1)}, u32[]{:S(2)}, u32[]{:S(2)}) async-start(bf16[2,256,256]{2,0,1:T(2,128)(2,1)} %copy.32), calls=%async_computation | async-start | bytes 524288 | tf_op jit(solution)/shard_map/all_to_all | solution.py:85
  43.7 1.0 %copy-start.5 = (f32[1,256,2,256]{3,1,0,2:T(8,128)S(1)}, f32[1,256,2,256]{3,1,0,2:T(8,128)}, u32[]{:S(2)}) copy-start(f32[1,256,2,256]{3,1,0,2:T(8,128)} %get-tuple-element.21) | copy-start | bytes 1572868
  43.7 1.2 %copy-start.7 = (f32[1,256,2,256]{3,1,0,2:T(8,128)S(1)}, f32[1,256,2,256]{3,1,0,2:T(8,128)}, u32[]{:S(2)}) copy-start(f32[1,256,2,256]{3,1,0,2:T(8,128)} %get-tuple-element.24) | copy-start | bytes 1572868
  51.9 1.0 %copy-start.6 = (f32[1,256,2,256]{3,1,0,2:T(8,128)S(1)}, f32[1,256,2,256]{3,1,0,2:T(8,128)}, u32[]{:S(2)}) copy-start(f32[1,256,2,256]{3,1,0,2:T(8,128)} %get-tuple-element.21) | copy-start | bytes 1572868
  51.9 1.2 %copy-start.8 = (f32[1,256,2,256]{3,1,0,2:T(8,128)S(1)}, f32[1,256,2,256]{3,1,0,2:T(8,128)}, u32[]{:S(2)}) copy-start(f32[1,256,2,256]{3,1,0,2:T(8,128)} %get-tuple-element.24) | copy-start | bytes 1572868
  56.3 1.0 %copy-start.9 = (f32[1,256,2,256]{3,1,2,0:T(8,128)S(1)}, f32[1,256,2,256]{3,1,2,0:T(8,128)}, u32[]{:S(2)}) copy-start(f32[1,256,2,256]{3,1,2,0:T(8,128)} %get-tuple-element.20) | copy-start | bytes 1572868
  56.3 1.2 %copy-start.10 = (f32[1,256,2,256]{3,1,2,0:T(8,128)S(1)}, f32[1,256,2,256]{3,1,2,0:T(8,128)}, u32[]{:S(2)}) copy-start(f32[1,256,2,256]{3,1,2,0:T(8,128)} %get-tuple-element.25) | copy-start | bytes 1572868
  60.6 12.2 %copy-start.2 = (f32[256,256]{1,0:T(8,128)S(1)}, f32[256,256]{1,0:T(8,128)}, u32[]{:S(2)}) copy-start(f32[256,256]{1,0:T(8,128)} %copy-done.1) | copy-start | bytes 786436
  60.6 12.2 %copy-start.12 = (f32[256]{0:T(256)S(1)}, f32[256]{0:T(256)}, u32[]{:S(2)}) copy-start(f32[256]{0:T(256)} %param.11) | copy-start | bytes 3076
  72.7 1.0 %copy-start.4 = (bf16[256,1024]{1,0:T(8,128)(2,1)S(1)}, bf16[256,1024]{1,0:T(8,128)(2,1)}, u32[]{:S(2)}) copy-start(bf16[256,1024]{1,0:T(8,128)(2,1)} %param.13) | copy-start | bytes 1572868
  74.2 8.0 %collective-permute-start.10 = (f32[3,2,256]{2,1,0:T(2,128)S(1)}, f32[3,2,256]{2,1,0:T(2,128)S(1)}, u32[]{:S(2)}, u32[]{:S(2)}) collective-permute-start(f32[3,2,256]{2,1,0:T(2,128)S(1)} %slice.132), channel_id=1, source_target_pairs={{4,0},{8,4},{12,8},{16,12},{20,16},{24,20},{28,24},{5,1},{9,5},{13... | collective-permute-start | bytes 18440 | tf_op jit(solution)/shard_map/ppermute | solution.py:17
  75.7 12.7 %collective-permute-start.8 = (bf16[256,256]{1,0:T(8,128)(2,1)S(1)}, bf16[256,256]{1,0:T(8,128)(2,1)S(1)}, u32[]{:S(2)}, u32[]{:S(2)}) collective-permute-start(bf16[256,256]{1,0:T(8,128)(2,1)S(1)} %convolution_convert_fusion.1), channel_id=1, source_target_pairs={{0,2},{1,3},{2,0},{3,1},{4,6},{5,7},{6,4},{7,5},{8,10},{9,11},{10,... | collective-permute-start | bytes 393224 | tf_op jit(solution)/shard_map/ppermute | solution.py:36
  78.4 10.1 %collective-permute-start.7 = (bf16[256,256]{1,0:T(8,128)(2,1)S(1)}, bf16[256,256]{1,0:T(8,128)(2,1)S(1)}, u32[]{:S(2)}, u32[]{:S(2)}) collective-permute-start(bf16[256,256]{1,0:T(8,128)(2,1)S(1)} %convolution_convert_fusion.2), channel_id=1, source_target_pairs={{0,1},{1,2},{2,3},{3,0},{4,5},{5,6},{6,7},{7,4},{8,9},{9,10},{10,1... | collective-permute-start | bytes 393224 | tf_op jit(solution)/shard_map/ppermute | solution.py:36
  78.4 11.8 %collective-permute-start.9 = (bf16[256,256]{1,0:T(8,128)(2,1)S(1)}, bf16[256,256]{1,0:T(8,128)(2,1)S(1)}, u32[]{:S(2)}, u32[]{:S(2)}) collective-permute-start(bf16[256,256]{1,0:T(8,128)(2,1)S(1)} %convolution_convert_fusion), channel_id=1, source_target_pairs={{0,3},{1,0},{2,1},{3,2},{4,7},{5,4},{6,5},{7,6},{8,11},{9,8},{10,9... | collective-permute-start | bytes 393224 | tf_op jit(solution)/shard_map/ppermute | solution.py:36
  83.2 16.4 %collective-permute-start.12 = (bf16[256,256]{1,0:T(8,128)(2,1)S(1)}, bf16[256,256]{1,0:T(8,128)(2,1)S(1)}, u32[]{:S(2)}, u32[]{:S(2)}) collective-permute-start(bf16[256,256]{1,0:T(8,128)(2,1)S(1)} %fusion.31), channel_id=1, source_target_pairs={{0,2},{1,3},{2,0},{3,1},{4,6},{5,7},{6,4},{7,5},{8,10},{9,11},{10,... | collective-permute-start | bytes 393224 | tf_op jit(solution)/shard_map/ppermute | solution.py:36
  83.2 16.4 %collective-permute-start.11 = (bf16[256,256]{1,0:T(8,128)(2,1)S(1)}, bf16[256,256]{1,0:T(8,128)(2,1)S(1)}, u32[]{:S(2)}, u32[]{:S(2)}) collective-permute-start(bf16[256,256]{1,0:T(8,128)(2,1)S(1)} %fusion.30), channel_id=1, source_target_pairs={{0,1},{1,2},{2,3},{3,0},{4,5},{5,6},{6,7},{7,4},{8,9},{9,10},{10,1... | collective-permute-start | bytes 393224 | tf_op jit(solution)/shard_map/ppermute | solution.py:36
  88.4 11.2 %collective-permute-start.13 = (bf16[256,256]{1,0:T(8,128)(2,1)S(1)}, bf16[256,256]{1,0:T(8,128)(2,1)S(1)}, u32[]{:S(2)}, u32[]{:S(2)}) collective-permute-start(bf16[256,256]{1,0:T(8,128)(2,1)S(1)} %fusion.32), channel_id=1, source_target_pairs={{0,3},{1,0},{2,1},{3,2},{4,7},{5,4},{6,5},{7,6},{8,11},{9,8},{10,9... | collective-permute-start | bytes 393224 | tf_op jit(solution)/shard_map/ppermute | solution.py:36

commit v12 on v11

--- a/solution.py
+++ b/solution.py
@@ -101,6 +101,38 @@
     spread = jnp.einsum("erkp,bcpm->bcerkm", stage_a, columns, precision=STAGE_A_PRECISION)
     spread = complex_scale(spread, twiddle[0], twiddle[1], 3)
     return jnp.einsum("bcerkm,rmsq->bceskq", spread, stage_b, precision=STAGE_B_PRECISION)
+
+
+def forward_packed(columns, tables):
+    stage_a, twiddle, stage_b, _, _ = tables
+    packed_a = jnp.stack(
+        [stage_a, jnp.stack([-stage_a[:, 1], stage_a[:, 0]], axis=1)], axis=3
+    )
+    spread = jnp.einsum("erkip,icpm->cerkm", packed_a, columns, precision=STAGE_A_PRECISION)
+    spread = complex_scale(spread[None], twiddle[0], twiddle[1], 3)
+    return jnp.einsum("bcerkm,rmsq->bceskq", spread, stage_b, precision=STAGE_B_PRECISION)
+
+
+def reversed_conjugate(spectrum):
+    shard_count = spectrum.shape[4]
+    even, odd = spectrum[:, :, 0], spectrum[:, :, 1]
+    odd_rev = jnp.flip(odd, axis=(-2, -1))
+    even_k = jnp.roll(jnp.flip(even, axis=-2), 1, axis=-2)
+    even_q = jnp.flip(even_k, axis=-1)
+    first_row = (jnp.arange(shard_count) == 0)[:, None]
+    even_rev = jnp.where(first_row, jnp.roll(even_q, 1, axis=-1), even_q)
+    rev = jnp.stack([even_rev, odd_rev], axis=2)
+    return jnp.stack([rev[:, :, :, 0], -rev[:, :, :, 1]], axis=3)
+
+
+def inverse_packed(spectrum, tables):
+    _, twiddle, _, stage_b_inv, stage_a_inv = tables
+    spread = jnp.einsum("bceskq,sqrm->bcerkm", spectrum, stage_b_inv, precision=STAGE_B_PRECISION)
+    spread = complex_scale(spread, twiddle[0], -twiddle[1], 3)
+    packed_a = jnp.stack(
+        [stage_a_inv, jnp.stack([-stage_a_inv[:, 1], stage_a_inv[:, 0]], axis=1)]
+    )
+    return jnp.einsum("oerkp,bcerkm->obcpm", packed_a, spread, precision=STAGE_A_PRECISION)
 
 
 def inverse_spectrum(spectrum, tables):
@@ -147,23 +179,17 @@
     gate_out, gate_in, value_path = (filtered[0], filtered[1], filtered[2])
     signal = value_path * gate_in
     grad_state = grad_gated * gate_out
-    spectra = forward_spectrum(to_columns(jnp.stack([signal, grad_state]), WIRE), tables)
+    spectrum = forward_packed(to_columns(jnp.stack([signal, grad_state]), WIRE), tables)
+    mirrored = reversed_conjugate(spectrum)
     filt_real, filt_imag = filt_spec[:, :, :, 0], filt_spec[:, :, :, 1]
-    sig_real, sig_imag = spectra[0:1, :, :, 0], spectra[0:1, :, :, 1]
-    grad_real, grad_imag = spectra[1:2, :, :, 0], spectra[1:2, :, :, 1]
-    product = jnp.concatenate(
+    product = jnp.stack(
         [
-            jnp.stack(
-                [sig_real * filt_real - sig_imag * filt_imag, sig_real * filt_imag + sig_imag * filt_real],
-                axis=3,
-            ),
-            jnp.stack(
-                [grad_real * filt_real + grad_imag * filt_imag, grad_imag * filt_real - grad_real * filt_imag],
-                axis=3,
-            ),
-        ]
-    )
-    convolved = to_rows(inverse_spectrum(product, tables), WIRE)
+            spectrum[:, :, :, 0] * filt_real - mirrored[:, :, :, 1] * filt_imag,
+            spectrum[:, :, :, 1] * filt_real + mirrored[:, :, :, 0] * filt_imag,
+        ],
+        axis=3,
+    )
+    convolved = to_rows(inverse_packed(product, tables)[:, 0], WIRE)
     conv_state = convolved[0] + skip_gain[None, :] * signal
     grad_signal = convolved[1] + skip_gain[None, :] * grad_state
     gated_state = (conv_state * gate_out).astype(jnp.bfloat16)

time: 102 us -> 117 us (1.15)
  local copies, waits for them, and re-layouts: 8.92 us -> 18.5 us
  other arithmetic: 13 us -> 18.4 us
  matrix products: 20.3 us -> 17.7 us
  waiting for transfers between devices: 19.1 us -> 21.5 us
    concatenate x1 -> x3, other arithmetic: 0.14 us -> 4.68 us  [reversed_conjugate(): even_k = jnp.roll(jnp.flip(even, axis=-2), 1, axis=-2)]
    rev x0 -> x2, local copies, waits for them, and re-layouts: none -> 3.88 us  [the longest x1 1.95 us: reversed_conjugate(): odd_rev = jnp.flip(odd, axis=(-2, -1))]
    slice x0 -> x3, local copies, waits for them, and re-layouts: none -> 2.66 us  [reversed_conjugate(): even_k = jnp.roll(jnp.flip(even, axis=-2), 1, axis=-2)]
    unnamed x27 -> x53, local copies, waits for them, and re-layouts: 4.24 us -> 6.88 us
    all_to_all x2, waiting for transfers between devices: 3.78 us -> 6.12 us  [to_columns(): lax.all_to_all(jnp.swapaxes(rows, 1, 2).astype(wire), 'seq', split_axis=1...]
    another operation x4 -> x7, other arithmetic: 3.05 us -> 4.95 us  [the longest x1 1.59 us: reversed_conjugate(): rev = jnp.stack([even_rev, odd_rev], axis=2)]
    dot_general x2 -> x1, matrix products: 2.29 us -> 0.58 us  [forward_spectrum(): jnp.einsum('erkp,bcpm->bcerkm', stage_a, columns, precision=STAGE_A_PRECI...]
    dot_general x2 -> x1, matrix products: 3.81 us -> 2.45 us  [forward_spectrum(): jnp.einsum('bcerkm,rmsq->bceskq', spread, stage_b, precision=STAGE_B_PREC...]
  transfers between devices with their start and end apart: 16 -> 16, of which waited for: 5 -> 5; matrix products, arithmetic and copies ran while one was open for 25% -> 18% of each run, Pallas kernels for 0% -> 0%
where the time goes in v12:
time: 117 us; the launch traced here: 115 us
  starting transfers between devices  28.8 us (25%)
  waiting for transfers between devices  21.5 us (18%)
  local copies, waits for them, and re-layouts  18.5 us (16%)
  other arithmetic  18.4 us (16%)
  matrix products  17.7 us (15%)
  blocking collectives  9.32 us (8%)
  between operations  1.26 us (1%)
    ppermute x6, waiting for transfers between devices, panel_reduce_scatter(): lax.ppermute(sent, 'panel', [(i, (i + k) % count) for i in range(count)])  14.7 us
    ppermute x6, starting transfers between devices, panel_parts(): lax.ppermute(value, 'panel', [(i, (i + k) % count) for i in range(count)])  10.4 us
    all_to_all x1, blocking collectives, to_rows(): lax.all_to_all(columns.astype(wire), 'seq', split_axis=2, concat_axis=1,...  9.32 us
    all_to_all x2, starting transfers between devices, to_columns(): lax.all_to_all(jnp.swapaxes(rows, 1, 2).astype(wire), 'seq', split_axis=1...  7.96 us
    ppermute x6, starting transfers between devices, panel_reduce_scatter(): lax.ppermute(sent, 'panel', [(i, (i + k) % count) for i in range(count)])  7.07 us
    unnamed x53, local copies, waits for them, and re-layouts  6.88 us
    all_to_all x2, waiting for transfers between devices, to_columns(): lax.all_to_all(jnp.swapaxes(rows, 1, 2).astype(wire), 'seq', split_axis=1...  6.12 us
    concatenate x3, other arithmetic, reversed_conjugate(): even_k = jnp.roll(jnp.flip(even, axis=-2), 1, axis=-2)  4.68 us
  transfers between devices with their start and end apart: 16, of which 5 were waited for; matrix products, arithmetic and copies ran while one was open for 18% of the time, Pallas kernels for 0%

profile of v12, /device:TPU:0, one launch (start us, length us, event | category | flops | bytes accessed | tf_op | source)
XLA Modules:
  0.0 115.3 jit_solution(1857140088433515272)
XLA Ops:
  0.7 3.1 %collective-permute-start = (bf16[256,256]{1,0:T(8,128)(2,1)}, bf16[256,256]{1,0:T(8,128)(2,1)}, u32[]{:S(2)}, u32[]{:S(2)}) collective-permute-start(bf16[256,256]{1,0:T(8,128)(2,1)} %param.7), channel_id=1, source_target_pairs={{0,1},{1,2},{2,3},{3,0},{4,5},{5,6},{6,7},{7,4},{8,9},{9,10},{10,1... | collective-permute-start | bytes 393224 | tf_op jit(solution)/shard_map/ppermute | solution.py:25
  3.8 2.1 %collective-permute-start.2 = (bf16[256,256]{1,0:T(8,128)(2,1)}, bf16[256,256]{1,0:T(8,128)(2,1)}, u32[]{:S(2)}, u32[]{:S(2)}) collective-permute-start(bf16[256,256]{1,0:T(8,128)(2,1)} %param.7), channel_id=1, source_target_pairs={{0,3},{1,0},{2,1},{3,2},{4,7},{5,4},{6,5},{7,6},{8,11},{9,8},{10,9... | collective-permute-start | bytes 393224 | tf_op jit(solution)/shard_map/ppermute | solution.py:25
  5.9 0.9 collective-permute-start.1
  6.8 1.6 %collective-permute-start.4 = (bf16[256,256]{1,0:T(8,128)(2,1)}, bf16[256,256]{1,0:T(8,128)(2,1)}, u32[]{:S(2)}, u32[]{:S(2)}) collective-permute-start(bf16[256,256]{1,0:T(8,128)(2,1)} %param.8), channel_id=1, source_target_pairs={{0,1},{1,2},{2,3},{3,0},{4,5},{5,6},{6,7},{7,4},{8,9},{9,10},{10,1... | collective-permute-start | bytes 393224 | tf_op jit(solution)/shard_map/ppermute | solution.py:25
  8.4 2.2 %collective-permute-start.6 = (bf16[256,256]{1,0:T(8,128)(2,1)}, bf16[256,256]{1,0:T(8,128)(2,1)}, u32[]{:S(2)}, u32[]{:S(2)}) collective-permute-start(bf16[256,256]{1,0:T(8,128)(2,1)} %param.8), channel_id=1, source_target_pairs={{0,3},{1,0},{2,1},{3,2},{4,7},{5,4},{6,5},{7,6},{8,11},{9,8},{10,9... | collective-permute-start | bytes 393224 | tf_op jit(solution)/shard_map/ppermute | solution.py:25
  10.6 1.9 %copy.79 = f32[1,256,256]{1,0,2:T(1,128)} copy(f32[1,256,256]{2,1,0:T(8,128)} %bitcast.260) | data formatting | bytes 524288 | tf_op jit(solution)/shard_map/broadcast_in_dim | solution.py:150
  12.5 3.7 %all-to-all-start.1 = ((f32[1,256,256]{2,0,1:T(1,128)}), f32[1,256,256]{2,0,1:T(1,128)S(1)}, u32[]{:S(2)}, u32[]{:S(2)}) async-start(f32[1,256,256]{2,0,1:T(1,128)} %bitcast.43), calls=%async_computation.1 | async-start | bytes 524288 | tf_op jit(solution)/shard_map/all_to_all | solution.py:85
  18.1 1.8 %fusion.81 = (f32[256,1,256]{2,0,1:T(8,128)}, f32[256,1,256]{2,0,1:T(8,128)}) fusion(), kind=kLoop, calls=%fused_computation.143 | loop fusion | flops 983040 | bytes 524288 | tf_op jit(solution)/shard_map/sin | solution.py:62
  19.9 1.7 %fusion.83 = f32[256,1,256]{2,0,1:T(8,128)} fusion(), kind=kLoop, calls=%fused_computation.145 | loop fusion | flops 1048576 | bytes 262144 | tf_op jit(solution)/shard_map/neg | solution.py:67
  23.1 1.4 %fusion.29 = (f32[1,256,2,256]{3,1,0,2:T(8,128)}, f32[1,256,2,256]{3,1,2,0:T(8,128)}, f32[1,256,2,256]{3,1,2,0:T(8,128)}, f32[1,256,2,256]{3,1,0,2:T(8,128)}) fusion(f32[256,1,256]{2,0,1:T(8,128)S(1)} %copy-done.14, f32[256,1,256]{2,0,1:T(8,128)S(1)} %copy-done.13, f32[256,1,256]{2,0,1:T(8,128)S(1)} %copy-done.15), kind=kLoop, calls=%fused_computation.70 | loop fusion | flops 524288 | bytes 2883584 | tf_op jit(solution)/shard_map/stack | solution.py:63
  25.6 1.2 %convolution_add_fusion.1 = f32[3,256,256]{1,2,0:T(8,128)S(1)} fusion(f32[3,256,256]{1,2,0:T(8,128)S(1)} %fusion.45, bf16[3,1024,256]{2,1,0:T(8,128)(2,1)S(1)} %copy-done, s32[]{:T(128)S(6)} %select_n.180, bf16[256,256]{1,0:T(8,128)(2,1)} %collective-permute-done), kind=kOutput, calls=%fused_computation.7 | convolution fusion | flops 100859904 | bytes 2097156 | tf_op jit(solution)/shard_map/td,jdc->jtc/dot_general | solution.py:154
  26.8 1.2 %fusion.38 = f32[3,256,256]{1,2,0:T(8,128)S(1)} fusion(bf16[3,1024,256]{2,1,0:T(8,128)(2,1)S(1)} %copy-done, s32[]{:T(128)S(6)} %select_n.184, bf16[256,256]{1,0:T(8,128)(2,1)} %collective-permute-done.2), kind=kOutput, calls=%fused_computation.95 | convolution fusion | flops 100663296 | bytes 1310724 | tf_op jit(solution)/shard_map/td,jdc->jtc/dot_general | solution.py:154
  28.0 1.2 %fusion.2 = bf16[3,256,256]{2,1,0:T(8,128)(2,1)S(1)} fusion(f32[3,256,256]{1,2,0:T(8,128)S(1)} %fusion.38, f32[3,256,256]{1,2,0:T(8,128)S(1)} %convolution_add_fusion.1, bf16[3,1024,256]{2,1,0:T(8,128)(2,1)S(1)} %copy-done, s32[]{:T(128)S(6)} %select_n.182, bf16[256,256]{1,0:T(8,128)(2,1)} %collective-permute-done.1), kind=kOutput, calls=%fused_computation.10 | convolution fusion | flops 101253120 | bytes 2490372 | tf_op jit(solution)/shard_map/td,jdc->jtc/dot_general | solution.py:154
  29.2 2.1 %collective-permute-start.3 = (bf16[3,2,256]{2,1,0:T(2,128)(2,1)S(1)}, bf16[3,2,256]{2,1,0:T(2,128)(2,1)S(1)}, u32[]{:S(2)}, u32[]{:S(2)}) collective-permute-start(bf16[3,2,256]{2,1,0:T(2,128)(2,1)S(1)} %slice.157), channel_id=1, source_target_pairs={{0,4},{4,8},{8,12},{12,16},{16,20},{20,24},{24,28},{1,5},{5,9},{9,... | collective-permute-start | bytes 9224 | tf_op jit(solution)/shard_map/ppermute | solution.py:17
  31.3 1.1 convolution_add_fusion.3
  32.5 1.1 fusion.85
  35.4 0.9 copy.44
  36.2 4.2 %all-to-all-start = ((bf16[2,256,256]{2,0,1:T(2,128)(2,1)}), bf16[2,256,256]{2,0,1:T(2,128)(2,1)}, u32[]{:S(2)}, u32[]{:S(2)}) async-start(bf16[2,256,256]{2,0,1:T(2,128)(2,1)} %copy.44), calls=%async_computation | async-start | bytes 524288 | tf_op jit(solution)/shard_map/all_to_all | solution.py:85
  41.1 6.1 %all-to-all-done = bf16[2,256,256]{2,0,1:T(2,128)(2,1)} async-done(((bf16[2,256,256]{2,0,1:T(2,128)(2,1)}), bf16[2,256,256]{2,0,1:T(2,128)(2,1)}, u32[]{:S(2)}, u32[]{:S(2)}) %all-to-all-start) | async-done | bytes 262176 | tf_op jit(solution)/shard_map/all_to_all | solution.py:85
  47.2 1.4 %convolution_bitcast_fusion.4 = f32[1,32,2,2,8,256]{5,4,3,2,1,0:T(8,128)S(1)} fusion(bf16[2,8,32,256]{3,0,2,1:T(2,128)(2,1)} %bitcast.20, f32[2,2,8,1,8]{4,2,3,1,0:T(8,128)S(1)} %get-tuple-element.38, f32[2,2,8,1,8]{4,2,3,1,0:T(8,128)S(1)} %get-tuple-element.31), kind=kOutput, calls=%fused_computation.4 | convolution fusion | flops 25166336 | bytes 1312768 | tf_op jit(solution)/shard_map/erkip,icpm->cerkm/dot_general | solution.py:111
  49.0 1.2 %maximum_bitcast_fusion.3 = (f32[32,2,2,8,256]{4,3,2,1,0:T(8,128)S(1)}, f32[32,2,2,8,256]{4,3,2,1,0:T(8,128)}) fusion(f32[1,32,2,1,8,256]{5,4,3,2,1,0:T(8,128)S(1)} %get-tuple-element.26, f32[1,32,2,1,8,256]{5,4,3,2,1,0:T(8,128)S(1)} %get-tuple-element.27, f32[1,32,2,1,8,256]{5,4,3,2,1,0:T(8,128)S(1)} %get-tuple-element.13, ...), kind=kLoop, calls=%fused_computation.31 | loop fusion | flops 524288 | bytes 4194304 | tf_op jit(solution)/shard_map/reshape.14
  50.4 1.5 %convolution_bitcast_fusion.3 = f32[1,32,2,2,8,256]{5,1,4,2,3,0:T(8,128)S(1)} fusion(f32[32,2,2,8,256]{4,3,2,1,0:T(8,128)S(1)} %get-tuple-element.46, f32[1,256,2,256]{3,1,0,2:T(8,128)S(1)} %copy-done.6, f32[1,256,2,256]{3,1,0,2:T(8,128)S(1)} %copy-done.4), kind=kOutput, calls=%fused_computation.3 | convolution fusion | flops 805568512 | bytes 3145728 | tf_op jit(solution)/shard_map/bcerkm,rmsq->bceskq/dot_general | solution.py:113
  51.9 0.9 slice_bitcast_fusion.1
  52.8 0.8 slice.172
  53.6 1.8 %slice.139 = f32[1,32,2,7,256]{4,1,3,2,0:T(8,128)} reverse(f32[1,32,2,7,256]{4,1,3,2,0:T(8,128)} %slice.172), dimensions={3} | reverse | bytes 917504 | tf_op jit(solution)/shard_map/jit(_roll_static)/slice | solution.py:120
  55.4 1.8 %fusion.63 = f32[1,32,2,8,1]{4,1,3,2,0:T(8,128)} fusion(f32[1,32,2,7,256]{4,1,3,2,0:T(8,128)} %slice.139, f32[1,32,2,1,256]{4,1,3,2,0:T(8,128)S(1)} %slice.171), kind=kLoop, calls=%fused_computation.112 | loop fusion | flops 512 | bytes 526336 | tf_op jit(solution)/shard_map/jit(_roll_static)/concatenate | solution.py:120
  57.3 2.0 %fusion.25 = f32[1,32,2,8,255]{4,1,3,2,0:T(8,128)} fusion(f32[1,32,2,7,256]{4,1,3,2,0:T(8,128)} %slice.139, f32[1,32,2,1,256]{4,1,3,2,0:T(8,128)S(1)} %slice.171), kind=kLoop, calls=%fused_computation.66 | loop fusion | flops 130560 | bytes 1046528 | tf_op jit(solution)/shard_map/jit(_roll_static)/concatenate | solution.py:120
  59.3 0.8 pad_maximum_fusion
  60.1 2.4 %convolution_bitcast_fusion.1 = f32[1,32,2,2,8,256]{5,1,4,2,3,0:T(8,128)} fusion(f32[32,2,2,8,256]{4,3,2,1,0:T(8,128)S(1)} %copy-done.2, f32[1,256,2,256]{3,1,0,2:T(8,128)S(1)} %copy-done.7, f32[1,256,2,256]{3,1,0,2:T(8,128)S(1)} %copy-done.5), kind=kOutput, calls=%fused_computation.1 | convolution fusion | flops 805568512 | bytes 3145728 | tf_op jit(solution)/shard_map/bcerkm,rmsq->bceskq/dot_general | solution.py:103
  62.6 1.9 %reverse.4 = f32[1,32,2,8,256]{4,1,3,2,0:T(8,128)} reverse(f32[1,32,2,8,256]{4,1,3,2,0:T(8,128)} %bitcast.256), dimensions={4} | reverse | bytes 1048576
  64.5 2.0 %slice.285 = f32[1,32,2,8,255]{4,1,3,2,0:T(8,128)} slice(f32[1,32,2,8,256]{4,1,3,2,0:T(8,128)} %reverse.4), slice={[0:1], [0:32], [0:2], [0:8], [1:256]} | slice | bytes 1044480
  66.6 1.9 %rev.10 = f32[1,32,2,8,256]{4,1,3,2,0:T(8,128)} reverse(f32[1,32,2,8,256]{4,1,3,2,0:T(8,128)} %pad_maximum_fusion), dimensions={4} | reverse | bytes 1048576 | tf_op jit(solution)/shard_map/jit(_flip)/rev | solution.py:121
  68.5 1.9 %rev.11 = f32[1,32,2,8,256]{4,1,3,2,0:T(8,128)} reverse(f32[1,32,2,8,256]{4,1,3,2,0:T(8,128)} %get-tuple-element.17), dimensions={3,4} | reverse | bytes 1048576 | tf_op jit(solution)/shard_map/jit(_flip)/rev | solution.py:119
  70.4 1.6 %fusion.36 = f32[1,32,1,2,8,256]{5,1,4,2,3,0:T(8,128)S(1)} fusion(f32[1,32,2,8,256]{4,1,3,2,0:T(8,128)} %rev.10, f32[1,32,2,8,255]{4,1,3,2,0:T(8,128)} %slice.285, f32[1,32,2,8,1]{4,1,3,2,0:T(8,128)} %fusion.63, pred[8]{0:T(512)(128)(4,1)S(1)} %iota_compare_fusion), kind=kLoop, calls=%fused_computation.83 | loop fusion | flops 262144 | bytes 1572872 | tf_op jit(solution)/shard_map/stack | solution.py:124
  72.6 0.9 copy-done.16
  73.7 1.4 %convolution_bitcast_fusion = f32[1,32,2,2,8,256]{5,4,3,2,1,0:T(8,128)S(1)} fusion(f32[1,256,2,256]{3,1,2,0:T(8,128)S(1)} %copy-done.16, f32[1,256,2,256]{3,1,2,0:T(8,128)S(1)} %copy-done.17, f32[32,2,2,8,256,1]{4,0,3,1,2,5:T(8,128)S(1)} %maximum_bitcast_fusion.5), kind=kOutput, calls=%fused_computation | convolution fusion | flops 805568512 | bytes 3145728 | tf_op jit(solution)/shard_map/bceskq,sqrm->bcerkm/dot_general | solution.py:130
  76.0 9.3 %all_to_all.39 = bf16[2,32,8,256]{3,0,1,2:T(2,128)(2,1)S(1)} all-to-all(bf16[2,32,8,256]{3,0,1,2:T(2,128)(2,1)S(1)} %copy.60), channel_id=1, replica_groups=mesh['seq'=8,'panel'=4] {'seq'}, dimensions={2} | all-to-all | bytes 524288 | tf_op jit(solution)/shard_map/all_to_all | solution.py:93
  85.3 0.9 bitcast_convert_fusion
  86.2 1.2 %copy.62 = f32[2,256,256]{1,2,0:T(8,128)S(1)} copy(f32[2,256,256]{2,1,0:T(8,128)} %bitcast.257) | data formatting | bytes 1048576 | tf_op jit(solution)/shard_map/transpose | solution.py:96
  87.6 0.8 copy-done.11
  88.9 1.3 %collective-permute-start.10 = (f32[3,2,256]{2,1,0:T(2,128)S(1)}, f32[3,2,256]{2,1,0:T(2,128)S(1)}, u32[]{:S(2)}, u32[]{:S(2)}) collective-permute-start(f32[3,2,256]{2,1,0:T(2,128)S(1)} %slice.188), channel_id=1, source_target_pairs={{4,0},{8,4},{12,8},{16,12},{20,16},{24,20},{28,24},{5,1},{9,5},{13... | collective-permute-start | bytes 18440 | tf_op jit(solution)/shard_map/ppermute | solution.py:17
  90.4 2.6 %collective-permute-start.8 = (bf16[256,256]{1,0:T(8,128)(2,1)S(1)}, bf16[256,256]{1,0:T(8,128)(2,1)S(1)}, u32[]{:S(2)}, u32[]{:S(2)}) collective-permute-start(bf16[256,256]{1,0:T(8,128)(2,1)S(1)} %convolution_convert_fusion.1), channel_id=1, source_target_pairs={{0,2},{1,3},{2,0},{3,1},{4,6},{5,7},{6,4},{7,5},{8,10},{9,11},{10,... | collective-permute-start | bytes 393224 | tf_op jit(solution)/shard_map/ppermute | solution.py:36
  93.1 3.8 %collective-permute-start.9 = (bf16[256,256]{1,0:T(8,128)(2,1)S(1)}, bf16[256,256]{1,0:T(8,128)(2,1)S(1)}, u32[]{:S(2)}, u32[]{:S(2)}) collective-permute-start(bf16[256,256]{1,0:T(8,128)(2,1)S(1)} %convolution_convert_fusion), channel_id=1, source_target_pairs={{0,3},{1,0},{2,1},{3,2},{4,7},{5,4},{6,5},{7,6},{8,11},{9,8},{10,9... | collective-permute-start | bytes 393224 | tf_op jit(solution)/shard_map/ppermute | solution.py:36
  98.8 4.3 %collective-permute-done.8 = bf16[256,256]{1,0:T(8,128)(2,1)S(1)} collective-permute-done((bf16[256,256]{1,0:T(8,128)(2,1)S(1)}, bf16[256,256]{1,0:T(8,128)(2,1)S(1)}, u32[]{:S(2)}, u32[]{:S(2)}) %collective-permute-start.8) | collective-permute-done | bytes 131104 | tf_op jit(solution)/shard_map/ppermute | solution.py:36
  103.2 1.7 %collective-permute-done.9 = bf16[256,256]{1,0:T(8,128)(2,1)S(1)} collective-permute-done((bf16[256,256]{1,0:T(8,128)(2,1)S(1)}, bf16[256,256]{1,0:T(8,128)(2,1)S(1)}, u32[]{:S(2)}, u32[]{:S(2)}) %collective-permute-start.9) | collective-permute-done | bytes 131104 | tf_op jit(solution)/shard_map/ppermute | solution.py:36
  104.8 0.9 add_convert_fusion
  105.7 8.6 %collective-permute-done.12 = bf16[256,256]{1,0:T(8,128)(2,1)S(1)} collective-permute-done((bf16[256,256]{1,0:T(8,128)(2,1)S(1)}, bf16[256,256]{1,0:T(8,128)(2,1)S(1)}, u32[]{:S(2)}, u32[]{:S(2)}) %collective-permute-start.12) | collective-permute-done | bytes 131104 | tf_op jit(solution)/shard_map/ppermute | solution.py:36
  114.3 1.0 fusion.56
  (108 shorter events, 11.5 us)
Async XLA Ops:
  0.6 20.9 %copy-start = (bf16[3,1024,256]{2,1,0:T(8,128)(2,1)S(1)}, bf16[3,1024,256]{2,1,0:T(8,128)(2,1)}, u32[]{:S(2)}) copy-start(bf16[3,1024,256]{2,1,0:T(8,128)(2,1)} %param.9) | copy-start | bytes 4718596
  0.6 20.9 %copy-start.18 = (bf16[256,256]{1,0:T(8,128)(2,1)S(1)}, bf16[256,256]{1,0:T(8,128)(2,1)}, u32[]{:S(2)}) copy-start(bf16[256,256]{1,0:T(8,128)(2,1)} %param.7) | copy-start | bytes 393220
  0.7 20.9 %copy-start.21 = (f32[3,3,256]{2,1,0:T(4,128)S(1)}, f32[3,3,256]{2,1,0:T(4,128)}, u32[]{:S(2)}) copy-start(f32[3,3,256]{2,1,0:T(4,128)} %param.10) | copy-start | bytes 27652
  0.7 24.5 %collective-permute-start = (bf16[256,256]{1,0:T(8,128)(2,1)}, bf16[256,256]{1,0:T(8,128)(2,1)}, u32[]{:S(2)}, u32[]{:S(2)}) collective-permute-start(bf16[256,256]{1,0:T(8,128)(2,1)} %param.7), channel_id=1, source_target_pairs={{0,1},{1,2},{2,3},{3,0},{4,5},{5,6},{6,7},{7,4},{8,9},{9,10},{10,1... | collective-permute-start | bytes 393224 | tf_op jit(solution)/shard_map/ppermute | solution.py:25
  3.8 23.0 %collective-permute-start.2 = (bf16[256,256]{1,0:T(8,128)(2,1)}, bf16[256,256]{1,0:T(8,128)(2,1)}, u32[]{:S(2)}, u32[]{:S(2)}) collective-permute-start(bf16[256,256]{1,0:T(8,128)(2,1)} %param.7), channel_id=1, source_target_pairs={{0,3},{1,0},{2,1},{3,2},{4,7},{5,4},{6,5},{7,6},{8,11},{9,8},{10,9... | collective-permute-start | bytes 393224 | tf_op jit(solution)/shard_map/ppermute | solution.py:25
  5.9 22.1 %collective-permute-start.1 = (bf16[256,256]{1,0:T(8,128)(2,1)}, bf16[256,256]{1,0:T(8,128)(2,1)}, u32[]{:S(2)}, u32[]{:S(2)}) collective-permute-start(bf16[256,256]{1,0:T(8,128)(2,1)} %param.7), channel_id=1, source_target_pairs={{0,2},{1,3},{2,0},{3,1},{4,6},{5,7},{6,4},{7,5},{8,10},{9,11},{10,... | collective-permute-start | bytes 393224 | tf_op jit(solution)/shard_map/ppermute | solution.py:25
  6.8 24.5 %collective-permute-start.4 = (bf16[256,256]{1,0:T(8,128)(2,1)}, bf16[256,256]{1,0:T(8,128)(2,1)}, u32[]{:S(2)}, u32[]{:S(2)}) collective-permute-start(bf16[256,256]{1,0:T(8,128)(2,1)} %param.8), channel_id=1, source_target_pairs={{0,1},{1,2},{2,3},{3,0},{4,5},{5,6},{6,7},{7,4},{8,9},{9,10},{10,1... | collective-permute-start | bytes 393224 | tf_op jit(solution)/shard_map/ppermute | solution.py:25
  8.4 24.1 %collective-permute-start.6 = (bf16[256,256]{1,0:T(8,128)(2,1)}, bf16[256,256]{1,0:T(8,128)(2,1)}, u32[]{:S(2)}, u32[]{:S(2)}) collective-permute-start(bf16[256,256]{1,0:T(8,128)(2,1)} %param.8), channel_id=1, source_target_pairs={{0,3},{1,0},{2,1},{3,2},{4,7},{5,4},{6,5},{7,6},{8,11},{9,8},{10,9... | collective-permute-start | bytes 393224 | tf_op jit(solution)/shard_map/ppermute | solution.py:25
  10.6 11.3 %copy-start.10 = (bf16[256,1024]{1,0:T(8,128)(2,1)S(1)}, bf16[256,1024]{1,0:T(8,128)(2,1)}, u32[]{:S(2)}) copy-start(bf16[256,1024]{1,0:T(8,128)(2,1)} %param.13) | copy-start | bytes 1572868
  10.6 11.3 %copy-start.19 = (bf16[256,256]{1,0:T(8,128)(2,1)S(1)}, bf16[256,256]{1,0:T(8,128)(2,1)}, u32[]{:S(2)}) copy-start(bf16[256,256]{1,0:T(8,128)(2,1)} %param.8) | copy-start | bytes 393220
  12.5 23.8 %all-to-all-start.1 = ((f32[1,256,256]{2,0,1:T(1,128)}), f32[1,256,256]{2,0,1:T(1,128)S(1)}, u32[]{:S(2)}, u32[]{:S(2)}) async-start(f32[1,256,256]{2,0,1:T(1,128)} %bitcast.43), calls=%async_computation.1 | async-start | bytes 524288 | tf_op jit(solution)/shard_map/all_to_all | solution.py:85
  21.6 0.7 copy-start.24
  21.6 1.4 %copy-start.20 = (s32[8,256]{1,0:T(8,128)S(1)}, s32[8,256]{1,0:T(8,128)}, u32[]{:S(2)}) copy-start(s32[8,256]{1,0:T(8,128)} %iota_multiply_fusion) | copy-start | bytes 24580
  21.6 1.4 %copy-start.22 = (s32[2,256]{1,0:T(2,128)S(1)}, s32[2,256]{1,0:T(2,128)}, u32[]{:S(2)}) copy-start(s32[2,256]{1,0:T(2,128)} %iota_multiply_fusion.2) | copy-start | bytes 6148
  21.6 1.4 %copy-start.13 = (f32[256,1,256]{2,0,1:T(8,128)S(1)}, f32[256,1,256]{2,0,1:T(8,128)}, u32[]{:S(2)}) copy-start(f32[256,1,256]{2,0,1:T(8,128)} %get-tuple-element.44) | copy-start | bytes 786436
  21.6 1.4 %copy-start.14 = (f32[256,1,256]{2,0,1:T(8,128)S(1)}, f32[256,1,256]{2,0,1:T(8,128)}, u32[]{:S(2)}) copy-start(f32[256,1,256]{2,0,1:T(8,128)} %get-tuple-element.45) | copy-start | bytes 786436
  21.6 1.4 %copy-start.15 = (f32[256,1,256]{2,0,1:T(8,128)S(1)}, f32[256,1,256]{2,0,1:T(8,128)}, u32[]{:S(2)}) copy-start(f32[256,1,256]{2,0,1:T(8,128)} %fusion.83) | copy-start | bytes 786436
  25.2 9.1 %collective-permute-start.5 = (bf16[256,256]{1,0:T(8,128)(2,1)}, bf16[256,256]{1,0:T(8,128)(2,1)S(1)}, u32[]{:S(2)}, u32[]{:S(2)}) collective-permute-start(bf16[256,256]{1,0:T(8,128)(2,1)} %param.8), channel_id=1, source_target_pairs={{0,2},{1,3},{2,0},{3,1},{4,6},{5,7},{6,4},{7,5},{8,10},{9,11},{10,... | collective-permute-start | bytes 393224 | tf_op jit(solution)/shard_map/ppermute | solution.py:25
  29.2 5.4 %collective-permute-start.3 = (bf16[3,2,256]{2,1,0:T(2,128)(2,1)S(1)}, bf16[3,2,256]{2,1,0:T(2,128)(2,1)S(1)}, u32[]{:S(2)}, u32[]{:S(2)}) collective-permute-start(bf16[3,2,256]{2,1,0:T(2,128)(2,1)S(1)} %slice.157), channel_id=1, source_target_pairs={{0,4},{4,8},{8,12},{12,16},{16,20},{20,24},{24,28},{1,5},{5,9},{9,... | collective-permute-start | bytes 9224 | tf_op jit(solution)/shard_map/ppermute | solution.py:17
  34.5 0.7 copy-start.8
  36.2 11.0 %all-to-all-start = ((bf16[2,256,256]{2,0,1:T(2,128)(2,1)}), bf16[2,256,256]{2,0,1:T(2,128)(2,1)}, u32[]{:S(2)}, u32[]{:S(2)}) async-start(bf16[2,256,256]{2,0,1:T(2,128)(2,1)} %copy.44), calls=%async_computation | async-start | bytes 524288 | tf_op jit(solution)/shard_map/all_to_all | solution.py:85
  49.0 1.2 %copy-start.4 = (f32[1,256,2,256]{3,1,0,2:T(8,128)S(1)}, f32[1,256,2,256]{3,1,0,2:T(8,128)}, u32[]{:S(2)}) copy-start(f32[1,256,2,256]{3,1,0,2:T(8,128)} %get-tuple-element.20) | copy-start | bytes 1572868
  49.0 1.5 %copy-start.6 = (f32[1,256,2,256]{3,1,0,2:T(8,128)S(1)}, f32[1,256,2,256]{3,1,0,2:T(8,128)}, u32[]{:S(2)}) copy-start(f32[1,256,2,256]{3,1,0,2:T(8,128)} %get-tuple-element.25) | copy-start | bytes 1572868
  55.4 3.9 %copy-start.1 = (f32[1,32,2,7,256]{4,1,3,2,0:T(8,128)S(1)}, f32[1,32,2,7,256]{4,1,3,2,0:T(8,128)}, u32[]{:S(2)}) copy-start(f32[1,32,2,7,256]{4,1,3,2,0:T(8,128)} %slice.139) | copy-start | bytes 1376260
  55.4 4.7 %copy-start.2 = (f32[32,2,2,8,256]{4,3,2,1,0:T(8,128)S(1)}, f32[32,2,2,8,256]{4,3,2,1,0:T(8,128)}, u32[]{:S(2)}) copy-start(f32[32,2,2,8,256]{4,3,2,1,0:T(8,128)} %get-tuple-element.47) | copy-start | bytes 3145732
  55.4 4.7 %copy-start.5 = (f32[1,256,2,256]{3,1,0,2:T(8,128)S(1)}, f32[1,256,2,256]{3,1,0,2:T(8,128)}, u32[]{:S(2)}) copy-start(f32[1,256,2,256]{3,1,0,2:T(8,128)} %get-tuple-element.20) | copy-start | bytes 1572868
  55.4 4.7 %copy-start.7 = (f32[1,256,2,256]{3,1,0,2:T(8,128)S(1)}, f32[1,256,2,256]{3,1,0,2:T(8,128)}, u32[]{:S(2)}) copy-start(f32[1,256,2,256]{3,1,0,2:T(8,128)} %get-tuple-element.25) | copy-start | bytes 1572868
  70.4 1.6 %copy-start.3 = (f32[1,32,2,2,8,256]{5,1,4,2,3,0:T(8,128)S(1)}, f32[1,32,2,2,8,256]{5,1,4,2,3,0:T(8,128)}, u32[]{:S(2)}) copy-start(f32[1,32,2,2,8,256]{5,1,4,2,3,0:T(8,128)} %convolution_bitcast_fusion.1) | copy-start | bytes 3145732
  70.4 1.7 %copy-start.12 = (f32[1,32,2,8,256]{4,1,3,2,0:T(8,128)S(1)}, f32[1,32,2,8,256]{4,1,3,2,0:T(8,128)}, u32[]{:S(2)}) copy-start(f32[1,32,2,8,256]{4,1,3,2,0:T(8,128)} %rev.11) | copy-start | bytes 1572868
  72.5 1.0 copy-start.16
  72.5 1.2 %copy-start.17 = (f32[1,256,2,256]{3,1,2,0:T(8,128)S(1)}, f32[1,256,2,256]{3,1,2,0:T(8,128)}, u32[]{:S(2)}) copy-start(f32[1,256,2,256]{3,1,2,0:T(8,128)} %get-tuple-element.24) | copy-start | bytes 1572868
  75.7 11.7 %copy-start.9 = (f32[256,256]{1,0:T(8,128)S(1)}, f32[256,256]{1,0:T(8,128)}, u32[]{:S(2)}) copy-start(f32[256,256]{1,0:T(8,128)} %copy-done.8) | copy-start | bytes 786436
  75.7 11.7 %copy-start.23 = (f32[256]{0:T(256)S(1)}, f32[256]{0:T(256)}, u32[]{:S(2)}) copy-start(f32[256]{0:T(256)} %param.11) | copy-start | bytes 3076
  87.4 1.0 copy-start.11
  88.9 8.0 %collective-permute-start.10 = (f32[3,2,256]{2,1,0:T(2,128)S(1)}, f32[3,2,256]{2,1,0:T(2,128)S(1)}, u32[]{:S(2)}, u32[]{:S(2)}) collective-permute-start(f32[3,2,256]{2,1,0:T(2,128)S(1)} %slice.188), channel_id=1, source_target_pairs={{4,0},{8,4},{12,8},{16,12},{20,16},{24,20},{28,24},{5,1},{9,5},{13... | collective-permute-start | bytes 18440 | tf_op jit(solution)/shard_map/ppermute | solution.py:17
  90.4 12.7 %collective-permute-start.8 = (bf16[256,256]{1,0:T(8,128)(2,1)S(1)}, bf16[256,256]{1,0:T(8,128)(2,1)S(1)}, u32[]{:S(2)}, u32[]{:S(2)}) collective-permute-start(bf16[256,256]{1,0:T(8,128)(2,1)S(1)} %convolution_convert_fusion.1), channel_id=1, source_target_pairs={{0,2},{1,3},{2,0},{3,1},{4,6},{5,7},{6,4},{7,5},{8,10},{9,11},{10,... | collective-permute-start | bytes 393224 | tf_op jit(solution)/shard_map/ppermute | solution.py:36
  93.1 10.1 %collective-permute-start.7 = (bf16[256,256]{1,0:T(8,128)(2,1)S(1)}, bf16[256,256]{1,0:T(8,128)(2,1)S(1)}, u32[]{:S(2)}, u32[]{:S(2)}) collective-permute-start(bf16[256,256]{1,0:T(8,128)(2,1)S(1)} %convolution_convert_fusion.2), channel_id=1, source_target_pairs={{0,1},{1,2},{2,3},{3,0},{4,5},{5,6},{6,7},{7,4},{8,9},{9,10},{10,1... | collective-permute-start | bytes 393224 | tf_op jit(solution)/shard_map/ppermute | solution.py:36
  93.1 11.8 %collective-permute-start.9 = (bf16[256,256]{1,0:T(8,128)(2,1)S(1)}, bf16[256,256]{1,0:T(8,128)(2,1)S(1)}, u32[]{:S(2)}, u32[]{:S(2)}) collective-permute-start(bf16[256,256]{1,0:T(8,128)(2,1)S(1)} %convolution_convert_fusion), channel_id=1, source_target_pairs={{0,3},{1,0},{2,1},{3,2},{4,7},{5,4},{6,5},{7,6},{8,11},{9,8},{10,9... | collective-permute-start | bytes 393224 | tf_op jit(solution)/shard_map/ppermute | solution.py:36
  97.9 16.5 %collective-permute-start.12 = (bf16[256,256]{1,0:T(8,128)(2,1)S(1)}, bf16[256,256]{1,0:T(8,128)(2,1)S(1)}, u32[]{:S(2)}, u32[]{:S(2)}) collective-permute-start(bf16[256,256]{1,0:T(8,128)(2,1)S(1)} %fusion.8), channel_id=1, source_target_pairs={{0,2},{1,3},{2,0},{3,1},{4,6},{5,7},{6,4},{7,5},{8,10},{9,11},{10,... | collective-permute-start | bytes 393224 | tf_op jit(solution)/shard_map/ppermute | solution.py:36
  97.9 16.4 %collective-permute-start.11 = (bf16[256,256]{1,0:T(8,128)(2,1)S(1)}, bf16[256,256]{1,0:T(8,128)(2,1)S(1)}, u32[]{:S(2)}, u32[]{:S(2)}) collective-permute-start(bf16[256,256]{1,0:T(8,128)(2,1)S(1)} %fusion.7), channel_id=1, source_target_pairs={{0,1},{1,2},{2,3},{3,0},{4,5},{5,6},{6,7},{7,4},{8,9},{9,10},{10,1... | collective-permute-start | bytes 393224 | tf_op jit(solution)/shard_map/ppermute | solution.py:36
  103.2 11.2 %collective-permute-start.13 = (bf16[256,256]{1,0:T(8,128)(2,1)S(1)}, bf16[256,256]{1,0:T(8,128)(2,1)S(1)}, u32[]{:S(2)}, u32[]{:S(2)}) collective-permute-start(bf16[256,256]{1,0:T(8,128)(2,1)S(1)} %fusion.9), channel_id=1, source_target_pairs={{0,3},{1,0},{2,1},{3,2},{4,7},{5,4},{6,5},{7,6},{8,11},{9,8},{10,9... | collective-permute-start | bytes 393224 | tf_op jit(solution)/shard_map/ppermute | solution.py:36

commit v13 on v11

--- a/solution.py
+++ b/solution.py
@@ -88,12 +88,19 @@
     return columns.reshape(batch, columns.shape[1], shard_count, row_count)
 
 
-def to_rows(columns, wire=jnp.float32):
+def to_rows(columns, wire=jnp.float32, rim=0):
     batch, chan_count, shard_count, row_count = columns.shape
+    if rim:
+        ahead = jnp.concatenate(
+            [columns[:, :, 1:, :rim], jnp.zeros_like(columns[:, :, :1, :rim])], axis=2
+        )
+        columns = jnp.concatenate([columns, ahead], axis=3)
     rows = lax.all_to_all(
         columns.astype(wire), "seq", split_axis=2, concat_axis=1, tiled=True
     ).astype(jnp.float32)
-    return jnp.swapaxes(rows.reshape(batch, shard_count * chan_count, row_count), 1, 2)
+    return jnp.swapaxes(
+        rows.reshape(batch, shard_count * chan_count, row_count + rim), 1, 2
+    )
 
 
 def forward_spectrum(columns, tables):
@@ -147,6 +154,10 @@
     gate_out, gate_in, value_path = (filtered[0], filtered[1], filtered[2])
     signal = value_path * gate_in
     grad_state = grad_gated * gate_out
+    rim = tap_count - 1
+    ahead = shifted(
+        jnp.stack([gate_out[:rim], gate_in[:rim], value_path[:rim], grad_gated[:rim]]), "seq", -1
+    )
     spectra = forward_spectrum(to_columns(jnp.stack([signal, grad_state]), WIRE), tables)
     filt_real, filt_imag = filt_spec[:, :, :, 0], filt_spec[:, :, :, 1]
     sig_real, sig_imag = spectra[0:1, :, :, 0], spectra[0:1, :, :, 1]
@@ -163,9 +174,14 @@
             ),
         ]
     )
-    convolved = to_rows(inverse_spectrum(product, tables), WIRE)
-    conv_state = convolved[0] + skip_gain[None, :] * signal
-    grad_signal = convolved[1] + skip_gain[None, :] * grad_state
+    convolved = to_rows(inverse_spectrum(product, tables), WIRE, rim)
+    conv_state = convolved[0, :row_count] + skip_gain[None, :] * signal
+    grad_signal = convolved[1, :row_count] + skip_gain[None, :] * grad_state
+    conv_ahead = convolved[0, row_count:] + skip_gain[None, :] * (ahead[2] * ahead[1])
+    grad_signal_ahead = convolved[1, row_count:] + skip_gain[None, :] * (ahead[3] * ahead[0])
+    upstream_ahead = jnp.stack(
+        [ahead[3] * conv_ahead, grad_signal_ahead * ahead[2], grad_signal_ahead * ahead[1]]
+    )
     gated_state = (conv_state * gate_out).astype(jnp.bfloat16)
     block_out = panel_reduce_scatter(
         lambda dest: jnp.dot(
@@ -178,8 +194,7 @@
     grad_value = grad_signal * gate_in
     grad_gate_in = grad_signal * value_path
     upstream = jnp.stack([grad_gate_out, grad_gate_in, grad_value])
-    after_rim = shifted(upstream[:, : tap_count - 1, :], "seq", -1)
-    widened = jnp.concatenate([upstream, after_rim], axis=1)
+    widened = jnp.concatenate([upstream, upstream_ahead], axis=1)
     grad_projected = short_kernel[0][:, None, :] * widened[:, :row_count, :]
     for tap_index in range(1, tap_count):
         grad_projected = (

time: 102 us -> 103 us (level)
  blocking collectives: 9.32 us -> 0 us
  waiting for transfers between devices: 19.1 us -> 25.4 us
  starting transfers between devices: 28.8 us -> 32.3 us
  other arithmetic: 13 us -> 14.2 us
    all_to_all x1 -> x0, blocking collectives: 9.32 us -> none  [to_rows(): lax.all_to_all(columns.astype(wire), 'seq', split_axis=2, concat_axis=1,...]
    all_to_all x0 -> x1, waiting for transfers between devices: none -> 6.66 us  [to_rows(): lax.all_to_all(columns.astype(wire), 'seq', split_axis=2, concat_axis=1,...]
    all_to_all x0 -> x1, starting transfers between devices: none -> 3.45 us  [to_rows(): lax.all_to_all(columns.astype(wire), 'seq', split_axis=2, concat_axis=1,...]
  transfers between devices with their start and end apart: 16 -> 17, of which waited for: 5 -> 5; matrix products, arithmetic and copies ran while one was open for 25% -> 26% of each run, Pallas kernels for 0% -> 0%
where the time goes in v13:
time: 103 us; the launch traced here: 102 us
  starting transfers between devices  32.3 us (31%)
  waiting for transfers between devices  25.4 us (25%)
  matrix products  20.3 us (20%)
  other arithmetic  14.2 us (14%)
  local copies, waits for them, and re-layouts  8.77 us (9%)
  between operations  1.22 us (1%)
    ppermute x6, waiting for transfers between devices, panel_reduce_scatter(): lax.ppermute(sent, 'panel', [(i, (i + k) % count) for i in range(count)])  14.3 us
    ppermute x6, starting transfers between devices, panel_parts(): lax.ppermute(value, 'panel', [(i, (i + k) % count) for i in range(count)])  10.3 us
    all_to_all x2, starting transfers between devices, to_columns(): lax.all_to_all(jnp.swapaxes(rows, 1, 2).astype(wire), 'seq', split_axis=1...  7.96 us
    ppermute x6, starting transfers between devices, panel_reduce_scatter(): lax.ppermute(sent, 'panel', [(i, (i + k) % count) for i in range(count)])  6.89 us
    all_to_all x1, waiting for transfers between devices, to_rows(): lax.all_to_all(columns.astype(wire), 'seq', split_axis=2, concat_axis=1,...  6.66 us
    dot_general x4, matrix products, local(): jnp.einsum('td,jdc->jtc', part, lax.dynamic_slice_in_dim(in_weight, sourc...  4.7 us
    dot_general x2, matrix products, forward_spectrum(): jnp.einsum('bcerkm,rmsq->bceskq', spread, stage_b, precision=STAGE_B_PREC...  3.81 us
    all_to_all x2, waiting for transfers between devices, to_columns(): lax.all_to_all(jnp.swapaxes(rows, 1, 2).astype(wire), 'seq', split_axis=1...  3.78 us
  transfers between devices with their start and end apart: 17, of which 5 were waited for; matrix products, arithmetic and copies ran while one was open for 26% of the time, Pallas kernels for 0%

profile of v13, /device:TPU:0, one launch (start us, length us, event | category | flops | bytes accessed | tf_op | source)
XLA Modules:
  0.0 102.2 jit_solution(16370592749146353908)
XLA Ops:
  0.7 3.1 %collective-permute-start = (bf16[256,256]{1,0:T(8,128)(2,1)}, bf16[256,256]{1,0:T(8,128)(2,1)}, u32[]{:S(2)}, u32[]{:S(2)}) collective-permute-start(bf16[256,256]{1,0:T(8,128)(2,1)} %param.7), channel_id=1, source_target_pairs={{0,1},{1,2},{2,3},{3,0},{4,5},{5,6},{6,7},{7,4},{8,9},{9,10},{10,1... | collective-permute-start | bytes 393224 | tf_op jit(solution)/shard_map/ppermute | solution.py:25
  3.8 2.1 %collective-permute-start.2 = (bf16[256,256]{1,0:T(8,128)(2,1)}, bf16[256,256]{1,0:T(8,128)(2,1)}, u32[]{:S(2)}, u32[]{:S(2)}) collective-permute-start(bf16[256,256]{1,0:T(8,128)(2,1)} %param.7), channel_id=1, source_target_pairs={{0,3},{1,0},{2,1},{3,2},{4,7},{5,4},{6,5},{7,6},{8,11},{9,8},{10,9... | collective-permute-start | bytes 393224 | tf_op jit(solution)/shard_map/ppermute | solution.py:25
  5.9 0.9 collective-permute-start.1
  6.8 1.6 %collective-permute-start.4 = (bf16[256,256]{1,0:T(8,128)(2,1)}, bf16[256,256]{1,0:T(8,128)(2,1)}, u32[]{:S(2)}, u32[]{:S(2)}) collective-permute-start(bf16[256,256]{1,0:T(8,128)(2,1)} %param.8), channel_id=1, source_target_pairs={{0,1},{1,2},{2,3},{3,0},{4,5},{5,6},{6,7},{7,4},{8,9},{9,10},{10,1... | collective-permute-start | bytes 393224 | tf_op jit(solution)/shard_map/ppermute | solution.py:25
  8.4 2.2 %collective-permute-start.6 = (bf16[256,256]{1,0:T(8,128)(2,1)}, bf16[256,256]{1,0:T(8,128)(2,1)}, u32[]{:S(2)}, u32[]{:S(2)}) collective-permute-start(bf16[256,256]{1,0:T(8,128)(2,1)} %param.8), channel_id=1, source_target_pairs={{0,3},{1,0},{2,1},{3,2},{4,7},{5,4},{6,5},{7,6},{8,11},{9,8},{10,9... | collective-permute-start | bytes 393224 | tf_op jit(solution)/shard_map/ppermute | solution.py:25
  10.6 1.8 %copy.63 = f32[1,256,256]{1,0,2:T(1,128)} copy(f32[1,256,256]{2,1,0:T(8,128)} %bitcast.224) | data formatting | bytes 524288 | tf_op jit(solution)/shard_map/broadcast_in_dim | solution.py:125
  12.4 3.7 %all-to-all-start.1 = ((f32[1,256,256]{2,0,1:T(1,128)}), f32[1,256,256]{2,0,1:T(1,128)S(1)}, u32[]{:S(2)}, u32[]{:S(2)}) async-start(f32[1,256,256]{2,0,1:T(1,128)} %bitcast.36), calls=%async_computation.1 | async-start | bytes 524288 | tf_op jit(solution)/shard_map/all_to_all | solution.py:85
  16.2 0.6 iota_multiply_fusion.3
  16.8 0.7 iota_multiply_fusion
  17.5 0.6 iota_multiply_fusion.2
  18.1 1.8 %fusion.93 = (f32[256,1,256]{2,0,1:T(8,128)}, f32[256,1,256]{2,0,1:T(8,128)}) fusion(), kind=kLoop, calls=%fused_computation.133 | loop fusion | flops 983040 | bytes 524288 | tf_op jit(solution)/shard_map/sin | solution.py:62
  19.8 1.7 %fusion.95 = f32[256,1,256]{2,0,1:T(8,128)} fusion(), kind=kLoop, calls=%fused_computation.135 | loop fusion | flops 1048576 | bytes 262144 | tf_op jit(solution)/shard_map/neg | solution.py:67
  21.5 0.7 slice_bitcast_fusion.5
  22.3 1.2 %fusion.58 = f32[3,256,256]{1,2,0:T(8,128)S(1)} fusion(bf16[3,1024,256]{2,1,0:T(8,128)(2,1)S(1)} %copy-done, s32[]{:T(128)S(6)} %select_n.148, bf16[256,256]{1,0:T(8,128)(2,1)} %param.7), kind=kOutput, calls=%fused_computation.94 | convolution fusion | flops 100663296 | bytes 1310724 | tf_op jit(solution)/shard_map/td,jdc->jtc/dot_general | solution.py:129
  23.7 0.7 fusion.123
  24.4 0.8 fusion.143
  25.2 2.8 %fusion.47 = (f32[1,256,2,256]{3,1,2,0:T(8,128)}, f32[1,256,2,256]{3,1,0,2:T(8,128)}, f32[1,256,2,256]{3,1,0,2:T(8,128)}, f32[1,256,2,256]{3,1,2,0:T(8,128)}) fusion(f32[256,1,256]{2,0,1:T(8,128)} %get-tuple-element.38, f32[256,1,256]{2,0,1:T(8,128)} %fusion.95, f32[256,1,256]{2,0,1:T(8,128)} %get-tuple-element.37), kind=kLoop, calls=%fused_computation.73 | loop fusion | flops 524288 | bytes 2883584 | tf_op jit(solution)/shard_map/stack | solution.py:66
  28.4 1.2 %convolution_add_fusion.1 = f32[3,256,256]{1,2,0:T(8,128)S(1)} fusion(f32[3,256,256]{1,2,0:T(8,128)S(1)} %fusion.58, bf16[3,1024,256]{2,1,0:T(8,128)(2,1)S(1)} %copy-done, s32[]{:T(128)S(6)} %select_n.150, bf16[256,256]{1,0:T(8,128)(2,1)} %collective-permute-done), kind=kOutput, calls=%fused_computation.19 | convolution fusion | flops 100859904 | bytes 2097156 | tf_op jit(solution)/shard_map/td,jdc->jtc/dot_general | solution.py:129
  29.6 1.2 %fusion.51 = f32[3,256,256]{1,2,0:T(8,128)S(1)} fusion(bf16[3,1024,256]{2,1,0:T(8,128)(2,1)S(1)} %copy-done, s32[]{:T(128)S(6)} %select_n.154, bf16[256,256]{1,0:T(8,128)(2,1)} %collective-permute-done.2), kind=kOutput, calls=%fused_computation.87 | convolution fusion | flops 100663296 | bytes 1310724 | tf_op jit(solution)/shard_map/td,jdc->jtc/dot_general | solution.py:129
  30.8 1.2 %fusion.21 = bf16[3,256,256]{2,1,0:T(8,128)(2,1)S(1)} fusion(f32[3,256,256]{1,2,0:T(8,128)S(1)} %fusion.51, f32[3,256,256]{1,2,0:T(8,128)S(1)} %convolution_add_fusion.1, bf16[3,1024,256]{2,1,0:T(8,128)(2,1)S(1)} %copy-done, s32[]{:T(128)S(6)} %select_n.152, bf16[256,256]{1,0:T(8,128)(2,1)} %collective-permute-done.1), kind=kOutput, calls=%fused_computation.22 | convolution fusion | flops 101253120 | bytes 2490372 | tf_op jit(solution)/shard_map/td,jdc->jtc/dot_general | solution.py:129
  32.0 2.1 %collective-permute-start.3 = (bf16[3,2,256]{2,1,0:T(2,128)(2,1)S(1)}, bf16[3,2,256]{2,1,0:T(2,128)(2,1)S(1)}, u32[]{:S(2)}, u32[]{:S(2)}) collective-permute-start(bf16[3,2,256]{2,1,0:T(2,128)(2,1)S(1)} %slice.156), channel_id=1, source_target_pairs={{0,4},{4,8},{8,12},{12,16},{16,20},{20,24},{24,28},{1,5},{5,9},{9,... | collective-permute-start | bytes 9224 | tf_op jit(solution)/shard_map/ppermute | solution.py:17
  34.1 1.1 %convolution_add_fusion.3 = f32[256,256]{0,1:T(8,128)S(1)} fusion(f32[256,256]{0,1:T(8,128)S(1)} %fusion.105, bf16[256,256]{1,0:T(8,128)(2,1)} %collective-permute-done.4, bf16[256,1024]{1,0:T(8,128)(2,1)S(1)} %copy-done.3, s32[]{:T(128)S(6)} %select_n.150), kind=kOutput, calls=%fused_computation.31 | convolution fusion | flops 33619968 | bytes 786436 | tf_op jit(solution)/shard_map/dot_general | solution.py:137
  35.3 1.1 %fusion.97 = f32[256,256]{0,1:T(8,128)S(1)} fusion(bf16[256,256]{1,0:T(8,128)(2,1)} %collective-permute-done.6, bf16[256,1024]{1,0:T(8,128)(2,1)S(1)} %copy-done.3, s32[]{:T(128)S(6)} %select_n.154), kind=kOutput, calls=%fused_computation.137 | convolution fusion | flops 33554432 | bytes 524292 | tf_op jit(solution)/shard_map/dot_general | solution.py:137
  36.4 0.7 collective-permute-done.5
  38.2 0.9 copy.32
  39.1 4.2 %all-to-all-start = ((bf16[2,256,256]{2,0,1:T(2,128)(2,1)}), bf16[2,256,256]{2,0,1:T(2,128)(2,1)}, u32[]{:S(2)}, u32[]{:S(2)}) async-start(bf16[2,256,256]{2,0,1:T(2,128)(2,1)} %copy.32), calls=%async_computation | async-start | bytes 524288 | tf_op jit(solution)/shard_map/all_to_all | solution.py:85
  44.2 0.8 copy-done.5
  45.1 1.1 %convolution_bitcast_fusion.1 = f32[1,32,2,2,8,256]{5,1,4,2,0,3:T(8,128)S(1)} fusion(f32[32,2,2,8,256]{4,3,0,2,1:T(8,128)S(1)} %maximum_bitcast_fusion.3, f32[1,256,2,256]{3,1,0,2:T(8,128)S(1)} %copy-done.5, f32[1,256,2,256]{3,1,0,2:T(8,128)S(1)} %copy-done.7), kind=kOutput, calls=%fused_computation.15 | convolution fusion | flops 805568512 | bytes 3145728 | tf_op jit(solution)/shard_map/bcerkm,rmsq->bceskq/dot_general | solution.py:110
  46.3 3.8 %all-to-all-done = bf16[2,256,256]{2,0,1:T(2,128)(2,1)} async-done(((bf16[2,256,256]{2,0,1:T(2,128)(2,1)}), bf16[2,256,256]{2,0,1:T(2,128)(2,1)}, u32[]{:S(2)}, u32[]{:S(2)}) %all-to-all-start) | async-done | bytes 262176 | tf_op jit(solution)/shard_map/all_to_all | solution.py:85
  50.1 1.7 %convolution_bitcast_fusion = f32[2,32,2,2,8,256]{5,4,3,2,1,0:T(8,128)S(1)} fusion(bf16[2,8,32,256]{3,0,2,1:T(2,128)(2,1)} %bitcast.20, f32[2,1,8,8]{3,2,1,0:T(8,128)S(1)} %get-tuple-element.36, f32[2,1,8,8]{3,2,1,0:T(8,128)S(1)} %get-tuple-element.35), kind=kOutput, calls=%fused_computation.14 | convolution fusion | flops 25166080 | bytes 2360320 | tf_op jit(solution)/shard_map/erkp,bcpm->bcerkm/dot_general | solution.py:108
  52.3 0.8 copy-done.6
  53.3 2.7 %fusion.10 = f32[2,32,2,2,8,256]{5,1,4,2,0,3:T(8,128)S(1)} fusion(f32[2,32,2,2,8,256]{5,4,3,2,1,0:T(8,128)S(1)} %pad_maximum_fusion, f32[1,256,2,256]{3,1,0,2:T(8,128)S(1)} %copy-done.6, f32[1,256,2,256]{3,1,0,2:T(8,128)S(1)} %copy-done.8), kind=kOutput, calls=%fused_computation.12 | convolution fusion | flops 1610874880 | bytes 5242880 | tf_op jit(solution)/shard_map/bcerkm,rmsq->bceskq/dot_general | solution.py:110
  56.7 0.9 copy-done.9
  57.7 2.7 %fusion.13 = f32[2,32,2,2,8,256]{5,4,3,2,1,0:T(8,128)S(1)} fusion(f32[2,32,2,2,8,256,1]{5,1,4,2,0,3,6:T(8,128)S(1)} %maximum_bitcast_fusion, f32[1,256,2,256]{3,1,2,0:T(8,128)S(1)} %copy-done.10, f32[1,256,2,256]{3,1,2,0:T(8,128)S(1)} %copy-done.9), kind=kOutput, calls=%fused_computation.13 | convolution fusion | flops 1610874880 | bytes 5242880 | tf_op jit(solution)/shard_map/bceskq,sqrm->bcerkm/dot_general | solution.py:115
  60.8 0.7 fusion.27
  61.6 0.8 copy.43
  62.4 3.5 %all-to-all-start.2 = ((bf16[2,32,8,258]{3,1,0,2:T(8,128)(2,1)}), bf16[2,32,8,258]{3,1,0,2:T(8,128)(2,1)S(1)}, u32[]{:S(2)}, u32[]{:S(2)}) async-start(bf16[2,32,8,258]{3,1,0,2:T(8,128)(2,1)} %copy.43), calls=%async_computation.2 | async-start | bytes 786432 | tf_op jit(solution)/shard_map/all_to_all | solution.py:98
  65.9 1.5 %collective-permute-start.10 = (f32[4,2,256]{2,1,0:T(2,128)S(1)}, f32[4,2,256]{2,1,0:T(2,128)S(1)}, u32[]{:S(2)}, u32[]{:S(2)}) collective-permute-start(f32[4,2,256]{2,1,0:T(2,128)S(1)} %pad_maximum_fusion.12), channel_id=1, source_target_pairs={{4,0},{8,4},{12,8},{16,12},{20,16},{24,20},{28,24},{5,1},{9,5},{13... | collective-permute-start | bytes 24584 | tf_op jit(solution)/shard_map/ppermute | solution.py:17
  67.4 6.7 %all-to-all-done.2 = bf16[2,32,8,258]{3,1,0,2:T(8,128)(2,1)S(1)} async-done(((bf16[2,32,8,258]{3,1,0,2:T(8,128)(2,1)}), bf16[2,32,8,258]{3,1,0,2:T(8,128)(2,1)S(1)}, u32[]{:S(2)}, u32[]{:S(2)}) %all-to-all-start.2) | async-done | bytes 264224 | tf_op jit(solution)/shard_map/all_to_all | solution.py:98
  74.2 1.0 %copy.45 = f32[2,256,258]{1,2,0:T(8,128)} copy(f32[2,256,258]{2,1,0:T(8,128)S(1)} %bitcast.220) | data formatting | bytes 1056768 | tf_op jit(solution)/shard_map/transpose | solution.py:101
  75.2 1.1 %fusion.82 = (f32[1,256,256]{2,1,0:T(8,128)S(1)}, f32[256,256]{1,0:T(8,128)S(1)}, f32[1,256,256]{2,1,0:T(8,128)S(1)}, f32[256,256]{1,0:T(8,128)S(1)}) fusion(f32[3,256,256]{2,1,0:T(8,128)S(1)} %fusion.42, f32[256,256]{1,0:T(8,128)S(1)} %copy-done.2, f32[256]{0:T(256)S(1)} %copy-done.12, f32[2,258,256]{2,1,0:T(8,128)} %bitcast.221), kind=kLoop, calls=%fused_computation.117 | loop fusion | flops 524288 | bytes 2622464 | tf_op jit(solution)/shard_map/stack | solution.py:196
  76.5 0.7 slice_multiply_fusion.7
  78.9 2.5 %collective-permute-start.12 = (bf16[256,256]{1,0:T(8,128)(2,1)S(1)}, bf16[256,256]{1,0:T(8,128)(2,1)S(1)}, u32[]{:S(2)}, u32[]{:S(2)}) collective-permute-start(bf16[256,256]{1,0:T(8,128)(2,1)S(1)} %fusion.31), channel_id=1, source_target_pairs={{0,2},{1,3},{2,0},{3,1},{4,6},{5,7},{6,4},{7,5},{8,10},{9,11},{10,... | collective-permute-start | bytes 393224 | tf_op jit(solution)/shard_map/ppermute | solution.py:36
  81.4 3.8 %collective-permute-start.13 = (bf16[256,256]{1,0:T(8,128)(2,1)S(1)}, bf16[256,256]{1,0:T(8,128)(2,1)S(1)}, u32[]{:S(2)}, u32[]{:S(2)}) collective-permute-start(bf16[256,256]{1,0:T(8,128)(2,1)S(1)} %fusion.32), channel_id=1, source_target_pairs={{0,3},{1,0},{2,1},{3,2},{4,7},{5,4},{6,5},{7,6},{8,11},{9,8},{10,9... | collective-permute-start | bytes 393224 | tf_op jit(solution)/shard_map/ppermute | solution.py:36
  86.0 7.3 %collective-permute-done.12 = bf16[256,256]{1,0:T(8,128)(2,1)S(1)} collective-permute-done((bf16[256,256]{1,0:T(8,128)(2,1)S(1)}, bf16[256,256]{1,0:T(8,128)(2,1)S(1)}, u32[]{:S(2)}, u32[]{:S(2)}) %collective-permute-start.12) | collective-permute-done | bytes 131104 | tf_op jit(solution)/shard_map/ppermute | solution.py:36
  93.3 1.0 fusion.69
  94.3 6.9 %collective-permute-done.8 = bf16[256,256]{1,0:T(8,128)(2,1)S(1)} collective-permute-done((bf16[256,256]{1,0:T(8,128)(2,1)S(1)}, bf16[256,256]{1,0:T(8,128)(2,1)S(1)}, u32[]{:S(2)}, u32[]{:S(2)}) %collective-permute-start.8) | collective-permute-done | bytes 131104 | tf_op jit(solution)/shard_map/ppermute | solution.py:36
  101.3 0.9 add_convert_fusion
  (76 shorter events, 7.2 us)
Async XLA Ops:
  0.6 21.6 %copy-start = (bf16[3,1024,256]{2,1,0:T(8,128)(2,1)S(1)}, bf16[3,1024,256]{2,1,0:T(8,128)(2,1)}, u32[]{:S(2)}) copy-start(bf16[3,1024,256]{2,1,0:T(8,128)(2,1)} %param.9) | copy-start | bytes 4718596
  0.6 22.8 %copy-start.11 = (bf16[256,256]{1,0:T(8,128)(2,1)S(1)}, bf16[256,256]{1,0:T(8,128)(2,1)}, u32[]{:S(2)}) copy-start(bf16[256,256]{1,0:T(8,128)(2,1)} %param.8) | copy-start | bytes 393220
  0.7 22.8 %copy-start.3 = (bf16[256,1024]{1,0:T(8,128)(2,1)S(1)}, bf16[256,1024]{1,0:T(8,128)(2,1)}, u32[]{:S(2)}) copy-start(bf16[256,1024]{1,0:T(8,128)(2,1)} %param.13) | copy-start | bytes 1572868
  0.7 27.4 %collective-permute-start = (bf16[256,256]{1,0:T(8,128)(2,1)}, bf16[256,256]{1,0:T(8,128)(2,1)}, u32[]{:S(2)}, u32[]{:S(2)}) collective-permute-start(bf16[256,256]{1,0:T(8,128)(2,1)} %param.7), channel_id=1, source_target_pairs={{0,1},{1,2},{2,3},{3,0},{4,5},{5,6},{6,7},{7,4},{8,9},{9,10},{10,1... | collective-permute-start | bytes 393224 | tf_op jit(solution)/shard_map/ppermute | solution.py:25
  3.8 25.8 %collective-permute-start.2 = (bf16[256,256]{1,0:T(8,128)(2,1)}, bf16[256,256]{1,0:T(8,128)(2,1)}, u32[]{:S(2)}, u32[]{:S(2)}) collective-permute-start(bf16[256,256]{1,0:T(8,128)(2,1)} %param.7), channel_id=1, source_target_pairs={{0,3},{1,0},{2,1},{3,2},{4,7},{5,4},{6,5},{7,6},{8,11},{9,8},{10,9... | collective-permute-start | bytes 393224 | tf_op jit(solution)/shard_map/ppermute | solution.py:25
  5.9 24.9 %collective-permute-start.1 = (bf16[256,256]{1,0:T(8,128)(2,1)}, bf16[256,256]{1,0:T(8,128)(2,1)}, u32[]{:S(2)}, u32[]{:S(2)}) collective-permute-start(bf16[256,256]{1,0:T(8,128)(2,1)} %param.7), channel_id=1, source_target_pairs={{0,2},{1,3},{2,0},{3,1},{4,6},{5,7},{6,4},{7,5},{8,10},{9,11},{10,... | collective-permute-start | bytes 393224 | tf_op jit(solution)/shard_map/ppermute | solution.py:25
  6.8 27.3 %collective-permute-start.4 = (bf16[256,256]{1,0:T(8,128)(2,1)}, bf16[256,256]{1,0:T(8,128)(2,1)}, u32[]{:S(2)}, u32[]{:S(2)}) collective-permute-start(bf16[256,256]{1,0:T(8,128)(2,1)} %param.8), channel_id=1, source_target_pairs={{0,1},{1,2},{2,3},{3,0},{4,5},{5,6},{6,7},{7,4},{8,9},{9,10},{10,1... | collective-permute-start | bytes 393224 | tf_op jit(solution)/shard_map/ppermute | solution.py:25
  8.4 26.9 %collective-permute-start.6 = (bf16[256,256]{1,0:T(8,128)(2,1)}, bf16[256,256]{1,0:T(8,128)(2,1)}, u32[]{:S(2)}, u32[]{:S(2)}) collective-permute-start(bf16[256,256]{1,0:T(8,128)(2,1)} %param.8), channel_id=1, source_target_pairs={{0,3},{1,0},{2,1},{3,2},{4,7},{5,4},{6,5},{7,6},{8,11},{9,8},{10,9... | collective-permute-start | bytes 393224 | tf_op jit(solution)/shard_map/ppermute | solution.py:25
  12.4 26.7 %all-to-all-start.1 = ((f32[1,256,256]{2,0,1:T(1,128)}), f32[1,256,256]{2,0,1:T(1,128)S(1)}, u32[]{:S(2)}, u32[]{:S(2)}) async-start(f32[1,256,256]{2,0,1:T(1,128)} %bitcast.36), calls=%async_computation.1 | async-start | bytes 524288 | tf_op jit(solution)/shard_map/all_to_all | solution.py:85
  28.1 9.1 %collective-permute-start.5 = (bf16[256,256]{1,0:T(8,128)(2,1)}, bf16[256,256]{1,0:T(8,128)(2,1)S(1)}, u32[]{:S(2)}, u32[]{:S(2)}) collective-permute-start(bf16[256,256]{1,0:T(8,128)(2,1)} %param.8), channel_id=1, source_target_pairs={{0,2},{1,3},{2,0},{3,1},{4,6},{5,7},{6,4},{7,5},{8,10},{9,11},{10,... | collective-permute-start | bytes 393224 | tf_op jit(solution)/shard_map/ppermute | solution.py:25
  32.0 5.4 %collective-permute-start.3 = (bf16[3,2,256]{2,1,0:T(2,128)(2,1)S(1)}, bf16[3,2,256]{2,1,0:T(2,128)(2,1)S(1)}, u32[]{:S(2)}, u32[]{:S(2)}) collective-permute-start(bf16[3,2,256]{2,1,0:T(2,128)(2,1)S(1)} %slice.156), channel_id=1, source_target_pairs={{0,4},{4,8},{8,12},{12,16},{16,20},{20,24},{24,28},{1,5},{5,9},{9,... | collective-permute-start | bytes 9224 | tf_op jit(solution)/shard_map/ppermute | solution.py:17
  37.4 0.7 copy-start.1
  39.1 11.0 %all-to-all-start = ((bf16[2,256,256]{2,0,1:T(2,128)(2,1)}), bf16[2,256,256]{2,0,1:T(2,128)(2,1)}, u32[]{:S(2)}, u32[]{:S(2)}) async-start(bf16[2,256,256]{2,0,1:T(2,128)(2,1)} %copy.32), calls=%async_computation | async-start | bytes 524288 | tf_op jit(solution)/shard_map/all_to_all | solution.py:85
  43.9 1.0 %copy-start.5 = (f32[1,256,2,256]{3,1,0,2:T(8,128)S(1)}, f32[1,256,2,256]{3,1,0,2:T(8,128)}, u32[]{:S(2)}) copy-start(f32[1,256,2,256]{3,1,0,2:T(8,128)} %get-tuple-element.24) | copy-start | bytes 1572868
  44.0 1.2 %copy-start.7 = (f32[1,256,2,256]{3,1,0,2:T(8,128)S(1)}, f32[1,256,2,256]{3,1,0,2:T(8,128)}, u32[]{:S(2)}) copy-start(f32[1,256,2,256]{3,1,0,2:T(8,128)} %get-tuple-element.27) | copy-start | bytes 1572868
  52.1 1.0 %copy-start.6 = (f32[1,256,2,256]{3,1,0,2:T(8,128)S(1)}, f32[1,256,2,256]{3,1,0,2:T(8,128)}, u32[]{:S(2)}) copy-start(f32[1,256,2,256]{3,1,0,2:T(8,128)} %get-tuple-element.24) | copy-start | bytes 1572868
  52.1 1.2 %copy-start.8 = (f32[1,256,2,256]{3,1,0,2:T(8,128)S(1)}, f32[1,256,2,256]{3,1,0,2:T(8,128)}, u32[]{:S(2)}) copy-start(f32[1,256,2,256]{3,1,0,2:T(8,128)} %get-tuple-element.27) | copy-start | bytes 1572868
  56.5 1.0 %copy-start.9 = (f32[1,256,2,256]{3,1,2,0:T(8,128)S(1)}, f32[1,256,2,256]{3,1,2,0:T(8,128)}, u32[]{:S(2)}) copy-start(f32[1,256,2,256]{3,1,2,0:T(8,128)} %get-tuple-element.23) | copy-start | bytes 1572868
  56.5 1.2 %copy-start.10 = (f32[1,256,2,256]{3,1,2,0:T(8,128)S(1)}, f32[1,256,2,256]{3,1,2,0:T(8,128)}, u32[]{:S(2)}) copy-start(f32[1,256,2,256]{3,1,2,0:T(8,128)} %get-tuple-element.28) | copy-start | bytes 1572868
  60.8 5.0 %copy-start.2 = (f32[256,256]{1,0:T(8,128)S(1)}, f32[256,256]{1,0:T(8,128)}, u32[]{:S(2)}) copy-start(f32[256,256]{1,0:T(8,128)} %copy-done.1) | copy-start | bytes 786436
  62.4 11.7 %all-to-all-start.2 = ((bf16[2,32,8,258]{3,1,0,2:T(8,128)(2,1)}), bf16[2,32,8,258]{3,1,0,2:T(8,128)(2,1)S(1)}, u32[]{:S(2)}, u32[]{:S(2)}) async-start(bf16[2,32,8,258]{3,1,0,2:T(8,128)(2,1)} %copy.43), calls=%async_computation.2 | async-start | bytes 786432 | tf_op jit(solution)/shard_map/all_to_all | solution.py:98
  65.8 9.4 %copy-start.12 = (f32[256]{0:T(256)S(1)}, f32[256]{0:T(256)}, u32[]{:S(2)}) copy-start(f32[256]{0:T(256)} %param.11) | copy-start | bytes 3076
  65.9 10.6 %collective-permute-start.10 = (f32[4,2,256]{2,1,0:T(2,128)S(1)}, f32[4,2,256]{2,1,0:T(2,128)S(1)}, u32[]{:S(2)}, u32[]{:S(2)}) collective-permute-start(f32[4,2,256]{2,1,0:T(2,128)S(1)} %pad_maximum_fusion.12), channel_id=1, source_target_pairs={{4,0},{8,4},{12,8},{16,12},{20,16},{24,20},{28,24},{5,1},{9,5},{13... | collective-permute-start | bytes 24584 | tf_op jit(solution)/shard_map/ppermute | solution.py:17
  77.3 1.2 %copy-start.4 = (bf16[256,1024]{1,0:T(8,128)(2,1)S(1)}, bf16[256,1024]{1,0:T(8,128)(2,1)}, u32[]{:S(2)}) copy-start(bf16[256,1024]{1,0:T(8,128)(2,1)} %param.13) | copy-start | bytes 1572868
  78.9 14.4 %collective-permute-start.12 = (bf16[256,256]{1,0:T(8,128)(2,1)S(1)}, bf16[256,256]{1,0:T(8,128)(2,1)S(1)}, u32[]{:S(2)}, u32[]{:S(2)}) collective-permute-start(bf16[256,256]{1,0:T(8,128)(2,1)S(1)} %fusion.31), channel_id=1, source_target_pairs={{0,2},{1,3},{2,0},{3,1},{4,6},{5,7},{6,4},{7,5},{8,10},{9,11},{10,... | collective-permute-start | bytes 393224 | tf_op jit(solution)/shard_map/ppermute | solution.py:36
  81.4 11.9 %collective-permute-start.11 = (bf16[256,256]{1,0:T(8,128)(2,1)S(1)}, bf16[256,256]{1,0:T(8,128)(2,1)S(1)}, u32[]{:S(2)}, u32[]{:S(2)}) collective-permute-start(bf16[256,256]{1,0:T(8,128)(2,1)S(1)} %fusion.30), channel_id=1, source_target_pairs={{0,1},{1,2},{2,3},{3,0},{4,5},{5,6},{6,7},{7,4},{8,9},{9,10},{10,1... | collective-permute-start | bytes 393224 | tf_op jit(solution)/shard_map/ppermute | solution.py:36
  81.4 11.9 %collective-permute-start.13 = (bf16[256,256]{1,0:T(8,128)(2,1)S(1)}, bf16[256,256]{1,0:T(8,128)(2,1)S(1)}, u32[]{:S(2)}, u32[]{:S(2)}) collective-permute-start(bf16[256,256]{1,0:T(8,128)(2,1)S(1)} %fusion.32), channel_id=1, source_target_pairs={{0,3},{1,0},{2,1},{3,2},{4,7},{5,4},{6,5},{7,6},{8,11},{9,8},{10,9... | collective-permute-start | bytes 393224 | tf_op jit(solution)/shard_map/ppermute | solution.py:36
  85.2 16.1 %collective-permute-start.8 = (bf16[256,256]{1,0:T(8,128)(2,1)S(1)}, bf16[256,256]{1,0:T(8,128)(2,1)S(1)}, u32[]{:S(2)}, u32[]{:S(2)}) collective-permute-start(bf16[256,256]{1,0:T(8,128)(2,1)S(1)} %convolution_convert_fusion.1), channel_id=1, source_target_pairs={{0,2},{1,3},{2,0},{3,1},{4,6},{5,7},{6,4},{7,5},{8,10},{9,11},{10,... | collective-permute-start | bytes 393224 | tf_op jit(solution)/shard_map/ppermute | solution.py:36
  85.2 16.1 %collective-permute-start.7 = (bf16[256,256]{1,0:T(8,128)(2,1)S(1)}, bf16[256,256]{1,0:T(8,128)(2,1)S(1)}, u32[]{:S(2)}, u32[]{:S(2)}) collective-permute-start(bf16[256,256]{1,0:T(8,128)(2,1)S(1)} %convolution_convert_fusion.2), channel_id=1, source_target_pairs={{0,1},{1,2},{2,3},{3,0},{4,5},{5,6},{6,7},{7,4},{8,9},{9,10},{10,1... | collective-permute-start | bytes 393224 | tf_op jit(solution)/shard_map/ppermute | solution.py:36
  93.3 8.0 %collective-permute-start.9 = (bf16[256,256]{1,0:T(8,128)(2,1)S(1)}, bf16[256,256]{1,0:T(8,128)(2,1)S(1)}, u32[]{:S(2)}, u32[]{:S(2)}) collective-permute-start(bf16[256,256]{1,0:T(8,128)(2,1)S(1)} %convolution_convert_fusion), channel_id=1, source_target_pairs={{0,3},{1,0},{2,1},{3,2},{4,7},{5,4},{6,5},{7,6},{8,11},{9,8},{10,9... | collective-permute-start | bytes 393224 | tf_op jit(solution)/shard_map/ppermute | solution.py:36

commit v14 on v13

--- a/solution.py
+++ b/solution.py
@@ -5,7 +5,7 @@
 from jax import lax
 from jax.sharding import PartitionSpec as P
 
-HIGHEST = lax.Precision.HIGHEST
+
 STAGE_A_PRECISION = lax.Precision.HIGH
 STAGE_B_PRECISION = lax.Precision.HIGH
 WIRE = jnp.bfloat16
@@ -117,7 +117,7 @@
     return jnp.einsum("erkp,bcerkm->bcpm", stage_a_inv, spread, precision=STAGE_A_PRECISION)
 
 
-def local(tokens, cotangent, in_weight, short_kernel, skip_gain, long_filter, out_weight):
+def local_body(tokens, cotangent, in_weight, short_kernel, skip_gain, long_filter, out_weight):
     row_count = tokens.shape[0]
     tap_count = short_kernel.shape[0]
     shard_count = lax.axis_size("seq")
@@ -156,9 +156,12 @@
     grad_state = grad_gated * gate_out
     rim = tap_count - 1
     ahead = shifted(
-        jnp.stack([gate_out[:rim], gate_in[:rim], value_path[:rim], grad_gated[:rim]]), "seq", -1
-    )
-    spectra = forward_spectrum(to_columns(jnp.stack([signal, grad_state]), WIRE), tables)
+        jnp.stack([gate_out[:rim], gate_in[:rim], value_path[:rim], grad_gated[:rim]]),
+        "seq",
+        -1,
+    )
+    columns = to_columns(jnp.stack([signal, grad_state]), WIRE)
+    spectra = forward_spectrum(columns, tables)
     filt_real, filt_imag = filt_spec[:, :, :, 0], filt_spec[:, :, :, 1]
     sig_real, sig_imag = spectra[0:1, :, :, 0], spectra[0:1, :, :, 1]
     grad_real, grad_imag = spectra[1:2, :, :, 0], spectra[1:2, :, :, 1]
@@ -224,7 +227,7 @@
         P("panel", None),
     )
     return jax.shard_map(
-        local,
+        local_body,
         mesh=mesh,
         in_specs=placed,
         out_specs=(P("seq", "panel"), P("seq", "panel")),

time: 103 us -> 103 us (level)
  no operation moved by 1% of the time
where the time goes in v14:
time: 103 us; the launch traced here: 102 us
  starting transfers between devices  32.3 us (31%)
  waiting for transfers between devices  25.4 us (25%)
  matrix products  20.3 us (20%)
  other arithmetic  14.2 us (14%)
  local copies, waits for them, and re-layouts  8.77 us (9%)
  between operations  1.22 us (1%)
    ppermute x6, waiting for transfers between devices, panel_reduce_scatter(): lax.ppermute(sent, 'panel', [(i, (i + k) % count) for i in range(count)])  14.3 us
    ppermute x6, starting transfers between devices, panel_parts(): lax.ppermute(value, 'panel', [(i, (i + k) % count) for i in range(count)])  10.3 us
    all_to_all x2, starting transfers between devices, to_columns(): lax.all_to_all(jnp.swapaxes(rows, 1, 2).astype(wire), 'seq', split_axis=1...  7.96 us
    ppermute x6, starting transfers between devices, panel_reduce_scatter(): lax.ppermute(sent, 'panel', [(i, (i + k) % count) for i in range(count)])  6.89 us
    all_to_all x1, waiting for transfers between devices, to_rows(): lax.all_to_all(columns.astype(wire), 'seq', split_axis=2, concat_axis=1,...  6.66 us
    dot_general x4, matrix products, local_body(): jnp.einsum('td,jdc->jtc', part, lax.dynamic_slice_in_dim(in_weight, sourc...  4.7 us
    dot_general x2, matrix products, forward_spectrum(): jnp.einsum('bcerkm,rmsq->bceskq', spread, stage_b, precision=STAGE_B_PREC...  3.81 us
    all_to_all x2, waiting for transfers between devices, to_columns(): lax.all_to_all(jnp.swapaxes(rows, 1, 2).astype(wire), 'seq', split_axis=1...  3.78 us
  transfers between devices with their start and end apart: 17, of which 5 were waited for; matrix products, arithmetic and copies ran while one was open for 26% of the time, Pallas kernels for 0%

profile of v14, /device:TPU:0, one launch (start us, length us, event | category | flops | bytes accessed | tf_op | source)
XLA Modules:
  0.0 102.2 jit_solution(16370592749146353908)
XLA Ops:
  0.7 3.1 %collective-permute-start = (bf16[256,256]{1,0:T(8,128)(2,1)}, bf16[256,256]{1,0:T(8,128)(2,1)}, u32[]{:S(2)}, u32[]{:S(2)}) collective-permute-start(bf16[256,256]{1,0:T(8,128)(2,1)} %param.7), channel_id=1, source_target_pairs={{0,1},{1,2},{2,3},{3,0},{4,5},{5,6},{6,7},{7,4},{8,9},{9,10},{10,1... | collective-permute-start | bytes 393224 | tf_op jit(solution)/shard_map/ppermute | solution.py:25
  3.8 2.1 %collective-permute-start.2 = (bf16[256,256]{1,0:T(8,128)(2,1)}, bf16[256,256]{1,0:T(8,128)(2,1)}, u32[]{:S(2)}, u32[]{:S(2)}) collective-permute-start(bf16[256,256]{1,0:T(8,128)(2,1)} %param.7), channel_id=1, source_target_pairs={{0,3},{1,0},{2,1},{3,2},{4,7},{5,4},{6,5},{7,6},{8,11},{9,8},{10,9... | collective-permute-start | bytes 393224 | tf_op jit(solution)/shard_map/ppermute | solution.py:25
  5.9 0.9 collective-permute-start.1
  6.8 1.6 %collective-permute-start.4 = (bf16[256,256]{1,0:T(8,128)(2,1)}, bf16[256,256]{1,0:T(8,128)(2,1)}, u32[]{:S(2)}, u32[]{:S(2)}) collective-permute-start(bf16[256,256]{1,0:T(8,128)(2,1)} %param.8), channel_id=1, source_target_pairs={{0,1},{1,2},{2,3},{3,0},{4,5},{5,6},{6,7},{7,4},{8,9},{9,10},{10,1... | collective-permute-start | bytes 393224 | tf_op jit(solution)/shard_map/ppermute | solution.py:25
  8.4 2.2 %collective-permute-start.6 = (bf16[256,256]{1,0:T(8,128)(2,1)}, bf16[256,256]{1,0:T(8,128)(2,1)}, u32[]{:S(2)}, u32[]{:S(2)}) collective-permute-start(bf16[256,256]{1,0:T(8,128)(2,1)} %param.8), channel_id=1, source_target_pairs={{0,3},{1,0},{2,1},{3,2},{4,7},{5,4},{6,5},{7,6},{8,11},{9,8},{10,9... | collective-permute-start | bytes 393224 | tf_op jit(solution)/shard_map/ppermute | solution.py:25
  10.6 1.8 %copy.63 = f32[1,256,256]{1,0,2:T(1,128)} copy(f32[1,256,256]{2,1,0:T(8,128)} %bitcast.224) | data formatting | bytes 524288 | tf_op jit(solution)/shard_map/broadcast_in_dim | solution.py:125
  12.4 3.7 %all-to-all-start.1 = ((f32[1,256,256]{2,0,1:T(1,128)}), f32[1,256,256]{2,0,1:T(1,128)S(1)}, u32[]{:S(2)}, u32[]{:S(2)}) async-start(f32[1,256,256]{2,0,1:T(1,128)} %bitcast.36), calls=%async_computation.1 | async-start | bytes 524288 | tf_op jit(solution)/shard_map/all_to_all | solution.py:85
  16.2 0.6 iota_multiply_fusion.3
  16.8 0.7 iota_multiply_fusion
  17.5 0.6 iota_multiply_fusion.2
  18.1 1.8 %fusion.93 = (f32[256,1,256]{2,0,1:T(8,128)}, f32[256,1,256]{2,0,1:T(8,128)}) fusion(), kind=kLoop, calls=%fused_computation.133 | loop fusion | flops 983040 | bytes 524288 | tf_op jit(solution)/shard_map/sin | solution.py:62
  19.8 1.7 %fusion.95 = f32[256,1,256]{2,0,1:T(8,128)} fusion(), kind=kLoop, calls=%fused_computation.135 | loop fusion | flops 1048576 | bytes 262144 | tf_op jit(solution)/shard_map/neg | solution.py:67
  21.5 0.7 slice_bitcast_fusion.5
  22.3 1.2 %fusion.58 = f32[3,256,256]{1,2,0:T(8,128)S(1)} fusion(bf16[3,1024,256]{2,1,0:T(8,128)(2,1)S(1)} %copy-done, s32[]{:T(128)S(6)} %select_n.148, bf16[256,256]{1,0:T(8,128)(2,1)} %param.7), kind=kOutput, calls=%fused_computation.94 | convolution fusion | flops 100663296 | bytes 1310724 | tf_op jit(solution)/shard_map/td,jdc->jtc/dot_general | solution.py:129
  23.7 0.7 fusion.123
  24.4 0.8 fusion.143
  25.2 2.8 %fusion.47 = (f32[1,256,2,256]{3,1,2,0:T(8,128)}, f32[1,256,2,256]{3,1,0,2:T(8,128)}, f32[1,256,2,256]{3,1,0,2:T(8,128)}, f32[1,256,2,256]{3,1,2,0:T(8,128)}) fusion(f32[256,1,256]{2,0,1:T(8,128)} %get-tuple-element.38, f32[256,1,256]{2,0,1:T(8,128)} %fusion.95, f32[256,1,256]{2,0,1:T(8,128)} %get-tuple-element.37), kind=kLoop, calls=%fused_computation.73 | loop fusion | flops 524288 | bytes 2883584 | tf_op jit(solution)/shard_map/stack | solution.py:66
  28.4 1.2 %convolution_add_fusion.1 = f32[3,256,256]{1,2,0:T(8,128)S(1)} fusion(f32[3,256,256]{1,2,0:T(8,128)S(1)} %fusion.58, bf16[3,1024,256]{2,1,0:T(8,128)(2,1)S(1)} %copy-done, s32[]{:T(128)S(6)} %select_n.150, bf16[256,256]{1,0:T(8,128)(2,1)} %collective-permute-done), kind=kOutput, calls=%fused_computation.19 | convolution fusion | flops 100859904 | bytes 2097156 | tf_op jit(solution)/shard_map/td,jdc->jtc/dot_general | solution.py:129
  29.6 1.2 %fusion.51 = f32[3,256,256]{1,2,0:T(8,128)S(1)} fusion(bf16[3,1024,256]{2,1,0:T(8,128)(2,1)S(1)} %copy-done, s32[]{:T(128)S(6)} %select_n.154, bf16[256,256]{1,0:T(8,128)(2,1)} %collective-permute-done.2), kind=kOutput, calls=%fused_computation.87 | convolution fusion | flops 100663296 | bytes 1310724 | tf_op jit(solution)/shard_map/td,jdc->jtc/dot_general | solution.py:129
  30.8 1.2 %fusion.21 = bf16[3,256,256]{2,1,0:T(8,128)(2,1)S(1)} fusion(f32[3,256,256]{1,2,0:T(8,128)S(1)} %fusion.51, f32[3,256,256]{1,2,0:T(8,128)S(1)} %convolution_add_fusion.1, bf16[3,1024,256]{2,1,0:T(8,128)(2,1)S(1)} %copy-done, s32[]{:T(128)S(6)} %select_n.152, bf16[256,256]{1,0:T(8,128)(2,1)} %collective-permute-done.1), kind=kOutput, calls=%fused_computation.22 | convolution fusion | flops 101253120 | bytes 2490372 | tf_op jit(solution)/shard_map/td,jdc->jtc/dot_general | solution.py:129
  32.0 2.1 %collective-permute-start.3 = (bf16[3,2,256]{2,1,0:T(2,128)(2,1)S(1)}, bf16[3,2,256]{2,1,0:T(2,128)(2,1)S(1)}, u32[]{:S(2)}, u32[]{:S(2)}) collective-permute-start(bf16[3,2,256]{2,1,0:T(2,128)(2,1)S(1)} %slice.156), channel_id=1, source_target_pairs={{0,4},{4,8},{8,12},{12,16},{16,20},{20,24},{24,28},{1,5},{5,9},{9,... | collective-permute-start | bytes 9224 | tf_op jit(solution)/shard_map/ppermute | solution.py:17
  34.1 1.1 %convolution_add_fusion.3 = f32[256,256]{0,1:T(8,128)S(1)} fusion(f32[256,256]{0,1:T(8,128)S(1)} %fusion.105, bf16[256,256]{1,0:T(8,128)(2,1)} %collective-permute-done.4, bf16[256,1024]{1,0:T(8,128)(2,1)S(1)} %copy-done.3, s32[]{:T(128)S(6)} %select_n.150), kind=kOutput, calls=%fused_computation.31 | convolution fusion | flops 33619968 | bytes 786436 | tf_op jit(solution)/shard_map/dot_general | solution.py:137
  35.3 1.1 %fusion.97 = f32[256,256]{0,1:T(8,128)S(1)} fusion(bf16[256,256]{1,0:T(8,128)(2,1)} %collective-permute-done.6, bf16[256,1024]{1,0:T(8,128)(2,1)S(1)} %copy-done.3, s32[]{:T(128)S(6)} %select_n.154), kind=kOutput, calls=%fused_computation.137 | convolution fusion | flops 33554432 | bytes 524292 | tf_op jit(solution)/shard_map/dot_general | solution.py:137
  36.4 0.7 collective-permute-done.5
  38.2 0.9 copy.32
  39.1 4.2 %all-to-all-start = ((bf16[2,256,256]{2,0,1:T(2,128)(2,1)}), bf16[2,256,256]{2,0,1:T(2,128)(2,1)}, u32[]{:S(2)}, u32[]{:S(2)}) async-start(bf16[2,256,256]{2,0,1:T(2,128)(2,1)} %copy.32), calls=%async_computation | async-start | bytes 524288 | tf_op jit(solution)/shard_map/all_to_all | solution.py:85
  44.2 0.8 copy-done.5
  45.1 1.1 %convolution_bitcast_fusion.1 = f32[1,32,2,2,8,256]{5,1,4,2,0,3:T(8,128)S(1)} fusion(f32[32,2,2,8,256]{4,3,0,2,1:T(8,128)S(1)} %maximum_bitcast_fusion.3, f32[1,256,2,256]{3,1,0,2:T(8,128)S(1)} %copy-done.5, f32[1,256,2,256]{3,1,0,2:T(8,128)S(1)} %copy-done.7), kind=kOutput, calls=%fused_computation.15 | convolution fusion | flops 805568512 | bytes 3145728 | tf_op jit(solution)/shard_map/bcerkm,rmsq->bceskq/dot_general | solution.py:110
  46.3 3.8 %all-to-all-done = bf16[2,256,256]{2,0,1:T(2,128)(2,1)} async-done(((bf16[2,256,256]{2,0,1:T(2,128)(2,1)}), bf16[2,256,256]{2,0,1:T(2,128)(2,1)}, u32[]{:S(2)}, u32[]{:S(2)}) %all-to-all-start) | async-done | bytes 262176 | tf_op jit(solution)/shard_map/all_to_all | solution.py:85
  50.1 1.7 %convolution_bitcast_fusion = f32[2,32,2,2,8,256]{5,4,3,2,1,0:T(8,128)S(1)} fusion(bf16[2,8,32,256]{3,0,2,1:T(2,128)(2,1)} %bitcast.20, f32[2,1,8,8]{3,2,1,0:T(8,128)S(1)} %get-tuple-element.36, f32[2,1,8,8]{3,2,1,0:T(8,128)S(1)} %get-tuple-element.35), kind=kOutput, calls=%fused_computation.14 | convolution fusion | flops 25166080 | bytes 2360320 | tf_op jit(solution)/shard_map/erkp,bcpm->bcerkm/dot_general | solution.py:108
  52.3 0.8 copy-done.6
  53.3 2.7 %fusion.10 = f32[2,32,2,2,8,256]{5,1,4,2,0,3:T(8,128)S(1)} fusion(f32[2,32,2,2,8,256]{5,4,3,2,1,0:T(8,128)S(1)} %pad_maximum_fusion, f32[1,256,2,256]{3,1,0,2:T(8,128)S(1)} %copy-done.6, f32[1,256,2,256]{3,1,0,2:T(8,128)S(1)} %copy-done.8), kind=kOutput, calls=%fused_computation.12 | convolution fusion | flops 1610874880 | bytes 5242880 | tf_op jit(solution)/shard_map/bcerkm,rmsq->bceskq/dot_general | solution.py:110
  56.7 0.9 copy-done.9
  57.7 2.7 %fusion.13 = f32[2,32,2,2,8,256]{5,4,3,2,1,0:T(8,128)S(1)} fusion(f32[2,32,2,2,8,256,1]{5,1,4,2,0,3,6:T(8,128)S(1)} %maximum_bitcast_fusion, f32[1,256,2,256]{3,1,2,0:T(8,128)S(1)} %copy-done.10, f32[1,256,2,256]{3,1,2,0:T(8,128)S(1)} %copy-done.9), kind=kOutput, calls=%fused_computation.13 | convolution fusion | flops 1610874880 | bytes 5242880 | tf_op jit(solution)/shard_map/bceskq,sqrm->bcerkm/dot_general | solution.py:115
  60.8 0.7 fusion.27
  61.6 0.8 copy.43
  62.4 3.5 %all-to-all-start.2 = ((bf16[2,32,8,258]{3,1,0,2:T(8,128)(2,1)}), bf16[2,32,8,258]{3,1,0,2:T(8,128)(2,1)S(1)}, u32[]{:S(2)}, u32[]{:S(2)}) async-start(bf16[2,32,8,258]{3,1,0,2:T(8,128)(2,1)} %copy.43), calls=%async_computation.2 | async-start | bytes 786432 | tf_op jit(solution)/shard_map/all_to_all | solution.py:98
  65.9 1.5 %collective-permute-start.10 = (f32[4,2,256]{2,1,0:T(2,128)S(1)}, f32[4,2,256]{2,1,0:T(2,128)S(1)}, u32[]{:S(2)}, u32[]{:S(2)}) collective-permute-start(f32[4,2,256]{2,1,0:T(2,128)S(1)} %pad_maximum_fusion.12), channel_id=1, source_target_pairs={{4,0},{8,4},{12,8},{16,12},{20,16},{24,20},{28,24},{5,1},{9,5},{13... | collective-permute-start | bytes 24584 | tf_op jit(solution)/shard_map/ppermute | solution.py:17
  67.4 6.7 %all-to-all-done.2 = bf16[2,32,8,258]{3,1,0,2:T(8,128)(2,1)S(1)} async-done(((bf16[2,32,8,258]{3,1,0,2:T(8,128)(2,1)}), bf16[2,32,8,258]{3,1,0,2:T(8,128)(2,1)S(1)}, u32[]{:S(2)}, u32[]{:S(2)}) %all-to-all-start.2) | async-done | bytes 264224 | tf_op jit(solution)/shard_map/all_to_all | solution.py:98
  74.2 1.0 %copy.45 = f32[2,256,258]{1,2,0:T(8,128)} copy(f32[2,256,258]{2,1,0:T(8,128)S(1)} %bitcast.220) | data formatting | bytes 1056768 | tf_op jit(solution)/shard_map/transpose | solution.py:101
  75.2 1.1 %fusion.82 = (f32[1,256,256]{2,1,0:T(8,128)S(1)}, f32[256,256]{1,0:T(8,128)S(1)}, f32[1,256,256]{2,1,0:T(8,128)S(1)}, f32[256,256]{1,0:T(8,128)S(1)}) fusion(f32[3,256,256]{2,1,0:T(8,128)S(1)} %fusion.42, f32[256,256]{1,0:T(8,128)S(1)} %copy-done.2, f32[256]{0:T(256)S(1)} %copy-done.12, f32[2,258,256]{2,1,0:T(8,128)} %bitcast.221), kind=kLoop, calls=%fused_computation.117 | loop fusion | flops 524288 | bytes 2622464 | tf_op jit(solution)/shard_map/stack | solution.py:199
  76.5 0.7 slice_multiply_fusion.7
  78.9 2.5 %collective-permute-start.12 = (bf16[256,256]{1,0:T(8,128)(2,1)S(1)}, bf16[256,256]{1,0:T(8,128)(2,1)S(1)}, u32[]{:S(2)}, u32[]{:S(2)}) collective-permute-start(bf16[256,256]{1,0:T(8,128)(2,1)S(1)} %fusion.31), channel_id=1, source_target_pairs={{0,2},{1,3},{2,0},{3,1},{4,6},{5,7},{6,4},{7,5},{8,10},{9,11},{10,... | collective-permute-start | bytes 393224 | tf_op jit(solution)/shard_map/ppermute | solution.py:36
  81.4 3.8 %collective-permute-start.13 = (bf16[256,256]{1,0:T(8,128)(2,1)S(1)}, bf16[256,256]{1,0:T(8,128)(2,1)S(1)}, u32[]{:S(2)}, u32[]{:S(2)}) collective-permute-start(bf16[256,256]{1,0:T(8,128)(2,1)S(1)} %fusion.32), channel_id=1, source_target_pairs={{0,3},{1,0},{2,1},{3,2},{4,7},{5,4},{6,5},{7,6},{8,11},{9,8},{10,9... | collective-permute-start | bytes 393224 | tf_op jit(solution)/shard_map/ppermute | solution.py:36
  86.0 7.3 %collective-permute-done.12 = bf16[256,256]{1,0:T(8,128)(2,1)S(1)} collective-permute-done((bf16[256,256]{1,0:T(8,128)(2,1)S(1)}, bf16[256,256]{1,0:T(8,128)(2,1)S(1)}, u32[]{:S(2)}, u32[]{:S(2)}) %collective-permute-start.12) | collective-permute-done | bytes 131104 | tf_op jit(solution)/shard_map/ppermute | solution.py:36
  93.3 1.0 fusion.69
  94.3 6.9 %collective-permute-done.8 = bf16[256,256]{1,0:T(8,128)(2,1)S(1)} collective-permute-done((bf16[256,256]{1,0:T(8,128)(2,1)S(1)}, bf16[256,256]{1,0:T(8,128)(2,1)S(1)}, u32[]{:S(2)}, u32[]{:S(2)}) %collective-permute-start.8) | collective-permute-done | bytes 131104 | tf_op jit(solution)/shard_map/ppermute | solution.py:36
  101.3 0.9 add_convert_fusion
  (76 shorter events, 7.2 us)
Async XLA Ops:
  0.6 21.6 %copy-start = (bf16[3,1024,256]{2,1,0:T(8,128)(2,1)S(1)}, bf16[3,1024,256]{2,1,0:T(8,128)(2,1)}, u32[]{:S(2)}) copy-start(bf16[3,1024,256]{2,1,0:T(8,128)(2,1)} %param.9) | copy-start | bytes 4718596
  0.6 22.8 %copy-start.11 = (bf16[256,256]{1,0:T(8,128)(2,1)S(1)}, bf16[256,256]{1,0:T(8,128)(2,1)}, u32[]{:S(2)}) copy-start(bf16[256,256]{1,0:T(8,128)(2,1)} %param.8) | copy-start | bytes 393220
  0.7 22.8 %copy-start.3 = (bf16[256,1024]{1,0:T(8,128)(2,1)S(1)}, bf16[256,1024]{1,0:T(8,128)(2,1)}, u32[]{:S(2)}) copy-start(bf16[256,1024]{1,0:T(8,128)(2,1)} %param.13) | copy-start | bytes 1572868
  0.7 27.4 %collective-permute-start = (bf16[256,256]{1,0:T(8,128)(2,1)}, bf16[256,256]{1,0:T(8,128)(2,1)}, u32[]{:S(2)}, u32[]{:S(2)}) collective-permute-start(bf16[256,256]{1,0:T(8,128)(2,1)} %param.7), channel_id=1, source_target_pairs={{0,1},{1,2},{2,3},{3,0},{4,5},{5,6},{6,7},{7,4},{8,9},{9,10},{10,1... | collective-permute-start | bytes 393224 | tf_op jit(solution)/shard_map/ppermute | solution.py:25
  3.8 25.8 %collective-permute-start.2 = (bf16[256,256]{1,0:T(8,128)(2,1)}, bf16[256,256]{1,0:T(8,128)(2,1)}, u32[]{:S(2)}, u32[]{:S(2)}) collective-permute-start(bf16[256,256]{1,0:T(8,128)(2,1)} %param.7), channel_id=1, source_target_pairs={{0,3},{1,0},{2,1},{3,2},{4,7},{5,4},{6,5},{7,6},{8,11},{9,8},{10,9... | collective-permute-start | bytes 393224 | tf_op jit(solution)/shard_map/ppermute | solution.py:25
  5.9 24.9 %collective-permute-start.1 = (bf16[256,256]{1,0:T(8,128)(2,1)}, bf16[256,256]{1,0:T(8,128)(2,1)}, u32[]{:S(2)}, u32[]{:S(2)}) collective-permute-start(bf16[256,256]{1,0:T(8,128)(2,1)} %param.7), channel_id=1, source_target_pairs={{0,2},{1,3},{2,0},{3,1},{4,6},{5,7},{6,4},{7,5},{8,10},{9,11},{10,... | collective-permute-start | bytes 393224 | tf_op jit(solution)/shard_map/ppermute | solution.py:25
  6.8 27.3 %collective-permute-start.4 = (bf16[256,256]{1,0:T(8,128)(2,1)}, bf16[256,256]{1,0:T(8,128)(2,1)}, u32[]{:S(2)}, u32[]{:S(2)}) collective-permute-start(bf16[256,256]{1,0:T(8,128)(2,1)} %param.8), channel_id=1, source_target_pairs={{0,1},{1,2},{2,3},{3,0},{4,5},{5,6},{6,7},{7,4},{8,9},{9,10},{10,1... | collective-permute-start | bytes 393224 | tf_op jit(solution)/shard_map/ppermute | solution.py:25
  8.4 26.9 %collective-permute-start.6 = (bf16[256,256]{1,0:T(8,128)(2,1)}, bf16[256,256]{1,0:T(8,128)(2,1)}, u32[]{:S(2)}, u32[]{:S(2)}) collective-permute-start(bf16[256,256]{1,0:T(8,128)(2,1)} %param.8), channel_id=1, source_target_pairs={{0,3},{1,0},{2,1},{3,2},{4,7},{5,4},{6,5},{7,6},{8,11},{9,8},{10,9... | collective-permute-start | bytes 393224 | tf_op jit(solution)/shard_map/ppermute | solution.py:25
  12.4 26.7 %all-to-all-start.1 = ((f32[1,256,256]{2,0,1:T(1,128)}), f32[1,256,256]{2,0,1:T(1,128)S(1)}, u32[]{:S(2)}, u32[]{:S(2)}) async-start(f32[1,256,256]{2,0,1:T(1,128)} %bitcast.36), calls=%async_computation.1 | async-start | bytes 524288 | tf_op jit(solution)/shard_map/all_to_all | solution.py:85
  28.1 9.1 %collective-permute-start.5 = (bf16[256,256]{1,0:T(8,128)(2,1)}, bf16[256,256]{1,0:T(8,128)(2,1)S(1)}, u32[]{:S(2)}, u32[]{:S(2)}) collective-permute-start(bf16[256,256]{1,0:T(8,128)(2,1)} %param.8), channel_id=1, source_target_pairs={{0,2},{1,3},{2,0},{3,1},{4,6},{5,7},{6,4},{7,5},{8,10},{9,11},{10,... | collective-permute-start | bytes 393224 | tf_op jit(solution)/shard_map/ppermute | solution.py:25
  32.0 5.4 %collective-permute-start.3 = (bf16[3,2,256]{2,1,0:T(2,128)(2,1)S(1)}, bf16[3,2,256]{2,1,0:T(2,128)(2,1)S(1)}, u32[]{:S(2)}, u32[]{:S(2)}) collective-permute-start(bf16[3,2,256]{2,1,0:T(2,128)(2,1)S(1)} %slice.156), channel_id=1, source_target_pairs={{0,4},{4,8},{8,12},{12,16},{16,20},{20,24},{24,28},{1,5},{5,9},{9,... | collective-permute-start | bytes 9224 | tf_op jit(solution)/shard_map/ppermute | solution.py:17
  37.4 0.7 copy-start.1
  39.1 11.0 %all-to-all-start = ((bf16[2,256,256]{2,0,1:T(2,128)(2,1)}), bf16[2,256,256]{2,0,1:T(2,128)(2,1)}, u32[]{:S(2)}, u32[]{:S(2)}) async-start(bf16[2,256,256]{2,0,1:T(2,128)(2,1)} %copy.32), calls=%async_computation | async-start | bytes 524288 | tf_op jit(solution)/shard_map/all_to_all | solution.py:85
  43.9 1.0 %copy-start.5 = (f32[1,256,2,256]{3,1,0,2:T(8,128)S(1)}, f32[1,256,2,256]{3,1,0,2:T(8,128)}, u32[]{:S(2)}) copy-start(f32[1,256,2,256]{3,1,0,2:T(8,128)} %get-tuple-element.24) | copy-start | bytes 1572868
  44.0 1.2 %copy-start.7 = (f32[1,256,2,256]{3,1,0,2:T(8,128)S(1)}, f32[1,256,2,256]{3,1,0,2:T(8,128)}, u32[]{:S(2)}) copy-start(f32[1,256,2,256]{3,1,0,2:T(8,128)} %get-tuple-element.27) | copy-start | bytes 1572868
  52.1 1.0 %copy-start.6 = (f32[1,256,2,256]{3,1,0,2:T(8,128)S(1)}, f32[1,256,2,256]{3,1,0,2:T(8,128)}, u32[]{:S(2)}) copy-start(f32[1,256,2,256]{3,1,0,2:T(8,128)} %get-tuple-element.24) | copy-start | bytes 1572868
  52.1 1.2 %copy-start.8 = (f32[1,256,2,256]{3,1,0,2:T(8,128)S(1)}, f32[1,256,2,256]{3,1,0,2:T(8,128)}, u32[]{:S(2)}) copy-start(f32[1,256,2,256]{3,1,0,2:T(8,128)} %get-tuple-element.27) | copy-start | bytes 1572868
  56.5 1.0 %copy-start.9 = (f32[1,256,2,256]{3,1,2,0:T(8,128)S(1)}, f32[1,256,2,256]{3,1,2,0:T(8,128)}, u32[]{:S(2)}) copy-start(f32[1,256,2,256]{3,1,2,0:T(8,128)} %get-tuple-element.23) | copy-start | bytes 1572868
  56.5 1.2 %copy-start.10 = (f32[1,256,2,256]{3,1,2,0:T(8,128)S(1)}, f32[1,256,2,256]{3,1,2,0:T(8,128)}, u32[]{:S(2)}) copy-start(f32[1,256,2,256]{3,1,2,0:T(8,128)} %get-tuple-element.28) | copy-start | bytes 1572868
  60.8 5.0 %copy-start.2 = (f32[256,256]{1,0:T(8,128)S(1)}, f32[256,256]{1,0:T(8,128)}, u32[]{:S(2)}) copy-start(f32[256,256]{1,0:T(8,128)} %copy-done.1) | copy-start | bytes 786436
  62.4 11.7 %all-to-all-start.2 = ((bf16[2,32,8,258]{3,1,0,2:T(8,128)(2,1)}), bf16[2,32,8,258]{3,1,0,2:T(8,128)(2,1)S(1)}, u32[]{:S(2)}, u32[]{:S(2)}) async-start(bf16[2,32,8,258]{3,1,0,2:T(8,128)(2,1)} %copy.43), calls=%async_computation.2 | async-start | bytes 786432 | tf_op jit(solution)/shard_map/all_to_all | solution.py:98
  65.8 9.4 %copy-start.12 = (f32[256]{0:T(256)S(1)}, f32[256]{0:T(256)}, u32[]{:S(2)}) copy-start(f32[256]{0:T(256)} %param.11) | copy-start | bytes 3076
  65.9 10.6 %collective-permute-start.10 = (f32[4,2,256]{2,1,0:T(2,128)S(1)}, f32[4,2,256]{2,1,0:T(2,128)S(1)}, u32[]{:S(2)}, u32[]{:S(2)}) collective-permute-start(f32[4,2,256]{2,1,0:T(2,128)S(1)} %pad_maximum_fusion.12), channel_id=1, source_target_pairs={{4,0},{8,4},{12,8},{16,12},{20,16},{24,20},{28,24},{5,1},{9,5},{13... | collective-permute-start | bytes 24584 | tf_op jit(solution)/shard_map/ppermute | solution.py:17
  77.3 1.2 %copy-start.4 = (bf16[256,1024]{1,0:T(8,128)(2,1)S(1)}, bf16[256,1024]{1,0:T(8,128)(2,1)}, u32[]{:S(2)}) copy-start(bf16[256,1024]{1,0:T(8,128)(2,1)} %param.13) | copy-start | bytes 1572868
  78.9 14.4 %collective-permute-start.12 = (bf16[256,256]{1,0:T(8,128)(2,1)S(1)}, bf16[256,256]{1,0:T(8,128)(2,1)S(1)}, u32[]{:S(2)}, u32[]{:S(2)}) collective-permute-start(bf16[256,256]{1,0:T(8,128)(2,1)S(1)} %fusion.31), channel_id=1, source_target_pairs={{0,2},{1,3},{2,0},{3,1},{4,6},{5,7},{6,4},{7,5},{8,10},{9,11},{10,... | collective-permute-start | bytes 393224 | tf_op jit(solution)/shard_map/ppermute | solution.py:36
  81.4 11.9 %collective-permute-start.11 = (bf16[256,256]{1,0:T(8,128)(2,1)S(1)}, bf16[256,256]{1,0:T(8,128)(2,1)S(1)}, u32[]{:S(2)}, u32[]{:S(2)}) collective-permute-start(bf16[256,256]{1,0:T(8,128)(2,1)S(1)} %fusion.30), channel_id=1, source_target_pairs={{0,1},{1,2},{2,3},{3,0},{4,5},{5,6},{6,7},{7,4},{8,9},{9,10},{10,1... | collective-permute-start | bytes 393224 | tf_op jit(solution)/shard_map/ppermute | solution.py:36
  81.4 11.9 %collective-permute-start.13 = (bf16[256,256]{1,0:T(8,128)(2,1)S(1)}, bf16[256,256]{1,0:T(8,128)(2,1)S(1)}, u32[]{:S(2)}, u32[]{:S(2)}) collective-permute-start(bf16[256,256]{1,0:T(8,128)(2,1)S(1)} %fusion.32), channel_id=1, source_target_pairs={{0,3},{1,0},{2,1},{3,2},{4,7},{5,4},{6,5},{7,6},{8,11},{9,8},{10,9... | collective-permute-start | bytes 393224 | tf_op jit(solution)/shard_map/ppermute | solution.py:36
  85.2 16.1 %collective-permute-start.8 = (bf16[256,256]{1,0:T(8,128)(2,1)S(1)}, bf16[256,256]{1,0:T(8,128)(2,1)S(1)}, u32[]{:S(2)}, u32[]{:S(2)}) collective-permute-start(bf16[256,256]{1,0:T(8,128)(2,1)S(1)} %convolution_convert_fusion.1), channel_id=1, source_target_pairs={{0,2},{1,3},{2,0},{3,1},{4,6},{5,7},{6,4},{7,5},{8,10},{9,11},{10,... | collective-permute-start | bytes 393224 | tf_op jit(solution)/shard_map/ppermute | solution.py:36
  85.2 16.1 %collective-permute-start.7 = (bf16[256,256]{1,0:T(8,128)(2,1)S(1)}, bf16[256,256]{1,0:T(8,128)(2,1)S(1)}, u32[]{:S(2)}, u32[]{:S(2)}) collective-permute-start(bf16[256,256]{1,0:T(8,128)(2,1)S(1)} %convolution_convert_fusion.2), channel_id=1, source_target_pairs={{0,1},{1,2},{2,3},{3,0},{4,5},{5,6},{6,7},{7,4},{8,9},{9,10},{10,1... | collective-permute-start | bytes 393224 | tf_op jit(solution)/shard_map/ppermute | solution.py:36
  93.3 8.0 %collective-permute-start.9 = (bf16[256,256]{1,0:T(8,128)(2,1)S(1)}, bf16[256,256]{1,0:T(8,128)(2,1)S(1)}, u32[]{:S(2)}, u32[]{:S(2)}) collective-permute-start(bf16[256,256]{1,0:T(8,128)(2,1)S(1)} %convolution_convert_fusion), channel_id=1, source_target_pairs={{0,3},{1,0},{2,1},{3,2},{4,7},{5,4},{6,5},{7,6},{8,11},{9,8},{10,9... | collective-permute-start | bytes 393224 | tf_op jit(solution)/shard_map/ppermute | solution.py:36

commit v15 on v11

--- a/solution.py
+++ b/solution.py
@@ -29,14 +29,9 @@
 
 def panel_reduce_scatter(block_of):
     count = lax.axis_size("panel")
-    me = lax.axis_index("panel")
-    total = block_of(me)
-    for k in range(1, count):
-        sent = block_of((me + k) % count).astype(jnp.bfloat16)
-        total = total + lax.ppermute(
-            sent, "panel", [(i, (i + k) % count) for i in range(count)]
-        ).astype(jnp.float32)
-    return total.astype(jnp.bfloat16)
+    blocks = jnp.stack([block_of(dest) for dest in range(count)]).astype(jnp.bfloat16)
+    received = lax.all_to_all(blocks, "panel", 0, 0, tiled=True)
+    return received.astype(jnp.float32).sum(axis=0).astype(jnp.bfloat16)
 
 
 def phase(numer, period):

time: 102 us -> 106 us (1.039)
  waiting for transfers between devices: 19.1 us -> 31.7 us
  other arithmetic: 13 us -> 9.53 us
  matrix products: 20.3 us -> 17.4 us
  local copies, waits for them, and re-layouts: 8.92 us -> 7.38 us
    all_to_all x0 -> x2, waiting for transfers between devices: none -> 26.4 us  [panel_reduce_scatter(): received = lax.all_to_all(blocks, 'panel', 0, 0, tiled=True)]
    ppermute x6 -> x0, waiting for transfers between devices: 14.6 us -> none  [panel_reduce_scatter(): lax.ppermute(sent, 'panel', [(i, (i + k) % count) for i in range(count)])]
    all_to_all x0 -> x2, starting transfers between devices: none -> 7.32 us  [panel_reduce_scatter(): received = lax.all_to_all(blocks, 'panel', 0, 0, tiled=True)]
    ppermute x6 -> x0, starting transfers between devices: 7.07 us -> none  [panel_reduce_scatter(): lax.ppermute(sent, 'panel', [(i, (i + k) % count) for i in range(count)])]
    another operation x2 -> x4, other arithmetic: 0.12 us -> 1.89 us  [the longest x2 1.77 us: panel_reduce_scatter(): jnp.stack([block_of(dest) for dest in range(count)]).astype(jnp.bfloat16)]
    reduce_sum x0 -> x2, other arithmetic: none -> 1.49 us  [panel_reduce_scatter(): return received.astype(jnp.float32).sum(axis=0).astype(jnp.bfloat16)]
    another operation x1, other arithmetic: 2.76 us -> 1.3 us  [transform_tables(): jnp.stack([jnp.stack([cos_b, -sin_b], axis=1), jnp.stack([sin_b, cos_b],...]
    unnamed x27 -> x19, local copies, waits for them, and re-layouts: 4.24 us -> 3.71 us
  transfers between devices with their start and end apart: 16 -> 12, of which waited for: 5 -> 4; matrix products, arithmetic and copies ran while one was open for 25% -> 19% of each run, Pallas kernels for 0% -> 0%
where the time goes in v15:
time: 106 us; the launch traced here: 105 us
  waiting for transfers between devices  31.7 us (30%)
  starting transfers between devices  28.9 us (27%)
  matrix products  17.4 us (16%)
  other arithmetic  9.53 us (9%)
  blocking collectives  9.32 us (9%)
  local copies, waits for them, and re-layouts  7.38 us (7%)
  between operations  1.18 us (1%)
    all_to_all x2, waiting for transfers between devices, panel_reduce_scatter(): received = lax.all_to_all(blocks, 'panel', 0, 0, tiled=True)  26.4 us
    ppermute x6, starting transfers between devices, panel_parts(): lax.ppermute(value, 'panel', [(i, (i + k) % count) for i in range(count)])  10.3 us
    all_to_all x1, blocking collectives, to_rows(): lax.all_to_all(columns.astype(wire), 'seq', split_axis=2, concat_axis=1,...  9.32 us
    all_to_all x2, starting transfers between devices, to_columns(): lax.all_to_all(jnp.swapaxes(rows, 1, 2).astype(wire), 'seq', split_axis=1...  7.86 us
    all_to_all x2, starting transfers between devices, panel_reduce_scatter(): received = lax.all_to_all(blocks, 'panel', 0, 0, tiled=True)  7.32 us
    dot_general x4, matrix products, local(): jnp.einsum('td,jdc->jtc', part, lax.dynamic_slice_in_dim(in_weight, sourc...  5.02 us
    all_to_all x2, waiting for transfers between devices, to_columns(): lax.all_to_all(jnp.swapaxes(rows, 1, 2).astype(wire), 'seq', split_axis=1...  4.11 us
    dot_general x2, matrix products, forward_spectrum(): jnp.einsum('bcerkm,rmsq->bceskq', spread, stage_b, precision=STAGE_B_PREC...  3.84 us
  transfers between devices with their start and end apart: 12, of which 4 were waited for; matrix products, arithmetic and copies ran while one was open for 19% of the time, Pallas kernels for 0%

profile of v15, /device:TPU:0, one launch (start us, length us, event | category | flops | bytes accessed | tf_op | source)
XLA Modules:
  0.0 105.4 jit_solution(13450745048445673913)
XLA Ops:
  0.7 3.1 %collective-permute-start = (bf16[256,256]{1,0:T(8,128)(2,1)}, bf16[256,256]{1,0:T(8,128)(2,1)}, u32[]{:S(2)}, u32[]{:S(2)}) collective-permute-start(bf16[256,256]{1,0:T(8,128)(2,1)} %param.7), channel_id=1, source_target_pairs={{0,1},{1,2},{2,3},{3,0},{4,5},{5,6},{6,7},{7,4},{8,9},{9,10},{10,1... | collective-permute-start | bytes 393224 | tf_op jit(solution)/shard_map/ppermute | solution.py:25
  3.8 2.1 %collective-permute-start.2 = (bf16[256,256]{1,0:T(8,128)(2,1)}, bf16[256,256]{1,0:T(8,128)(2,1)}, u32[]{:S(2)}, u32[]{:S(2)}) collective-permute-start(bf16[256,256]{1,0:T(8,128)(2,1)} %param.7), channel_id=1, source_target_pairs={{0,3},{1,0},{2,1},{3,2},{4,7},{5,4},{6,5},{7,6},{8,11},{9,8},{10,9... | collective-permute-start | bytes 393224 | tf_op jit(solution)/shard_map/ppermute | solution.py:25
  5.8 0.9 collective-permute-start.1
  6.8 1.6 %collective-permute-start.4 = (bf16[256,256]{1,0:T(8,128)(2,1)}, bf16[256,256]{1,0:T(8,128)(2,1)}, u32[]{:S(2)}, u32[]{:S(2)}) collective-permute-start(bf16[256,256]{1,0:T(8,128)(2,1)} %param.8), channel_id=1, source_target_pairs={{0,1},{1,2},{2,3},{3,0},{4,5},{5,6},{6,7},{7,4},{8,9},{9,10},{10,1... | collective-permute-start | bytes 393224 | tf_op jit(solution)/shard_map/ppermute | solution.py:25
  8.4 2.2 %collective-permute-start.6 = (bf16[256,256]{1,0:T(8,128)(2,1)}, bf16[256,256]{1,0:T(8,128)(2,1)S(1)}, u32[]{:S(2)}, u32[]{:S(2)}) collective-permute-start(bf16[256,256]{1,0:T(8,128)(2,1)} %param.8), channel_id=1, source_target_pairs={{0,3},{1,0},{2,1},{3,2},{4,7},{5,4},{6,5},{7,6},{8,11},{9,8},{10,9... | collective-permute-start | bytes 393224 | tf_op jit(solution)/shard_map/ppermute | solution.py:25
  10.6 1.8 %copy.63 = f32[1,256,256]{1,0,2:T(1,128)} copy(f32[1,256,256]{2,1,0:T(8,128)} %bitcast.240) | data formatting | bytes 524288 | tf_op jit(solution)/shard_map/broadcast_in_dim | solution.py:113
  12.4 3.7 %all-to-all-start.1 = ((f32[1,256,256]{2,0,1:T(1,128)}), f32[1,256,256]{2,0,1:T(1,128)S(1)}, u32[]{:S(2)}, u32[]{:S(2)}) async-start(f32[1,256,256]{2,0,1:T(1,128)} %bitcast.36), calls=%async_computation.1 | async-start | bytes 524288 | tf_op jit(solution)/shard_map/all_to_all | solution.py:80
  16.3 1.0 fusion.98
  17.4 1.0 fusion.100
  18.3 0.7 slice_bitcast_fusion.5
  19.1 1.3 %fusion.65 = f32[3,256,256]{1,2,0:T(8,128)S(1)} fusion(bf16[3,1024,256]{2,1,0:T(8,128)(2,1)} %param.9, s32[]{:T(128)S(6)} %select_n.128, bf16[256,256]{1,0:T(8,128)(2,1)} %param.7), kind=kOutput, calls=%fused_computation.99 | convolution fusion | flops 100663296 | bytes 1310724 | tf_op jit(solution)/shard_map/td,jdc->jtc/dot_general | solution.py:117
  20.8 1.3 %fusion.55 = (f32[1,256,2,256]{3,1,2,0:T(8,128)}, f32[1,256,2,256]{3,1,0,2:T(8,128)S(1)}, f32[1,256,2,256]{3,1,0,2:T(8,128)}, f32[1,256,2,256]{3,1,2,0:T(8,128)}) fusion(f32[256,1,256]{2,0,1:T(8,128)S(1)} %get-tuple-element.35, f32[256,1,256]{2,0,1:T(8,128)S(1)} %fusion.100, f32[256,1,256]{2,0,1:T(8,128)S(1)} %get-tuple-element.34), kind=kLoop, calls=%fused_computation.80 | loop fusion | flops 524288 | bytes 2883584 | tf_op jit(solution)/shard_map/stack | solution.py:61
  22.1 0.3 collective-permute-start.5
  22.5 1.3 %convolution_add_fusion.1 = f32[3,256,256]{1,2,0:T(8,128)S(1)} fusion(f32[3,256,256]{1,2,0:T(8,128)S(1)} %fusion.65, bf16[3,1024,256]{2,1,0:T(8,128)(2,1)} %param.9, s32[]{:T(128)S(6)} %select_n.130, bf16[256,256]{1,0:T(8,128)(2,1)} %collective-permute-done), kind=kOutput, calls=%fused_computation.19 | convolution fusion | flops 100859904 | bytes 2097156 | tf_op jit(solution)/shard_map/td,jdc->jtc/dot_general | solution.py:117
  23.8 1.2 %fusion.61 = f32[3,256,256]{1,2,0:T(8,128)S(1)} fusion(bf16[3,1024,256]{2,1,0:T(8,128)(2,1)S(1)} %copy-done.3, s32[]{:T(128)S(6)} %select_n.134, bf16[256,256]{1,0:T(8,128)(2,1)} %collective-permute-done.2), kind=kOutput, calls=%fused_computation.95 | convolution fusion | flops 100663296 | bytes 1310724 | tf_op jit(solution)/shard_map/td,jdc->jtc/dot_general | solution.py:117
  25.0 1.2 %fusion.21 = bf16[3,256,256]{2,1,0:T(8,128)(2,1)S(1)} fusion(f32[3,256,256]{1,2,0:T(8,128)S(1)} %fusion.61, f32[3,256,256]{1,2,0:T(8,128)S(1)} %convolution_add_fusion.1, bf16[3,1024,256]{2,1,0:T(8,128)(2,1)S(1)} %copy-done.3, s32[]{:T(128)S(6)} %select_n.132, bf16[256,256]{1,0:T(8,128)(2,1)} %collective-permute-done.1), kind=kOutput, calls=%fused_computation.22 | convolution fusion | flops 101253120 | bytes 2490372 | tf_op jit(solution)/shard_map/td,jdc->jtc/dot_general | solution.py:117
  26.2 2.1 %collective-permute-start.3 = (bf16[3,2,256]{2,1,0:T(2,128)(2,1)S(1)}, bf16[3,2,256]{2,1,0:T(2,128)(2,1)S(1)}, u32[]{:S(2)}, u32[]{:S(2)}) collective-permute-start(bf16[3,2,256]{2,1,0:T(2,128)(2,1)S(1)} %slice.111), channel_id=1, source_target_pairs={{0,4},{4,8},{8,12},{12,16},{16,20},{20,24},{24,28},{1,5},{5,9},{9,... | collective-permute-start | bytes 9224 | tf_op jit(solution)/shard_map/ppermute | solution.py:17
  28.4 1.1 %convolution_add_fusion.3 = f32[256,256]{0,1:T(8,128)S(1)} fusion(f32[256,256]{0,1:T(8,128)S(1)} %fusion.96, bf16[256,256]{1,0:T(8,128)(2,1)} %collective-permute-done.4, bf16[256,1024]{1,0:T(8,128)(2,1)S(1)} %copy-done, s32[]{:T(128)S(6)} %select_n.130), kind=kOutput, calls=%fused_computation.31 | convolution fusion | flops 33619968 | bytes 786436 | tf_op jit(solution)/shard_map/dot_general | solution.py:125
  29.8 1.2 %collective-permute-done.5 = bf16[256,256]{1,0:T(8,128)(2,1)S(1)} collective-permute-done((bf16[256,256]{1,0:T(8,128)(2,1)S(1)}, bf16[256,256]{1,0:T(8,128)(2,1)S(1)}, u32[]{:S(2)}, u32[]{:S(2)}) %collective-permute-start.5) | collective-permute-done | bytes 131104 | tf_op jit(solution)/shard_map/ppermute | solution.py:25
  31.7 0.9 copy.32
  32.5 4.1 %all-to-all-start = ((bf16[2,256,256]{2,0,1:T(2,128)(2,1)}), bf16[2,256,256]{2,0,1:T(2,128)(2,1)S(1)}, u32[]{:S(2)}, u32[]{:S(2)}) async-start(bf16[2,256,256]{2,0,1:T(2,128)(2,1)} %copy.32), calls=%async_computation | async-start | bytes 524288 | tf_op jit(solution)/shard_map/all_to_all | solution.py:80
  36.7 0.6 convolution_bitcast_fusion.2
  37.5 0.8 copy-done.1
  38.3 1.1 %convolution_bitcast_fusion.1 = f32[1,32,2,2,8,256]{5,1,4,2,0,3:T(8,128)S(1)} fusion(f32[32,2,2,8,256]{4,3,0,2,1:T(8,128)S(1)} %maximum_bitcast_fusion.3, f32[1,256,2,256]{3,1,0,2:T(8,128)S(1)} %get-tuple-element.21, f32[1,256,2,256]{3,1,0,2:T(8,128)S(1)} %copy-done.1), kind=kOutput, calls=%fused_computation.15 | convolution fusion | flops 805568512 | bytes 3145728 | tf_op jit(solution)/shard_map/bcerkm,rmsq->bceskq/dot_general | solution.py:98
  39.5 4.1 %all-to-all-done = bf16[2,256,256]{2,0,1:T(2,128)(2,1)S(1)} async-done(((bf16[2,256,256]{2,0,1:T(2,128)(2,1)}), bf16[2,256,256]{2,0,1:T(2,128)(2,1)S(1)}, u32[]{:S(2)}, u32[]{:S(2)}) %all-to-all-start) | async-done | bytes 262176 | tf_op jit(solution)/shard_map/all_to_all | solution.py:80
  43.6 0.8 convolution_bitcast_fusion
  44.4 0.3 multiply_subtract_fusion.1
  44.9 0.9 copy-done.2
  45.7 2.7 %fusion.10 = f32[2,32,2,2,8,256]{5,1,4,2,0,3:T(8,128)S(1)} fusion(f32[2,32,2,2,8,256]{5,4,3,2,1,0:T(8,128)S(1)} %pad_maximum_fusion, f32[1,256,2,256]{3,1,0,2:T(8,128)S(1)} %get-tuple-element.21, f32[1,256,2,256]{3,1,0,2:T(8,128)S(1)} %copy-done.2), kind=kOutput, calls=%fused_computation.12 | convolution fusion | flops 1610874880 | bytes 5242880 | tf_op jit(solution)/shard_map/bcerkm,rmsq->bceskq/dot_general | solution.py:98
  48.4 0.4 multiply_subtract_fusion.3
  49.1 0.8 copy-done.5
  50.1 2.7 %fusion.13 = f32[2,32,2,2,8,256]{5,4,3,2,1,0:T(8,128)S(1)} fusion(f32[2,32,2,2,8,256,1]{5,1,4,2,0,3,6:T(8,128)S(1)} %maximum_bitcast_fusion, f32[1,256,2,256]{3,1,2,0:T(8,128)S(1)} %copy-done.6, f32[1,256,2,256]{3,1,2,0:T(8,128)S(1)} %copy-done.5), kind=kOutput, calls=%fused_computation.13 | convolution fusion | flops 1610874880 | bytes 5242880 | tf_op jit(solution)/shard_map/bceskq,sqrm->bcerkm/dot_general | solution.py:103
  53.1 0.7 fusion.27
  53.8 9.3 %all_to_all.49 = bf16[2,32,8,256]{3,1,0,2:T(8,128)(2,1)S(1)} all-to-all(bf16[2,32,8,256]{3,1,0,2:T(8,128)(2,1)S(1)} %copy.43), channel_id=1, replica_groups=mesh['seq'=8,'panel'=4] {'seq'}, dimensions={2} | all-to-all | bytes 524288 | tf_op jit(solution)/shard_map/all_to_all | solution.py:88
  64.5 1.3 %collective-permute-start.7 = (f32[3,2,256]{2,1,0:T(2,128)S(1)}, f32[3,2,256]{2,1,0:T(2,128)S(1)}, u32[]{:S(2)}, u32[]{:S(2)}) collective-permute-start(f32[3,2,256]{2,1,0:T(2,128)S(1)} %slice.132), channel_id=1, source_target_pairs={{4,0},{8,4},{12,8},{16,12},{20,16},{24,20},{28,24},{5,1},{9,5},{13... | collective-permute-start | bytes 18440 | tf_op jit(solution)/shard_map/ppermute | solution.py:17
  65.8 0.9 pad_maximum_fusion.10
  66.7 3.9 %all-to-all-start.3 = ((bf16[4,256,256]{2,1,0:T(8,128)(2,1)}), bf16[4,256,256]{2,1,0:T(8,128)(2,1)S(1)}, u32[]{:S(2)}, u32[]{:S(2)}) async-start(bf16[4,256,256]{2,1,0:T(8,128)(2,1)} %pad_maximum_fusion.10), calls=%async_computation.3 | async-start | bytes 1048576 | tf_op jit(solution)/shard_map/all_to_all | solution.py:33
  70.8 1.1 %copy-done.4 = bf16[3,1024,256]{2,1,0:T(8,128)(2,1)S(1)} copy-done((bf16[3,1024,256]{2,1,0:T(8,128)(2,1)S(1)}, bf16[3,1024,256]{2,1,0:T(8,128)(2,1)}, u32[]{:S(2)}) %copy-start.4) | copy-done | bytes 1572888
  71.9 0.3 fusion.34
  72.2 0.3 fusion.35
  72.5 0.3 fusion.36
  72.8 0.3 fusion.37
  73.2 0.9 pad_maximum_fusion.11
  74.0 12.3 %all-to-all-done.3 = bf16[4,256,256]{2,1,0:T(8,128)(2,1)S(1)} async-done(((bf16[4,256,256]{2,1,0:T(8,128)(2,1)}), bf16[4,256,256]{2,1,0:T(8,128)(2,1)S(1)}, u32[]{:S(2)}, u32[]{:S(2)}) %all-to-all-start.3) | async-done | bytes 524320 | tf_op jit(solution)/shard_map/all_to_all | solution.py:33
  86.3 3.5 %all-to-all-start.4 = ((bf16[4,256,256]{2,1,0:T(8,128)(2,1)}), bf16[4,256,256]{2,1,0:T(8,128)(2,1)S(1)}, u32[]{:S(2)}, u32[]{:S(2)}) async-start(bf16[4,256,256]{2,1,0:T(8,128)(2,1)} %pad_maximum_fusion.11), calls=%async_computation.4 | async-start | bytes 1048576 | tf_op jit(solution)/shard_map/all_to_all | solution.py:33
  89.8 0.7 reduce_sum.24
  90.5 14.1 %all-to-all-done.4 = bf16[4,256,256]{2,1,0:T(8,128)(2,1)S(1)} async-done(((bf16[4,256,256]{2,1,0:T(8,128)(2,1)}), bf16[4,256,256]{2,1,0:T(8,128)(2,1)S(1)}, u32[]{:S(2)}, u32[]{:S(2)}) %all-to-all-start.4) | async-done | bytes 524320 | tf_op jit(solution)/shard_map/all_to_all | solution.py:33
  104.7 0.7 reduce_sum.25
  (57 shorter events, 4.2 us)
Async XLA Ops:
  0.6 19.8 %copy-start.7 = (bf16[256,256]{1,0:T(8,128)(2,1)S(1)}, bf16[256,256]{1,0:T(8,128)(2,1)}, u32[]{:S(2)}) copy-start(bf16[256,256]{1,0:T(8,128)(2,1)} %param.8) | copy-start | bytes 393220
  0.6 19.8 %copy-start = (bf16[256,1024]{1,0:T(8,128)(2,1)S(1)}, bf16[256,1024]{1,0:T(8,128)(2,1)}, u32[]{:S(2)}) copy-start(bf16[256,1024]{1,0:T(8,128)(2,1)} %param.13) | copy-start | bytes 1572868
  0.7 21.5 %collective-permute-start = (bf16[256,256]{1,0:T(8,128)(2,1)}, bf16[256,256]{1,0:T(8,128)(2,1)}, u32[]{:S(2)}, u32[]{:S(2)}) collective-permute-start(bf16[256,256]{1,0:T(8,128)(2,1)} %param.7), channel_id=1, source_target_pairs={{0,1},{1,2},{2,3},{3,0},{4,5},{5,6},{6,7},{7,4},{8,9},{9,10},{10,1... | collective-permute-start | bytes 393224 | tf_op jit(solution)/shard_map/ppermute | solution.py:25
  3.8 20.1 %collective-permute-start.2 = (bf16[256,256]{1,0:T(8,128)(2,1)}, bf16[256,256]{1,0:T(8,128)(2,1)}, u32[]{:S(2)}, u32[]{:S(2)}) collective-permute-start(bf16[256,256]{1,0:T(8,128)(2,1)} %param.7), channel_id=1, source_target_pairs={{0,3},{1,0},{2,1},{3,2},{4,7},{5,4},{6,5},{7,6},{8,11},{9,8},{10,9... | collective-permute-start | bytes 393224 | tf_op jit(solution)/shard_map/ppermute | solution.py:25
  5.8 19.2 %collective-permute-start.1 = (bf16[256,256]{1,0:T(8,128)(2,1)}, bf16[256,256]{1,0:T(8,128)(2,1)}, u32[]{:S(2)}, u32[]{:S(2)}) collective-permute-start(bf16[256,256]{1,0:T(8,128)(2,1)} %param.7), channel_id=1, source_target_pairs={{0,2},{1,3},{2,0},{3,1},{4,6},{5,7},{6,4},{7,5},{8,10},{9,11},{10,... | collective-permute-start | bytes 393224 | tf_op jit(solution)/shard_map/ppermute | solution.py:25
  6.8 21.6 %collective-permute-start.4 = (bf16[256,256]{1,0:T(8,128)(2,1)}, bf16[256,256]{1,0:T(8,128)(2,1)}, u32[]{:S(2)}, u32[]{:S(2)}) collective-permute-start(bf16[256,256]{1,0:T(8,128)(2,1)} %param.8), channel_id=1, source_target_pairs={{0,1},{1,2},{2,3},{3,0},{4,5},{5,6},{6,7},{7,4},{8,9},{9,10},{10,1... | collective-permute-start | bytes 393224 | tf_op jit(solution)/shard_map/ppermute | solution.py:25
  8.4 21.2 %collective-permute-start.6 = (bf16[256,256]{1,0:T(8,128)(2,1)}, bf16[256,256]{1,0:T(8,128)(2,1)S(1)}, u32[]{:S(2)}, u32[]{:S(2)}) collective-permute-start(bf16[256,256]{1,0:T(8,128)(2,1)} %param.8), channel_id=1, source_target_pairs={{0,3},{1,0},{2,1},{3,2},{4,7},{5,4},{6,5},{7,6},{8,11},{9,8},{10,9... | collective-permute-start | bytes 393224 | tf_op jit(solution)/shard_map/ppermute | solution.py:25
  12.4 20.1 %all-to-all-start.1 = ((f32[1,256,256]{2,0,1:T(1,128)}), f32[1,256,256]{2,0,1:T(1,128)S(1)}, u32[]{:S(2)}, u32[]{:S(2)}) async-start(f32[1,256,256]{2,0,1:T(1,128)} %bitcast.36), calls=%async_computation.1 | async-start | bytes 524288 | tf_op jit(solution)/shard_map/all_to_all | solution.py:80
  20.8 3.0 %copy-start.3 = (bf16[3,1024,256]{2,1,0:T(8,128)(2,1)S(1)}, bf16[3,1024,256]{2,1,0:T(8,128)(2,1)}, u32[]{:S(2)}) copy-start(bf16[3,1024,256]{2,1,0:T(8,128)(2,1)} %param.9) | copy-start | bytes 4718596
  22.1 8.8 %collective-permute-start.5 = (bf16[256,256]{1,0:T(8,128)(2,1)S(1)}, bf16[256,256]{1,0:T(8,128)(2,1)S(1)}, u32[]{:S(2)}, u32[]{:S(2)}) collective-permute-start(bf16[256,256]{1,0:T(8,128)(2,1)S(1)} %copy-done.7), channel_id=1, source_target_pairs={{0,2},{1,3},{2,0},{3,1},{4,6},{5,7},{6,4},{7,5},{8,10},{9,11},{10,... | collective-permute-start | bytes 393224 | tf_op jit(solution)/shard_map/ppermute | solution.py:25
  26.2 5.0 %collective-permute-start.3 = (bf16[3,2,256]{2,1,0:T(2,128)(2,1)S(1)}, bf16[3,2,256]{2,1,0:T(2,128)(2,1)S(1)}, u32[]{:S(2)}, u32[]{:S(2)}) collective-permute-start(bf16[3,2,256]{2,1,0:T(2,128)(2,1)S(1)} %slice.111), channel_id=1, source_target_pairs={{0,4},{4,8},{8,12},{12,16},{16,20},{20,24},{24,28},{1,5},{5,9},{9,... | collective-permute-start | bytes 9224 | tf_op jit(solution)/shard_map/ppermute | solution.py:17
  32.5 11.0 %all-to-all-start = ((bf16[2,256,256]{2,0,1:T(2,128)(2,1)}), bf16[2,256,256]{2,0,1:T(2,128)(2,1)S(1)}, u32[]{:S(2)}, u32[]{:S(2)}) async-start(bf16[2,256,256]{2,0,1:T(2,128)(2,1)} %copy.32), calls=%async_computation | async-start | bytes 524288 | tf_op jit(solution)/shard_map/all_to_all | solution.py:80
  37.3 1.0 copy-start.1
  44.7 1.0 copy-start.2
  48.9 1.0 copy-start.5
  48.9 1.2 %copy-start.6 = (f32[1,256,2,256]{3,1,2,0:T(8,128)S(1)}, f32[1,256,2,256]{3,1,2,0:T(8,128)}, u32[]{:S(2)}) copy-start(f32[1,256,2,256]{3,1,2,0:T(8,128)} %get-tuple-element.25) | copy-start | bytes 1572868
  53.1 10.3 %copy-start.8 = (f32[256]{0:T(256)S(1)}, f32[256]{0:T(256)}, u32[]{:S(2)}) copy-start(f32[256]{0:T(256)} %param.11) | copy-start | bytes 3076
  64.5 6.1 %collective-permute-start.7 = (f32[3,2,256]{2,1,0:T(2,128)S(1)}, f32[3,2,256]{2,1,0:T(2,128)S(1)}, u32[]{:S(2)}, u32[]{:S(2)}) collective-permute-start(f32[3,2,256]{2,1,0:T(2,128)S(1)} %slice.132), channel_id=1, source_target_pairs={{4,0},{8,4},{12,8},{16,12},{20,16},{24,20},{28,24},{5,1},{9,5},{13... | collective-permute-start | bytes 18440 | tf_op jit(solution)/shard_map/ppermute | solution.py:17
  66.7 19.6 %all-to-all-start.3 = ((bf16[4,256,256]{2,1,0:T(8,128)(2,1)}), bf16[4,256,256]{2,1,0:T(8,128)(2,1)S(1)}, u32[]{:S(2)}, u32[]{:S(2)}) async-start(bf16[4,256,256]{2,1,0:T(8,128)(2,1)} %pad_maximum_fusion.10), calls=%async_computation.3 | async-start | bytes 1048576 | tf_op jit(solution)/shard_map/all_to_all | solution.py:33
  70.5 1.4 %copy-start.4 = (bf16[3,1024,256]{2,1,0:T(8,128)(2,1)S(1)}, bf16[3,1024,256]{2,1,0:T(8,128)(2,1)}, u32[]{:S(2)}) copy-start(bf16[3,1024,256]{2,1,0:T(8,128)(2,1)} %param.9) | copy-start | bytes 4718596
  86.3 18.4 %all-to-all-start.4 = ((bf16[4,256,256]{2,1,0:T(8,128)(2,1)}), bf16[4,256,256]{2,1,0:T(8,128)(2,1)S(1)}, u32[]{:S(2)}, u32[]{:S(2)}) async-start(bf16[4,256,256]{2,1,0:T(8,128)(2,1)} %pad_maximum_fusion.11), calls=%async_computation.4 | async-start | bytes 1048576 | tf_op jit(solution)/shard_map/all_to_all | solution.py:33

commit v16 on v11

--- a/solution.py
+++ b/solution.py
@@ -63,11 +63,8 @@
     stage_b = jnp.stack(
         [jnp.stack([cos_b, sin_b], axis=1), jnp.stack([-sin_b, cos_b], axis=1)]
     )
-    stage_b_inv = jnp.stack(
-        [jnp.stack([cos_b, -sin_b], axis=1), jnp.stack([sin_b, cos_b], axis=1)]
-    )
     stage_a_inv = stage_a * (0.5 / length)
-    return stage_a, twiddle, stage_b, stage_b_inv, stage_a_inv
+    return stage_a, twiddle, stage_b, stage_a_inv
 
 
 def complex_scale(value, cos_part, sin_part, axis):
@@ -97,15 +94,15 @@
 
 
 def forward_spectrum(columns, tables):
-    stage_a, twiddle, stage_b, _, _ = tables
+    stage_a, twiddle, stage_b, _ = tables
     spread = jnp.einsum("erkp,bcpm->bcerkm", stage_a, columns, precision=STAGE_A_PRECISION)
     spread = complex_scale(spread, twiddle[0], twiddle[1], 3)
     return jnp.einsum("bcerkm,rmsq->bceskq", spread, stage_b, precision=STAGE_B_PRECISION)
 
 
 def inverse_spectrum(spectrum, tables):
-    _, twiddle, _, stage_b_inv, stage_a_inv = tables
-    spread = jnp.einsum("bceskq,sqrm->bcerkm", spectrum, stage_b_inv, precision=STAGE_B_PRECISION)
+    _, twiddle, stage_b, stage_a_inv = tables
+    spread = jnp.einsum("bceskq,rmsq->bcerkm", spectrum, stage_b, precision=STAGE_B_PRECISION)
     spread = complex_scale(spread, twiddle[0], -twiddle[1], 3)
     return jnp.einsum("erkp,bcerkm->bcpm", stage_a_inv, spread, precision=STAGE_A_PRECISION)
 

time: 102 us -> 101 us (level)
  other arithmetic: 13 us -> 11.6 us
    unnamed x27 -> x25, local copies, waits for them, and re-layouts: 4.24 us -> 4.12 us
  transfers between devices with their start and end apart: 16 -> 16, of which waited for: 5 -> 5; matrix products, arithmetic and copies ran while one was open for 25% -> 26% of each run, Pallas kernels for 0% -> 0%
where the time goes in v16:
time: 101 us; the launch traced here: 99 us
  starting transfers between devices  28.9 us (29%)
  matrix products  21 us (21%)
  waiting for transfers between devices  18.2 us (18%)
  other arithmetic  11.6 us (11%)
  blocking collectives  9.32 us (9%)
  local copies, waits for them, and re-layouts  8.8 us (9%)
  between operations  1.22 us (1%)
    ppermute x6, waiting for transfers between devices, panel_reduce_scatter(): lax.ppermute(sent, 'panel', [(i, (i + k) % count) for i in range(count)])  14.6 us
    ppermute x6, starting transfers between devices, panel_parts(): lax.ppermute(value, 'panel', [(i, (i + k) % count) for i in range(count)])  10.2 us
    all_to_all x1, blocking collectives, to_rows(): lax.all_to_all(columns.astype(wire), 'seq', split_axis=2, concat_axis=1,...  9.32 us
    all_to_all x2, starting transfers between devices, to_columns(): lax.all_to_all(jnp.swapaxes(rows, 1, 2).astype(wire), 'seq', split_axis=1...  8.29 us
    ppermute x6, starting transfers between devices, panel_reduce_scatter(): lax.ppermute(sent, 'panel', [(i, (i + k) % count) for i in range(count)])  7.15 us
    dot_general x4, matrix products, local(): jnp.einsum('td,jdc->jtc', part, lax.dynamic_slice_in_dim(in_weight, sourc...  4.74 us
    unnamed x25, local copies, waits for them, and re-layouts  4.12 us
    dot_general x2, matrix products, forward_spectrum(): jnp.einsum('bcerkm,rmsq->bceskq', spread, stage_b, precision=STAGE_B_PREC...  3.82 us
  transfers between devices with their start and end apart: 16, of which 5 were waited for; matrix products, arithmetic and copies ran while one was open for 26% of the time, Pallas kernels for 0%

profile of v16, /device:TPU:0, one launch (start us, length us, event | category | flops | bytes accessed | tf_op | source)
XLA Modules:
  0.0 99.0 jit_solution(11845898490907962866)
XLA Ops:
  0.7 3.1 %collective-permute-start = (bf16[256,256]{1,0:T(8,128)(2,1)}, bf16[256,256]{1,0:T(8,128)(2,1)}, u32[]{:S(2)}, u32[]{:S(2)}) collective-permute-start(bf16[256,256]{1,0:T(8,128)(2,1)} %param.7), channel_id=1, source_target_pairs={{0,1},{1,2},{2,3},{3,0},{4,5},{5,6},{6,7},{7,4},{8,9},{9,10},{10,1... | collective-permute-start | bytes 393224 | tf_op jit(solution)/shard_map/ppermute | solution.py:25
  3.8 2.1 %collective-permute-start.2 = (bf16[256,256]{1,0:T(8,128)(2,1)}, bf16[256,256]{1,0:T(8,128)(2,1)}, u32[]{:S(2)}, u32[]{:S(2)}) collective-permute-start(bf16[256,256]{1,0:T(8,128)(2,1)} %param.7), channel_id=1, source_target_pairs={{0,3},{1,0},{2,1},{3,2},{4,7},{5,4},{6,5},{7,6},{8,11},{9,8},{10,9... | collective-permute-start | bytes 393224 | tf_op jit(solution)/shard_map/ppermute | solution.py:25
  5.9 0.9 collective-permute-start.1
  6.8 1.6 %collective-permute-start.4 = (bf16[256,256]{1,0:T(8,128)(2,1)}, bf16[256,256]{1,0:T(8,128)(2,1)}, u32[]{:S(2)}, u32[]{:S(2)}) collective-permute-start(bf16[256,256]{1,0:T(8,128)(2,1)} %param.8), channel_id=1, source_target_pairs={{0,1},{1,2},{2,3},{3,0},{4,5},{5,6},{6,7},{7,4},{8,9},{9,10},{10,1... | collective-permute-start | bytes 393224 | tf_op jit(solution)/shard_map/ppermute | solution.py:25
  8.4 2.2 %collective-permute-start.6 = (bf16[256,256]{1,0:T(8,128)(2,1)}, bf16[256,256]{1,0:T(8,128)(2,1)}, u32[]{:S(2)}, u32[]{:S(2)}) collective-permute-start(bf16[256,256]{1,0:T(8,128)(2,1)} %param.8), channel_id=1, source_target_pairs={{0,3},{1,0},{2,1},{3,2},{4,7},{5,4},{6,5},{7,6},{8,11},{9,8},{10,9... | collective-permute-start | bytes 393224 | tf_op jit(solution)/shard_map/ppermute | solution.py:25
  10.6 1.8 %copy.63 = f32[1,256,256]{1,0,2:T(1,128)} copy(f32[1,256,256]{2,1,0:T(8,128)} %bitcast.217) | data formatting | bytes 524288 | tf_op jit(solution)/shard_map/broadcast_in_dim | solution.py:115
  12.4 4.1 %all-to-all-start.1 = ((f32[1,256,256]{2,0,1:T(1,128)}), f32[1,256,256]{2,0,1:T(1,128)}, u32[]{:S(2)}, u32[]{:S(2)}) async-start(f32[1,256,256]{2,0,1:T(1,128)} %bitcast.34), calls=%async_computation.1 | async-start | bytes 524288 | tf_op jit(solution)/shard_map/all_to_all | solution.py:82
  17.2 0.7 iota_multiply_fusion
  17.9 0.6 iota_multiply_fusion.2
  18.4 1.0 %fusion.86 = (f32[256,1,256]{2,0,1:T(8,128)S(1)}, f32[256,1,256]{2,0,1:T(8,128)S(1)}) fusion(), kind=kLoop, calls=%fused_computation.122 | loop fusion | flops 983040 | bytes 524288 | tf_op jit(solution)/shard_map/sin | solution.py:62
  19.5 1.7 %fusion.88 = f32[256,1,256]{2,0,1:T(8,128)} fusion(), kind=kLoop, calls=%fused_computation.124 | loop fusion | flops 1048576 | bytes 262144 | tf_op jit(solution)/shard_map/neg | solution.py:64
  21.2 0.7 slice_bitcast_fusion.5
  21.9 1.2 %fusion.51 = f32[3,256,256]{1,2,0:T(8,128)S(1)} fusion(bf16[3,1024,256]{2,1,0:T(8,128)(2,1)S(1)} %copy-done, s32[]{:T(128)S(6)} %select_n.140, bf16[256,256]{1,0:T(8,128)(2,1)} %param.7), kind=kOutput, calls=%fused_computation.82 | convolution fusion | flops 100663296 | bytes 1310724 | tf_op jit(solution)/shard_map/td,jdc->jtc/dot_general | solution.py:119
  23.1 0.9 fusion.98
  24.0 0.7 fusion.116
  24.7 0.8 fusion.133
  25.5 2.0 %maximum_bitcast_fusion.2 = (f32[1,256,2,256]{3,1,0,2:T(8,128)}, f32[1,256,2,256]{3,1,0,2:T(8,128)}) fusion(f32[256,1,256]{2,0,1:T(8,128)S(1)} %get-tuple-element.30, f32[256,1,256]{2,0,1:T(8,128)S(1)} %get-tuple-element.31, f32[256,1,256]{2,0,1:T(8,128)} %fusion.88), kind=kLoop, calls=%fused_computation.62 | loop fusion | flops 262144 | bytes 1835008 | tf_op jit(solution)/shard_map/stack | solution.py:63
  27.7 1.2 %convolution_add_fusion.1 = f32[3,256,256]{1,2,0:T(8,128)S(1)} fusion(f32[3,256,256]{1,2,0:T(8,128)S(1)} %fusion.51, bf16[3,1024,256]{2,1,0:T(8,128)(2,1)S(1)} %copy-done, s32[]{:T(128)S(6)} %select_n.142, bf16[256,256]{1,0:T(8,128)(2,1)} %collective-permute-done), kind=kOutput, calls=%fused_computation.19 | convolution fusion | flops 100859904 | bytes 2097156 | tf_op jit(solution)/shard_map/td,jdc->jtc/dot_general | solution.py:119
  28.9 1.2 %fusion.44 = f32[3,256,256]{1,2,0:T(8,128)S(1)} fusion(bf16[3,1024,256]{2,1,0:T(8,128)(2,1)S(1)} %copy-done, s32[]{:T(128)S(6)} %select_n.146, bf16[256,256]{1,0:T(8,128)(2,1)} %collective-permute-done.2), kind=kOutput, calls=%fused_computation.75 | convolution fusion | flops 100663296 | bytes 1310724 | tf_op jit(solution)/shard_map/td,jdc->jtc/dot_general | solution.py:119
  30.2 1.2 %fusion.21 = bf16[3,256,256]{2,1,0:T(8,128)(2,1)S(1)} fusion(f32[3,256,256]{1,2,0:T(8,128)S(1)} %fusion.44, f32[3,256,256]{1,2,0:T(8,128)S(1)} %convolution_add_fusion.1, bf16[3,1024,256]{2,1,0:T(8,128)(2,1)S(1)} %copy-done, s32[]{:T(128)S(6)} %select_n.144, bf16[256,256]{1,0:T(8,128)(2,1)} %collective-permute-done.1), kind=kOutput, calls=%fused_computation.22 | convolution fusion | flops 101253120 | bytes 2490372 | tf_op jit(solution)/shard_map/td,jdc->jtc/dot_general | solution.py:119
  31.4 2.0 %collective-permute-start.3 = (bf16[3,2,256]{2,1,0:T(2,128)(2,1)S(1)}, bf16[3,2,256]{2,1,0:T(2,128)(2,1)S(1)}, u32[]{:S(2)}, u32[]{:S(2)}) collective-permute-start(bf16[3,2,256]{2,1,0:T(2,128)(2,1)S(1)} %slice.111), channel_id=1, source_target_pairs={{0,4},{4,8},{8,12},{12,16},{16,20},{20,24},{24,28},{1,5},{5,9},{9,... | collective-permute-start | bytes 9224 | tf_op jit(solution)/shard_map/ppermute | solution.py:17
  33.5 1.1 %convolution_add_fusion.3 = f32[256,256]{0,1:T(8,128)S(1)} fusion(f32[256,256]{0,1:T(8,128)S(1)} %copy-done.9, bf16[256,256]{1,0:T(8,128)(2,1)} %collective-permute-done.4, bf16[256,1024]{1,0:T(8,128)(2,1)S(1)} %copy-done.7, s32[]{:T(128)S(6)} %select_n.142), kind=kOutput, calls=%fused_computation.31 | convolution fusion | flops 33619968 | bytes 786436 | tf_op jit(solution)/shard_map/dot_general | solution.py:127
  34.6 1.1 %fusion.90 = f32[256,256]{0,1:T(8,128)S(1)} fusion(bf16[256,256]{1,0:T(8,128)(2,1)} %collective-permute-done.6, bf16[256,1024]{1,0:T(8,128)(2,1)S(1)} %copy-done.7, s32[]{:T(128)S(6)} %select_n.146), kind=kOutput, calls=%fused_computation.126 | convolution fusion | flops 33554432 | bytes 524292 | tf_op jit(solution)/shard_map/dot_general | solution.py:127
  35.7 0.7 collective-permute-done.5
  37.5 0.9 copy.32
  38.3 4.2 %all-to-all-start = ((bf16[2,256,256]{2,0,1:T(2,128)(2,1)}), bf16[2,256,256]{2,0,1:T(2,128)(2,1)}, u32[]{:S(2)}, u32[]{:S(2)}) async-start(bf16[2,256,256]{2,0,1:T(2,128)(2,1)} %copy.32), calls=%async_computation | async-start | bytes 524288 | tf_op jit(solution)/shard_map/all_to_all | solution.py:82
  42.6 1.0 copy.68
  43.6 0.6 convolution_bitcast_fusion.2
  44.4 0.8 copy-done.1
  45.4 1.1 %convolution_bitcast_fusion.1 = f32[1,32,2,2,8,256]{5,1,4,2,0,3:T(8,128)S(1)} fusion(f32[32,2,2,8,256]{4,3,0,2,1:T(8,128)S(1)} %maximum_bitcast_fusion.1, f32[1,256,2,256]{3,1,0,2:T(8,128)S(1)} %copy-done.3, f32[1,256,2,256]{3,1,0,2:T(8,128)S(1)} %copy-done.1), kind=kOutput, calls=%fused_computation.15 | convolution fusion | flops 805568512 | bytes 3145728 | tf_op jit(solution)/shard_map/bcerkm,rmsq->bceskq/dot_general | solution.py:100
  46.5 2.8 %all-to-all-done = bf16[2,256,256]{2,0,1:T(2,128)(2,1)} async-done(((bf16[2,256,256]{2,0,1:T(2,128)(2,1)}), bf16[2,256,256]{2,0,1:T(2,128)(2,1)}, u32[]{:S(2)}, u32[]{:S(2)}) %all-to-all-start) | async-done | bytes 262176 | tf_op jit(solution)/shard_map/all_to_all | solution.py:82
  49.3 1.7 %convolution_bitcast_fusion = f32[2,32,2,2,8,256]{5,4,3,2,1,0:T(8,128)S(1)} fusion(bf16[2,8,32,256]{3,0,2,1:T(2,128)(2,1)} %bitcast.18, f32[2,1,8,8]{3,2,1,0:T(8,128)S(1)} %get-tuple-element.29, f32[2,1,8,8]{3,2,1,0:T(8,128)S(1)} %get-tuple-element.28), kind=kOutput, calls=%fused_computation.14 | convolution fusion | flops 25166080 | bytes 2360320 | tf_op jit(solution)/shard_map/erkp,bcpm->bcerkm/dot_general | solution.py:98
  51.5 0.8 copy-done.2
  52.5 2.7 %fusion.10 = f32[2,32,2,2,8,256]{5,1,4,2,0,3:T(8,128)S(1)} fusion(f32[2,32,2,2,8,256]{5,4,3,2,1,0:T(8,128)S(1)} %pad_maximum_fusion, f32[1,256,2,256]{3,1,0,2:T(8,128)S(1)} %copy-done.4, f32[1,256,2,256]{3,1,0,2:T(8,128)S(1)} %copy-done.2), kind=kOutput, calls=%fused_computation.12 | convolution fusion | flops 1610874880 | bytes 5242880 | tf_op jit(solution)/shard_map/bcerkm,rmsq->bceskq/dot_general | solution.py:100
  55.9 2.7 %fusion.13 = f32[2,32,2,2,8,256]{5,4,3,2,1,0:T(8,128)S(1)} fusion(f32[2,32,2,2,8,256,1]{5,1,4,2,0,3,6:T(8,128)S(1)} %maximum_bitcast_fusion, f32[1,256,2,256]{3,1,0,2:T(8,128)S(1)} %copy-done.4, f32[1,256,2,256]{3,1,0,2:T(8,128)S(1)} %copy-done.2), kind=kOutput, calls=%fused_computation.13 | convolution fusion | flops 1610874880 | bytes 5242880 | tf_op jit(solution)/shard_map/bceskq,rmsq->bcerkm/dot_general | solution.py:105
  58.9 0.7 fusion.27
  59.6 9.3 %all_to_all.39 = bf16[2,32,8,256]{3,1,0,2:T(8,128)(2,1)S(1)} all-to-all(bf16[2,32,8,256]{3,1,0,2:T(8,128)(2,1)S(1)} %copy.43), channel_id=1, replica_groups=mesh['seq'=8,'panel'=4] {'seq'}, dimensions={2} | all-to-all | bytes 524288 | tf_op jit(solution)/shard_map/all_to_all | solution.py:90
  69.0 0.8 bitcast_convert_fusion
  69.8 1.2 %copy.45 = f32[2,256,256]{1,2,0:T(8,128)S(1)} copy(f32[2,256,256]{2,1,0:T(8,128)} %bitcast.215) | data formatting | bytes 1048576 | tf_op jit(solution)/shard_map/transpose | solution.py:93
  71.3 0.8 copy-done.8
  72.6 1.3 %collective-permute-start.10 = (f32[3,2,256]{2,1,0:T(2,128)S(1)}, f32[3,2,256]{2,1,0:T(2,128)S(1)}, u32[]{:S(2)}, u32[]{:S(2)}) collective-permute-start(f32[3,2,256]{2,1,0:T(2,128)S(1)} %slice.132), channel_id=1, source_target_pairs={{4,0},{8,4},{12,8},{16,12},{20,16},{24,20},{28,24},{5,1},{9,5},{13... | collective-permute-start | bytes 18440 | tf_op jit(solution)/shard_map/ppermute | solution.py:17
  74.1 2.7 %collective-permute-start.8 = (bf16[256,256]{1,0:T(8,128)(2,1)S(1)}, bf16[256,256]{1,0:T(8,128)(2,1)S(1)}, u32[]{:S(2)}, u32[]{:S(2)}) collective-permute-start(bf16[256,256]{1,0:T(8,128)(2,1)S(1)} %convolution_convert_fusion.1), channel_id=1, source_target_pairs={{0,2},{1,3},{2,0},{3,1},{4,6},{5,7},{6,4},{7,5},{8,10},{9,11},{10,... | collective-permute-start | bytes 393224 | tf_op jit(solution)/shard_map/ppermute | solution.py:36
  76.8 3.8 %collective-permute-start.9 = (bf16[256,256]{1,0:T(8,128)(2,1)S(1)}, bf16[256,256]{1,0:T(8,128)(2,1)S(1)}, u32[]{:S(2)}, u32[]{:S(2)}) collective-permute-start(bf16[256,256]{1,0:T(8,128)(2,1)S(1)} %convolution_convert_fusion), channel_id=1, source_target_pairs={{0,3},{1,0},{2,1},{3,2},{4,7},{5,4},{6,5},{7,6},{8,11},{9,8},{10,9... | collective-permute-start | bytes 393224 | tf_op jit(solution)/shard_map/ppermute | solution.py:36
  82.5 4.3 %collective-permute-done.8 = bf16[256,256]{1,0:T(8,128)(2,1)S(1)} collective-permute-done((bf16[256,256]{1,0:T(8,128)(2,1)S(1)}, bf16[256,256]{1,0:T(8,128)(2,1)S(1)}, u32[]{:S(2)}, u32[]{:S(2)}) %collective-permute-start.8) | collective-permute-done | bytes 131104 | tf_op jit(solution)/shard_map/ppermute | solution.py:36
  86.9 1.7 %collective-permute-done.9 = bf16[256,256]{1,0:T(8,128)(2,1)S(1)} collective-permute-done((bf16[256,256]{1,0:T(8,128)(2,1)S(1)}, bf16[256,256]{1,0:T(8,128)(2,1)S(1)}, u32[]{:S(2)}, u32[]{:S(2)}) %collective-permute-start.9) | collective-permute-done | bytes 131104 | tf_op jit(solution)/shard_map/ppermute | solution.py:36
  88.6 0.9 add_convert_fusion
  89.4 8.6 %collective-permute-done.12 = bf16[256,256]{1,0:T(8,128)(2,1)S(1)} collective-permute-done((bf16[256,256]{1,0:T(8,128)(2,1)S(1)}, bf16[256,256]{1,0:T(8,128)(2,1)S(1)}, u32[]{:S(2)}, u32[]{:S(2)}) %collective-permute-start.12) | collective-permute-done | bytes 131104 | tf_op jit(solution)/shard_map/ppermute | solution.py:36
  98.0 1.0 %fusion.62 = bf16[256,256]{1,0:T(8,128)(2,1)} fusion(bf16[3,256,256]{2,1,0:T(8,128)(2,1)S(1)} %fusion.39, bf16[3,1024,256]{2,1,0:T(8,128)(2,1)S(1)} %copy-done, s32[]{:T(128)S(6)} %select_n.140, bf16[256,256]{1,0:T(8,128)(2,1)S(1)} %collective-permute-done.13, bf16[256,256]{1,0:T(8,128)(2,1)S(1)} %collective-permute-done.12, ...), kind=kOutput, calls=%fused_computation.87 | convolution fusion | flops 101122048 | bytes 1310724 | tf_op jit(solution)/shard_map/jtc,jdc->td/dot_general | solution.py:188
  (67 shorter events, 6.6 us)
Async XLA Ops:
  0.6 21.3 %copy-start = (bf16[3,1024,256]{2,1,0:T(8,128)(2,1)S(1)}, bf16[3,1024,256]{2,1,0:T(8,128)(2,1)}, u32[]{:S(2)}) copy-start(bf16[3,1024,256]{2,1,0:T(8,128)(2,1)} %param.9) | copy-start | bytes 4718596
  0.6 22.4 %copy-start.10 = (bf16[256,256]{1,0:T(8,128)(2,1)S(1)}, bf16[256,256]{1,0:T(8,128)(2,1)}, u32[]{:S(2)}) copy-start(bf16[256,256]{1,0:T(8,128)(2,1)} %param.8) | copy-start | bytes 393220
  0.7 22.4 %copy-start.7 = (bf16[256,1024]{1,0:T(8,128)(2,1)S(1)}, bf16[256,1024]{1,0:T(8,128)(2,1)}, u32[]{:S(2)}) copy-start(bf16[256,1024]{1,0:T(8,128)(2,1)} %param.13) | copy-start | bytes 1572868
  0.7 26.9 %collective-permute-start = (bf16[256,256]{1,0:T(8,128)(2,1)}, bf16[256,256]{1,0:T(8,128)(2,1)}, u32[]{:S(2)}, u32[]{:S(2)}) collective-permute-start(bf16[256,256]{1,0:T(8,128)(2,1)} %param.7), channel_id=1, source_target_pairs={{0,1},{1,2},{2,3},{3,0},{4,5},{5,6},{6,7},{7,4},{8,9},{9,10},{10,1... | collective-permute-start | bytes 393224 | tf_op jit(solution)/shard_map/ppermute | solution.py:25
  3.8 25.2 %collective-permute-start.2 = (bf16[256,256]{1,0:T(8,128)(2,1)}, bf16[256,256]{1,0:T(8,128)(2,1)}, u32[]{:S(2)}, u32[]{:S(2)}) collective-permute-start(bf16[256,256]{1,0:T(8,128)(2,1)} %param.7), channel_id=1, source_target_pairs={{0,3},{1,0},{2,1},{3,2},{4,7},{5,4},{6,5},{7,6},{8,11},{9,8},{10,9... | collective-permute-start | bytes 393224 | tf_op jit(solution)/shard_map/ppermute | solution.py:25
  5.9 24.3 %collective-permute-start.1 = (bf16[256,256]{1,0:T(8,128)(2,1)}, bf16[256,256]{1,0:T(8,128)(2,1)}, u32[]{:S(2)}, u32[]{:S(2)}) collective-permute-start(bf16[256,256]{1,0:T(8,128)(2,1)} %param.7), channel_id=1, source_target_pairs={{0,2},{1,3},{2,0},{3,1},{4,6},{5,7},{6,4},{7,5},{8,10},{9,11},{10,... | collective-permute-start | bytes 393224 | tf_op jit(solution)/shard_map/ppermute | solution.py:25
  6.8 26.6 %collective-permute-start.4 = (bf16[256,256]{1,0:T(8,128)(2,1)}, bf16[256,256]{1,0:T(8,128)(2,1)}, u32[]{:S(2)}, u32[]{:S(2)}) collective-permute-start(bf16[256,256]{1,0:T(8,128)(2,1)} %param.8), channel_id=1, source_target_pairs={{0,1},{1,2},{2,3},{3,0},{4,5},{5,6},{6,7},{7,4},{8,9},{9,10},{10,1... | collective-permute-start | bytes 393224 | tf_op jit(solution)/shard_map/ppermute | solution.py:25
  8.4 26.2 %collective-permute-start.6 = (bf16[256,256]{1,0:T(8,128)(2,1)}, bf16[256,256]{1,0:T(8,128)(2,1)}, u32[]{:S(2)}, u32[]{:S(2)}) collective-permute-start(bf16[256,256]{1,0:T(8,128)(2,1)} %param.8), channel_id=1, source_target_pairs={{0,3},{1,0},{2,1},{3,2},{4,7},{5,4},{6,5},{7,6},{8,11},{9,8},{10,9... | collective-permute-start | bytes 393224 | tf_op jit(solution)/shard_map/ppermute | solution.py:25
  12.4 25.9 %all-to-all-start.1 = ((f32[1,256,256]{2,0,1:T(1,128)}), f32[1,256,256]{2,0,1:T(1,128)}, u32[]{:S(2)}, u32[]{:S(2)}) async-start(f32[1,256,256]{2,0,1:T(1,128)} %bitcast.34), calls=%async_computation.1 | async-start | bytes 524288 | tf_op jit(solution)/shard_map/all_to_all | solution.py:82
  27.6 8.9 %collective-permute-start.5 = (bf16[256,256]{1,0:T(8,128)(2,1)}, bf16[256,256]{1,0:T(8,128)(2,1)S(1)}, u32[]{:S(2)}, u32[]{:S(2)}) collective-permute-start(bf16[256,256]{1,0:T(8,128)(2,1)} %param.8), channel_id=1, source_target_pairs={{0,2},{1,3},{2,0},{3,1},{4,6},{5,7},{6,4},{7,5},{8,10},{9,11},{10,... | collective-permute-start | bytes 393224 | tf_op jit(solution)/shard_map/ppermute | solution.py:25
  28.9 4.5 %copy-start.9 = (f32[256,256]{0,1:T(8,128)S(1)}, f32[256,256]{0,1:T(8,128)}, u32[]{:S(2)}) copy-start(f32[256,256]{0,1:T(8,128)} %fusion.98) | copy-start | bytes 786436
  31.4 5.3 %collective-permute-start.3 = (bf16[3,2,256]{2,1,0:T(2,128)(2,1)S(1)}, bf16[3,2,256]{2,1,0:T(2,128)(2,1)S(1)}, u32[]{:S(2)}, u32[]{:S(2)}) collective-permute-start(bf16[3,2,256]{2,1,0:T(2,128)(2,1)S(1)} %slice.111), channel_id=1, source_target_pairs={{0,4},{4,8},{8,12},{12,16},{16,20},{20,24},{24,28},{1,5},{5,9},{9,... | collective-permute-start | bytes 9224 | tf_op jit(solution)/shard_map/ppermute | solution.py:17
  36.7 0.7 copy-start.5
  38.3 11.0 %all-to-all-start = ((bf16[2,256,256]{2,0,1:T(2,128)(2,1)}), bf16[2,256,256]{2,0,1:T(2,128)(2,1)}, u32[]{:S(2)}, u32[]{:S(2)}) async-start(bf16[2,256,256]{2,0,1:T(2,128)(2,1)} %copy.32), calls=%async_computation | async-start | bytes 524288 | tf_op jit(solution)/shard_map/all_to_all | solution.py:82
  44.1 1.0 %copy-start.1 = (f32[1,256,2,256]{3,1,0,2:T(8,128)S(1)}, f32[1,256,2,256]{3,1,0,2:T(8,128)}, u32[]{:S(2)}) copy-start(f32[1,256,2,256]{3,1,0,2:T(8,128)} %get-tuple-element.20) | copy-start | bytes 1572868
  44.2 1.2 %copy-start.3 = (f32[1,256,2,256]{3,1,0,2:T(8,128)S(1)}, f32[1,256,2,256]{3,1,0,2:T(8,128)}, u32[]{:S(2)}) copy-start(f32[1,256,2,256]{3,1,0,2:T(8,128)} %get-tuple-element.21) | copy-start | bytes 1572868
  51.3 1.0 %copy-start.2 = (f32[1,256,2,256]{3,1,0,2:T(8,128)S(1)}, f32[1,256,2,256]{3,1,0,2:T(8,128)}, u32[]{:S(2)}) copy-start(f32[1,256,2,256]{3,1,0,2:T(8,128)} %get-tuple-element.20) | copy-start | bytes 1572868
  51.3 1.2 %copy-start.4 = (f32[1,256,2,256]{3,1,0,2:T(8,128)S(1)}, f32[1,256,2,256]{3,1,0,2:T(8,128)}, u32[]{:S(2)}) copy-start(f32[1,256,2,256]{3,1,0,2:T(8,128)} %get-tuple-element.21) | copy-start | bytes 1572868
  58.9 12.2 %copy-start.6 = (f32[256,256]{1,0:T(8,128)S(1)}, f32[256,256]{1,0:T(8,128)}, u32[]{:S(2)}) copy-start(f32[256,256]{1,0:T(8,128)} %copy-done.5) | copy-start | bytes 786436
  58.9 12.2 %copy-start.11 = (f32[256]{0:T(256)S(1)}, f32[256]{0:T(256)}, u32[]{:S(2)}) copy-start(f32[256]{0:T(256)} %param.11) | copy-start | bytes 3076
  71.1 1.0 %copy-start.8 = (bf16[256,1024]{1,0:T(8,128)(2,1)S(1)}, bf16[256,1024]{1,0:T(8,128)(2,1)}, u32[]{:S(2)}) copy-start(bf16[256,1024]{1,0:T(8,128)(2,1)} %param.13) | copy-start | bytes 1572868
  72.6 8.0 %collective-permute-start.10 = (f32[3,2,256]{2,1,0:T(2,128)S(1)}, f32[3,2,256]{2,1,0:T(2,128)S(1)}, u32[]{:S(2)}, u32[]{:S(2)}) collective-permute-start(f32[3,2,256]{2,1,0:T(2,128)S(1)} %slice.132), channel_id=1, source_target_pairs={{4,0},{8,4},{12,8},{16,12},{20,16},{24,20},{28,24},{5,1},{9,5},{13... | collective-permute-start | bytes 18440 | tf_op jit(solution)/shard_map/ppermute | solution.py:17
  74.1 12.8 %collective-permute-start.8 = (bf16[256,256]{1,0:T(8,128)(2,1)S(1)}, bf16[256,256]{1,0:T(8,128)(2,1)S(1)}, u32[]{:S(2)}, u32[]{:S(2)}) collective-permute-start(bf16[256,256]{1,0:T(8,128)(2,1)S(1)} %convolution_convert_fusion.1), channel_id=1, source_target_pairs={{0,2},{1,3},{2,0},{3,1},{4,6},{5,7},{6,4},{7,5},{8,10},{9,11},{10,... | collective-permute-start | bytes 393224 | tf_op jit(solution)/shard_map/ppermute | solution.py:36
  76.8 10.1 %collective-permute-start.7 = (bf16[256,256]{1,0:T(8,128)(2,1)S(1)}, bf16[256,256]{1,0:T(8,128)(2,1)S(1)}, u32[]{:S(2)}, u32[]{:S(2)}) collective-permute-start(bf16[256,256]{1,0:T(8,128)(2,1)S(1)} %convolution_convert_fusion.2), channel_id=1, source_target_pairs={{0,1},{1,2},{2,3},{3,0},{4,5},{5,6},{6,7},{7,4},{8,9},{9,10},{10,1... | collective-permute-start | bytes 393224 | tf_op jit(solution)/shard_map/ppermute | solution.py:36
  76.8 11.8 %collective-permute-start.9 = (bf16[256,256]{1,0:T(8,128)(2,1)S(1)}, bf16[256,256]{1,0:T(8,128)(2,1)S(1)}, u32[]{:S(2)}, u32[]{:S(2)}) collective-permute-start(bf16[256,256]{1,0:T(8,128)(2,1)S(1)} %convolution_convert_fusion), channel_id=1, source_target_pairs={{0,3},{1,0},{2,1},{3,2},{4,7},{5,4},{6,5},{7,6},{8,11},{9,8},{10,9... | collective-permute-start | bytes 393224 | tf_op jit(solution)/shard_map/ppermute | solution.py:36
  81.6 16.5 %collective-permute-start.12 = (bf16[256,256]{1,0:T(8,128)(2,1)S(1)}, bf16[256,256]{1,0:T(8,128)(2,1)S(1)}, u32[]{:S(2)}, u32[]{:S(2)}) collective-permute-start(bf16[256,256]{1,0:T(8,128)(2,1)S(1)} %fusion.31), channel_id=1, source_target_pairs={{0,2},{1,3},{2,0},{3,1},{4,6},{5,7},{6,4},{7,5},{8,10},{9,11},{10,... | collective-permute-start | bytes 393224 | tf_op jit(solution)/shard_map/ppermute | solution.py:36
  81.7 16.4 %collective-permute-start.11 = (bf16[256,256]{1,0:T(8,128)(2,1)S(1)}, bf16[256,256]{1,0:T(8,128)(2,1)S(1)}, u32[]{:S(2)}, u32[]{:S(2)}) collective-permute-start(bf16[256,256]{1,0:T(8,128)(2,1)S(1)} %fusion.30), channel_id=1, source_target_pairs={{0,1},{1,2},{2,3},{3,0},{4,5},{5,6},{6,7},{7,4},{8,9},{9,10},{10,1... | collective-permute-start | bytes 393224 | tf_op jit(solution)/shard_map/ppermute | solution.py:36
  86.9 11.2 %collective-permute-start.13 = (bf16[256,256]{1,0:T(8,128)(2,1)S(1)}, bf16[256,256]{1,0:T(8,128)(2,1)S(1)}, u32[]{:S(2)}, u32[]{:S(2)}) collective-permute-start(bf16[256,256]{1,0:T(8,128)(2,1)S(1)} %fusion.32), channel_id=1, source_target_pairs={{0,3},{1,0},{2,1},{3,2},{4,7},{5,4},{6,5},{7,6},{8,11},{9,8},{10,9... | collective-permute-start | bytes 393224 | tf_op jit(solution)/shard_map/ppermute | solution.py:36

commit v17 on v16

--- a/solution.py
+++ b/solution.py
@@ -2,6 +2,7 @@
 
 import jax
 import jax.numpy as jnp
+import numpy as np
 from jax import lax
 from jax.sharding import PartitionSpec as P
 
@@ -48,22 +49,31 @@
     branch = jnp.arange(2, dtype=jnp.int32)
     shard = jnp.arange(shard_count, dtype=jnp.int32)
     row = jnp.arange(row_count, dtype=jnp.int32)
-    theta = -phase(
-        (2 * shard[:, None] * shard[None, :])[None] + branch[:, None, None] * shard[None, None, :],
-        2 * shard_count,
-    )
-    stage_a = jnp.stack([jnp.cos(theta), jnp.sin(theta)], axis=1)
-    phi = -phase(
-        (2 * shard[:, None] * row[None, :])[None] + branch[:, None, None] * row[None, :][None],
-        2 * length,
-    )
-    twiddle = (jnp.cos(phi), jnp.sin(phi))
+    small_shard, small_row = np.arange(shard_count), np.arange(row_count)
+    small_branch = np.arange(2)
+    theta = (-2.0 * math.pi / (2 * shard_count)) * (
+        (
+            (2 * small_shard[:, None] * small_shard[None, :])[None]
+            + small_branch[:, None, None] * small_shard[None, None, :]
+        )
+        % (2 * shard_count)
+    )
+    stage_a_np = np.stack([np.cos(theta), np.sin(theta)], axis=1)
+    stage_a = jnp.asarray(stage_a_np, dtype=jnp.float32)
+    phi = (-2.0 * math.pi / (2 * length)) * (
+        (
+            (2 * small_shard[:, None] * small_row[None, :])[None]
+            + small_branch[:, None, None] * small_row[None, :][None]
+        )
+        % (2 * length)
+    )
+    twiddle = (jnp.asarray(np.cos(phi), jnp.float32), jnp.asarray(np.sin(phi), jnp.float32))
     psi = -phase(row[:, None] * row[None, :], row_count)
     cos_b, sin_b = jnp.cos(psi), jnp.sin(psi)
     stage_b = jnp.stack(
         [jnp.stack([cos_b, sin_b], axis=1), jnp.stack([-sin_b, cos_b], axis=1)]
     )
-    stage_a_inv = stage_a * (0.5 / length)
+    stage_a_inv = jnp.asarray(stage_a_np * (0.5 / length), dtype=jnp.float32)
     return stage_a, twiddle, stage_b, stage_a_inv
 
 

time: 101 us -> 96.3 us (0.953)
  other arithmetic: 11.6 us -> 6.54 us
  starting transfers between devices: 28.9 us -> 30.4 us
    mul x5 -> x0, other arithmetic: 1.89 us -> none  [the longest x1 0.67 us: transform_tables(): 2 * shard[:, None] * row[None, :]]
    ppermute x6, starting transfers between devices: 7.15 us -> 8.68 us  [panel_reduce_scatter(): lax.ppermute(sent, 'panel', [(i, (i + k) % count) for i in range(count)])]
    ppermute x6, waiting for transfers between devices: 14.6 us -> 13.6 us  [panel_reduce_scatter(): lax.ppermute(sent, 'panel', [(i, (i + k) % count) for i in range(count)])]
    unnamed x25 -> x37, local copies, waits for them, and re-layouts: 4.12 us -> 3.63 us
  transfers between devices with their start and end apart: 16 -> 16, of which waited for: 5 -> 6; matrix products, arithmetic and copies ran while one was open for 26% -> 20% of each run, Pallas kernels for 0% -> 0%
where the time goes in v17:
time: 96.3 us; the launch traced here: 94.9 us
  starting transfers between devices  30.4 us (32%)
  matrix products  21.1 us (22%)
  waiting for transfers between devices  17.9 us (19%)
  blocking collectives  9.39 us (10%)
  local copies, waits for them, and re-layouts  8.3 us (9%)
  other arithmetic  6.54 us (7%)
  between operations  1.23 us (1%)
    ppermute x6, waiting for transfers between devices, panel_reduce_scatter(): lax.ppermute(sent, 'panel', [(i, (i + k) % count) for i in range(count)])  13.6 us
    ppermute x6, starting transfers between devices, panel_parts(): lax.ppermute(value, 'panel', [(i, (i + k) % count) for i in range(count)])  10.3 us
    all_to_all x1, blocking collectives, to_rows(): lax.all_to_all(columns.astype(wire), 'seq', split_axis=2, concat_axis=1,...  9.39 us
    ppermute x6, starting transfers between devices, panel_reduce_scatter(): lax.ppermute(sent, 'panel', [(i, (i + k) % count) for i in range(count)])  8.68 us
    all_to_all x2, starting transfers between devices, to_columns(): lax.all_to_all(jnp.swapaxes(rows, 1, 2).astype(wire), 'seq', split_axis=1...  7.96 us
    dot_general x4, matrix products, local(): lax.dot_general(part, lax.dynamic_slice_in_dim(out_weight, source * width...  4.42 us
    dot_general x4, matrix products, local(): jnp.einsum('td,jdc->jtc', part, lax.dynamic_slice_in_dim(in_weight, sourc...  3.86 us
    dot_general x2, matrix products, forward_spectrum(): jnp.einsum('bcerkm,rmsq->bceskq', spread, stage_b, precision=STAGE_B_PREC...  3.82 us
  transfers between devices with their start and end apart: 16, of which 6 were waited for; matrix products, arithmetic and copies ran while one was open for 20% of the time, Pallas kernels for 0%

profile of v17, /device:TPU:0, one launch (start us, length us, event | category | flops | bytes accessed | tf_op | source)
XLA Modules:
  0.0 94.9 jit_solution(1160381794692749451)
XLA Ops:
  0.7 3.1 %collective-permute-start = (bf16[256,256]{1,0:T(8,128)(2,1)}, bf16[256,256]{1,0:T(8,128)(2,1)}, u32[]{:S(2)}, u32[]{:S(2)}) collective-permute-start(bf16[256,256]{1,0:T(8,128)(2,1)} %param.11), channel_id=1, source_target_pairs={{0,1},{1,2},{2,3},{3,0},{4,5},{5,6},{6,7},{7,4},{8,9},{9,10},{10,1... | collective-permute-start | bytes 393224 | tf_op jit(solution)/shard_map/ppermute | solution.py:26
  3.8 2.1 %collective-permute-start.2 = (bf16[256,256]{1,0:T(8,128)(2,1)}, bf16[256,256]{1,0:T(8,128)(2,1)}, u32[]{:S(2)}, u32[]{:S(2)}) collective-permute-start(bf16[256,256]{1,0:T(8,128)(2,1)} %param.11), channel_id=1, source_target_pairs={{0,3},{1,0},{2,1},{3,2},{4,7},{5,4},{6,5},{7,6},{8,11},{9,8},{10,9... | collective-permute-start | bytes 393224 | tf_op jit(solution)/shard_map/ppermute | solution.py:26
  5.9 0.9 collective-permute-start.1
  6.8 1.6 %collective-permute-start.4 = (bf16[256,256]{1,0:T(8,128)(2,1)}, bf16[256,256]{1,0:T(8,128)(2,1)}, u32[]{:S(2)}, u32[]{:S(2)}) collective-permute-start(bf16[256,256]{1,0:T(8,128)(2,1)} %param.12), channel_id=1, source_target_pairs={{0,1},{1,2},{2,3},{3,0},{4,5},{5,6},{6,7},{7,4},{8,9},{9,10},{10,1... | collective-permute-start | bytes 393224 | tf_op jit(solution)/shard_map/ppermute | solution.py:26
  8.4 2.2 %collective-permute-start.6 = (bf16[256,256]{1,0:T(8,128)(2,1)}, bf16[256,256]{1,0:T(8,128)(2,1)}, u32[]{:S(2)}, u32[]{:S(2)}) collective-permute-start(bf16[256,256]{1,0:T(8,128)(2,1)} %param.12), channel_id=1, source_target_pairs={{0,3},{1,0},{2,1},{3,2},{4,7},{5,4},{6,5},{7,6},{8,11},{9,8},{10,9... | collective-permute-start | bytes 393224 | tf_op jit(solution)/shard_map/ppermute | solution.py:26
  10.6 1.8 %copy.64 = f32[1,256,256]{1,0,2:T(1,128)} copy(f32[1,256,256]{2,1,0:T(8,128)} %bitcast.216) | data formatting | bytes 524288 | tf_op jit(solution)/shard_map/broadcast_in_dim | solution.py:125
  12.4 3.7 %all-to-all-start.1 = ((f32[1,256,256]{2,0,1:T(1,128)}), f32[1,256,256]{2,0,1:T(1,128)S(1)}, u32[]{:S(2)}, u32[]{:S(2)}) async-start(f32[1,256,256]{2,0,1:T(1,128)} %bitcast.34), calls=%async_computation.1 | async-start | bytes 524288 | tf_op jit(solution)/shard_map/all_to_all | solution.py:92
  16.1 1.0 %fusion.88 = f32[256,1,256]{2,0,1:T(8,128)S(1)} fusion(), kind=kLoop, calls=%fused_computation.124 | loop fusion | flops 1048576 | bytes 262144 | tf_op jit(solution)/shard_map/neg | solution.py:74
  17.1 1.0 %fusion.86 = (f32[256,1,256]{2,0,1:T(8,128)S(1)}, f32[256,1,256]{2,0,1:T(8,128)S(1)}) fusion(), kind=kLoop, calls=%fused_computation.122 | loop fusion | flops 983040 | bytes 524288 | tf_op jit(solution)/shard_map/sin | solution.py:72
  18.2 0.7 slice_bitcast_fusion.5
  18.9 1.9 %fusion.98 = f32[256,256]{0,1:T(8,128)} fusion(bf16[256,256]{1,0:T(8,128)(2,1)} %param.12, bf16[256,1024]{1,0:T(8,128)(2,1)} %param.17, s32[]{:T(128)S(6)} %select_n.85), kind=kOutput, calls=%fused_computation.134 | convolution fusion | flops 33554432 | bytes 524292 | tf_op jit(solution)/shard_map/dot_general | solution.py:137
  21.1 1.1 %maximum_bitcast_fusion.2 = (f32[1,256,2,256]{3,1,0,2:T(8,128)}, f32[1,256,2,256]{3,1,0,2:T(8,128)}) fusion(f32[256,1,256]{2,0,1:T(8,128)S(1)} %get-tuple-element.25, f32[256,1,256]{2,0,1:T(8,128)S(1)} %get-tuple-element.26, f32[256,1,256]{2,0,1:T(8,128)S(1)} %fusion.88), kind=kLoop, calls=%fused_computation.62 | loop fusion | flops 262144 | bytes 1835008 | tf_op jit(solution)/shard_map/stack | solution.py:73
  22.5 1.2 %convolution_add_fusion.1 = f32[3,256,256]{1,2,0:T(8,128)S(1)} fusion(f32[3,256,256]{1,2,0:T(8,128)S(1)} %fusion.51, bf16[3,1024,256]{2,1,0:T(8,128)(2,1)S(1)} %copy-done, s32[]{:T(128)S(6)} %select_n.87, bf16[256,256]{1,0:T(8,128)(2,1)} %collective-permute-done), kind=kOutput, calls=%fused_computation.19 | convolution fusion | flops 100859904 | bytes 2097156 | tf_op jit(solution)/shard_map/td,jdc->jtc/dot_general | solution.py:129
  23.7 1.2 %fusion.44 = f32[3,256,256]{1,2,0:T(8,128)S(1)} fusion(bf16[3,1024,256]{2,1,0:T(8,128)(2,1)S(1)} %copy-done, s32[]{:T(128)S(6)} %select_n.91, bf16[256,256]{1,0:T(8,128)(2,1)} %collective-permute-done.2), kind=kOutput, calls=%fused_computation.75 | convolution fusion | flops 100663296 | bytes 1310724 | tf_op jit(solution)/shard_map/td,jdc->jtc/dot_general | solution.py:129
  25.0 1.2 %fusion.21 = bf16[3,256,256]{2,1,0:T(8,128)(2,1)S(1)} fusion(f32[3,256,256]{1,2,0:T(8,128)S(1)} %fusion.44, f32[3,256,256]{1,2,0:T(8,128)S(1)} %convolution_add_fusion.1, bf16[3,1024,256]{2,1,0:T(8,128)(2,1)S(1)} %copy-done, s32[]{:T(128)S(6)} %select_n.89, bf16[256,256]{1,0:T(8,128)(2,1)} %collective-permute-done.1), kind=kOutput, calls=%fused_computation.22 | convolution fusion | flops 101253120 | bytes 2490372 | tf_op jit(solution)/shard_map/td,jdc->jtc/dot_general | solution.py:129
  26.2 2.1 %collective-permute-start.3 = (bf16[3,2,256]{2,1,0:T(2,128)(2,1)S(1)}, bf16[3,2,256]{2,1,0:T(2,128)(2,1)S(1)}, u32[]{:S(2)}, u32[]{:S(2)}) collective-permute-start(bf16[3,2,256]{2,1,0:T(2,128)(2,1)S(1)} %slice.111), channel_id=1, source_target_pairs={{0,4},{4,8},{8,12},{12,16},{16,20},{20,24},{24,28},{1,5},{5,9},{9,... | collective-permute-start | bytes 9224 | tf_op jit(solution)/shard_map/ppermute | solution.py:18
  28.4 1.1 %convolution_add_fusion.3 = f32[256,256]{0,1:T(8,128)S(1)} fusion(f32[256,256]{0,1:T(8,128)S(1)} %copy-done.9, bf16[256,256]{1,0:T(8,128)(2,1)} %collective-permute-done.4, bf16[256,1024]{1,0:T(8,128)(2,1)S(1)} %copy-done.7, s32[]{:T(128)S(6)} %select_n.87), kind=kOutput, calls=%fused_computation.31 | convolution fusion | flops 33619968 | bytes 786436 | tf_op jit(solution)/shard_map/dot_general | solution.py:137
  29.5 1.1 %fusion.90 = f32[256,256]{0,1:T(8,128)S(1)} fusion(bf16[256,256]{1,0:T(8,128)(2,1)} %collective-permute-done.6, bf16[256,1024]{1,0:T(8,128)(2,1)S(1)} %copy-done.7, s32[]{:T(128)S(6)} %select_n.91), kind=kOutput, calls=%fused_computation.126 | convolution fusion | flops 33554432 | bytes 524292 | tf_op jit(solution)/shard_map/dot_general | solution.py:137
  30.7 0.6 collective-permute-done.5
  31.8 0.4 copy-done.5
  32.3 0.9 copy.34
  33.2 4.2 %all-to-all-start = ((bf16[2,256,256]{2,0,1:T(2,128)(2,1)}), bf16[2,256,256]{2,0,1:T(2,128)(2,1)}, u32[]{:S(2)}, u32[]{:S(2)}) async-start(bf16[2,256,256]{2,0,1:T(2,128)(2,1)} %copy.34), calls=%async_computation | async-start | bytes 524288 | tf_op jit(solution)/shard_map/all_to_all | solution.py:92
  37.5 0.6 convolution_bitcast_fusion.2
  38.3 0.8 copy-done.1
  39.3 1.1 %convolution_bitcast_fusion.1 = f32[1,32,2,2,8,256]{5,1,4,2,0,3:T(8,128)S(1)} fusion(f32[32,2,2,8,256]{4,3,0,2,1:T(8,128)S(1)} %maximum_bitcast_fusion.1, f32[1,256,2,256]{3,1,0,2:T(8,128)S(1)} %copy-done.3, f32[1,256,2,256]{3,1,0,2:T(8,128)S(1)} %copy-done.1), kind=kOutput, calls=%fused_computation.15 | convolution fusion | flops 805568512 | bytes 3145728 | tf_op jit(solution)/shard_map/bcerkm,rmsq->bceskq/dot_general | solution.py:110
  40.4 3.7 %all-to-all-done = bf16[2,256,256]{2,0,1:T(2,128)(2,1)} async-done(((bf16[2,256,256]{2,0,1:T(2,128)(2,1)}), bf16[2,256,256]{2,0,1:T(2,128)(2,1)}, u32[]{:S(2)}, u32[]{:S(2)}) %all-to-all-start) | async-done | bytes 262176 | tf_op jit(solution)/shard_map/all_to_all | solution.py:92
  44.2 1.7 %convolution_bitcast_fusion = f32[2,32,2,2,8,256]{5,4,3,2,1,0:T(8,128)S(1)} fusion(f32[2,2,8,8,1,1]{3,2,1,0,5,4:T(8,128)S(1)} %copy-done.15, bf16[2,8,32,256]{3,0,2,1:T(2,128)(2,1)} %bitcast.18), kind=kOutput, calls=%fused_computation.14 | convolution fusion | flops 25165824 | bytes 2360320 | tf_op jit(solution)/shard_map/erkp,bcpm->bcerkm/dot_general | solution.py:108
  46.4 0.8 copy-done.2
  47.3 2.7 %fusion.10 = f32[2,32,2,2,8,256]{5,1,4,2,0,3:T(8,128)S(1)} fusion(f32[2,32,2,2,8,256]{5,4,3,2,1,0:T(8,128)S(1)} %pad_maximum_fusion, f32[1,256,2,256]{3,1,0,2:T(8,128)S(1)} %copy-done.4, f32[1,256,2,256]{3,1,0,2:T(8,128)S(1)} %copy-done.2), kind=kOutput, calls=%fused_computation.12 | convolution fusion | flops 1610874880 | bytes 5242880 | tf_op jit(solution)/shard_map/bcerkm,rmsq->bceskq/dot_general | solution.py:110
  50.0 0.5 multiply_subtract_fusion.3
  50.7 2.7 %fusion.13 = f32[2,32,2,2,8,256]{5,4,3,2,1,0:T(8,128)S(1)} fusion(f32[2,32,2,2,8,256,1]{5,1,4,2,0,3,6:T(8,128)S(1)} %maximum_bitcast_fusion, f32[1,256,2,256]{3,1,0,2:T(8,128)S(1)} %copy-done.4, f32[1,256,2,256]{3,1,0,2:T(8,128)S(1)} %copy-done.2), kind=kOutput, calls=%fused_computation.13 | convolution fusion | flops 1610874880 | bytes 5242880 | tf_op jit(solution)/shard_map/bceskq,rmsq->bcerkm/dot_general | solution.py:115
  53.8 0.4 copy-done.13
  54.2 0.7 fusion.27
  54.9 9.4 %all_to_all.39 = bf16[2,32,8,256]{3,1,0,2:T(8,128)(2,1)S(1)} all-to-all(bf16[2,32,8,256]{3,1,0,2:T(8,128)(2,1)S(1)} %copy.44), channel_id=1, replica_groups=mesh['seq'=8,'panel'=4] {'seq'}, dimensions={2} | all-to-all | bytes 524288 | tf_op jit(solution)/shard_map/all_to_all | solution.py:100
  64.3 0.8 bitcast_convert_fusion
  65.1 1.2 %copy.46 = f32[2,256,256]{1,2,0:T(8,128)S(1)} copy(f32[2,256,256]{2,1,0:T(8,128)} %bitcast.214) | data formatting | bytes 1048576 | tf_op jit(solution)/shard_map/transpose | solution.py:103
  66.6 0.8 copy-done.8
  67.9 1.3 %collective-permute-start.10 = (f32[3,2,256]{2,1,0:T(2,128)S(1)}, f32[3,2,256]{2,1,0:T(2,128)S(1)}, u32[]{:S(2)}, u32[]{:S(2)}) collective-permute-start(f32[3,2,256]{2,1,0:T(2,128)S(1)} %slice.132), channel_id=1, source_target_pairs={{4,0},{8,4},{12,8},{16,12},{20,16},{24,20},{28,24},{5,1},{9,5},{13... | collective-permute-start | bytes 18440 | tf_op jit(solution)/shard_map/ppermute | solution.py:18
  69.7 2.4 %collective-permute-start.8 = (bf16[256,256]{1,0:T(8,128)(2,1)S(1)}, bf16[256,256]{1,0:T(8,128)(2,1)S(1)}, u32[]{:S(2)}, u32[]{:S(2)}) collective-permute-start(bf16[256,256]{1,0:T(8,128)(2,1)S(1)} %convolution_convert_fusion.1), channel_id=1, source_target_pairs={{0,2},{1,3},{2,0},{3,1},{4,6},{5,7},{6,4},{7,5},{8,10},{9,11},{10,... | collective-permute-start | bytes 393224 | tf_op jit(solution)/shard_map/ppermute | solution.py:37
  72.1 2.8 %collective-permute-start.9 = (bf16[256,256]{1,0:T(8,128)(2,1)S(1)}, bf16[256,256]{1,0:T(8,128)(2,1)S(1)}, u32[]{:S(2)}, u32[]{:S(2)}) collective-permute-start(bf16[256,256]{1,0:T(8,128)(2,1)S(1)} %convolution_convert_fusion), channel_id=1, source_target_pairs={{0,3},{1,0},{2,1},{3,2},{4,7},{5,4},{6,5},{7,6},{8,11},{9,8},{10,9... | collective-permute-start | bytes 393224 | tf_op jit(solution)/shard_map/ppermute | solution.py:37
  76.0 0.6 collective-permute-start.12
  76.9 0.8 collective-permute-done.7
  77.7 2.5 %collective-permute-start.13 = (bf16[256,256]{1,0:T(8,128)(2,1)S(1)}, bf16[256,256]{1,0:T(8,128)(2,1)S(1)}, u32[]{:S(2)}, u32[]{:S(2)}) collective-permute-start(bf16[256,256]{1,0:T(8,128)(2,1)S(1)} %fusion.32), channel_id=1, source_target_pairs={{0,3},{1,0},{2,1},{3,2},{4,7},{5,4},{6,5},{7,6},{8,11},{9,8},{10,9... | collective-permute-start | bytes 393224 | tf_op jit(solution)/shard_map/ppermute | solution.py:37
  80.2 2.4 %collective-permute-done.8 = bf16[256,256]{1,0:T(8,128)(2,1)S(1)} collective-permute-done((bf16[256,256]{1,0:T(8,128)(2,1)S(1)}, bf16[256,256]{1,0:T(8,128)(2,1)S(1)}, u32[]{:S(2)}, u32[]{:S(2)}) %collective-permute-start.8) | collective-permute-done | bytes 131104 | tf_op jit(solution)/shard_map/ppermute | solution.py:37
  82.6 0.9 add_convert_fusion
  83.5 2.6 %collective-permute-done.11 = bf16[256,256]{1,0:T(8,128)(2,1)S(1)} collective-permute-done((bf16[256,256]{1,0:T(8,128)(2,1)S(1)}, bf16[256,256]{1,0:T(8,128)(2,1)S(1)}, u32[]{:S(2)}, u32[]{:S(2)}) %collective-permute-start.11) | collective-permute-done | bytes 131104 | tf_op jit(solution)/shard_map/ppermute | solution.py:37
  86.1 7.8 %collective-permute-done.12 = bf16[256,256]{1,0:T(8,128)(2,1)S(1)} collective-permute-done((bf16[256,256]{1,0:T(8,128)(2,1)S(1)}, bf16[256,256]{1,0:T(8,128)(2,1)S(1)}, u32[]{:S(2)}, u32[]{:S(2)}) %collective-permute-start.12) | collective-permute-done | bytes 131104 | tf_op jit(solution)/shard_map/ppermute | solution.py:37
  93.9 1.0 %fusion.62 = bf16[256,256]{1,0:T(8,128)(2,1)} fusion(bf16[3,256,256]{2,1,0:T(8,128)(2,1)S(1)} %fusion.39, bf16[3,1024,256]{2,1,0:T(8,128)(2,1)S(1)} %copy-done, s32[]{:T(128)S(6)} %select_n.85, bf16[256,256]{1,0:T(8,128)(2,1)S(1)} %collective-permute-done.13, bf16[256,256]{1,0:T(8,128)(2,1)S(1)} %collective-permute-done.12, ...), kind=kOutput, calls=%fused_computation.87 | convolution fusion | flops 101122048 | bytes 1310724 | tf_op jit(solution)/shard_map/jtc,jdc->td/dot_general | solution.py:198
  (72 shorter events, 5.3 us)
Async XLA Ops:
  0.6 20.2 %copy-start = (bf16[3,1024,256]{2,1,0:T(8,128)(2,1)S(1)}, bf16[3,1024,256]{2,1,0:T(8,128)(2,1)}, u32[]{:S(2)}) copy-start(bf16[3,1024,256]{2,1,0:T(8,128)(2,1)} %param.13) | copy-start | bytes 4718596
  0.6 20.2 %copy-start.11 = (bf16[256,256]{1,0:T(8,128)(2,1)S(1)}, bf16[256,256]{1,0:T(8,128)(2,1)}, u32[]{:S(2)}) copy-start(bf16[256,256]{1,0:T(8,128)(2,1)} %param.11) | copy-start | bytes 393220
  0.7 21.5 %collective-permute-start = (bf16[256,256]{1,0:T(8,128)(2,1)}, bf16[256,256]{1,0:T(8,128)(2,1)}, u32[]{:S(2)}, u32[]{:S(2)}) collective-permute-start(bf16[256,256]{1,0:T(8,128)(2,1)} %param.11), channel_id=1, source_target_pairs={{0,1},{1,2},{2,3},{3,0},{4,5},{5,6},{6,7},{7,4},{8,9},{9,10},{10,1... | collective-permute-start | bytes 393224 | tf_op jit(solution)/shard_map/ppermute | solution.py:26
  3.8 20.0 %collective-permute-start.2 = (bf16[256,256]{1,0:T(8,128)(2,1)}, bf16[256,256]{1,0:T(8,128)(2,1)}, u32[]{:S(2)}, u32[]{:S(2)}) collective-permute-start(bf16[256,256]{1,0:T(8,128)(2,1)} %param.11), channel_id=1, source_target_pairs={{0,3},{1,0},{2,1},{3,2},{4,7},{5,4},{6,5},{7,6},{8,11},{9,8},{10,9... | collective-permute-start | bytes 393224 | tf_op jit(solution)/shard_map/ppermute | solution.py:26
  5.9 19.1 %collective-permute-start.1 = (bf16[256,256]{1,0:T(8,128)(2,1)}, bf16[256,256]{1,0:T(8,128)(2,1)}, u32[]{:S(2)}, u32[]{:S(2)}) collective-permute-start(bf16[256,256]{1,0:T(8,128)(2,1)} %param.11), channel_id=1, source_target_pairs={{0,2},{1,3},{2,0},{3,1},{4,6},{5,7},{6,4},{7,5},{8,10},{9,11},{10,... | collective-permute-start | bytes 393224 | tf_op jit(solution)/shard_map/ppermute | solution.py:26
  6.8 21.5 %collective-permute-start.4 = (bf16[256,256]{1,0:T(8,128)(2,1)}, bf16[256,256]{1,0:T(8,128)(2,1)}, u32[]{:S(2)}, u32[]{:S(2)}) collective-permute-start(bf16[256,256]{1,0:T(8,128)(2,1)} %param.12), channel_id=1, source_target_pairs={{0,1},{1,2},{2,3},{3,0},{4,5},{5,6},{6,7},{7,4},{8,9},{9,10},{10,1... | collective-permute-start | bytes 393224 | tf_op jit(solution)/shard_map/ppermute | solution.py:26
  8.4 21.1 %collective-permute-start.6 = (bf16[256,256]{1,0:T(8,128)(2,1)}, bf16[256,256]{1,0:T(8,128)(2,1)}, u32[]{:S(2)}, u32[]{:S(2)}) collective-permute-start(bf16[256,256]{1,0:T(8,128)(2,1)} %param.12), channel_id=1, source_target_pairs={{0,3},{1,0},{2,1},{3,2},{4,7},{5,4},{6,5},{7,6},{8,11},{9,8},{10,9... | collective-permute-start | bytes 393224 | tf_op jit(solution)/shard_map/ppermute | solution.py:26
  12.4 20.8 %all-to-all-start.1 = ((f32[1,256,256]{2,0,1:T(1,128)}), f32[1,256,256]{2,0,1:T(1,128)S(1)}, u32[]{:S(2)}, u32[]{:S(2)}) async-start(f32[1,256,256]{2,0,1:T(1,128)} %bitcast.34), calls=%async_computation.1 | async-start | bytes 524288 | tf_op jit(solution)/shard_map/all_to_all | solution.py:92
  22.2 9.0 %collective-permute-start.5 = (bf16[256,256]{1,0:T(8,128)(2,1)}, bf16[256,256]{1,0:T(8,128)(2,1)S(1)}, u32[]{:S(2)}, u32[]{:S(2)}) collective-permute-start(bf16[256,256]{1,0:T(8,128)(2,1)} %param.12), channel_id=1, source_target_pairs={{0,2},{1,3},{2,0},{3,1},{4,6},{5,7},{6,4},{7,5},{8,10},{9,11},{10,... | collective-permute-start | bytes 393224 | tf_op jit(solution)/shard_map/ppermute | solution.py:26
  23.7 4.6 %copy-start.7 = (bf16[256,1024]{1,0:T(8,128)(2,1)S(1)}, bf16[256,1024]{1,0:T(8,128)(2,1)}, u32[]{:S(2)}) copy-start(bf16[256,1024]{1,0:T(8,128)(2,1)} %param.17) | copy-start | bytes 1572868
  23.7 4.6 %copy-start.9 = (f32[256,256]{0,1:T(8,128)S(1)}, f32[256,256]{0,1:T(8,128)}, u32[]{:S(2)}) copy-start(f32[256,256]{0,1:T(8,128)} %fusion.98) | copy-start | bytes 786436
  26.2 5.3 %collective-permute-start.3 = (bf16[3,2,256]{2,1,0:T(2,128)(2,1)S(1)}, bf16[3,2,256]{2,1,0:T(2,128)(2,1)S(1)}, u32[]{:S(2)}, u32[]{:S(2)}) collective-permute-start(bf16[3,2,256]{2,1,0:T(2,128)(2,1)S(1)} %slice.111), channel_id=1, source_target_pairs={{0,4},{4,8},{8,12},{12,16},{16,20},{20,24},{24,28},{1,5},{5,9},{9,... | collective-permute-start | bytes 9224 | tf_op jit(solution)/shard_map/ppermute | solution.py:18
  31.5 0.7 copy-start.5
  32.2 5.3 %copy-start.16 = (f32[2,2,8,8,1]{3,2,4,1,0:T(8,128)S(1)}, f32[2,2,8,8,1]{3,2,4,1,0:T(8,128)}, u32[]{:S(2)}) copy-start(f32[2,2,8,8,1]{3,2,4,1,0:T(8,128)} %constant.93) | copy-start | bytes 3076
  32.2 5.8 %copy-start.10 = (f32[2,8,256]{2,1,0:T(8,128)S(1)}, f32[2,8,256]{2,1,0:T(8,128)}, u32[]{:S(2)}) copy-start(f32[2,8,256]{2,1,0:T(8,128)} %constant.88.clone) | copy-start | bytes 49156
  32.3 5.8 %copy-start.12 = (f32[2,8,256]{2,1,0:T(8,128)S(1)}, f32[2,8,256]{2,1,0:T(8,128)}, u32[]{:S(2)}) copy-start(f32[2,8,256]{2,1,0:T(8,128)} %constant.89.clone) | copy-start | bytes 49156
  33.2 11.0 %all-to-all-start = ((bf16[2,256,256]{2,0,1:T(2,128)(2,1)}), bf16[2,256,256]{2,0,1:T(2,128)(2,1)}, u32[]{:S(2)}, u32[]{:S(2)}) async-start(bf16[2,256,256]{2,0,1:T(2,128)(2,1)} %copy.34), calls=%async_computation | async-start | bytes 524288 | tf_op jit(solution)/shard_map/all_to_all | solution.py:92
  38.1 1.0 %copy-start.1 = (f32[1,256,2,256]{3,1,0,2:T(8,128)S(1)}, f32[1,256,2,256]{3,1,0,2:T(8,128)}, u32[]{:S(2)}) copy-start(f32[1,256,2,256]{3,1,0,2:T(8,128)} %get-tuple-element.20) | copy-start | bytes 1572868
  38.1 1.2 %copy-start.3 = (f32[1,256,2,256]{3,1,0,2:T(8,128)S(1)}, f32[1,256,2,256]{3,1,0,2:T(8,128)}, u32[]{:S(2)}) copy-start(f32[1,256,2,256]{3,1,0,2:T(8,128)} %get-tuple-element.21) | copy-start | bytes 1572868
  39.3 4.9 %copy-start.15 = (f32[2,2,8,8,1,1]{3,2,1,0,5,4:T(8,128)S(1)}, f32[2,2,8,8,1,1]{3,2,1,0,5,4:T(8,128)}, u32[]{:S(2)}) copy-start(f32[2,2,8,8,1,1]{3,2,1,0,5,4:T(8,128)} %constant.92) | copy-start | bytes 3076
  46.1 1.0 %copy-start.2 = (f32[1,256,2,256]{3,1,0,2:T(8,128)S(1)}, f32[1,256,2,256]{3,1,0,2:T(8,128)}, u32[]{:S(2)}) copy-start(f32[1,256,2,256]{3,1,0,2:T(8,128)} %get-tuple-element.20) | copy-start | bytes 1572868
  46.1 1.2 %copy-start.4 = (f32[1,256,2,256]{3,1,0,2:T(8,128)S(1)}, f32[1,256,2,256]{3,1,0,2:T(8,128)}, u32[]{:S(2)}) copy-start(f32[1,256,2,256]{3,1,0,2:T(8,128)} %get-tuple-element.21) | copy-start | bytes 1572868
  50.7 2.7 %copy-start.14 = (f32[2,8,256]{2,1,0:T(8,128)S(1)}, f32[2,8,256]{2,1,0:T(8,128)}, u32[]{:S(2)}) copy-start(f32[2,8,256]{2,1,0:T(8,128)} %constant.91) | copy-start | bytes 49156
  53.4 0.7 copy-start.13
  54.2 12.2 %copy-start.6 = (f32[256,256]{1,0:T(8,128)S(1)}, f32[256,256]{1,0:T(8,128)}, u32[]{:S(2)}) copy-start(f32[256,256]{1,0:T(8,128)} %copy-done.5) | copy-start | bytes 786436
  54.2 12.2 %copy-start.17 = (f32[256]{0:T(256)S(1)}, f32[256]{0:T(256)}, u32[]{:S(2)}) copy-start(f32[256]{0:T(256)} %param.15) | copy-start | bytes 3076
  66.4 1.0 %copy-start.8 = (bf16[256,1024]{1,0:T(8,128)(2,1)S(1)}, bf16[256,1024]{1,0:T(8,128)(2,1)}, u32[]{:S(2)}) copy-start(bf16[256,1024]{1,0:T(8,128)(2,1)} %param.17) | copy-start | bytes 1572868
  67.9 7.1 %collective-permute-start.10 = (f32[3,2,256]{2,1,0:T(2,128)S(1)}, f32[3,2,256]{2,1,0:T(2,128)S(1)}, u32[]{:S(2)}, u32[]{:S(2)}) collective-permute-start(f32[3,2,256]{2,1,0:T(2,128)S(1)} %slice.132), channel_id=1, source_target_pairs={{4,0},{8,4},{12,8},{16,12},{20,16},{24,20},{28,24},{5,1},{9,5},{13... | collective-permute-start | bytes 18440 | tf_op jit(solution)/shard_map/ppermute | solution.py:18
  69.4 8.3 %collective-permute-start.7 = (bf16[256,256]{1,0:T(8,128)(2,1)S(1)}, bf16[256,256]{1,0:T(8,128)(2,1)S(1)}, u32[]{:S(2)}, u32[]{:S(2)}) collective-permute-start(bf16[256,256]{1,0:T(8,128)(2,1)S(1)} %convolution_convert_fusion.2), channel_id=1, source_target_pairs={{0,1},{1,2},{2,3},{3,0},{4,5},{5,6},{6,7},{7,4},{8,9},{9,10},{10,1... | collective-permute-start | bytes 393224 | tf_op jit(solution)/shard_map/ppermute | solution.py:37
  69.7 12.9 %collective-permute-start.8 = (bf16[256,256]{1,0:T(8,128)(2,1)S(1)}, bf16[256,256]{1,0:T(8,128)(2,1)S(1)}, u32[]{:S(2)}, u32[]{:S(2)}) collective-permute-start(bf16[256,256]{1,0:T(8,128)(2,1)S(1)} %convolution_convert_fusion.1), channel_id=1, source_target_pairs={{0,2},{1,3},{2,0},{3,1},{4,6},{5,7},{6,4},{7,5},{8,10},{9,11},{10,... | collective-permute-start | bytes 393224 | tf_op jit(solution)/shard_map/ppermute | solution.py:37
  72.1 10.5 %collective-permute-start.9 = (bf16[256,256]{1,0:T(8,128)(2,1)S(1)}, bf16[256,256]{1,0:T(8,128)(2,1)S(1)}, u32[]{:S(2)}, u32[]{:S(2)}) collective-permute-start(bf16[256,256]{1,0:T(8,128)(2,1)S(1)} %convolution_convert_fusion), channel_id=1, source_target_pairs={{0,3},{1,0},{2,1},{3,2},{4,7},{5,4},{6,5},{7,6},{8,11},{9,8},{10,9... | collective-permute-start | bytes 393224 | tf_op jit(solution)/shard_map/ppermute | solution.py:37
  75.9 10.2 %collective-permute-start.11 = (bf16[256,256]{1,0:T(8,128)(2,1)S(1)}, bf16[256,256]{1,0:T(8,128)(2,1)S(1)}, u32[]{:S(2)}, u32[]{:S(2)}) collective-permute-start(bf16[256,256]{1,0:T(8,128)(2,1)S(1)} %fusion.30), channel_id=1, source_target_pairs={{0,1},{1,2},{2,3},{3,0},{4,5},{5,6},{6,7},{7,4},{8,9},{9,10},{10,1... | collective-permute-start | bytes 393224 | tf_op jit(solution)/shard_map/ppermute | solution.py:37
  76.0 17.9 %collective-permute-start.12 = (bf16[256,256]{1,0:T(8,128)(2,1)S(1)}, bf16[256,256]{1,0:T(8,128)(2,1)S(1)}, u32[]{:S(2)}, u32[]{:S(2)}) collective-permute-start(bf16[256,256]{1,0:T(8,128)(2,1)S(1)} %fusion.31), channel_id=1, source_target_pairs={{0,2},{1,3},{2,0},{3,1},{4,6},{5,7},{6,4},{7,5},{8,10},{9,11},{10,... | collective-permute-start | bytes 393224 | tf_op jit(solution)/shard_map/ppermute | solution.py:37
  77.7 16.2 %collective-permute-start.13 = (bf16[256,256]{1,0:T(8,128)(2,1)S(1)}, bf16[256,256]{1,0:T(8,128)(2,1)S(1)}, u32[]{:S(2)}, u32[]{:S(2)}) collective-permute-start(bf16[256,256]{1,0:T(8,128)(2,1)S(1)} %fusion.32), channel_id=1, source_target_pairs={{0,3},{1,0},{2,1},{3,2},{4,7},{5,4},{6,5},{7,6},{8,11},{9,8},{10,9... | collective-permute-start | bytes 393224 | tf_op jit(solution)/shard_map/ppermute | solution.py:37

commit v18 on v17

--- a/solution.py
+++ b/solution.py
@@ -68,8 +68,10 @@
         % (2 * length)
     )
     twiddle = (jnp.asarray(np.cos(phi), jnp.float32), jnp.asarray(np.sin(phi), jnp.float32))
-    psi = -phase(row[:, None] * row[None, :], row_count)
-    cos_b, sin_b = jnp.cos(psi), jnp.sin(psi)
+    base = (-2.0 * math.pi / row_count) * small_row
+    index = (row[:, None] * row[None, :]) % row_count
+    cos_b = jnp.take(jnp.asarray(np.cos(base), jnp.float32), index)
+    sin_b = jnp.take(jnp.asarray(np.sin(base), jnp.float32), index)
     stage_b = jnp.stack(
         [jnp.stack([cos_b, sin_b], axis=1), jnp.stack([-sin_b, cos_b], axis=1)]
     )

time: 96.3 us -> 907 us (9.42)
  local copies, waits for them, and re-layouts: 8.3 us -> 822 us
    gather x0 -> x4, local copies, waits for them, and re-layouts: none -> 812 us  [the longest x2 406 us: transform_tables(): sin_b = jnp.take(jnp.asarray(np.sin(base), jnp.float32), index)]
  transfers between devices with their start and end apart: 16 -> 16, of which waited for: 6 -> 6; matrix products, arithmetic and copies ran while one was open for 20% -> 92% of each run, Pallas kernels for 0% -> 0%
where the time goes in v18:
time: 907 us; the launch traced here: 906 us
  local copies, waits for them, and re-layouts  822 us (91%)
  starting transfers between devices  30.8 us (3%)
  matrix products  20.1 us (2%)
  waiting for transfers between devices  16.7 us (2%)
  blocking collectives  9.45 us (1%)
    gather x2, local copies, waits for them, and re-layouts, transform_tables(): sin_b = jnp.take(jnp.asarray(np.sin(base), jnp.float32), index)  406 us
    gather x2, local copies, waits for them, and re-layouts, transform_tables(): cos_b = jnp.take(jnp.asarray(np.cos(base), jnp.float32), index)  406 us
  transfers between devices with their start and end apart: 16, of which 6 were waited for; matrix products, arithmetic and copies ran while one was open for 92% of the time, Pallas kernels for 0%

profile of v18, /device:TPU:0, one launch (start us, length us, event | category | flops | bytes accessed | tf_op | source)
XLA Modules:
  0.0 905.6 jit_solution(13585472198427818526)
XLA Ops:
  0.7 3.1 collective-permute-start
  3.8 2.1 collective-permute-start.2
  5.9 0.9 collective-permute-start.1
  6.8 1.6 collective-permute-start.4
  8.4 2.2 collective-permute-start.6
  10.6 1.8 copy.66
  12.4 4.0 all-to-all-start.1
  16.7 1.3 slice_bitcast_fusion.5
  18.2 406.1 %gather_fusion.1 = f32[65536]{0:T(1024)S(1)} fusion(f32[256]{0:T(256)S(1)} %copy-done.2, s32[65536]{0:T(1024)S(1)} %broadcast_clamp_fusion), kind=kCustom, calls=%fused_computation.1.clone | custom fusion | bytes 786432 | tf_op jit(solution)/shard_map/jit(_take)/gather | solution.py:74
  424.3 406.1 %gather_fusion = f32[65536]{0:T(1024)S(1)} fusion(f32[256]{0:T(256)S(1)} %copy-done.1, s32[65536]{0:T(1024)S(1)} %broadcast_clamp_fusion), kind=kCustom, calls=%fused_computation.clone | custom fusion | bytes 786432 | tf_op jit(solution)/shard_map/jit(_take)/gather | solution.py:73
  830.6 0.9 fusion.93
  832.1 1.1 maximum_bitcast_fusion.2
  833.3 1.2 convolution_add_fusion.1
  834.5 1.2 fusion.44
  835.7 1.2 fusion.21
  837.0 2.1 collective-permute-start.3
  839.1 1.1 convolution_add_fusion.3
  840.3 1.1 fusion.85
  841.4 0.4 collective-permute-done.5
  842.9 0.9 copy.36
  843.7 4.2 all-to-all-start
  848.0 1.0 copy.70
  848.9 0.6 convolution_bitcast_fusion.2
  849.8 0.8 copy-done.3
  850.8 1.1 convolution_bitcast_fusion.1
  851.9 2.8 all-to-all-done
  854.7 1.7 convolution_bitcast_fusion
  856.9 0.8 copy-done.4
  857.9 2.7 fusion.10
  860.6 0.5 multiply_subtract_fusion.3
  861.3 2.7 fusion.13
  864.7 0.7 fusion.27
  865.4 9.5 %all_to_all.39 = bf16[2,32,8,256]{3,1,0,2:T(8,128)(2,1)S(1)} all-to-all(bf16[2,32,8,256]{3,1,0,2:T(8,128)(2,1)S(1)} %copy.46), channel_id=1, replica_groups=mesh['seq'=8,'panel'=4] {'seq'}, dimensions={2} | all-to-all | bytes 524288 | tf_op jit(solution)/shard_map/all_to_all | solution.py:102
  874.9 0.8 bitcast_convert_fusion
  875.7 1.2 copy.48
  877.2 0.8 copy-done.10
  878.5 1.3 collective-permute-start.10
  880.0 0.4 collective-permute-start.7
  880.5 2.4 collective-permute-start.8
  882.9 2.8 collective-permute-start.9
  886.8 0.6 collective-permute-start.12
  887.6 0.6 collective-permute-done.7
  888.3 2.7 collective-permute-start.13
  891.0 2.4 collective-permute-done.8
  893.4 0.9 add_convert_fusion
  894.3 2.4 collective-permute-done.11
  896.7 7.9 collective-permute-done.12
  904.6 1.0 fusion.62
  (92 shorter events, 6.3 us)
Async XLA Ops:
  0.6 830.9 %copy-start = (bf16[3,1024,256]{2,1,0:T(8,128)(2,1)S(1)}, bf16[3,1024,256]{2,1,0:T(8,128)(2,1)}, u32[]{:S(2)}) copy-start(bf16[3,1024,256]{2,1,0:T(8,128)(2,1)} %param.17) | copy-start | bytes 4718596
  0.6 17.5 %copy-start.2 = (f32[256]{0:T(256)S(1)}, f32[256]{0:T(256)}, u32[]{:S(2)}) copy-start(f32[256]{0:T(256)} %constant.103.clone2.1) | copy-start | bytes 3076
  0.7 832.5 %collective-permute-start = (bf16[256,256]{1,0:T(8,128)(2,1)}, bf16[256,256]{1,0:T(8,128)(2,1)}, u32[]{:S(2)}, u32[]{:S(2)}) collective-permute-start(bf16[256,256]{1,0:T(8,128)(2,1)} %param.15), channel_id=1, source_target_pairs={{0,1},{1,2},{2,3},{3,0},{4,5},{5,6},{6,7},{7,4},{8,9},{9,10},{10,1... | collective-permute-start | bytes 393224 | tf_op jit(solution)/shard_map/ppermute | solution.py:26
  3.8 830.7 %collective-permute-start.2 = (bf16[256,256]{1,0:T(8,128)(2,1)}, bf16[256,256]{1,0:T(8,128)(2,1)}, u32[]{:S(2)}, u32[]{:S(2)}) collective-permute-start(bf16[256,256]{1,0:T(8,128)(2,1)} %param.15), channel_id=1, source_target_pairs={{0,3},{1,0},{2,1},{3,2},{4,7},{5,4},{6,5},{7,6},{8,11},{9,8},{10,9... | collective-permute-start | bytes 393224 | tf_op jit(solution)/shard_map/ppermute | solution.py:26
  5.9 829.9 %collective-permute-start.1 = (bf16[256,256]{1,0:T(8,128)(2,1)}, bf16[256,256]{1,0:T(8,128)(2,1)}, u32[]{:S(2)}, u32[]{:S(2)}) collective-permute-start(bf16[256,256]{1,0:T(8,128)(2,1)} %param.15), channel_id=1, source_target_pairs={{0,2},{1,3},{2,0},{3,1},{4,6},{5,7},{6,4},{7,5},{8,10},{9,11},{10,... | collective-permute-start | bytes 393224 | tf_op jit(solution)/shard_map/ppermute | solution.py:26
  6.8 832.3 %collective-permute-start.4 = (bf16[256,256]{1,0:T(8,128)(2,1)}, bf16[256,256]{1,0:T(8,128)(2,1)}, u32[]{:S(2)}, u32[]{:S(2)}) collective-permute-start(bf16[256,256]{1,0:T(8,128)(2,1)} %param.16), channel_id=1, source_target_pairs={{0,1},{1,2},{2,3},{3,0},{4,5},{5,6},{6,7},{7,4},{8,9},{9,10},{10,1... | collective-permute-start | bytes 393224 | tf_op jit(solution)/shard_map/ppermute | solution.py:26
  8.4 831.9 %collective-permute-start.6 = (bf16[256,256]{1,0:T(8,128)(2,1)}, bf16[256,256]{1,0:T(8,128)(2,1)}, u32[]{:S(2)}, u32[]{:S(2)}) collective-permute-start(bf16[256,256]{1,0:T(8,128)(2,1)} %param.16), channel_id=1, source_target_pairs={{0,3},{1,0},{2,1},{3,2},{4,7},{5,4},{6,5},{7,6},{8,11},{9,8},{10,9... | collective-permute-start | bytes 393224 | tf_op jit(solution)/shard_map/ppermute | solution.py:26
  12.4 831.3 %all-to-all-start.1 = ((f32[1,256,256]{2,0,1:T(1,128)}), f32[1,256,256]{2,0,1:T(1,128)}, u32[]{:S(2)}, u32[]{:S(2)}) async-start(f32[1,256,256]{2,0,1:T(1,128)} %bitcast.37), calls=%async_computation.1 | async-start | bytes 524288 | tf_op jit(solution)/shard_map/all_to_all | solution.py:94
  18.2 406.1 %copy-start.1 = (f32[256]{0:T(256)S(1)}, f32[256]{0:T(256)}, u32[]{:S(2)}) copy-start(f32[256]{0:T(256)} %constant.102.clone2.1) | copy-start | bytes 3076
  424.3 406.3 %copy-start.9 = (bf16[256,1024]{1,0:T(8,128)(2,1)S(1)}, bf16[256,1024]{1,0:T(8,128)(2,1)}, u32[]{:S(2)}) copy-start(bf16[256,1024]{1,0:T(8,128)(2,1)} %param.21) | copy-start | bytes 1572868
  424.3 406.3 %copy-start.14 = (bf16[256,256]{1,0:T(8,128)(2,1)S(1)}, bf16[256,256]{1,0:T(8,128)(2,1)}, u32[]{:S(2)}) copy-start(bf16[256,256]{1,0:T(8,128)(2,1)} %param.16) | copy-start | bytes 393220
  424.3 407.2 %copy-start.13 = (bf16[256,256]{1,0:T(8,128)(2,1)S(1)}, bf16[256,256]{1,0:T(8,128)(2,1)}, u32[]{:S(2)}) copy-start(bf16[256,256]{1,0:T(8,128)(2,1)} %param.15) | copy-start | bytes 393220
  831.8 1.3 copy-start.15
  833.1 8.6 collective-permute-start.5
  834.5 4.6 copy-start.11
  836.9 5.2 copy-start.17
  836.9 5.2 copy-start.18
  837.0 5.2 copy-start.19
  837.0 5.1 collective-permute-start.3
  842.0 0.7 copy-start.7
  842.7 6.2 copy-start.23
  842.8 6.8 copy-start.12
  842.8 6.8 copy-start.16
  843.7 11.0 %all-to-all-start = ((bf16[2,256,256]{2,0,1:T(2,128)(2,1)}), bf16[2,256,256]{2,0,1:T(2,128)(2,1)}, u32[]{:S(2)}, u32[]{:S(2)}) async-start(bf16[2,256,256]{2,0,1:T(2,128)(2,1)} %copy.36), calls=%async_computation | async-start | bytes 524288 | tf_op jit(solution)/shard_map/all_to_all | solution.py:94
  849.5 1.0 copy-start.3
  849.6 1.2 copy-start.5
  850.8 4.0 copy-start.22
  856.7 1.0 copy-start.4
  856.7 1.2 copy-start.6
  861.3 2.7 copy-start.21
  864.0 0.7 copy-start.20
  864.7 12.3 %copy-start.8 = (f32[256,256]{1,0:T(8,128)S(1)}, f32[256,256]{1,0:T(8,128)}, u32[]{:S(2)}) copy-start(f32[256,256]{1,0:T(8,128)} %copy-done.7) | copy-start | bytes 786436
  864.7 12.3 %copy-start.24 = (f32[256]{0:T(256)S(1)}, f32[256]{0:T(256)}, u32[]{:S(2)}) copy-start(f32[256]{0:T(256)} %param.19) | copy-start | bytes 3076
  877.0 1.0 copy-start.10
  878.5 7.2 collective-permute-start.10
  880.0 8.3 collective-permute-start.7
  880.5 12.9 %collective-permute-start.8 = (bf16[256,256]{1,0:T(8,128)(2,1)S(1)}, bf16[256,256]{1,0:T(8,128)(2,1)S(1)}, u32[]{:S(2)}, u32[]{:S(2)}) collective-permute-start(bf16[256,256]{1,0:T(8,128)(2,1)S(1)} %convolution_convert_fusion.1), channel_id=1, source_target_pairs={{0,2},{1,3},{2,0},{3,1},{4,6},{5,7},{6,4},{7,5},{8,10},{9,11},{10,... | collective-permute-start | bytes 393224 | tf_op jit(solution)/shard_map/ppermute | solution.py:37
  882.9 10.5 %collective-permute-start.9 = (bf16[256,256]{1,0:T(8,128)(2,1)S(1)}, bf16[256,256]{1,0:T(8,128)(2,1)S(1)}, u32[]{:S(2)}, u32[]{:S(2)}) collective-permute-start(bf16[256,256]{1,0:T(8,128)(2,1)S(1)} %convolution_convert_fusion), channel_id=1, source_target_pairs={{0,3},{1,0},{2,1},{3,2},{4,7},{5,4},{6,5},{7,6},{8,11},{9,8},{10,9... | collective-permute-start | bytes 393224 | tf_op jit(solution)/shard_map/ppermute | solution.py:37
  886.7 10.0 %collective-permute-start.11 = (bf16[256,256]{1,0:T(8,128)(2,1)S(1)}, bf16[256,256]{1,0:T(8,128)(2,1)S(1)}, u32[]{:S(2)}, u32[]{:S(2)}) collective-permute-start(bf16[256,256]{1,0:T(8,128)(2,1)S(1)} %fusion.30), channel_id=1, source_target_pairs={{0,1},{1,2},{2,3},{3,0},{4,5},{5,6},{6,7},{7,4},{8,9},{9,10},{10,1... | collective-permute-start | bytes 393224 | tf_op jit(solution)/shard_map/ppermute | solution.py:37
  886.8 17.9 %collective-permute-start.12 = (bf16[256,256]{1,0:T(8,128)(2,1)S(1)}, bf16[256,256]{1,0:T(8,128)(2,1)S(1)}, u32[]{:S(2)}, u32[]{:S(2)}) collective-permute-start(bf16[256,256]{1,0:T(8,128)(2,1)S(1)} %fusion.31), channel_id=1, source_target_pairs={{0,2},{1,3},{2,0},{3,1},{4,6},{5,7},{6,4},{7,5},{8,10},{9,11},{10,... | collective-permute-start | bytes 393224 | tf_op jit(solution)/shard_map/ppermute | solution.py:37
  888.3 16.3 %collective-permute-start.13 = (bf16[256,256]{1,0:T(8,128)(2,1)S(1)}, bf16[256,256]{1,0:T(8,128)(2,1)S(1)}, u32[]{:S(2)}, u32[]{:S(2)}) collective-permute-start(bf16[256,256]{1,0:T(8,128)(2,1)S(1)} %fusion.32), channel_id=1, source_target_pairs={{0,3},{1,0},{2,1},{3,2},{4,7},{5,4},{6,5},{7,6},{8,11},{9,8},{10,9... | collective-permute-start | bytes 393224 | tf_op jit(solution)/shard_map/ppermute | solution.py:37
